TPU v7x, 32 devices: a whole 2x2x4 slice. The times are simulated.
32 devices in a mesh: tm: 8 (over z, y), cal: 4 (over x, core).
Axes of the slice: x: 2, y: 2, z: 4, core: 2. Of those that a mesh axis runs over, the one named last changes fastest.
Arguments:
- src_design: float32 [5, 4096, 128], P(None, ('tm', 'cal')), may hold values from -6 to 6
- att_design: float32 [3, 4096, 128], P(None, ('tm', 'cal')), may hold values from -6 to 6
- obs_phase: float32 [4096, 128], P(('tm', 'cal')), may hold values from 0 to 1
- cal_design: float32 [4096, 128], P(('tm', 'cal')), may hold values from -6 to 6
- obs_weight: float32 [4096, 128], P(('tm', 'cal')), may hold values from 0.1 to 12
- knot_index: int32 [4096, 128], P(('tm', 'cal')), may hold values from 0 to 4092, as said below
- cal_block: int32 [4096, 128], P(('tm', 'cal')), may hold values from 0 to 7
- cal_column: int32 [4096, 128], P(('tm', 'cal')), may hold values from 0 to 4095
- obs_count: int32 [4096], P(('tm', 'cal')), may hold values from 32 to 128
- src_res: float32 [5, 4096], P(None, ('tm', 'cal')), may hold values from -6 to 6
- att_res: float32 [3, 4096], P(None, ('tm', 'cal')), may hold values from -6 to 6
- cal_res: float32 [8, 4096], P('cal'), may hold values from -6 to 6
- src_dir: float32 [5, 4096], P(None, ('tm', 'cal')), may hold values from -6 to 6
- att_dir: float32 [3, 4096], P(None, ('tm', 'cal')), may hold values from -6 to 6
- cal_dir: float32 [8, 4096], P('cal'), may hold values from -6 to 6
Outputs:
- new_src_res: float32 [5, 4096], P(None, ('tm', 'cal'))
- new_att_res: float32 [3, 4096], P(None, ('tm', 'cal'))
- new_cal_res: float32 [8, 4096], P('cal')
- new_src_dir: float32 [5, 4096], P(None, ('tm', 'cal'))
- new_att_dir: float32 [3, 4096], P(None, ('tm', 'cal'))
- new_cal_dir: float32 [8, 4096], P('cal')
Inputs may be any that keep to these rules, and one draw needn't show every extreme that they name: The observations of source row s have knot intervals from (s // 128) * 128 to (s // 128) * 128 + 127, and knot_index + 3 < 4096.
All inputs are finite; a program needn't handle non-finite values.
Results may differ from a plain program's by a relative error of at most 0.00015.
Values sent between devices are 32-bit elements; how exact they have to be, the bound alone decides.
No kernel may reach another device: no remote copies, remote signals or barrier semaphores. Data moves between devices by JAX's collectives and lax.ppermute only.
A program may use at most 64 MiB of HBM per device.

v0:
```python
import math

import jax
import jax.numpy as jnp
from jax import lax
from jax.sharding import PartitionSpec as P


def passed_along(block, axis, distance):
    devices = range(lax.axis_size(axis))
    route = [(i - distance, i) for i in devices if i - distance in devices]
    return lax.ppermute(block, axis, route)


def spline(phase):
    rest = 1.0 - phase
    cube = phase * phase * phase
    square = phase * phase
    first = rest * rest * rest / 6.0
    second = (3.0 * cube - 6.0 * square + 4.0) / 6.0
    third = (-3.0 * cube + 3.0 * square + 3.0 * phase + 1.0) / 6.0
    fourth = cube / 6.0
    return (first, second, third, fourth)


def local(
    src_design,
    att_design,
    obs_phase,
    cal_design,
    obs_weight,
    knot_index,
    cal_block,
    cal_column,
    obs_count,
    src_res,
    att_res,
    cal_res,
    src_dir,
    att_dir,
    cal_dir,
):
    knot_count = att_dir.shape[1]
    extended = knot_count + 3
    blocks, col_width = cal_dir.shape
    all_blocks = blocks * lax.axis_size("cal")
    src_rows, slots = obs_phase.shape
    group = math.gcd(src_rows, 16)
    group_count = src_rows // group
    first_row = (lax.axis_index("tm") == 0).astype(jnp.float32)
    cal_values = lax.all_gather(cal_dir, "cal", axis=0, tiled=True)
    edge_knots = passed_along(att_dir[:, :3], ("tm", "cal"), -1)
    att_ext = jnp.concatenate([att_dir, edge_knots], axis=1)
    live_mask = (lax.broadcasted_iota(jnp.int32, obs_phase.shape, 1) < obs_count[:, None]).astype(
        jnp.float32
    )
    local_knot = knot_index - lax.axis_index(("tm", "cal")) * knot_count
    knot_iota = lax.broadcasted_iota(jnp.int32, (1, 1, extended), 2)

    def block_inputs(which):
        start = which * group
        knots = lax.dynamic_slice_in_dim(local_knot, start, group, 0)
        design = lax.dynamic_slice_in_dim(att_design, start, group, 1)
        phases = lax.dynamic_slice_in_dim(obs_phase, start, group, 0)
        return (start, knots, design, spline(phases))

    def forward(which):
        start, knots, design, weights = block_inputs(which)
        total = jnp.zeros((group, slots), jnp.float32)
        for offset in range(4):
            onehot = ((knots + offset)[:, :, None] == knot_iota).astype(jnp.float32)
            picked = jnp.einsum("bok,ck->cbo", onehot, att_ext, precision=lax.Precision.HIGHEST)
            total = total + weights[offset] * jnp.sum(design * picked, axis=0)
        return total

    y_att = lax.map(forward, jnp.arange(group_count, dtype=jnp.int32)).reshape(src_rows, slots)
    y_src = jnp.sum(src_design * src_dir[:, :, None], axis=0)
    flat_index = cal_block * col_width + cal_column
    y_cal = cal_design * jnp.take(cal_values.reshape(-1), flat_index)
    response = live_mask * (y_src + y_att + y_cal)
    weighted = obs_weight * response
    curv_local = jnp.sum(weighted * response)
    norm_local = (
        jnp.sum(src_res * src_res)
        + jnp.sum(att_res * att_res)
        + first_row * jnp.sum(cal_res * cal_res)
    )
    cal_term = jax.ops.segment_sum(
        (cal_design * weighted).reshape(-1),
        flat_index.reshape(-1),
        num_segments=all_blocks * col_width,
    ).reshape(all_blocks, col_width)
    q_src = jnp.sum(src_design * weighted[None], axis=2)

    def backward(which, grad_sum):
        start, knots, design, weights = block_inputs(which)
        scaled = design * lax.dynamic_slice_in_dim(weighted, start, group, 0)[None]
        for offset in range(4):
            onehot = ((knots + offset)[:, :, None] == knot_iota).astype(jnp.float32)
            grad_sum = grad_sum + jnp.einsum(
                "cbo,bok->ck",
                weights[offset][None] * scaled,
                onehot,
                precision=lax.Precision.HIGHEST,
            )
        return grad_sum

    grad_ext = lax.fori_loop(0, group_count, backward, jnp.zeros((3, extended), jnp.float32))
    incoming = passed_along(grad_ext[:, knot_count:], ("tm", "cal"), 1)
    q_att = jnp.concatenate([grad_ext[:, :3] + incoming, grad_ext[:, 3:knot_count]], axis=1)
    norm_now, curvature = lax.psum((norm_local, curv_local), ("tm", "cal"))
    shared = lax.psum_scatter(cal_term, "cal", scatter_dimension=0, tiled=True)
    q_cal = lax.psum(shared, "tm")
    step_len = norm_now / curvature
    new_src_res = src_res - step_len * q_src
    new_att_res = att_res - step_len * q_att
    new_cal_res = cal_res - step_len * q_cal
    next_local = (
        jnp.sum(new_src_res * new_src_res)
        + jnp.sum(new_att_res * new_att_res)
        + first_row * jnp.sum(new_cal_res * new_cal_res)
    )
    norm_next = lax.psum(next_local, ("tm", "cal"))
    ratio = norm_next / norm_now
    return (
        new_src_res,
        new_att_res,
        new_cal_res,
        new_src_res + ratio * src_dir,
        new_att_res + ratio * att_dir,
        new_cal_res + ratio * cal_dir,
    )


def solution(mesh):
    return jax.shard_map(
        local,
        mesh=mesh,
        in_specs=(
            P(None, ("tm", "cal"), None),
            P(None, ("tm", "cal"), None),
            P(("tm", "cal"), None),
            P(("tm", "cal"), None),
            P(("tm", "cal"), None),
            P(("tm", "cal"), None),
            P(("tm", "cal"), None),
            P(("tm", "cal"), None),
            P(("tm", "cal")),
            P(None, ("tm", "cal")),
            P(None, ("tm", "cal")),
            P("cal", None),
            P(None, ("tm", "cal")),
            P(None, ("tm", "cal")),
            P("cal", None),
        ),
        out_specs=(
            P(None, ("tm", "cal")),
            P(None, ("tm", "cal")),
            P("cal", None),
            P(None, ("tm", "cal")),
            P(None, ("tm", "cal")),
            P("cal", None),
        ),
        check_vma=False,
    )
```

profile of v0, /device:TPU:0, one launch (start us, length us, event | category | flops | bytes accessed | tf_op | source)
XLA Modules:
  0.0 394.6 jit_solution(5462069088811584754)
XLA Ops:
  7.2 1.3 collective-permute-start
  8.5 0.9 bitcast_clamp_fusion
  9.5 0.9 fusion.84
  10.4 7.4 %all-gather = f32[4,2,4096]{2,1,0:T(2,128)S(1)} all-gather(f32[1,2,4096]{2,1,0:T(2,128)S(1)} %bitcast.109), channel_id=1, replica_groups=mesh['tm'=8,'cal'=4] {'cal'}, dimensions={0}, use_global_device_ids=true | all-gather | bytes 163840 | tf_op jit(solution)/shard_map/all_gather | solution.py:51
  20.4 90.5 %gather_fusion = f32[16384]{0:T(1024)S(1)} fusion(f32[32768]{0:T(1024)S(1)} %bitcast.107, s32[16384]{0:T(1024)S(1)} %bitcast_clamp_fusion), kind=kCustom, calls=%fused_computation | custom fusion | bytes 196608 | tf_op jit(solution)/shard_map/jit(_take)/gather | solution.py:79
  111.1 0.6 copy-done.9
  115.1 31.6 %while.27 = (s32[]{:T(128)}, f32[8,16,128]{2,1,0:T(8,128)S(1)}, s32[8]{0:T(128)S(1)}, f32[128,128]{1,0:T(8,128)}, f32[3,128,128]{2,0,1:T(4,128)S(1)}, /*index=5*...) while((s32[]{:T(128)}, f32[8,16,128]{2,1,0:T(8,128)S(1)}, ...), condition=%wide.region_10.11_spmd.clone.clone, body=%wide.region_5.10_spmd.clone.clone.sunk | while | flops 39806980 | bytes 268635 | solution.py:76
  118.3 0.7 fusion.113
  122.3 0.7 fusion.113
  126.2 0.7 fusion.113
  130.2 0.7 fusion.113
  134.1 0.7 fusion.113
  138.1 0.7 fusion.113
  142.0 0.7 fusion.113
  146.0 0.7 fusion.113
  147.0 26.0 %while.28 = (s32[]{:T(128)}, f32[3,131]{1,0:T(4,128)S(1)}, f32[128,128]{1,0:T(8,128)}, f32[3,128,128]{2,0,1:T(4,128)S(1)}, f32[128,128]{1,0:T(8,128)S(1)}, /*ind...) while((s32[]{:T(128)}, f32[3,131]{1,0:T(4,128)S(1)}, ...), condition=%wide.region_15.16_spmd.clone.clone, body=%wide.region_14.15_spmd.clone.clone.sunk | while | flops 39802800 | bytes 358733 | solution.py:108
  147.1 0.7 fusion.118
  150.3 0.7 fusion.118
  153.6 0.7 fusion.118
  156.8 0.7 fusion.118
  160.1 0.7 fusion.118
  163.3 0.7 fusion.118
  166.6 0.7 fusion.118
  169.8 0.7 fusion.118
  173.8 2.2 collective-permute-start.1
  176.0 85.9 %scatter_custom_fusion = f32[32768]{0:T(1024)S(1)} fusion(s32[16384]{0:T(1024)S(1)} %fusion.84, f32[16384]{0:T(1024)S(1)} %get-tuple-element.350, f32[]{:T(128)} %constant.148.clone.1), kind=kCustom, calls=%fused_computation.114 | custom fusion | flops 16384 | bytes 131076 | tf_op jit(solution)/shard_map/scatter-add | solution.py:88
  261.9 0.7 reshape.50
  262.6 41.9 %all-reduce.1 = (f32[]{:T(128)}, f32[]{:T(128)}) all-reduce(f32[]{:T(128)S(6)} %add.198, f32[]{:T(128)} %multiply_reduce_fusion.2), channel_id=1, replica_groups=mesh['tm'=8,'cal'=4] {'tm','cal'}, use_global_device_ids=true, to_apply=%region_3.0 | all-reduce | flops 2 | bytes 16 | tf_op jit(solution)/shard_map/psum | solution.py:111
  306.4 0.7 multiply_reduce_fusion.7
  308.4 0.9 constant_dynamic-slice_fusion.3
  309.3 37.0 %psum.30 = f32[2,4096]{1,0:T(2,128)S(1)} all-reduce(f32[2,4096]{1,0:T(2,128)S(1)} %constant_dynamic-slice_fusion.3), channel_id=1, replica_groups=mesh['tm'=8,'cal'=4] {'tm'}, use_global_device_ids=true, to_apply=%region_18.19 | all-reduce | flops 8192 | bytes 65536 | tf_op jit(solution)/shard_map/psum | solution.py:113
  347.7 36.9 %psum.31 = f32[]{:T(128)} all-reduce(f32[]{:T(128)S(6)} %add.207), channel_id=1, replica_groups=mesh['tm'=8,'cal'=4] {'tm','cal'}, use_global_device_ids=true, to_apply=%region_22.23 | all-reduce | flops 1 | bytes 8 | tf_op jit(solution)/shard_map/psum | solution.py:123
  (167 shorter events, 47.6 us)
Async XLA Ops:
  7.2 3.2 copy-start.4
  7.2 301.2 %all-reduce.4.cloned.1.call-start = ((), (), s32[]{:S(2)}) async-start(), calls=%async_computation | async-start | bytes 262144
  7.2 107.8 %collective-permute-start = (f32[3,3]{1,0:T(4,128)}, f32[3,3]{1,0:T(4,128)S(1)}, u32[]{:S(2)}, u32[]{:S(2)}) collective-permute-start(f32[3,3]{1,0:T(4,128)} %bitcast.110), channel_id=1, source_target_pairs={{1,0},{2,1},{3,2},{4,3},{5,4},{6,5},{7,6},{8,7},{9,8},{10,9},{11,1... | collective-permute-start | bytes 116 | tf_op jit(solution)/shard_map/ppermute | solution.py:12
  9.4 8.4 %copy-start.3 = (f32[3,128,128]{2,1,0:T(8,128)S(1)}, f32[3,128,128]{2,1,0:T(8,128)}, u32[]{:S(2)}) copy-start(f32[3,128,128]{2,1,0:T(8,128)} %param.20) | copy-start | bytes 589828
  17.8 0.7 copy-start.12
  17.8 1.3 copy-start.13
  17.8 1.9 copy-start.6
  20.4 90.5 %copy-start = (f32[5,128,128]{2,1,0:T(8,128)S(1)}, f32[5,128,128]{2,1,0:T(8,128)}, u32[]{:S(2)}) copy-start(f32[5,128,128]{2,1,0:T(8,128)} %param.19) | copy-start | bytes 983044
  20.4 90.5 %copy-start.10 = (f32[5,128]{1,0:T(8,128)S(1)}, f32[5,128]{1,0:T(8,128)}, u32[]{:S(2)}) copy-start(f32[5,128]{1,0:T(8,128)} %param.31) | copy-start | bytes 7684
  110.9 0.8 copy-start.9
  110.9 2.8 copy-start.17
  110.9 4.0 %copy-start.14 = (f32[3,128]{1,0:T(4,128)S(1)}, f32[3,128]{1,0:T(4,128)}, u32[]{:S(2)}) copy-start(f32[3,128]{1,0:T(4,128)} %param.32) | copy-start | bytes 4612
  115.0 31.7 %copy-start.1 = (s32[128,128]{1,0:T(8,128)S(1)}, s32[128,128]{1,0:T(8,128)}, u32[]{:S(2)}) copy-start(s32[128,128]{1,0:T(8,128)} %param.26) | copy-start | bytes 196612
  115.0 31.7 %copy-start.2 = (s32[128,128]{1,0:T(8,128)S(1)}, s32[128,128]{1,0:T(8,128)}, u32[]{:S(2)}) copy-start(s32[128,128]{1,0:T(8,128)} %param.25) | copy-start | bytes 196612
  115.0 31.7 %copy-start.7 = (f32[128,128]{1,0:T(8,128)S(1)}, f32[128,128]{1,0:T(8,128)}, u32[]{:S(2)}) copy-start(f32[128,128]{1,0:T(8,128)} %param.22) | copy-start | bytes 196612
  115.1 31.7 %copy-start.8 = (f32[128,128]{1,0:T(8,128)S(1)}, f32[128,128]{1,0:T(8,128)}, u32[]{:S(2)}) copy-start(f32[128,128]{1,0:T(8,128)} %param.23) | copy-start | bytes 196612
  115.1 31.7 %copy-start.16 = (s32[128]{0:T(128)S(1)}, s32[128]{0:T(128)}, u32[]{:S(2)}) copy-start(s32[128]{0:T(128)} %param.27) | copy-start | bytes 1540
  173.8 132.6 %collective-permute-start.1 = (f32[3,3]{1,0:T(4,128)S(1)}, f32[3,3]{1,0:T(4,128)S(1)}, u32[]{:S(2)}, u32[]{:S(2)}) collective-permute-start(f32[3,3]{1,0:T(4,128)S(1)} %slice.14), channel_id=1, source_target_pairs={{0,1},{1,2},{2,3},{3,4},{4,5},{5,6},{6,7},{7,8},{8,9},{9,10},{10,1... | collective-permute-start | bytes 116 | tf_op jit(solution)/shard_map/ppermute | solution.py:12
  306.4 81.3 %copy-start.11 = (f32[5,128]{1,0:T(8,128)}, f32[5,128]{1,0:T(8,128)S(1)}, u32[]{:S(2)}) copy-start(f32[5,128]{1,0:T(8,128)S(1)} %get-tuple-element.349) | copy-start | bytes 7684
  307.1 80.7 %copy-start.15 = (f32[3,128]{1,0:T(4,128)}, f32[3,128]{1,0:T(4,128)S(1)}, u32[]{:S(2)}) copy-start(f32[3,128]{1,0:T(4,128)S(1)} %get-tuple-element.347) | copy-start | bytes 4612
  347.0 40.7 %copy-start.5 = (f32[2,4096]{1,0:T(2,128)}, f32[2,4096]{1,0:T(2,128)S(1)}, u32[]{:S(2)}) copy-start(f32[2,4096]{1,0:T(2,128)S(1)} %get-tuple-element.345) | copy-start | bytes 98308
Sparse Core Ops, SparseCore 0:
  262.7 34.3 all-reduce.3
where the time goes:
time: 398 us; the launch traced here: 395 us
  blocking collectives  123 us (31%)
  other arithmetic  106 us (27%)
  local copies, waits for them, and re-layouts  98.9 us (25%)
  matrix products  35.3 us (9%)
  between operations  21.6 us (5%)
  loops' own time  6.01 us (2%)
    gather x1, local copies, waits for them, and re-layouts, local(): y_cal = cal_design * jnp.take(cal_values.reshape(-1), flat_index)  90.5 us
    scatter-add x1, other arithmetic, local(): jax.ops.segment_sum((cal_design * weighted).reshape(-1), flat_index.resha...  85.9 us
    psum x1, blocking collectives, local(): norm_now, curvature = lax.psum((norm_local, curv_local), ('tm', 'cal'))  41.9 us
    psum x1, blocking collectives, local(): q_cal = lax.psum(shared, 'tm')  37 us
    psum x1, blocking collectives, local(): norm_next = lax.psum(next_local, ('tm', 'cal'))  36.9 us
    dot_general x32, matrix products, backward(): jnp.einsum('cbo,bok->ck', weights[offset][None] * scaled, onehot, precisi...  19.8 us
    dot_general x32, matrix products, forward(): jnp.einsum('bok,ck->cbo', onehot, att_ext, precision=lax.Precision.HIGHEST)  15.4 us
  transfers between devices with their start and end apart: 3, of which 0 were waited for; matrix products, arithmetic and copies ran while one was open for 46% of the time, Pallas kernels for 0%

commit v1 on v0

v1 whole, which is shorter than its diff:
```python
import jax
import jax.numpy as jnp
from jax import lax
from jax.sharding import PartitionSpec as P


EXACT = lax.Precision.HIGHEST


def passed_along(block, axis, distance):
    devices = range(lax.axis_size(axis))
    route = [(i - distance, i) for i in devices if i - distance in devices]
    return lax.ppermute(block, axis, route)


def spline(phase):
    rest = 1.0 - phase
    cube = phase * phase * phase
    square = phase * phase
    first = rest * rest * rest / 6.0
    second = (3.0 * cube - 6.0 * square + 4.0) / 6.0
    third = (-3.0 * cube + 3.0 * square + 3.0 * phase + 1.0) / 6.0
    fourth = cube / 6.0
    return (first, second, third, fourth)


def local(
    src_design,
    att_design,
    obs_phase,
    cal_design,
    obs_weight,
    knot_index,
    cal_block,
    cal_column,
    obs_count,
    src_res,
    att_res,
    cal_res,
    src_dir,
    att_dir,
    cal_dir,
):
    knot_count = att_dir.shape[1]
    blocks, col_width = cal_dir.shape
    all_blocks = blocks * lax.axis_size("cal")
    cal_size = all_blocks * col_width
    lane = 128
    rows = cal_size // lane
    src_rows, slots = obs_phase.shape
    first_row = (lax.axis_index("tm") == 0).astype(jnp.float32)

    cal_values = lax.all_gather(cal_dir, "cal", axis=0, tiled=True)
    edge_knots = passed_along(att_dir[:, :3], ("tm", "cal"), -1)
    att_ext = jnp.concatenate([att_dir, edge_knots], axis=1)

    live_mask = (lax.broadcasted_iota(jnp.int32, obs_phase.shape, 1) < obs_count[:, None]).astype(
        jnp.float32
    )
    basis = spline(obs_phase)
    local_knot = knot_index - lax.axis_index(("tm", "cal")) * knot_count

    knot_iota = lax.broadcasted_iota(jnp.int32, (knot_count, 1, 1), 0)
    knot_hot = (local_knot[None] == knot_iota).astype(jnp.float32)

    table = jnp.stack([att_ext[:, m : m + knot_count].T for m in range(4)], axis=1)
    table = table.reshape(knot_count, 12)
    picked = jnp.einsum("jq,jso->qso", table, knot_hot, precision=EXACT).reshape(4, 3, src_rows, slots)
    y_att = jnp.zeros_like(obs_phase)
    for m in range(4):
        y_att = y_att + basis[m] * jnp.sum(att_design * picked[m], axis=0)

    flat_index = cal_block * col_width + cal_column
    high = flat_index // lane
    low = flat_index % lane
    high_hot = (high[None] == lax.broadcasted_iota(jnp.int32, (rows, 1, 1), 0)).astype(jnp.float32)
    low_hot = (low[None] == lax.broadcasted_iota(jnp.int32, (lane, 1, 1), 0)).astype(jnp.float32)
    cal_table = cal_values.reshape(rows, lane)
    row_vals = jnp.einsum("hl,hso->lso", cal_table, high_hot, precision=EXACT)
    y_cal = cal_design * jnp.sum(row_vals * low_hot, axis=0)

    y_src = jnp.sum(src_design * src_dir[:, :, None], axis=0)
    response = live_mask * (y_src + y_att + y_cal)
    weighted = obs_weight * response
    curv_local = jnp.sum(weighted * response)
    norm_local = (
        jnp.sum(src_res * src_res)
        + jnp.sum(att_res * att_res)
        + first_row * jnp.sum(cal_res * cal_res)
    )
    q_src = jnp.sum(src_design * weighted[None], axis=2)

    scaled = att_design * weighted[None]
    spread = jnp.stack([basis[m][None] * scaled for m in range(4)], axis=0).reshape(12, src_rows, slots)
    gathered = jnp.einsum("qso,jso->jq", spread, knot_hot, precision=EXACT).reshape(knot_count, 4, 3)
    grad_ext = jnp.zeros((3, knot_count + 3), jnp.float32)
    for m in range(4):
        grad_ext = grad_ext + jnp.pad(gathered[:, m, :].T, ((0, 0), (m, 3 - m)))
    incoming = passed_along(grad_ext[:, knot_count:], ("tm", "cal"), 1)
    q_att = jnp.concatenate([grad_ext[:, :3] + incoming, grad_ext[:, 3:knot_count]], axis=1)

    cal_weighted = (cal_design * weighted)[None] * low_hot
    cal_term = jnp.einsum("hso,lso->hl", high_hot, cal_weighted, precision=EXACT)
    scalars = jnp.zeros((1, lane), jnp.float32).at[0, 0].set(norm_local).at[0, 1].set(curv_local)
    packed = jnp.concatenate([cal_term, scalars], axis=0)
    summed = lax.psum(packed, ("tm", "cal"))
    norm_now = summed[rows, 0]
    curvature = summed[rows, 1]
    own = lax.axis_index("cal") * (blocks * col_width // lane)
    q_cal = lax.dynamic_slice_in_dim(summed, own, blocks * col_width // lane, 0).reshape(blocks, col_width)

    step_len = norm_now / curvature
    new_src_res = src_res - step_len * q_src
    new_att_res = att_res - step_len * q_att
    new_cal_res = cal_res - step_len * q_cal
    next_local = (
        jnp.sum(new_src_res * new_src_res)
        + jnp.sum(new_att_res * new_att_res)
        + first_row * jnp.sum(new_cal_res * new_cal_res)
    )
    norm_next = lax.psum(jnp.zeros((1, lane), jnp.float32).at[0, 0].set(next_local), ("tm", "cal"))[0, 0]
    ratio = norm_next / norm_now
    return (
        new_src_res,
        new_att_res,
        new_cal_res,
        new_src_res + ratio * src_dir,
        new_att_res + ratio * att_dir,
        new_cal_res + ratio * cal_dir,
    )


def solution(mesh):
    return jax.shard_map(
        local,
        mesh=mesh,
        in_specs=(
            P(None, ("tm", "cal"), None),
            P(None, ("tm", "cal"), None),
            P(("tm", "cal"), None),
            P(("tm", "cal"), None),
            P(("tm", "cal"), None),
            P(("tm", "cal"), None),
            P(("tm", "cal"), None),
            P(("tm", "cal"), None),
            P(("tm", "cal")),
            P(None, ("tm", "cal")),
            P(None, ("tm", "cal")),
            P("cal", None),
            P(None, ("tm", "cal")),
            P(None, ("tm", "cal")),
            P("cal", None),
        ),
        out_specs=(
            P(None, ("tm", "cal")),
            P(None, ("tm", "cal")),
            P("cal", None),
            P(None, ("tm", "cal")),
            P(None, ("tm", "cal")),
            P("cal", None),
        ),
        check_vma=False,
    )
```

time: 398 us -> 324 us (0.81)
  waiting for transfers between devices: 0.04 us -> 123 us
  other arithmetic: 106 us -> 25.7 us
  blocking collectives: 123 us -> 50.1 us
  local copies, waits for them, and re-layouts: 98.9 us -> 73.3 us
  matrix products: 35.3 us -> 25.8 us
  loops' own time: 6.01 us -> 0 us
    psum x0 -> x1, waiting for transfers between devices: none -> 123 us  [local(): summed = lax.psum(packed, ('tm', 'cal'))]
    gather x1 -> x0, local copies, waits for them, and re-layouts: 90.5 us -> none  [local(): y_cal = cal_design * jnp.take(cal_values.reshape(-1), flat_index)]
    scatter-add x1 -> x0, other arithmetic: 85.9 us -> none  [local(): jax.ops.segment_sum((cal_design * weighted).reshape(-1), flat_index.resha...]
    psum x3 -> x1, blocking collectives: 116 us -> 42.5 us  [local(): lax.psum(jnp.zeros((1, lane), jnp.float32).at[0, 0].set(next_local), ('tm...]
    eq x0 -> x2, local copies, waits for them, and re-layouts: none -> 59 us  [the longest x1 38.5 us: local(): knot_hot = (local_knot[None] == knot_iota).astype(jnp.float32)]
    dot_general x64 -> x4, matrix products: 35.3 us -> 25.8 us  [the longest x1 11.2 us: local(): jnp.einsum('hso,lso->hl', high_hot, cal_weighted, precision=EXACT)]
    mul x0 -> x2, local copies, waits for them, and re-layouts: none -> 9.34 us  [the longest x1 9.32 us: local(): cal_weighted = (cal_design * weighted)[None] * low_hot]
    another operation x2 -> x0, loops' own time: 6.01 us -> none  [the longest x1 5.63 us: local(): lax.map(forward, jnp.arange(group_count, dtype=jnp.int32))]
  transfers between devices with their start and end apart: 3 -> 3, of which waited for: 0 -> 1; matrix products, arithmetic and copies ran while one was open for 46% -> 34% of each run, Pallas kernels for 0% -> 0%
where the time goes in v1:
time: 324 us
  waiting for transfers between devices  123 us (38%)
  local copies, waits for them, and re-layouts  73.3 us (23%)
  blocking collectives  50.1 us (15%)
  matrix products  25.8 us (8%)
  other arithmetic  25.7 us (8%)
  between operations  21.7 us (7%)
  starting transfers between devices  3.56 us (1%)
    psum x1, waiting for transfers between devices, local(): summed = lax.psum(packed, ('tm', 'cal'))  123 us
    psum x1, blocking collectives, local(): lax.psum(jnp.zeros((1, lane), jnp.float32).at[0, 0].set(next_local), ('tm...  42.5 us
    eq x1, local copies, waits for them, and re-layouts, local(): knot_hot = (local_knot[None] == knot_iota).astype(jnp.float32)  38.5 us
    eq x1, local copies, waits for them, and re-layouts, local(): high[None] == lax.broadcasted_iota(jnp.int32, (rows, 1, 1), 0)  20.5 us
    dot_general x1, matrix products, local(): jnp.einsum('hso,lso->hl', high_hot, cal_weighted, precision=EXACT)  11.2 us
    mul x1, local copies, waits for them, and re-layouts, local(): cal_weighted = (cal_design * weighted)[None] * low_hot  9.32 us
    dot_general x1, matrix products, local(): row_vals = jnp.einsum('hl,hso->lso', cal_table, high_hot, precision=EXACT)  8.23 us
    all_gather x1, blocking collectives, local(): cal_values = lax.all_gather(cal_dir, 'cal', axis=0, tiled=True)  7.65 us
  transfers between devices with their start and end apart: 3, of which 1 were waited for; matrix products, arithmetic and copies ran while one was open for 34% of the time, Pallas kernels for 0%

profile of v1, /device:TPU:0, one launch (start us, length us, event | category | flops | bytes accessed | tf_op | source)
XLA Modules:
  0.0 323.5 jit_solution(16515309153429786869)
XLA Ops:
  7.2 1.3 collective-permute-start
  8.5 0.6 compare_reduce_fusion.1
  9.2 0.6 compare_reduce_fusion
  9.8 0.7 constant_dynamic-update-slice_fusion.1
  10.5 1.4 multiply_reduce_fusion.4
  11.9 1.3 multiply_reduce_fusion.8
  13.2 1.3 multiply_reduce_fusion.6
  17.7 0.8 broadcast_subtract_fusion
  18.6 7.7 %all-gather = f32[4,2,4096]{2,1,0:T(2,128)S(1)} all-gather(f32[1,2,4096]{2,1,0:T(2,128)} %bitcast.78), channel_id=1, replica_groups=mesh['tm'=8,'cal'=4] {'cal'}, dimensions={0}, use_global_device_ids=true | all-gather | bytes 163840 | tf_op jit(solution)/shard_map/all_gather | solution.py:53
  26.4 0.9 add_select_fusion.1
  27.4 1.3 iota_compare_fusion.1
  28.7 38.5 %copy.50 = pred[128,128,128]{2,0,1:T(32,128)(4,1)S(1)} copy(pred[128,128,128]{1,0,2:T(32,128)(4,1)S(1)} %iota_compare_fusion.1) | data formatting | bytes 4194304 | tf_op jit(solution)/shard_map/eq | solution.py:64
  67.2 2.7 iota_compare_fusion
  70.0 20.5 %copy.55 = pred[256,128,128]{2,0,1:T(32,128)(4,1)} copy(pred[256,128,128]{1,0,2:T(32,128)(4,1)S(1)} %iota_compare_fusion) | data formatting | bytes 8388608 | tf_op jit(solution)/shard_map/eq | solution.py:76
  90.7 8.2 %fusion = f32[128,128]{1,0:T(8,128)S(1)} fusion(s32[128,128]{1,0:T(8,128)S(1)} %get-tuple-element.62, pred[256,128,128]{2,0,1:T(32,128)(4,1)} %copy.55, f32[256,128]{1,0:T(8,128)S(1)} %reshape.140), kind=kOutput, calls=%fused_computation.2 | convolution fusion | flops 6448726016 | bytes 4456448 | tf_op jit(solution)/shard_map/hl,hso->lso/dot_general | solution.py:79
  99.1 2.2 fusion.29
  101.3 0.8 fusion.7
  102.9 4.2 %fusion.4 = f32[128,4,3]{0,1,2:T(4,128)S(1)} fusion(f32[4,3,128,128]{3,0,2,1:T(4,128)S(1)} %copy.59, s32[128,128]{0,1:T(8,128)S(1)} %copy.49), kind=kOutput, calls=%fused_computation.9 | convolution fusion | flops 304087040 | bytes 858112 | tf_op jit(solution)/shard_map/qso,jso->jq/dot_general | solution.py:95
  107.9 2.2 collective-permute-start.1
  110.1 4.7 %fusion.1 = f32[128,128,128]{2,0,1:T(8,128)} fusion(f32[128,128]{1,0:T(8,128)S(1)} %get-tuple-element.52, s32[128,128]{1,0:T(8,128)S(1)} %get-tuple-element.62), kind=kLoop, calls=%fused_computation.5 | loop fusion | flops 4194304 | bytes 8519680 | tf_op jit(solution)/shard_map/mul | solution.py:102
  114.8 9.3 %copy.57 = f32[128,128,128]{1,0,2:T(8,128)} copy(f32[128,128,128]{2,0,1:T(8,128)} %fusion.1) | data formatting | bytes 16777216 | tf_op jit(solution)/shard_map/mul | solution.py:102
  124.2 11.2 %convolution_bitcast_fusion = f32[256,128]{1,0:T(8,128)S(1)} fusion(f32[128,128,128]{1,0,2:T(8,128)} %copy.57, s32[128,128]{0,1:T(8,128)S(1)} %copy.48), kind=kOutput, calls=%fused_computation.8 | convolution fusion | flops 6446645248 | bytes 8585216 | tf_op jit(solution)/shard_map/hso,lso->hl/dot_general | solution.py:103
  135.3 2.5 fusion.28
  137.9 1.4 scatter.11
  139.3 0.7 pad_maximum_fusion
  140.0 123.3 %all-reduce.8.cloned.1.call-done = f32[257,128]{1,0:T(8,128)} async-done(((f32[257,128]{1,0:T(8,128)}), f32[257,128]{1,0:T(8,128)}) %all-reduce.8.cloned.1.call-update) | async-done | bytes 131600 | tf_op jit(solution)/shard_map/psum | solution.py:106
  263.3 1.3 fusion.26
  266.0 0.8 dynamic-slice_multiply_fusion
  267.4 0.7 multiply_reduce_fusion.3
  268.8 0.8 multiply_reduce_fusion.7
  271.6 42.5 %psum.15 = f32[1,128]{1,0:T(1,128)S(1)} all-reduce(f32[1,128]{1,0:T(1,128)S(1)} %scatter.14), channel_id=1, replica_groups=mesh['tm'=8,'cal'=4] {'tm','cal'}, use_global_device_ids=true, to_apply=%region_17.18 | all-reduce | flops 128 | bytes 1024 | tf_op jit(solution)/shard_map/psum | solution.py:121
  316.0 0.6 multiply_add_fusion.1
  (63 shorter events, 4.6 us)
Async XLA Ops:
  7.2 256.2 %all-reduce.8.cloned.1.call-start = ((), (), s32[]{:S(2)}) async-start(), calls=%async_computation | async-start | bytes 270336 | tf_op jit(solution)/shard_map/psum | solution.py:106
  7.2 91.8 %collective-permute-start = (f32[3,3]{1,0:T(4,128)}, f32[3,3]{1,0:T(4,128)S(1)}, u32[]{:S(2)}, u32[]{:S(2)}) collective-permute-start(f32[3,3]{1,0:T(4,128)} %bitcast.79), channel_id=1, source_target_pairs={{1,0},{2,1},{3,2},{4,3},{5,4},{6,5},{7,6},{8,7},{9,8},{10,9},{11,1... | collective-permute-start | bytes 116 | tf_op jit(solution)/shard_map/ppermute | solution.py:13
  69.9 20.6 %copy-start = (f32[5,128,128]{2,1,0:T(8,128)S(1)}, f32[5,128,128]{2,1,0:T(8,128)}, u32[]{:S(2)}) copy-start(f32[5,128,128]{2,1,0:T(8,128)} %param.21) | copy-start | bytes 983044
  69.9 20.6 %copy-start.9 = (f32[5,128]{1,0:T(8,128)S(1)}, f32[5,128]{1,0:T(8,128)}, u32[]{:S(2)}) copy-start(f32[5,128]{1,0:T(8,128)} %param.33) | copy-start | bytes 7684
  90.7 8.4 %copy-start.8 = (f32[3,128]{1,0:T(4,128)S(1)}, f32[3,128]{1,0:T(4,128)}, u32[]{:S(2)}) copy-start(f32[3,128]{1,0:T(4,128)} %param.34) | copy-start | bytes 4612
  90.7 10.6 %copy-start.1 = (f32[3,128,128]{2,1,0:T(8,128)S(1)}, f32[3,128,128]{2,1,0:T(8,128)}, u32[]{:S(2)}) copy-start(f32[3,128,128]{2,1,0:T(8,128)} %param.22) | copy-start | bytes 589828
  98.9 3.2 copy-start.5
  98.9 3.2 copy-start.6
  98.9 3.2 copy-start.7
  99.0 3.2 copy-start.14
  107.9 32.1 %collective-permute-start.1 = (f32[3,3]{1,0:T(4,128)S(1)}, f32[3,3]{1,0:T(4,128)S(1)}, u32[]{:S(2)}, u32[]{:S(2)}) collective-permute-start(f32[3,3]{1,0:T(4,128)S(1)} %slice.142), channel_id=1, source_target_pairs={{0,1},{1,2},{2,3},{3,4},{4,5},{5,6},{6,7},{7,8},{8,9},{9,10},{10,1... | collective-permute-start | bytes 116 | tf_op jit(solution)/shard_map/ppermute | solution.py:13
  124.2 142.6 %copy-start.11 = (f32[5,128]{1,0:T(8,128)S(1)}, f32[5,128]{1,0:T(8,128)}, u32[]{:S(2)}) copy-start(f32[5,128]{1,0:T(8,128)} %param.30) | copy-start | bytes 7684
  124.2 143.3 %copy-start.4 = (f32[2,4096]{1,0:T(2,128)S(1)}, f32[2,4096]{1,0:T(2,128)}, u32[]{:S(2)}) copy-start(f32[2,4096]{1,0:T(2,128)} %param.32) | copy-start | bytes 98308
  124.2 144.7 %copy-start.12 = (f32[3,128]{1,0:T(4,128)S(1)}, f32[3,128]{1,0:T(4,128)}, u32[]{:S(2)}) copy-start(f32[3,128]{1,0:T(4,128)} %param.31) | copy-start | bytes 4612
  124.2 191.8 %copy-start.2 = (f32[2,4096]{1,0:T(2,128)S(1)}, f32[2,4096]{1,0:T(2,128)}, u32[]{:S(2)}) copy-start(f32[2,4096]{1,0:T(2,128)} %param.35) | copy-start | bytes 98308
  267.4 49.2 %copy-start.10 = (f32[5,128]{1,0:T(8,128)}, f32[5,128]{1,0:T(8,128)S(1)}, u32[]{:S(2)}) copy-start(f32[5,128]{1,0:T(8,128)S(1)} %get-tuple-element.51) | copy-start | bytes 7684
  268.1 48.5 %copy-start.3 = (f32[2,4096]{1,0:T(2,128)}, f32[2,4096]{1,0:T(2,128)S(1)}, u32[]{:S(2)}) copy-start(f32[2,4096]{1,0:T(2,128)S(1)} %get-tuple-element.47) | copy-start | bytes 98308
  269.6 47.1 %copy-start.13 = (f32[3,128]{1,0:T(4,128)}, f32[3,128]{1,0:T(4,128)S(1)}, u32[]{:S(2)}) copy-start(f32[3,128]{1,0:T(4,128)S(1)} %get-tuple-element.49) | copy-start | bytes 4612
Sparse Core Ops, SparseCore 0:
  140.1 123.1 all-reduce.7

commit v2 on v1

--- a/solution.py
+++ b/solution.py
@@ -11,6 +11,36 @@
     devices = range(lax.axis_size(axis))
     route = [(i - distance, i) for i in devices if i - distance in devices]
     return lax.ppermute(block, axis, route)
+
+
+def exchanged(block, axis, distance):
+    devices = range(lax.axis_size(axis))
+    return lax.ppermute(block, axis, [(i, i ^ distance) for i in devices])
+
+
+def halving_sum(rows, extra, axis):
+    count = lax.axis_size(axis)
+    me = lax.axis_index(axis)
+    distance = count // 2
+    while distance >= 1:
+        half = rows.shape[0] // 2
+        upper = (me // distance) % 2
+        keep = lax.dynamic_slice_in_dim(rows, upper * half, half, 0)
+        send = lax.dynamic_slice_in_dim(rows, (1 - upper) * half, half, 0)
+        got = exchanged(jnp.concatenate([send, extra], axis=0), axis, distance)
+        rows = keep + got[:half]
+        extra = extra + got[half:]
+        distance //= 2
+    return rows, extra
+
+
+def doubling_sum(rows, axis):
+    count = lax.axis_size(axis)
+    distance = 1
+    while distance < count:
+        rows = rows + exchanged(rows, axis, distance)
+        distance *= 2
+    return rows
 
 
 def spline(phase):
@@ -60,24 +90,23 @@
     basis = spline(obs_phase)
     local_knot = knot_index - lax.axis_index(("tm", "cal")) * knot_count
 
-    knot_iota = lax.broadcasted_iota(jnp.int32, (knot_count, 1, 1), 0)
-    knot_hot = (local_knot[None] == knot_iota).astype(jnp.float32)
+    n_obs = src_rows * slots
+    flat = lambda a: a.reshape(1, n_obs)
 
-    table = jnp.stack([att_ext[:, m : m + knot_count].T for m in range(4)], axis=1)
-    table = table.reshape(knot_count, 12)
-    picked = jnp.einsum("jq,jso->qso", table, knot_hot, precision=EXACT).reshape(4, 3, src_rows, slots)
+    knot_hot = (flat(local_knot) == lax.broadcasted_iota(jnp.int32, (knot_count, 1), 0)).astype(jnp.float32)
+
+    table = jnp.stack([att_ext[:, m : m + knot_count] for m in range(4)], axis=0).reshape(12, knot_count)
+    picked = jnp.dot(table, knot_hot, precision=EXACT).reshape(4, 3, src_rows, slots)
     y_att = jnp.zeros_like(obs_phase)
     for m in range(4):
         y_att = y_att + basis[m] * jnp.sum(att_design * picked[m], axis=0)
 
-    flat_index = cal_block * col_width + cal_column
-    high = flat_index // lane
-    low = flat_index % lane
-    high_hot = (high[None] == lax.broadcasted_iota(jnp.int32, (rows, 1, 1), 0)).astype(jnp.float32)
-    low_hot = (low[None] == lax.broadcasted_iota(jnp.int32, (lane, 1, 1), 0)).astype(jnp.float32)
+    flat_index = flat(cal_block * col_width + cal_column)
+    high_hot = (flat_index // lane == lax.broadcasted_iota(jnp.int32, (rows, 1), 0)).astype(jnp.float32)
+    low_hot = (flat_index % lane == lax.broadcasted_iota(jnp.int32, (lane, 1), 0)).astype(jnp.float32)
     cal_table = cal_values.reshape(rows, lane)
-    row_vals = jnp.einsum("hl,hso->lso", cal_table, high_hot, precision=EXACT)
-    y_cal = cal_design * jnp.sum(row_vals * low_hot, axis=0)
+    row_vals = lax.dot_general(cal_table, high_hot, (((0,), (0,)), ((), ())), precision=EXACT)
+    y_cal = cal_design * jnp.sum(row_vals * low_hot, axis=0).reshape(src_rows, slots)
 
     y_src = jnp.sum(src_design * src_dir[:, :, None], axis=0)
     response = live_mask * (y_src + y_att + y_cal)
@@ -91,23 +120,23 @@
     q_src = jnp.sum(src_design * weighted[None], axis=2)
 
     scaled = att_design * weighted[None]
-    spread = jnp.stack([basis[m][None] * scaled for m in range(4)], axis=0).reshape(12, src_rows, slots)
-    gathered = jnp.einsum("qso,jso->jq", spread, knot_hot, precision=EXACT).reshape(knot_count, 4, 3)
+    spread = jnp.stack([basis[m][None] * scaled for m in range(4)], axis=0).reshape(12, n_obs)
+    gathered = lax.dot_general(spread, knot_hot, (((1,), (1,)), ((), ())), precision=EXACT)
+    gathered = gathered.reshape(4, 3, knot_count)
     grad_ext = jnp.zeros((3, knot_count + 3), jnp.float32)
     for m in range(4):
-        grad_ext = grad_ext + jnp.pad(gathered[:, m, :].T, ((0, 0), (m, 3 - m)))
+        grad_ext = grad_ext + jnp.pad(gathered[m], ((0, 0), (m, 3 - m)))
     incoming = passed_along(grad_ext[:, knot_count:], ("tm", "cal"), 1)
     q_att = jnp.concatenate([grad_ext[:, :3] + incoming, grad_ext[:, 3:knot_count]], axis=1)
 
-    cal_weighted = (cal_design * weighted)[None] * low_hot
-    cal_term = jnp.einsum("hso,lso->hl", high_hot, cal_weighted, precision=EXACT)
+    cal_weighted = flat(cal_design * weighted) * low_hot
+    cal_term = lax.dot_general(high_hot, cal_weighted, (((1,), (1,)), ((), ())), precision=EXACT)
     scalars = jnp.zeros((1, lane), jnp.float32).at[0, 0].set(norm_local).at[0, 1].set(curv_local)
-    packed = jnp.concatenate([cal_term, scalars], axis=0)
-    summed = lax.psum(packed, ("tm", "cal"))
-    norm_now = summed[rows, 0]
-    curvature = summed[rows, 1]
-    own = lax.axis_index("cal") * (blocks * col_width // lane)
-    q_cal = lax.dynamic_slice_in_dim(summed, own, blocks * col_width // lane, 0).reshape(blocks, col_width)
+    q_cal, scalars = halving_sum(cal_term, scalars, "cal")
+    summed = doubling_sum(jnp.concatenate([q_cal, scalars], axis=0), "tm")
+    norm_now = summed[-1, 0]
+    curvature = summed[-1, 1]
+    q_cal = summed[:-1].reshape(blocks, col_width)
 
     step_len = norm_now / curvature
     new_src_res = src_res - step_len * q_src
@@ -118,7 +147,8 @@
         + jnp.sum(new_att_res * new_att_res)
         + first_row * jnp.sum(new_cal_res * new_cal_res)
     )
-    norm_next = lax.psum(jnp.zeros((1, lane), jnp.float32).at[0, 0].set(next_local), ("tm", "cal"))[0, 0]
+    norm_next = jnp.zeros((1, lane), jnp.float32).at[0, 0].set(next_local)
+    norm_next = doubling_sum(doubling_sum(norm_next, "cal"), "tm")[0, 0]
     ratio = norm_next / norm_now
     return (
         new_src_res,

time: 324 us -> 99.7 us (0.31)
  waiting for transfers between devices: 123 us -> 16.4 us
  local copies, waits for them, and re-layouts: 73.3 us -> 4.68 us
  blocking collectives: 50.1 us -> 7.63 us
  starting transfers between devices: 3.56 us -> 18 us
  between operations: 21.7 us -> 8.43 us
  other arithmetic: 25.7 us -> 18.1 us
    psum x1 -> x0, waiting for transfers between devices: 123 us -> none  [local(): summed = lax.psum(packed, ('tm', 'cal'))]
    eq x2 -> x0, local copies, waits for them, and re-layouts: 59 us -> none  [the longest x1 38.5 us: local(): knot_hot = (local_knot[None] == knot_iota).astype(jnp.float32)]
    psum x1 -> x0, blocking collectives: 42.5 us -> none  [local(): lax.psum(jnp.zeros((1, lane), jnp.float32).at[0, 0].set(next_local), ('tm...]
    ppermute x0 -> x10, waiting for transfers between devices: none -> 16.4 us  [exchanged(): return lax.ppermute(block, axis, [(i, i ^ distance) for i in devices])]
    ppermute x0 -> x10, starting transfers between devices: none -> 15.3 us  [exchanged(): return lax.ppermute(block, axis, [(i, i ^ distance) for i in devices])]
    mul x1 -> x0, local copies, waits for them, and re-layouts: 9.32 us -> none  [local(): cal_weighted = (cal_design * weighted)[None] * low_hot]
    mul x2 -> x1, other arithmetic: 4.81 us -> 0.09 us  [local(): cal_weighted = flat(cal_design * weighted) * low_hot]
    dot_general x1, other arithmetic: 0.05 us -> 4.09 us  [local(): lax.dot_general(high_hot, cal_weighted, (((1,), (1,)), ((), ())), precisi...]
  transfers between devices with their start and end apart: 3 -> 12, of which waited for: 1 -> 9; matrix products, arithmetic and copies ran while one was open for 34% -> 23% of each run, Pallas kernels for 0% -> 0%
where the time goes in v2:
time: 99.7 us; the launch traced here: 99.2 us
  matrix products  26 us (26%)
  other arithmetic  18.1 us (18%)
  starting transfers between devices  18 us (18%)
  waiting for transfers between devices  16.4 us (16%)
  between operations  8.43 us (8%)
  blocking collectives  7.63 us (8%)
  local copies, waits for them, and re-layouts  4.68 us (5%)
    ppermute x10, waiting for transfers between devices, exchanged(): return lax.ppermute(block, axis, [(i, i ^ distance) for i in devices])  16.4 us
    ppermute x10, starting transfers between devices, exchanged(): return lax.ppermute(block, axis, [(i, i ^ distance) for i in devices])  15.3 us
    dot_general x1, matrix products, local(): lax.dot_general(high_hot, cal_weighted, (((1,), (1,)), ((), ())), precisi...  12.4 us
    all_gather x1, blocking collectives, local(): cal_values = lax.all_gather(cal_dir, 'cal', axis=0, tiled=True)  7.63 us
    dot_general x1, matrix products, local(): lax.dot_general(cal_table, high_hot, (((0,), (0,)), ((), ())), precision=...  6.93 us
    dot_general x1, other arithmetic, local(): lax.dot_general(high_hot, cal_weighted, (((1,), (1,)), ((), ())), precisi...  4.09 us
    dot_general x1, matrix products, local(): lax.dot_general(spread, knot_hot, (((1,), (1,)), ((), ())), precision=EXACT)  3.92 us
    another operation x3, other arithmetic  3.8 us
  transfers between devices with their start and end apart: 12, of which 9 were waited for; matrix products, arithmetic and copies ran while one was open for 23% of the time, Pallas kernels for 0%

profile of v2, /device:TPU:0, one launch (start us, length us, event | category | flops | bytes accessed | tf_op | source)
XLA Modules:
  0.0 99.2 jit_solution(12310585510139875100)
XLA Ops:
  0.7 1.4 %collective-permute-start = (f32[3,3]{1,0:T(4,128)}, f32[3,3]{1,0:T(4,128)S(1)}, u32[]{:S(2)}, u32[]{:S(2)}) collective-permute-start(f32[3,3]{1,0:T(4,128)} %bitcast.104), channel_id=1, source_target_pairs={{1,0},{2,1},{3,2},{4,3},{5,4},{6,5},{7,6},{8,7},{9,8},{10,9},{11,1... | collective-permute-start | bytes 116 | tf_op jit(solution)/shard_map/ppermute | solution.py:13
  4.1 1.4 %multiply_reduce_fusion.4 = f32[]{:T(128)} fusion(f32[2,4096]{1,0:T(2,128)} %param.32), kind=kLoop, calls=%fused_computation.75 | loop fusion | flops 16383 | bytes 32772 | tf_op jit(solution)/shard_map/reduce_sum | solution.py:118
  5.5 1.3 %multiply_reduce_fusion.8 = f32[]{:T(128)} fusion(f32[3,128]{1,0:T(4,128)} %param.31), kind=kLoop, calls=%fused_computation.92 | loop fusion | flops 767 | bytes 1540 | tf_op jit(solution)/shard_map/reduce_sum | solution.py:117
  6.7 1.3 %multiply_reduce_fusion.6 = f32[]{:T(128)} fusion(f32[5,128]{1,0:T(8,128)} %param.30), kind=kLoop, calls=%fused_computation.83 | loop fusion | flops 1279 | bytes 2564 | tf_op jit(solution)/shard_map/reduce_sum | solution.py:116
  11.2 7.6 %all-gather = f32[4,2,4096]{2,1,0:T(2,128)S(1)} all-gather(f32[1,2,4096]{2,1,0:T(2,128)} %bitcast.103), channel_id=1, replica_groups=mesh['tm'=8,'cal'=4] {'cal'}, dimensions={0}, use_global_device_ids=true | all-gather | bytes 163840 | tf_op jit(solution)/shard_map/all_gather | solution.py:83
  19.0 0.9 add_select_fusion
  19.9 4.1 %iota_compare_fusion.14 = pred[256,16384]{1,0:T(32,128)(4,1)} fusion(s32[16384]{0:T(1024)S(1)} %get-tuple-element.64), kind=kLoop, calls=%fused_computation.2.clone.clone.2 | loop fusion | flops 4194304 | bytes 4259840 | tf_op jit(solution)/shard_map/dot_general | solution.py:133
  24.2 6.9 %fusion.12 = f32[16384]{0:T(1024)S(1)} fusion(f32[256,128]{1,0:T(8,128)S(1)} %reshape.241, s32[16384]{0:T(1024)S(1)} %get-tuple-element.64, s32[16384]{0:T(1024)S(1)} %get-tuple-element.63), kind=kOutput, calls=%fused_computation.16 | convolution fusion | flops 6452920320 | bytes 327680 | tf_op jit(solution)/shard_map/dot_general | solution.py:108
  31.3 2.7 %fusion.4 = f32[12,16384]{1,0:T(8,128)S(1)} fusion(f32[12,128]{1,0:T(8,128)S(1)} %reshape.240, s32[16384]{0:T(1024)S(1)} %subtract_bitcast_fusion), kind=kOutput, calls=%fused_computation.7 | convolution fusion | flops 304087040 | bytes 858112 | tf_op jit(solution)/shard_map/dot_general | solution.py:99
  35.9 2.5 %fusion.38 = f32[1,1]{1,0:T(1,128)} fusion(pred[1,1]{1,0:T(4,128)(4,1)} %bitcast.11, f32[1,1]{1,0:T(1,128)} %bitcast.12, s32[]{:T(128)} %bitcast.13, f32[1,1]{1,0:T(1,128)} %bitcast.10), kind=kLoop, calls=%fused_computation.106 | loop fusion | flops 1 | bytes 17 | tf_op jit(solution)/shard_map/select.4
  38.4 1.5 %scatter.11 = f32[1,128]{1,0:T(1,128)S(1)} dynamic-update-slice(f32[1,128]{1,0:T(1,128)S(1)} %scatter.10, f32[1,1]{1,0:T(1,128)} %fusion.38, s32[]{:T(128)} %constant.154.clone.1, s32[]{:T(128)} %bitcast.13) | dynamic-update-slice | bytes 12 | tf_op jit(solution)/shard_map/scatter | solution.py:134
  40.0 12.4 %fusion.1 = f32[256,128]{1,0:T(8,128)S(1)} fusion(f32[16384]{0:T(1024)S(1)} %get-tuple-element.52, s32[16384]{0:T(1024)S(1)} %get-tuple-element.63, pred[256,16384]{1,0:T(32,128)(4,1)} %iota_compare_fusion.14), kind=kOutput, calls=%fused_computation.3 | convolution fusion | flops 6446645248 | bytes 4456448 | tf_op jit(solution)/shard_map/dot_general | solution.py:133
  52.5 1.6 %collective-permute-start.1 = (f32[129,128]{1,0:T(8,128)S(1)}, f32[129,128]{1,0:T(8,128)S(1)}, u32[]{:S(2)}, u32[]{:S(2)}) collective-permute-start(f32[129,128]{1,0:T(8,128)S(1)} %pad_maximum_fusion.1), channel_id=1, source_target_pairs={{0,2},{1,3},{2,0},{3,1},{4,6},{5,7},{6,4},{7,5},{8,10},{9,11},{10,... | collective-permute-start | bytes 198152 | tf_op jit(solution)/shard_map/ppermute | solution.py:18
  54.1 3.9 %fusion.3 = f32[12,128]{1,0:T(8,128)S(1)} fusion(f32[12,16384]{1,0:T(8,128)S(1)} %bitcast.102, s32[16384]{0:T(1024)S(1)} %subtract_bitcast_fusion), kind=kOutput, calls=%fused_computation.6 | convolution fusion | flops 304087040 | bytes 858112 | tf_op jit(solution)/shard_map/dot_general | solution.py:124
  58.2 1.1 %collective-permute-done.2 = f32[65,128]{1,0:T(8,128)S(1)} collective-permute-done((f32[65,128]{1,0:T(8,128)S(1)}, f32[65,128]{1,0:T(8,128)S(1)}, u32[]{:S(2)}, u32[]{:S(2)}) %collective-permute-start.2) | collective-permute-done | bytes 33312 | tf_op jit(solution)/shard_map/ppermute | solution.py:18
  59.4 1.6 %collective-permute-start.3 = (f32[65,128]{1,0:T(8,128)S(1)}, f32[65,128]{1,0:T(8,128)S(1)}, u32[]{:S(2)}, u32[]{:S(2)}) collective-permute-start(f32[65,128]{1,0:T(8,128)S(1)} %pad_maximum_fusion.3), channel_id=1, source_target_pairs={{0,4},{4,0},{8,12},{12,8},{16,20},{20,16},{24,28},{28,24},{1,5},{5... | collective-permute-start | bytes 99848 | tf_op jit(solution)/shard_map/ppermute | solution.py:18
  61.2 2.3 %collective-permute-done.3 = f32[65,128]{1,0:T(8,128)S(1)} collective-permute-done((f32[65,128]{1,0:T(8,128)S(1)}, f32[65,128]{1,0:T(8,128)S(1)}, u32[]{:S(2)}, u32[]{:S(2)}) %collective-permute-start.3) | collective-permute-done | bytes 33312 | tf_op jit(solution)/shard_map/ppermute | solution.py:18
  63.4 2.3 %collective-permute-start.4 = (f32[65,128]{1,0:T(8,128)S(1)}, f32[65,128]{1,0:T(8,128)S(1)}, u32[]{:S(2)}, u32[]{:S(2)}) collective-permute-start(f32[65,128]{1,0:T(8,128)S(1)} %fusion.33), channel_id=1, source_target_pairs={{0,8},{4,12},{8,0},{12,4},{16,24},{20,28},{24,16},{28,20},{1,9},{5... | collective-permute-start | bytes 99848 | tf_op jit(solution)/shard_map/ppermute | solution.py:18
  65.9 1.3 %collective-permute-start.6 = (f32[3,3]{1,0:T(4,128)S(1)}, f32[3,3]{1,0:T(4,128)S(1)}, u32[]{:S(2)}, u32[]{:S(2)}) collective-permute-start(f32[3,3]{1,0:T(4,128)S(1)} %slice.170), channel_id=1, source_target_pairs={{0,1},{1,2},{2,3},{3,4},{4,5},{5,6},{6,7},{7,8},{8,9},{9,10},{10,1... | collective-permute-start | bytes 116 | tf_op jit(solution)/shard_map/ppermute | solution.py:13
  67.7 3.0 %collective-permute-start.5 = (f32[65,128]{1,0:T(8,128)S(1)}, f32[65,128]{1,0:T(8,128)S(1)}, u32[]{:S(2)}, u32[]{:S(2)}) collective-permute-start(f32[65,128]{1,0:T(8,128)S(1)} %add.187), channel_id=1, source_target_pairs={{0,16},{4,20},{8,24},{12,28},{16,0},{20,4},{24,8},{28,12},{1,17},{... | collective-permute-start | bytes 99848 | tf_op jit(solution)/shard_map/ppermute | solution.py:18
  70.7 1.9 %collective-permute-done.5 = f32[65,128]{1,0:T(8,128)S(1)} collective-permute-done((f32[65,128]{1,0:T(8,128)S(1)}, f32[65,128]{1,0:T(8,128)S(1)}, u32[]{:S(2)}, u32[]{:S(2)}) %collective-permute-start.5) | collective-permute-done | bytes 33312 | tf_op jit(solution)/shard_map/ppermute | solution.py:18
  76.7 0.8 multiply_reduce_fusion.7
  79.5 1.3 %collective-permute-start.7 = (f32[1,128]{1,0:T(1,128)S(1)}, f32[1,128]{1,0:T(1,128)S(1)}, u32[]{:S(2)}, u32[]{:S(2)}) collective-permute-start(f32[1,128]{1,0:T(1,128)S(1)} %scatter.14), channel_id=1, source_target_pairs={{0,1},{1,0},{2,3},{3,2},{4,5},{5,4},{6,7},{7,6},{8,9},{9,8},{10,11... | collective-permute-start | bytes 1544 | tf_op jit(solution)/shard_map/ppermute | solution.py:18
  80.7 0.8 collective-permute-done.7
  81.6 1.2 %collective-permute-start.8 = (f32[1,128]{1,0:T(1,128)S(1)}, f32[1,128]{1,0:T(1,128)S(1)}, u32[]{:S(2)}, u32[]{:S(2)}) collective-permute-start(f32[1,128]{1,0:T(1,128)S(1)} %pad_add_fusion.1), channel_id=1, source_target_pairs={{0,2},{1,3},{2,0},{3,1},{4,6},{5,7},{6,4},{7,5},{8,10},{9,11},{10,... | collective-permute-start | bytes 1544 | tf_op jit(solution)/shard_map/ppermute | solution.py:18
  82.8 2.3 %collective-permute-done.8 = f32[1,128]{1,0:T(1,128)S(1)} collective-permute-done((f32[1,128]{1,0:T(1,128)S(1)}, f32[1,128]{1,0:T(1,128)S(1)}, u32[]{:S(2)}, u32[]{:S(2)}) %collective-permute-start.8) | collective-permute-done | bytes 544 | tf_op jit(solution)/shard_map/ppermute | solution.py:18
  85.1 0.9 collective-permute-start.9
  86.0 2.7 %collective-permute-done.9 = f32[1,128]{1,0:T(1,128)S(1)} collective-permute-done((f32[1,128]{1,0:T(1,128)S(1)}, f32[1,128]{1,0:T(1,128)S(1)}, u32[]{:S(2)}, u32[]{:S(2)}) %collective-permute-start.9) | collective-permute-done | bytes 544 | tf_op jit(solution)/shard_map/ppermute | solution.py:18
  88.7 1.0 collective-permute-start.10
  89.7 2.6 %collective-permute-done.10 = f32[1,128]{1,0:T(1,128)S(1)} collective-permute-done((f32[1,128]{1,0:T(1,128)S(1)}, f32[1,128]{1,0:T(1,128)S(1)}, u32[]{:S(2)}, u32[]{:S(2)}) %collective-permute-start.10) | collective-permute-done | bytes 544 | tf_op jit(solution)/shard_map/ppermute | solution.py:18
  92.2 2.2 %collective-permute-start.11 = (f32[1,128]{1,0:T(1,128)S(1)}, f32[1,128]{1,0:T(1,128)S(1)}, u32[]{:S(2)}, u32[]{:S(2)}) collective-permute-start(f32[1,128]{1,0:T(1,128)S(1)} %add.198), channel_id=1, source_target_pairs={{0,16},{4,20},{8,24},{12,28},{16,0},{20,4},{24,8},{28,12},{1,17},{... | collective-permute-start | bytes 1544 | tf_op jit(solution)/shard_map/ppermute | solution.py:18
  94.4 2.2 %collective-permute-done.11 = f32[1,128]{1,0:T(1,128)S(1)} collective-permute-done((f32[1,128]{1,0:T(1,128)S(1)}, f32[1,128]{1,0:T(1,128)S(1)}, u32[]{:S(2)}, u32[]{:S(2)}) %collective-permute-start.11) | collective-permute-done | bytes 544 | tf_op jit(solution)/shard_map/ppermute | solution.py:18
  (90 shorter events, 9.6 us)
Async XLA Ops:
  0.6 23.4 %copy-start.5 = (s32[128,128]{1,0:T(8,128)S(1)}, s32[128,128]{1,0:T(8,128)}, u32[]{:S(2)}) copy-start(s32[128,128]{1,0:T(8,128)} %param.26) | copy-start | bytes 196612
  0.6 23.4 %copy-start.10 = (f32[5,128]{1,0:T(8,128)S(1)}, f32[5,128]{1,0:T(8,128)}, u32[]{:S(2)}) copy-start(f32[5,128]{1,0:T(8,128)} %param.33) | copy-start | bytes 7684
  0.7 23.4 %copy-start = (f32[5,128,128]{2,1,0:T(8,128)S(1)}, f32[5,128,128]{2,1,0:T(8,128)}, u32[]{:S(2)}) copy-start(f32[5,128,128]{2,1,0:T(8,128)} %param.21) | copy-start | bytes 983044
  0.7 30.6 %collective-permute-start = (f32[3,3]{1,0:T(4,128)}, f32[3,3]{1,0:T(4,128)S(1)}, u32[]{:S(2)}, u32[]{:S(2)}) collective-permute-start(f32[3,3]{1,0:T(4,128)} %bitcast.104), channel_id=1, source_target_pairs={{1,0},{2,1},{3,2},{4,3},{5,4},{6,5},{7,6},{8,7},{9,8},{10,9},{11,1... | collective-permute-start | bytes 116 | tf_op jit(solution)/shard_map/ppermute | solution.py:13
  24.2 7.1 %copy-start.9 = (f32[3,128]{1,0:T(4,128)S(1)}, f32[3,128]{1,0:T(4,128)}, u32[]{:S(2)}) copy-start(f32[3,128]{1,0:T(4,128)} %param.34) | copy-start | bytes 4612
  31.2 3.1 %copy-start.1 = (f32[3,128,128]{2,1,0:T(8,128)S(1)}, f32[3,128,128]{2,1,0:T(8,128)}, u32[]{:S(2)}) copy-start(f32[3,128,128]{2,1,0:T(8,128)} %param.22) | copy-start | bytes 589828
  31.2 3.1 %copy-start.6 = (f32[128,128]{1,0:T(8,128)S(1)}, f32[128,128]{1,0:T(8,128)}, u32[]{:S(2)}) copy-start(f32[128,128]{1,0:T(8,128)} %param.24) | copy-start | bytes 196612
  31.2 3.1 %copy-start.7 = (f32[128,128]{1,0:T(8,128)S(1)}, f32[128,128]{1,0:T(8,128)}, u32[]{:S(2)}) copy-start(f32[128,128]{1,0:T(8,128)} %param.25) | copy-start | bytes 196612
  31.2 3.1 %copy-start.8 = (f32[128,128]{1,0:T(8,128)S(1)}, f32[128,128]{1,0:T(8,128)}, u32[]{:S(2)}) copy-start(f32[128,128]{1,0:T(8,128)} %param.23) | copy-start | bytes 196612
  31.2 3.1 %copy-start.15 = (s32[128]{0:T(128)S(1)}, s32[128]{0:T(128)}, u32[]{:S(2)}) copy-start(s32[128]{0:T(128)} %param.29) | copy-start | bytes 1540
  40.0 34.7 %copy-start.12 = (f32[5,128]{1,0:T(8,128)S(1)}, f32[5,128]{1,0:T(8,128)}, u32[]{:S(2)}) copy-start(f32[5,128]{1,0:T(8,128)} %param.30) | copy-start | bytes 7684
  40.0 35.3 %copy-start.4 = (f32[2,4096]{1,0:T(2,128)S(1)}, f32[2,4096]{1,0:T(2,128)}, u32[]{:S(2)}) copy-start(f32[2,4096]{1,0:T(2,128)} %param.32) | copy-start | bytes 98308
  40.0 36.7 %copy-start.13 = (f32[3,128]{1,0:T(4,128)S(1)}, f32[3,128]{1,0:T(4,128)}, u32[]{:S(2)}) copy-start(f32[3,128]{1,0:T(4,128)} %param.31) | copy-start | bytes 4612
  40.0 58.6 %copy-start.2 = (f32[2,4096]{1,0:T(2,128)S(1)}, f32[2,4096]{1,0:T(2,128)}, u32[]{:S(2)}) copy-start(f32[2,4096]{1,0:T(2,128)} %param.35) | copy-start | bytes 98308
  52.5 5.5 %collective-permute-start.1 = (f32[129,128]{1,0:T(8,128)S(1)}, f32[129,128]{1,0:T(8,128)S(1)}, u32[]{:S(2)}, u32[]{:S(2)}) collective-permute-start(f32[129,128]{1,0:T(8,128)S(1)} %pad_maximum_fusion.1), channel_id=1, source_target_pairs={{0,2},{1,3},{2,0},{3,1},{4,6},{5,7},{6,4},{7,5},{8,10},{9,11},{10,... | collective-permute-start | bytes 198152 | tf_op jit(solution)/shard_map/ppermute | solution.py:18
  58.1 1.3 %collective-permute-start.2 = (f32[65,128]{1,0:T(8,128)S(1)}, f32[65,128]{1,0:T(8,128)S(1)}, u32[]{:S(2)}, u32[]{:S(2)}) collective-permute-start(f32[65,128]{1,0:T(8,128)S(1)} %pad_maximum_fusion.2), channel_id=1, source_target_pairs={{0,1},{1,0},{2,3},{3,2},{4,5},{5,4},{6,7},{7,6},{8,9},{9,8},{10,11... | collective-permute-start | bytes 99848 | tf_op jit(solution)/shard_map/ppermute | solution.py:18
  59.4 4.0 %collective-permute-start.3 = (f32[65,128]{1,0:T(8,128)S(1)}, f32[65,128]{1,0:T(8,128)S(1)}, u32[]{:S(2)}, u32[]{:S(2)}) collective-permute-start(f32[65,128]{1,0:T(8,128)S(1)} %pad_maximum_fusion.3), channel_id=1, source_target_pairs={{0,4},{4,0},{8,12},{12,8},{16,20},{20,16},{24,28},{28,24},{1,5},{5... | collective-permute-start | bytes 99848 | tf_op jit(solution)/shard_map/ppermute | solution.py:18
  63.4 4.3 %collective-permute-start.4 = (f32[65,128]{1,0:T(8,128)S(1)}, f32[65,128]{1,0:T(8,128)S(1)}, u32[]{:S(2)}, u32[]{:S(2)}) collective-permute-start(f32[65,128]{1,0:T(8,128)S(1)} %fusion.33), channel_id=1, source_target_pairs={{0,8},{4,12},{8,0},{12,4},{16,24},{20,28},{24,16},{28,20},{1,9},{5... | collective-permute-start | bytes 99848 | tf_op jit(solution)/shard_map/ppermute | solution.py:18
  65.9 4.8 %collective-permute-start.6 = (f32[3,3]{1,0:T(4,128)S(1)}, f32[3,3]{1,0:T(4,128)S(1)}, u32[]{:S(2)}, u32[]{:S(2)}) collective-permute-start(f32[3,3]{1,0:T(4,128)S(1)} %slice.170), channel_id=1, source_target_pairs={{0,1},{1,2},{2,3},{3,4},{4,5},{5,6},{6,7},{7,8},{8,9},{9,10},{10,1... | collective-permute-start | bytes 116 | tf_op jit(solution)/shard_map/ppermute | solution.py:13
  67.7 5.0 %collective-permute-start.5 = (f32[65,128]{1,0:T(8,128)S(1)}, f32[65,128]{1,0:T(8,128)S(1)}, u32[]{:S(2)}, u32[]{:S(2)}) collective-permute-start(f32[65,128]{1,0:T(8,128)S(1)} %add.187), channel_id=1, source_target_pairs={{0,16},{4,20},{8,24},{12,28},{16,0},{20,4},{24,8},{28,12},{1,17},{... | collective-permute-start | bytes 99848 | tf_op jit(solution)/shard_map/ppermute | solution.py:18
  75.3 23.9 %copy-start.11 = (f32[5,128]{1,0:T(8,128)}, f32[5,128]{1,0:T(8,128)S(1)}, u32[]{:S(2)}) copy-start(f32[5,128]{1,0:T(8,128)S(1)} %get-tuple-element.51) | copy-start | bytes 7684
  76.0 23.2 %copy-start.3 = (f32[2,4096]{1,0:T(2,128)}, f32[2,4096]{1,0:T(2,128)S(1)}, u32[]{:S(2)}) copy-start(f32[2,4096]{1,0:T(2,128)S(1)} %get-tuple-element.47) | copy-start | bytes 98308
  77.4 21.8 %copy-start.14 = (f32[3,128]{1,0:T(4,128)}, f32[3,128]{1,0:T(4,128)S(1)}, u32[]{:S(2)}) copy-start(f32[3,128]{1,0:T(4,128)S(1)} %get-tuple-element.49) | copy-start | bytes 4612
  79.5 2.1 %collective-permute-start.7 = (f32[1,128]{1,0:T(1,128)S(1)}, f32[1,128]{1,0:T(1,128)S(1)}, u32[]{:S(2)}, u32[]{:S(2)}) collective-permute-start(f32[1,128]{1,0:T(1,128)S(1)} %scatter.14), channel_id=1, source_target_pairs={{0,1},{1,0},{2,3},{3,2},{4,5},{5,4},{6,7},{7,6},{8,9},{9,8},{10,11... | collective-permute-start | bytes 1544 | tf_op jit(solution)/shard_map/ppermute | solution.py:18
  81.6 3.5 %collective-permute-start.8 = (f32[1,128]{1,0:T(1,128)S(1)}, f32[1,128]{1,0:T(1,128)S(1)}, u32[]{:S(2)}, u32[]{:S(2)}) collective-permute-start(f32[1,128]{1,0:T(1,128)S(1)} %pad_add_fusion.1), channel_id=1, source_target_pairs={{0,2},{1,3},{2,0},{3,1},{4,6},{5,7},{6,4},{7,5},{8,10},{9,11},{10,... | collective-permute-start | bytes 1544 | tf_op jit(solution)/shard_map/ppermute | solution.py:18
  85.1 3.5 %collective-permute-start.9 = (f32[1,128]{1,0:T(1,128)S(1)}, f32[1,128]{1,0:T(1,128)S(1)}, u32[]{:S(2)}, u32[]{:S(2)}) collective-permute-start(f32[1,128]{1,0:T(1,128)S(1)} %fusion.42), channel_id=1, source_target_pairs={{0,4},{4,0},{8,12},{12,8},{16,20},{20,16},{24,28},{28,24},{1,5},{5... | collective-permute-start | bytes 1544 | tf_op jit(solution)/shard_map/ppermute | solution.py:18
  88.7 3.5 %collective-permute-start.10 = (f32[1,128]{1,0:T(1,128)S(1)}, f32[1,128]{1,0:T(1,128)S(1)}, u32[]{:S(2)}, u32[]{:S(2)}) collective-permute-start(f32[1,128]{1,0:T(1,128)S(1)} %add.197), channel_id=1, source_target_pairs={{0,8},{4,12},{8,0},{12,4},{16,24},{20,28},{24,16},{28,20},{1,9},{5... | collective-permute-start | bytes 1544 | tf_op jit(solution)/shard_map/ppermute | solution.py:18
  92.2 4.4 %collective-permute-start.11 = (f32[1,128]{1,0:T(1,128)S(1)}, f32[1,128]{1,0:T(1,128)S(1)}, u32[]{:S(2)}, u32[]{:S(2)}) collective-permute-start(f32[1,128]{1,0:T(1,128)S(1)} %add.198), channel_id=1, source_target_pairs={{0,16},{4,20},{8,24},{12,28},{16,0},{20,4},{24,8},{28,12},{1,17},{... | collective-permute-start | bytes 1544 | tf_op jit(solution)/shard_map/ppermute | solution.py:18

commit v3 on v2

--- a/solution.py
+++ b/solution.py
@@ -41,6 +41,48 @@
         rows = rows + exchanged(rows, axis, distance)
         distance *= 2
     return rows
+
+
+def from_all(block, axis):
+    count = lax.axis_size(axis)
+    me = lax.axis_index(axis)
+    got = [block] + [
+        lax.ppermute(block, axis, [(i, (i + shift) % count) for i in range(count)])
+        for shift in range(1, count)
+    ]
+    stacked = jnp.stack(got[::-1] + got[::-1], axis=0)
+    return lax.dynamic_slice_in_dim(stacked, count - 1 - me, count, 0)
+
+
+def ordered_sum(parts):
+    total = parts[0]
+    for k in range(1, parts.shape[0]):
+        total = total + parts[k]
+    return total
+
+
+def all_sum(block, axis):
+    if lax.axis_size(axis) > 8:
+        return doubling_sum(block, axis)
+    return ordered_sum(from_all(block, axis))
+
+
+def scatter_sum(rows, extra, axis):
+    count = lax.axis_size(axis)
+    if count > 8:
+        return halving_sum(rows, extra, axis)
+    me = lax.axis_index(axis)
+    share = rows.shape[0] // count
+    got = []
+    for shift in range(count):
+        target = (me + shift) % count
+        part = jnp.concatenate([lax.dynamic_slice_in_dim(rows, target * share, share, 0), extra], axis=0)
+        if shift:
+            part = lax.ppermute(part, axis, [(i, (i + shift) % count) for i in range(count)])
+        got.append(part)
+    stacked = jnp.stack(got[::-1] + got[::-1], axis=0)
+    total = ordered_sum(lax.dynamic_slice_in_dim(stacked, count - 1 - me, count, 0))
+    return total[:share], total[share:]
 
 
 def spline(phase):
@@ -80,7 +122,7 @@
     src_rows, slots = obs_phase.shape
     first_row = (lax.axis_index("tm") == 0).astype(jnp.float32)
 
-    cal_values = lax.all_gather(cal_dir, "cal", axis=0, tiled=True)
+    cal_values = from_all(cal_dir, "cal").reshape(all_blocks, col_width)
     edge_knots = passed_along(att_dir[:, :3], ("tm", "cal"), -1)
     att_ext = jnp.concatenate([att_dir, edge_knots], axis=1)
 
@@ -132,8 +174,8 @@
     cal_weighted = flat(cal_design * weighted) * low_hot
     cal_term = lax.dot_general(high_hot, cal_weighted, (((1,), (1,)), ((), ())), precision=EXACT)
     scalars = jnp.zeros((1, lane), jnp.float32).at[0, 0].set(norm_local).at[0, 1].set(curv_local)
-    q_cal, scalars = halving_sum(cal_term, scalars, "cal")
-    summed = doubling_sum(jnp.concatenate([q_cal, scalars], axis=0), "tm")
+    q_cal, scalars = scatter_sum(cal_term, scalars, "cal")
+    summed = all_sum(jnp.concatenate([q_cal, scalars], axis=0), "tm")
     norm_now = summed[-1, 0]
     curvature = summed[-1, 1]
     q_cal = summed[:-1].reshape(blocks, col_width)
@@ -148,7 +190,7 @@
         + first_row * jnp.sum(new_cal_res * new_cal_res)
     )
     norm_next = jnp.zeros((1, lane), jnp.float32).at[0, 0].set(next_local)
-    norm_next = doubling_sum(doubling_sum(norm_next, "cal"), "tm")[0, 0]
+    norm_next = all_sum(all_sum(norm_next, "cal"), "tm")[0, 0]
     ratio = norm_next / norm_now
     return (
         new_src_res,

time: 99.7 us -> 116 us (1.16)
  starting transfers between devices: 18 us -> 41 us
  blocking collectives: 7.63 us -> 0 us
    ppermute x10 -> x23, starting transfers between devices: 15.3 us -> 37.7 us  [the longest x20 33.3 us: from_all(): lax.ppermute(block, axis, [(i, (i + shift) % count) for i in range(count)])]
    all_gather x1 -> x0, blocking collectives: 7.63 us -> none  [local(): cal_values = lax.all_gather(cal_dir, 'cal', axis=0, tiled=True)]
    ppermute x10 -> x23, waiting for transfers between devices: 16.4 us -> 15.5 us  [the longest x20 13.1 us: from_all(): lax.ppermute(block, axis, [(i, (i + shift) % count) for i in range(count)])]
    another operation x3 -> x6, other arithmetic: 3.8 us -> 3.85 us
  transfers between devices with their start and end apart: 12 -> 25, of which waited for: 9 -> 7; matrix products, arithmetic and copies ran while one was open for 23% -> 13% of each run, Pallas kernels for 0% -> 0%
where the time goes in v3:
time: 116 us; the launch traced here: 115 us
  starting transfers between devices  41 us (35%)
  matrix products  26.2 us (23%)
  other arithmetic  18.3 us (16%)
  waiting for transfers between devices  15.5 us (13%)
  between operations  8.73 us (8%)
  local copies, waits for them, and re-layouts  4.92 us (4%)
    ppermute x20, starting transfers between devices, from_all(): lax.ppermute(block, axis, [(i, (i + shift) % count) for i in range(count)])  33.3 us
    ppermute x20, waiting for transfers between devices, from_all(): lax.ppermute(block, axis, [(i, (i + shift) % count) for i in range(count)])  13.1 us
    dot_general x1, matrix products, local(): lax.dot_general(high_hot, cal_weighted, (((1,), (1,)), ((), ())), precisi...  12.4 us
    dot_general x1, matrix products, local(): lax.dot_general(cal_table, high_hot, (((0,), (0,)), ((), ())), precision=...  7.12 us
    ppermute x3, starting transfers between devices, scatter_sum(): lax.ppermute(part, axis, [(i, (i + shift) % count) for i in range(count)])  4.37 us
    dot_general x1, other arithmetic, local(): lax.dot_general(high_hot, cal_weighted, (((1,), (1,)), ((), ())), precisi...  4.11 us
    dot_general x1, matrix products, local(): lax.dot_general(spread, knot_hot, (((1,), (1,)), ((), ())), precision=EXACT)  3.92 us
    another operation x3, other arithmetic  3.8 us
  transfers between devices with their start and end apart: 25, of which 7 were waited for; matrix products, arithmetic and copies ran while one was open for 13% of the time, Pallas kernels for 0%

profile of v3, /device:TPU:0, one launch (start us, length us, event | category | flops | bytes accessed | tf_op | source)
XLA Modules:
  0.0 114.6 jit_solution(18185706723334146975)
XLA Ops:
  1.2 2.6 %collective-permute-start.2 = (f32[2,4096]{1,0:T(2,128)}, f32[2,4096]{1,0:T(2,128)S(1)}, u32[]{:S(2)}, u32[]{:S(2)}) collective-permute-start(f32[2,4096]{1,0:T(2,128)} %param.35), channel_id=1, source_target_pairs={{0,2},{1,3},{2,0},{3,1},{4,6},{5,7},{6,4},{7,5},{8,10},{9,11},{10,... | collective-permute-start | bytes 98312 | tf_op jit(solution)/shard_map/ppermute | solution.py:50
  3.7 1.4 %collective-permute-start.1 = (f32[2,4096]{1,0:T(2,128)}, f32[2,4096]{1,0:T(2,128)S(1)}, u32[]{:S(2)}, u32[]{:S(2)}) collective-permute-start(f32[2,4096]{1,0:T(2,128)} %param.35), channel_id=1, source_target_pairs={{0,3},{1,0},{2,1},{3,2},{4,7},{5,4},{6,5},{7,6},{8,11},{9,8},{10,9... | collective-permute-start | bytes 98312 | tf_op jit(solution)/shard_map/ppermute | solution.py:50
  5.1 1.3 %collective-permute-start = (f32[3,3]{1,0:T(4,128)}, f32[3,3]{1,0:T(4,128)S(1)}, u32[]{:S(2)}, u32[]{:S(2)}) collective-permute-start(f32[3,3]{1,0:T(4,128)} %bitcast.185), channel_id=1, source_target_pairs={{1,0},{2,1},{3,2},{4,3},{5,4},{6,5},{7,6},{8,7},{9,8},{10,9},{11,1... | collective-permute-start | bytes 116 | tf_op jit(solution)/shard_map/ppermute | solution.py:13
  8.4 1.4 %multiply_reduce_fusion.4 = f32[]{:T(128)} fusion(f32[2,4096]{1,0:T(2,128)} %param.32), kind=kLoop, calls=%fused_computation.142 | loop fusion | flops 16383 | bytes 32772 | tf_op jit(solution)/shard_map/reduce_sum | solution.py:160
  9.8 1.3 %multiply_reduce_fusion.8 = f32[]{:T(128)} fusion(f32[3,128]{1,0:T(4,128)} %param.31), kind=kLoop, calls=%fused_computation.175 | loop fusion | flops 767 | bytes 1540 | tf_op jit(solution)/shard_map/reduce_sum | solution.py:159
  11.1 1.3 %multiply_reduce_fusion.6 = f32[]{:T(128)} fusion(f32[5,128]{1,0:T(8,128)} %param.30), kind=kLoop, calls=%fused_computation.166 | loop fusion | flops 1279 | bytes 2564 | tf_op jit(solution)/shard_map/reduce_sum | solution.py:158
  16.5 4.1 %iota_compare_fusion.14 = pred[256,16384]{1,0:T(32,128)(4,1)} fusion(s32[16384]{0:T(1024)S(1)} %get-tuple-element.68), kind=kLoop, calls=%fused_computation.1.clone.clone.2 | loop fusion | flops 4194304 | bytes 4259840 | tf_op jit(solution)/shard_map/dot_general | solution.py:175
  20.9 2.7 %fusion.3 = f32[12,16384]{1,0:T(8,128)S(1)} fusion(f32[12,128]{1,0:T(8,128)S(1)} %reshape.387, s32[16384]{0:T(1024)S(1)} %subtract_bitcast_fusion), kind=kOutput, calls=%fused_computation.6 | convolution fusion | flops 304087040 | bytes 858112 | tf_op jit(solution)/shard_map/dot_general | solution.py:141
  24.2 7.1 %fusion.11 = f32[16384]{0:T(1024)S(1)} fusion(f32[256,128]{1,0:T(8,128)S(1)} %reshape_reshape.3, s32[16384]{0:T(1024)S(1)} %get-tuple-element.68, s32[16384]{0:T(1024)S(1)} %get-tuple-element.67), kind=kOutput, calls=%fused_computation.15 | convolution fusion | flops 6452920320 | bytes 327680 | tf_op jit(solution)/shard_map/dot_general | solution.py:150
  33.2 3.9 %fusion.2 = f32[12,128]{1,0:T(8,128)S(1)} fusion(f32[12,16384]{1,0:T(8,128)S(1)} %bitcast.184, s32[16384]{0:T(1024)S(1)} %subtract_bitcast_fusion), kind=kOutput, calls=%fused_computation.5 | convolution fusion | flops 304087040 | bytes 858112 | tf_op jit(solution)/shard_map/dot_general | solution.py:166
  37.1 2.5 %fusion.48 = f32[1,1]{1,0:T(1,128)} fusion(pred[1,1]{1,0:T(4,128)(4,1)} %bitcast.13, f32[1,1]{1,0:T(1,128)} %bitcast.14, s32[]{:T(128)} %bitcast.15, f32[1,1]{1,0:T(1,128)} %bitcast.12), kind=kLoop, calls=%fused_computation.193 | loop fusion | flops 1 | bytes 17 | tf_op jit(solution)/shard_map/select.4
  39.6 1.4 %scatter.11 = f32[1,128]{1,0:T(1,128)S(1)} dynamic-update-slice(f32[1,128]{1,0:T(1,128)S(1)} %scatter.10, f32[1,1]{1,0:T(1,128)} %fusion.48, s32[]{:T(128)} %constant.150.clone.1, s32[]{:T(128)} %bitcast.15) | dynamic-update-slice | bytes 12 | tf_op jit(solution)/shard_map/scatter | solution.py:176
  41.1 12.4 %fusion = f32[256,128]{1,0:T(8,128)S(1)} fusion(f32[16384]{0:T(1024)S(1)} %get-tuple-element.52, s32[16384]{0:T(1024)S(1)} %get-tuple-element.67, pred[256,16384]{1,0:T(32,128)(4,1)} %iota_compare_fusion.14), kind=kOutput, calls=%fused_computation.2 | convolution fusion | flops 6446645248 | bytes 4456448 | tf_op jit(solution)/shard_map/dot_general | solution.py:175
  53.5 1.1 collective-permute-start.4
  54.8 2.0 %collective-permute-start.14 = (f32[3,3]{1,0:T(4,128)S(1)}, f32[3,3]{1,0:T(4,128)S(1)}, u32[]{:S(2)}, u32[]{:S(2)}) collective-permute-start(f32[3,3]{1,0:T(4,128)S(1)} %slice.250), channel_id=1, source_target_pairs={{0,1},{1,2},{2,3},{3,4},{4,5},{5,6},{6,7},{7,8},{8,9},{9,10},{10,1... | collective-permute-start | bytes 116 | tf_op jit(solution)/shard_map/ppermute | solution.py:13
  56.8 1.8 %collective-permute-start.6 = (f32[65,128]{1,0:T(8,128)S(1)}, f32[65,128]{1,0:T(8,128)S(1)}, u32[]{:S(2)}, u32[]{:S(2)}) collective-permute-start(f32[65,128]{1,0:T(8,128)S(1)} %get-tuple-element.82), channel_id=1, source_target_pairs={{0,1},{1,2},{2,3},{3,0},{4,5},{5,6},{6,7},{7,4},{8,9},{9,10},{10,1... | collective-permute-start | bytes 99848 | tf_op jit(solution)/shard_map/ppermute | solution.py:81
  58.6 1.5 %collective-permute-start.5 = (f32[65,128]{1,0:T(8,128)S(1)}, f32[65,128]{1,0:T(8,128)S(1)}, u32[]{:S(2)}, u32[]{:S(2)}) collective-permute-start(f32[65,128]{1,0:T(8,128)S(1)} %get-tuple-element.83), channel_id=1, source_target_pairs={{0,2},{1,3},{2,0},{3,1},{4,6},{5,7},{6,4},{7,5},{8,10},{9,11},{10,... | collective-permute-start | bytes 99848 | tf_op jit(solution)/shard_map/ppermute | solution.py:81
  60.1 2.5 %collective-permute-done.5 = f32[65,128]{1,0:T(8,128)S(1)} collective-permute-done((f32[65,128]{1,0:T(8,128)S(1)}, f32[65,128]{1,0:T(8,128)S(1)}, u32[]{:S(2)}, u32[]{:S(2)}) %collective-permute-start.5) | collective-permute-done | bytes 33312 | tf_op jit(solution)/shard_map/ppermute | solution.py:81
  62.6 4.6 %collective-permute-start.7 = (f32[65,128]{1,0:T(8,128)S(1)}, f32[65,128]{1,0:T(8,128)S(1)}, u32[]{:S(2)}, u32[]{:S(2)}) collective-permute-start(f32[65,128]{1,0:T(8,128)S(1)} %fusion.54), channel_id=1, source_target_pairs={{0,28},{4,0},{8,4},{12,8},{16,12},{20,16},{24,20},{28,24},{1,29},{... | collective-permute-start | bytes 99848 | tf_op jit(solution)/shard_map/ppermute | solution.py:50
  67.3 2.4 %collective-permute-start.11 = (f32[65,128]{1,0:T(8,128)S(1)}, f32[65,128]{1,0:T(8,128)S(1)}, u32[]{:S(2)}, u32[]{:S(2)}) collective-permute-start(f32[65,128]{1,0:T(8,128)S(1)} %fusion.54), channel_id=1, source_target_pairs={{0,12},{4,16},{8,20},{12,24},{16,28},{20,0},{24,4},{28,8},{1,13},{... | collective-permute-start | bytes 99848 | tf_op jit(solution)/shard_map/ppermute | solution.py:50
  69.7 2.8 %collective-permute-start.10 = (f32[65,128]{1,0:T(8,128)S(1)}, f32[65,128]{1,0:T(8,128)S(1)}, u32[]{:S(2)}, u32[]{:S(2)}) collective-permute-start(f32[65,128]{1,0:T(8,128)S(1)} %fusion.54), channel_id=1, source_target_pairs={{0,16},{4,20},{8,24},{12,28},{16,0},{20,4},{24,8},{28,12},{1,17},{... | collective-permute-start | bytes 99848 | tf_op jit(solution)/shard_map/ppermute | solution.py:50
  72.6 2.9 %collective-permute-start.8 = (f32[65,128]{1,0:T(8,128)S(1)}, f32[65,128]{1,0:T(8,128)S(1)}, u32[]{:S(2)}, u32[]{:S(2)}) collective-permute-start(f32[65,128]{1,0:T(8,128)S(1)} %fusion.54), channel_id=1, source_target_pairs={{0,24},{4,28},{8,0},{12,4},{16,8},{20,12},{24,16},{28,20},{1,25},{... | collective-permute-start | bytes 99848 | tf_op jit(solution)/shard_map/ppermute | solution.py:50
  75.5 1.6 %collective-permute-done.8 = f32[65,128]{1,0:T(8,128)S(1)} collective-permute-done((f32[65,128]{1,0:T(8,128)S(1)}, f32[65,128]{1,0:T(8,128)S(1)}, u32[]{:S(2)}, u32[]{:S(2)}) %collective-permute-start.8) | collective-permute-done | bytes 33312 | tf_op jit(solution)/shard_map/ppermute | solution.py:50
  77.9 4.1 %collective-permute-done.9 = f32[65,128]{1,0:T(8,128)S(1)} collective-permute-done((f32[65,128]{1,0:T(8,128)S(1)}, f32[65,128]{1,0:T(8,128)S(1)}, u32[]{:S(2)}, u32[]{:S(2)}) %collective-permute-start.9) | collective-permute-done | bytes 33312 | tf_op jit(solution)/shard_map/ppermute | solution.py:50
  90.4 2.7 %collective-permute-done.16 = f32[1,128]{1,0:T(1,128)S(1)} collective-permute-done((f32[1,128]{1,0:T(1,128)S(1)}, f32[1,128]{1,0:T(1,128)S(1)}, u32[]{:S(2)}, u32[]{:S(2)}) %collective-permute-start.16) | collective-permute-done | bytes 544 | tf_op jit(solution)/shard_map/ppermute | solution.py:50
  93.3 4.6 %collective-permute-start.18 = (f32[1,128]{1,0:T(1,128)S(1)}, f32[1,128]{1,0:T(1,128)S(1)}, u32[]{:S(2)}, u32[]{:S(2)}) collective-permute-start(f32[1,128]{1,0:T(1,128)S(1)} %fusion.52), channel_id=1, source_target_pairs={{0,28},{4,0},{8,4},{12,8},{16,12},{20,16},{24,20},{28,24},{1,29},{... | collective-permute-start | bytes 1544 | tf_op jit(solution)/shard_map/ppermute | solution.py:50
  97.8 3.5 %collective-permute-start.22 = (f32[1,128]{1,0:T(1,128)S(1)}, f32[1,128]{1,0:T(1,128)S(1)}, u32[]{:S(2)}, u32[]{:S(2)}) collective-permute-start(f32[1,128]{1,0:T(1,128)S(1)} %fusion.52), channel_id=1, source_target_pairs={{0,12},{4,16},{8,20},{12,24},{16,28},{20,0},{24,4},{28,8},{1,13},{... | collective-permute-start | bytes 1544 | tf_op jit(solution)/shard_map/ppermute | solution.py:50
  101.4 1.8 %collective-permute-start.21 = (f32[1,128]{1,0:T(1,128)S(1)}, f32[1,128]{1,0:T(1,128)S(1)}, u32[]{:S(2)}, u32[]{:S(2)}) collective-permute-start(f32[1,128]{1,0:T(1,128)S(1)} %fusion.52), channel_id=1, source_target_pairs={{0,16},{4,20},{8,24},{12,28},{16,0},{20,4},{24,8},{28,12},{1,17},{... | collective-permute-start | bytes 1544 | tf_op jit(solution)/shard_map/ppermute | solution.py:50
  103.1 2.9 %collective-permute-start.19 = (f32[1,128]{1,0:T(1,128)S(1)}, f32[1,128]{1,0:T(1,128)S(1)}, u32[]{:S(2)}, u32[]{:S(2)}) collective-permute-start(f32[1,128]{1,0:T(1,128)S(1)} %fusion.52), channel_id=1, source_target_pairs={{0,24},{4,28},{8,0},{12,4},{16,8},{20,12},{24,16},{28,20},{1,25},{... | collective-permute-start | bytes 1544 | tf_op jit(solution)/shard_map/ppermute | solution.py:50
  106.1 1.3 %collective-permute-done.19 = f32[1,128]{1,0:T(1,128)S(1)} collective-permute-done((f32[1,128]{1,0:T(1,128)S(1)}, f32[1,128]{1,0:T(1,128)S(1)}, u32[]{:S(2)}, u32[]{:S(2)}) %collective-permute-start.19) | collective-permute-done | bytes 544 | tf_op jit(solution)/shard_map/ppermute | solution.py:50
  107.4 1.9 %collective-permute-start.20 = (f32[1,128]{1,0:T(1,128)S(1)}, f32[1,128]{1,0:T(1,128)S(1)}, u32[]{:S(2)}, u32[]{:S(2)}) collective-permute-start(f32[1,128]{1,0:T(1,128)S(1)} %fusion.52), channel_id=1, source_target_pairs={{0,20},{4,24},{8,28},{12,0},{16,4},{20,8},{24,12},{28,16},{1,21},{... | collective-permute-start | bytes 1544 | tf_op jit(solution)/shard_map/ppermute | solution.py:50
  109.2 2.6 %collective-permute-done.20 = f32[1,128]{1,0:T(1,128)S(1)} collective-permute-done((f32[1,128]{1,0:T(1,128)S(1)}, f32[1,128]{1,0:T(1,128)S(1)}, u32[]{:S(2)}, u32[]{:S(2)}) %collective-permute-start.20) | collective-permute-done | bytes 544 | tf_op jit(solution)/shard_map/ppermute | solution.py:50
  (162 shorter events, 13.9 us)
Async XLA Ops:
  0.6 20.3 %copy-start.9 = (f32[3,128]{1,0:T(4,128)S(1)}, f32[3,128]{1,0:T(4,128)}, u32[]{:S(2)}) copy-start(f32[3,128]{1,0:T(4,128)} %param.34) | copy-start | bytes 4612
  0.7 23.3 %collective-permute-start.3 = (f32[2,4096]{1,0:T(2,128)}, f32[2,4096]{1,0:T(2,128)S(1)}, u32[]{:S(2)}, u32[]{:S(2)}) collective-permute-start(f32[2,4096]{1,0:T(2,128)} %param.35), channel_id=1, source_target_pairs={{0,1},{1,2},{2,3},{3,0},{4,5},{5,6},{6,7},{7,4},{8,9},{9,10},{10,1... | collective-permute-start | bytes 98312 | tf_op jit(solution)/shard_map/ppermute | solution.py:50
  1.2 22.7 %collective-permute-start.2 = (f32[2,4096]{1,0:T(2,128)}, f32[2,4096]{1,0:T(2,128)S(1)}, u32[]{:S(2)}, u32[]{:S(2)}) collective-permute-start(f32[2,4096]{1,0:T(2,128)} %param.35), channel_id=1, source_target_pairs={{0,2},{1,3},{2,0},{3,1},{4,6},{5,7},{6,4},{7,5},{8,10},{9,11},{10,... | collective-permute-start | bytes 98312 | tf_op jit(solution)/shard_map/ppermute | solution.py:50
  3.7 20.1 %collective-permute-start.1 = (f32[2,4096]{1,0:T(2,128)}, f32[2,4096]{1,0:T(2,128)S(1)}, u32[]{:S(2)}, u32[]{:S(2)}) collective-permute-start(f32[2,4096]{1,0:T(2,128)} %param.35), channel_id=1, source_target_pairs={{0,3},{1,0},{2,1},{3,2},{4,7},{5,4},{6,5},{7,6},{8,11},{9,8},{10,9... | collective-permute-start | bytes 98312 | tf_op jit(solution)/shard_map/ppermute | solution.py:50
  5.1 15.7 %collective-permute-start = (f32[3,3]{1,0:T(4,128)}, f32[3,3]{1,0:T(4,128)S(1)}, u32[]{:S(2)}, u32[]{:S(2)}) collective-permute-start(f32[3,3]{1,0:T(4,128)} %bitcast.185), channel_id=1, source_target_pairs={{1,0},{2,1},{3,2},{4,3},{5,4},{6,5},{7,6},{8,7},{9,8},{10,9},{11,1... | collective-permute-start | bytes 116 | tf_op jit(solution)/shard_map/ppermute | solution.py:13
  41.0 43.2 %copy-start.12 = (f32[5,128]{1,0:T(8,128)S(1)}, f32[5,128]{1,0:T(8,128)}, u32[]{:S(2)}) copy-start(f32[5,128]{1,0:T(8,128)} %param.30) | copy-start | bytes 7684
  41.0 43.8 %copy-start.4 = (f32[2,4096]{1,0:T(2,128)S(1)}, f32[2,4096]{1,0:T(2,128)}, u32[]{:S(2)}) copy-start(f32[2,4096]{1,0:T(2,128)} %param.32) | copy-start | bytes 98308
  41.0 45.2 %copy-start.13 = (f32[3,128]{1,0:T(4,128)S(1)}, f32[3,128]{1,0:T(4,128)}, u32[]{:S(2)}) copy-start(f32[3,128]{1,0:T(4,128)} %param.31) | copy-start | bytes 4612
  53.5 6.5 %collective-permute-start.4 = (f32[65,128]{1,0:T(8,128)S(1)}, f32[65,128]{1,0:T(8,128)S(1)}, u32[]{:S(2)}, u32[]{:S(2)}) collective-permute-start(f32[65,128]{1,0:T(8,128)S(1)} %get-tuple-element.84), channel_id=1, source_target_pairs={{0,3},{1,0},{2,1},{3,2},{4,7},{5,4},{6,5},{7,6},{8,11},{9,8},{10,9... | collective-permute-start | bytes 99848 | tf_op jit(solution)/shard_map/ppermute | solution.py:81
  54.8 12.5 %collective-permute-start.14 = (f32[3,3]{1,0:T(4,128)S(1)}, f32[3,3]{1,0:T(4,128)S(1)}, u32[]{:S(2)}, u32[]{:S(2)}) collective-permute-start(f32[3,3]{1,0:T(4,128)S(1)} %slice.250), channel_id=1, source_target_pairs={{0,1},{1,2},{2,3},{3,4},{4,5},{5,6},{6,7},{7,8},{8,9},{9,10},{10,1... | collective-permute-start | bytes 116 | tf_op jit(solution)/shard_map/ppermute | solution.py:13
  56.8 5.8 %collective-permute-start.6 = (f32[65,128]{1,0:T(8,128)S(1)}, f32[65,128]{1,0:T(8,128)S(1)}, u32[]{:S(2)}, u32[]{:S(2)}) collective-permute-start(f32[65,128]{1,0:T(8,128)S(1)} %get-tuple-element.82), channel_id=1, source_target_pairs={{0,1},{1,2},{2,3},{3,0},{4,5},{5,6},{6,7},{7,4},{8,9},{9,10},{10,1... | collective-permute-start | bytes 99848 | tf_op jit(solution)/shard_map/ppermute | solution.py:81
  58.6 4.0 %collective-permute-start.5 = (f32[65,128]{1,0:T(8,128)S(1)}, f32[65,128]{1,0:T(8,128)S(1)}, u32[]{:S(2)}, u32[]{:S(2)}) collective-permute-start(f32[65,128]{1,0:T(8,128)S(1)} %get-tuple-element.83), channel_id=1, source_target_pairs={{0,2},{1,3},{2,0},{3,1},{4,6},{5,7},{6,4},{7,5},{8,10},{9,11},{10,... | collective-permute-start | bytes 99848 | tf_op jit(solution)/shard_map/ppermute | solution.py:81
  62.6 9.9 %collective-permute-start.7 = (f32[65,128]{1,0:T(8,128)S(1)}, f32[65,128]{1,0:T(8,128)S(1)}, u32[]{:S(2)}, u32[]{:S(2)}) collective-permute-start(f32[65,128]{1,0:T(8,128)S(1)} %fusion.54), channel_id=1, source_target_pairs={{0,28},{4,0},{8,4},{12,8},{16,12},{20,16},{24,20},{28,24},{1,29},{... | collective-permute-start | bytes 99848 | tf_op jit(solution)/shard_map/ppermute | solution.py:50
  67.3 14.8 %collective-permute-start.13 = (f32[65,128]{1,0:T(8,128)S(1)}, f32[65,128]{1,0:T(8,128)S(1)}, u32[]{:S(2)}, u32[]{:S(2)}) collective-permute-start(f32[65,128]{1,0:T(8,128)S(1)} %fusion.54), channel_id=1, source_target_pairs={{0,4},{4,8},{8,12},{12,16},{16,20},{20,24},{24,28},{28,0},{1,5},{5... | collective-permute-start | bytes 99848 | tf_op jit(solution)/shard_map/ppermute | solution.py:50
  67.3 14.7 %collective-permute-start.12 = (f32[65,128]{1,0:T(8,128)S(1)}, f32[65,128]{1,0:T(8,128)S(1)}, u32[]{:S(2)}, u32[]{:S(2)}) collective-permute-start(f32[65,128]{1,0:T(8,128)S(1)} %fusion.54), channel_id=1, source_target_pairs={{0,8},{4,12},{8,16},{12,20},{16,24},{20,28},{24,0},{28,4},{1,9},{5... | collective-permute-start | bytes 99848 | tf_op jit(solution)/shard_map/ppermute | solution.py:50
  67.3 14.7 %collective-permute-start.11 = (f32[65,128]{1,0:T(8,128)S(1)}, f32[65,128]{1,0:T(8,128)S(1)}, u32[]{:S(2)}, u32[]{:S(2)}) collective-permute-start(f32[65,128]{1,0:T(8,128)S(1)} %fusion.54), channel_id=1, source_target_pairs={{0,12},{4,16},{8,20},{12,24},{16,28},{20,0},{24,4},{28,8},{1,13},{... | collective-permute-start | bytes 99848 | tf_op jit(solution)/shard_map/ppermute | solution.py:50
  69.7 12.2 %collective-permute-start.10 = (f32[65,128]{1,0:T(8,128)S(1)}, f32[65,128]{1,0:T(8,128)S(1)}, u32[]{:S(2)}, u32[]{:S(2)}) collective-permute-start(f32[65,128]{1,0:T(8,128)S(1)} %fusion.54), channel_id=1, source_target_pairs={{0,16},{4,20},{8,24},{12,28},{16,0},{20,4},{24,8},{28,12},{1,17},{... | collective-permute-start | bytes 99848 | tf_op jit(solution)/shard_map/ppermute | solution.py:50
  72.6 4.6 %collective-permute-start.8 = (f32[65,128]{1,0:T(8,128)S(1)}, f32[65,128]{1,0:T(8,128)S(1)}, u32[]{:S(2)}, u32[]{:S(2)}) collective-permute-start(f32[65,128]{1,0:T(8,128)S(1)} %fusion.54), channel_id=1, source_target_pairs={{0,24},{4,28},{8,0},{12,4},{16,8},{20,12},{24,16},{28,20},{1,25},{... | collective-permute-start | bytes 99848 | tf_op jit(solution)/shard_map/ppermute | solution.py:50
  77.1 4.9 %collective-permute-start.9 = (f32[65,128]{1,0:T(8,128)S(1)}, f32[65,128]{1,0:T(8,128)S(1)}, u32[]{:S(2)}, u32[]{:S(2)}) collective-permute-start(f32[65,128]{1,0:T(8,128)S(1)} %fusion.54), channel_id=1, source_target_pairs={{0,20},{4,24},{8,28},{12,0},{16,4},{20,8},{24,12},{28,16},{1,21},{... | collective-permute-start | bytes 99848 | tf_op jit(solution)/shard_map/ppermute | solution.py:50
  84.9 29.7 %copy-start.11 = (f32[5,128]{1,0:T(8,128)}, f32[5,128]{1,0:T(8,128)S(1)}, u32[]{:S(2)}) copy-start(f32[5,128]{1,0:T(8,128)S(1)} %get-tuple-element.51) | copy-start | bytes 7684
  85.6 29.0 %copy-start.3 = (f32[2,4096]{1,0:T(2,128)}, f32[2,4096]{1,0:T(2,128)S(1)}, u32[]{:S(2)}) copy-start(f32[2,4096]{1,0:T(2,128)S(1)} %get-tuple-element.47) | copy-start | bytes 98308
  87.1 27.5 %copy-start.14 = (f32[3,128]{1,0:T(4,128)}, f32[3,128]{1,0:T(4,128)S(1)}, u32[]{:S(2)}) copy-start(f32[3,128]{1,0:T(4,128)S(1)} %get-tuple-element.49) | copy-start | bytes 4612
  89.1 1.4 %collective-permute-start.15 = (f32[1,128]{1,0:T(1,128)S(1)}, f32[1,128]{1,0:T(1,128)S(1)}, u32[]{:S(2)}, u32[]{:S(2)}) collective-permute-start(f32[1,128]{1,0:T(1,128)S(1)} %scatter.14), channel_id=1, source_target_pairs={{0,3},{1,0},{2,1},{3,2},{4,7},{5,4},{6,5},{7,6},{8,11},{9,8},{10,9... | collective-permute-start | bytes 1544 | tf_op jit(solution)/shard_map/ppermute | solution.py:50
  89.1 4.0 %collective-permute-start.17 = (f32[1,128]{1,0:T(1,128)S(1)}, f32[1,128]{1,0:T(1,128)S(1)}, u32[]{:S(2)}, u32[]{:S(2)}) collective-permute-start(f32[1,128]{1,0:T(1,128)S(1)} %scatter.14), channel_id=1, source_target_pairs={{0,1},{1,2},{2,3},{3,0},{4,5},{5,6},{6,7},{7,4},{8,9},{9,10},{10,1... | collective-permute-start | bytes 1544 | tf_op jit(solution)/shard_map/ppermute | solution.py:50
  89.6 3.5 %collective-permute-start.16 = (f32[1,128]{1,0:T(1,128)S(1)}, f32[1,128]{1,0:T(1,128)S(1)}, u32[]{:S(2)}, u32[]{:S(2)}) collective-permute-start(f32[1,128]{1,0:T(1,128)S(1)} %scatter.14), channel_id=1, source_target_pairs={{0,2},{1,3},{2,0},{3,1},{4,6},{5,7},{6,4},{7,5},{8,10},{9,11},{10,... | collective-permute-start | bytes 1544 | tf_op jit(solution)/shard_map/ppermute | solution.py:50
  93.3 9.9 %collective-permute-start.18 = (f32[1,128]{1,0:T(1,128)S(1)}, f32[1,128]{1,0:T(1,128)S(1)}, u32[]{:S(2)}, u32[]{:S(2)}) collective-permute-start(f32[1,128]{1,0:T(1,128)S(1)} %fusion.52), channel_id=1, source_target_pairs={{0,28},{4,0},{8,4},{12,8},{16,12},{20,16},{24,20},{28,24},{1,29},{... | collective-permute-start | bytes 1544 | tf_op jit(solution)/shard_map/ppermute | solution.py:50
  97.8 14.0 %collective-permute-start.24 = (f32[1,128]{1,0:T(1,128)S(1)}, f32[1,128]{1,0:T(1,128)S(1)}, u32[]{:S(2)}, u32[]{:S(2)}) collective-permute-start(f32[1,128]{1,0:T(1,128)S(1)} %fusion.52), channel_id=1, source_target_pairs={{0,4},{4,8},{8,12},{12,16},{16,20},{20,24},{24,28},{28,0},{1,5},{5... | collective-permute-start | bytes 1544 | tf_op jit(solution)/shard_map/ppermute | solution.py:50
  97.8 14.0 %collective-permute-start.23 = (f32[1,128]{1,0:T(1,128)S(1)}, f32[1,128]{1,0:T(1,128)S(1)}, u32[]{:S(2)}, u32[]{:S(2)}) collective-permute-start(f32[1,128]{1,0:T(1,128)S(1)} %fusion.52), channel_id=1, source_target_pairs={{0,8},{4,12},{8,16},{12,20},{16,24},{20,28},{24,0},{28,4},{1,9},{5... | collective-permute-start | bytes 1544 | tf_op jit(solution)/shard_map/ppermute | solution.py:50
  97.8 14.0 %collective-permute-start.22 = (f32[1,128]{1,0:T(1,128)S(1)}, f32[1,128]{1,0:T(1,128)S(1)}, u32[]{:S(2)}, u32[]{:S(2)}) collective-permute-start(f32[1,128]{1,0:T(1,128)S(1)} %fusion.52), channel_id=1, source_target_pairs={{0,12},{4,16},{8,20},{12,24},{16,28},{20,0},{24,4},{28,8},{1,13},{... | collective-permute-start | bytes 1544 | tf_op jit(solution)/shard_map/ppermute | solution.py:50
  101.4 10.4 %collective-permute-start.21 = (f32[1,128]{1,0:T(1,128)S(1)}, f32[1,128]{1,0:T(1,128)S(1)}, u32[]{:S(2)}, u32[]{:S(2)}) collective-permute-start(f32[1,128]{1,0:T(1,128)S(1)} %fusion.52), channel_id=1, source_target_pairs={{0,16},{4,20},{8,24},{12,28},{16,0},{20,4},{24,8},{28,12},{1,17},{... | collective-permute-start | bytes 1544 | tf_op jit(solution)/shard_map/ppermute | solution.py:50
  103.1 4.2 %collective-permute-start.19 = (f32[1,128]{1,0:T(1,128)S(1)}, f32[1,128]{1,0:T(1,128)S(1)}, u32[]{:S(2)}, u32[]{:S(2)}) collective-permute-start(f32[1,128]{1,0:T(1,128)S(1)} %fusion.52), channel_id=1, source_target_pairs={{0,24},{4,28},{8,0},{12,4},{16,8},{20,12},{24,16},{28,20},{1,25},{... | collective-permute-start | bytes 1544 | tf_op jit(solution)/shard_map/ppermute | solution.py:50
  107.4 4.4 %collective-permute-start.20 = (f32[1,128]{1,0:T(1,128)S(1)}, f32[1,128]{1,0:T(1,128)S(1)}, u32[]{:S(2)}, u32[]{:S(2)}) collective-permute-start(f32[1,128]{1,0:T(1,128)S(1)} %fusion.52), channel_id=1, source_target_pairs={{0,20},{4,24},{8,28},{12,0},{16,4},{20,8},{24,12},{28,16},{1,21},{... | collective-permute-start | bytes 1544 | tf_op jit(solution)/shard_map/ppermute | solution.py:50
  (9 other events, 99.3 us)

commit v4 on v2

--- a/solution.py
+++ b/solution.py
@@ -78,9 +78,10 @@
     lane = 128
     rows = cal_size // lane
     src_rows, slots = obs_phase.shape
-    first_row = (lax.axis_index("tm") == 0).astype(jnp.float32)
 
-    cal_values = lax.all_gather(cal_dir, "cal", axis=0, tiled=True)
+    cal_both = lax.all_gather(jnp.stack([cal_dir, cal_res]), "cal", axis=1, tiled=True)
+    cal_values = cal_both[0]
+    cal_res_all = cal_both[1]
     edge_knots = passed_along(att_dir[:, :3], ("tm", "cal"), -1)
     att_ext = jnp.concatenate([att_dir, edge_knots], axis=1)
 
@@ -112,11 +113,6 @@
     response = live_mask * (y_src + y_att + y_cal)
     weighted = obs_weight * response
     curv_local = jnp.sum(weighted * response)
-    norm_local = (
-        jnp.sum(src_res * src_res)
-        + jnp.sum(att_res * att_res)
-        + first_row * jnp.sum(cal_res * cal_res)
-    )
     q_src = jnp.sum(src_design * weighted[None], axis=2)
 
     scaled = att_design * weighted[None]
@@ -131,25 +127,25 @@
 
     cal_weighted = flat(cal_design * weighted) * low_hot
     cal_term = lax.dot_general(high_hot, cal_weighted, (((1,), (1,)), ((), ())), precision=EXACT)
-    scalars = jnp.zeros((1, lane), jnp.float32).at[0, 0].set(norm_local).at[0, 1].set(curv_local)
-    q_cal, scalars = halving_sum(cal_term, scalars, "cal")
-    summed = doubling_sum(jnp.concatenate([q_cal, scalars], axis=0), "tm")
-    norm_now = summed[-1, 0]
-    curvature = summed[-1, 1]
-    q_cal = summed[:-1].reshape(blocks, col_width)
+    res_sq = jnp.sum(src_res * src_res) + jnp.sum(att_res * att_res)
+    res_q = jnp.sum(src_res * q_src) + jnp.sum(att_res * q_att)
+    q_sq = jnp.sum(q_src * q_src) + jnp.sum(q_att * q_att)
+    scalars = jnp.zeros((1, lane), jnp.float32)
+    scalars = scalars.at[0, 0].set(res_sq).at[0, 1].set(curv_local)
+    scalars = scalars.at[0, 2].set(res_q).at[0, 3].set(q_sq)
+    summed = doubling_sum(doubling_sum(jnp.concatenate([cal_term, scalars], axis=0), "cal"), "tm")
+    res_sq, curvature, res_q, q_sq = (summed[rows, k] for k in range(4))
+    q_cal_all = summed[:rows].reshape(all_blocks, col_width)
 
+    norm_now = res_sq + jnp.sum(cal_res_all * cal_res_all)
     step_len = norm_now / curvature
     new_src_res = src_res - step_len * q_src
     new_att_res = att_res - step_len * q_att
-    new_cal_res = cal_res - step_len * q_cal
-    next_local = (
-        jnp.sum(new_src_res * new_src_res)
-        + jnp.sum(new_att_res * new_att_res)
-        + first_row * jnp.sum(new_cal_res * new_cal_res)
-    )
-    norm_next = jnp.zeros((1, lane), jnp.float32).at[0, 0].set(next_local)
-    norm_next = doubling_sum(doubling_sum(norm_next, "cal"), "tm")[0, 0]
+    new_cal_all = cal_res_all - step_len * q_cal_all
+    kept = res_sq - step_len * (2.0 * res_q - step_len * q_sq)
+    norm_next = kept + jnp.sum(new_cal_all * new_cal_all)
     ratio = norm_next / norm_now
+    new_cal_res = lax.dynamic_slice_in_dim(new_cal_all, lax.axis_index("cal") * blocks, blocks, 0)
     return (
         new_src_res,
         new_att_res,

time: 99.7 us -> 101 us (1.013)
  local copies, waits for them, and re-layouts: 4.68 us -> 10.3 us
  matrix products: 26 us -> 22.1 us
  starting transfers between devices: 18 us -> 14.3 us
  between operations: 8.43 us -> 10.2 us
  other arithmetic: 18.1 us -> 19.2 us
    ppermute x10 -> x5, starting transfers between devices: 15.3 us -> 10.6 us  [exchanged(): return lax.ppermute(block, axis, [(i, i ^ distance) for i in devices])]
    another operation x3 -> x9, other arithmetic: 3.8 us -> 8.08 us
    dot_general x1, matrix products: 12.4 us -> 8.4 us  [local(): lax.dot_general(high_hot, cal_weighted, (((1,), (1,)), ((), ())), precisi...]
    reduce_sum x6 -> x4, other arithmetic: 6.05 us -> 2.72 us  [the longest x2 1.37 us: local(): q_sq = jnp.sum(q_src * q_src) + jnp.sum(q_att * q_att)]
    another operation x2 -> x6, local copies, waits for them, and re-layouts: 0.58 us -> 3.45 us
    scatter x3 -> x4, local copies, waits for them, and re-layouts: 1.54 us -> 4.19 us  [the longest x2 2.75 us: local(): scalars = scalars.at[0, 2].set(res_q).at[0, 3].set(q_sq)]
    ppermute x2, starting transfers between devices: 2.7 us -> 3.75 us  [passed_along(): return lax.ppermute(block, axis, route)]
    ppermute x10 -> x5, waiting for transfers between devices: 16.4 us -> 16.2 us  [exchanged(): return lax.ppermute(block, axis, [(i, i ^ distance) for i in devices])]
  transfers between devices with their start and end apart: 12 -> 7, of which waited for: 9 -> 5; matrix products, arithmetic and copies ran while one was open for 23% -> 29% of each run, Pallas kernels for 0% -> 0%
where the time goes in v4:
time: 101 us; the launch traced here: 100 us
  matrix products  22.1 us (22%)
  other arithmetic  19.2 us (19%)
  waiting for transfers between devices  16.2 us (16%)
  starting transfers between devices  14.3 us (14%)
  local copies, waits for them, and re-layouts  10.3 us (10%)
  between operations  10.2 us (10%)
  blocking collectives  7.84 us (8%)
    ppermute x5, waiting for transfers between devices, exchanged(): return lax.ppermute(block, axis, [(i, i ^ distance) for i in devices])  16.2 us
    ppermute x5, starting transfers between devices, exchanged(): return lax.ppermute(block, axis, [(i, i ^ distance) for i in devices])  10.6 us
    dot_general x1, matrix products, local(): lax.dot_general(high_hot, cal_weighted, (((1,), (1,)), ((), ())), precisi...  8.4 us
    another operation x8, other arithmetic  8.02 us
    all_gather x1, blocking collectives, local(): lax.all_gather(jnp.stack([cal_dir, cal_res]), 'cal', axis=1, tiled=True)  7.84 us
    dot_general x1, matrix products, local(): lax.dot_general(cal_table, high_hot, (((0,), (0,)), ((), ())), precision=...  7.11 us
    dot_general x1, other arithmetic, local(): lax.dot_general(high_hot, cal_weighted, (((1,), (1,)), ((), ())), precisi...  4.09 us
    dot_general x1, matrix products, local(): lax.dot_general(spread, knot_hot, (((1,), (1,)), ((), ())), precision=EXACT)  3.92 us
  transfers between devices with their start and end apart: 7, of which 5 were waited for; matrix products, arithmetic and copies ran while one was open for 29% of the time, Pallas kernels for 0%

profile of v4, /device:TPU:0, one launch (start us, length us, event | category | flops | bytes accessed | tf_op | source)
XLA Modules:
  0.0 100.2 jit_solution(6230862101835744385)
XLA Ops:
  0.6 1.3 %collective-permute-start = (f32[3,3]{1,0:T(4,128)}, f32[3,3]{1,0:T(4,128)S(1)}, u32[]{:S(2)}, u32[]{:S(2)}) collective-permute-start(f32[3,3]{1,0:T(4,128)} %bitcast.110), channel_id=1, source_target_pairs={{1,0},{2,1},{3,2},{4,3},{5,4},{6,5},{7,6},{8,7},{9,8},{10,9},{11,1... | collective-permute-start | bytes 116 | tf_op jit(solution)/shard_map/ppermute | solution.py:13
  2.6 0.7 constant_dynamic-update-slice_fusion.1
  3.9 0.7 and_reduce_fusion
  4.6 0.8 stack.45
  5.3 0.8 stack.44
  6.2 7.8 %all_gather.3 = f32[2,8,4096]{2,0,1:T(2,128)S(1)} all-gather(f32[2,2,4096]{2,0,1:T(2,128)S(1)} %pad_maximum_fusion.2), channel_id=1, replica_groups=mesh['tm'=8,'cal'=4] {'cal'}, dimensions={1}, use_global_device_ids=true | all-gather | bytes 327680 | tf_op jit(solution)/shard_map/all_gather | solution.py:82
  16.2 0.9 add_select_fusion
  17.1 4.1 %iota_compare_fusion.14 = pred[256,16384]{1,0:T(32,128)(4,1)} fusion(s32[16384]{0:T(1024)S(1)} %get-tuple-element.90), kind=kLoop, calls=%fused_computation.1.clone.clone.2 | loop fusion | flops 4194304 | bytes 4259840 | tf_op jit(solution)/shard_map/dot_general | solution.py:129
  21.2 7.1 %fusion.11 = f32[16384]{0:T(1024)S(1)} fusion(f32[256,128]{1,0:T(8,128)S(1)} %bitcast.109, s32[16384]{0:T(1024)S(1)} %get-tuple-element.90, s32[16384]{0:T(1024)S(1)} %get-tuple-element.89), kind=kOutput, calls=%fused_computation.15 | convolution fusion | flops 6452920320 | bytes 327680 | tf_op jit(solution)/shard_map/dot_general | solution.py:109
  28.7 2.7 %fusion.3 = f32[12,16384]{1,0:T(8,128)S(1)} fusion(f32[12,128]{1,0:T(8,128)S(1)} %reshape.278, s32[16384]{0:T(1024)S(1)} %subtract_bitcast_fusion), kind=kOutput, calls=%fused_computation.6 | convolution fusion | flops 304087040 | bytes 858112 | tf_op jit(solution)/shard_map/dot_general | solution.py:100
  32.9 3.9 %fusion.2 = f32[12,128]{1,0:T(8,128)S(1)} fusion(f32[12,16384]{1,0:T(8,128)S(1)} %bitcast.108, s32[16384]{0:T(1024)S(1)} %subtract_bitcast_fusion), kind=kOutput, calls=%fused_computation.5 | convolution fusion | flops 304087040 | bytes 858112 | tf_op jit(solution)/shard_map/dot_general | solution.py:120
  37.0 2.5 %collective-permute-start.1 = (f32[3,3]{1,0:T(4,128)S(1)}, f32[3,3]{1,0:T(4,128)S(1)}, u32[]{:S(2)}, u32[]{:S(2)}) collective-permute-start(f32[3,3]{1,0:T(4,128)S(1)} %slice.187), channel_id=1, source_target_pairs={{0,1},{1,2},{2,3},{3,4},{4,5},{5,6},{6,7},{7,8},{8,9},{9,10},{10,1... | collective-permute-start | bytes 116 | tf_op jit(solution)/shard_map/ppermute | solution.py:13
  40.7 8.4 %fusion = f32[256,128]{1,0:T(8,128)S(1)} fusion(f32[16384]{0:T(1024)S(1)} %get-tuple-element.72, s32[16384]{0:T(1024)S(1)} %get-tuple-element.89, pred[256,16384]{1,0:T(32,128)(4,1)S(1)} %copy-done), kind=kOutput, calls=%fused_computation.2 | convolution fusion | flops 6446645248 | bytes 4456448 | tf_op jit(solution)/shard_map/dot_general | solution.py:129
  49.2 0.8 multiply_reduce_fusion.7
  53.2 2.4 %fusion.37 = f32[1,1]{1,0:T(1,128)} fusion(pred[1,1]{1,0:T(4,128)(4,1)} %bitcast.10, f32[1,1]{1,0:T(1,128)} %bitcast.11, s32[]{:T(128)} %bitcast.12, f32[1,1]{1,0:T(1,128)} %bitcast.9), kind=kLoop, calls=%fused_computation.109 | loop fusion | flops 1 | bytes 17 | tf_op jit(solution)/shard_map/select.5
  55.7 1.4 %scatter.15 = f32[1,128]{1,0:T(1,128)S(1)} dynamic-update-slice(f32[1,128]{1,0:T(1,128)S(1)} %scatter.14, f32[1,1]{1,0:T(1,128)} %fusion.37, s32[]{:T(128)} %constant.146.clone.1, s32[]{:T(128)} %bitcast.12) | dynamic-update-slice | bytes 12 | tf_op jit(solution)/shard_map/scatter | solution.py:134
  57.1 1.8 %fusion.38 = f32[1,1]{1,0:T(1,128)} fusion(pred[1,1]{1,0:T(4,128)(4,1)} %bitcast.13, f32[1,1]{1,0:T(1,128)} %bitcast.18, f32[1,128]{1,0:T(1,128)S(1)} %scatter.15, s32[]{:T(128)} %bitcast.19), kind=kLoop, calls=%fused_computation.110 | loop fusion | flops 1 | bytes 17 | tf_op jit(solution)/shard_map/select.6
  58.8 1.3 %scatter.16 = f32[1,128]{1,0:T(1,128)S(1)} dynamic-update-slice(f32[1,128]{1,0:T(1,128)S(1)} %scatter.15, f32[1,1]{1,0:T(1,128)} %fusion.38, s32[]{:T(128)} %constant.146.clone.1, s32[]{:T(128)} %bitcast.19) | dynamic-update-slice | bytes 12 | tf_op jit(solution)/shard_map/scatter | solution.py:135
  61.5 1.9 %fusion.39 = f32[1,1]{1,0:T(1,128)} fusion(pred[1,1]{1,0:T(4,128)(4,1)} %bitcast.20, f32[1,1]{1,0:T(1,128)} %bitcast.21, f32[1,128]{1,0:T(1,128)S(1)} %scatter.16, s32[]{:T(128)} %bitcast.22), kind=kLoop, calls=%fused_computation.111 | loop fusion | flops 1 | bytes 17 | tf_op jit(solution)/shard_map/select.7
  63.3 1.4 %scatter.19 = f32[1,128]{1,0:T(1,128)S(1)} dynamic-update-slice(f32[1,128]{1,0:T(1,128)S(1)} %scatter.16, f32[1,1]{1,0:T(1,128)} %fusion.39, s32[]{:T(128)} %constant.146.clone.1, s32[]{:T(128)} %bitcast.22) | dynamic-update-slice | bytes 12 | tf_op jit(solution)/shard_map/scatter | solution.py:135
  64.8 1.6 %collective-permute-start.2 = (f32[257,128]{1,0:T(8,128)S(1)}, f32[257,128]{1,0:T(8,128)S(1)}, u32[]{:S(2)}, u32[]{:S(2)}) collective-permute-start(f32[257,128]{1,0:T(8,128)S(1)} %pad_maximum_fusion.1), channel_id=1, source_target_pairs={{0,1},{1,0},{2,3},{3,2},{4,5},{5,4},{6,7},{7,6},{8,9},{9,8},{10,11... | collective-permute-start | bytes 394760 | tf_op jit(solution)/shard_map/ppermute | solution.py:18
  66.4 1.0 collective-permute-done.2
  67.4 2.2 %collective-permute-start.3 = (f32[257,128]{1,0:T(8,128)S(1)}, f32[257,128]{1,0:T(8,128)S(1)}, u32[]{:S(2)}, u32[]{:S(2)}) collective-permute-start(f32[257,128]{1,0:T(8,128)S(1)} %fusion.32), channel_id=1, source_target_pairs={{0,2},{1,3},{2,0},{3,1},{4,6},{5,7},{6,4},{7,5},{8,10},{9,11},{10,... | collective-permute-start | bytes 394760 | tf_op jit(solution)/shard_map/ppermute | solution.py:18
  69.6 4.1 %collective-permute-done.3 = f32[257,128]{1,0:T(8,128)S(1)} collective-permute-done((f32[257,128]{1,0:T(8,128)S(1)}, f32[257,128]{1,0:T(8,128)S(1)}, u32[]{:S(2)}, u32[]{:S(2)}) %collective-permute-start.3) | collective-permute-done | bytes 131616 | tf_op jit(solution)/shard_map/ppermute | solution.py:18
  73.7 2.5 %collective-permute-start.4 = (f32[257,128]{1,0:T(8,128)S(1)}, f32[257,128]{1,0:T(8,128)S(1)}, u32[]{:S(2)}, u32[]{:S(2)}) collective-permute-start(f32[257,128]{1,0:T(8,128)S(1)} %add.146), channel_id=1, source_target_pairs={{0,4},{4,0},{8,12},{12,8},{16,20},{20,16},{24,28},{28,24},{1,5},{5... | collective-permute-start | bytes 394760 | tf_op jit(solution)/shard_map/ppermute | solution.py:18
  76.2 3.5 %collective-permute-done.4 = f32[257,128]{1,0:T(8,128)S(1)} collective-permute-done((f32[257,128]{1,0:T(8,128)S(1)}, f32[257,128]{1,0:T(8,128)S(1)}, u32[]{:S(2)}, u32[]{:S(2)}) %collective-permute-start.4) | collective-permute-done | bytes 131616 | tf_op jit(solution)/shard_map/ppermute | solution.py:18
  79.8 1.6 %collective-permute-start.5 = (f32[257,128]{1,0:T(8,128)S(1)}, f32[257,128]{1,0:T(8,128)S(1)}, u32[]{:S(2)}, u32[]{:S(2)}) collective-permute-start(f32[257,128]{1,0:T(8,128)S(1)} %add.147), channel_id=1, source_target_pairs={{0,8},{4,12},{8,0},{12,4},{16,24},{20,28},{24,16},{28,20},{1,9},{5... | collective-permute-start | bytes 394760 | tf_op jit(solution)/shard_map/ppermute | solution.py:18
  81.4 3.4 %collective-permute-done.5 = f32[257,128]{1,0:T(8,128)S(1)} collective-permute-done((f32[257,128]{1,0:T(8,128)S(1)}, f32[257,128]{1,0:T(8,128)S(1)}, u32[]{:S(2)}, u32[]{:S(2)}) %collective-permute-start.5) | collective-permute-done | bytes 131616 | tf_op jit(solution)/shard_map/ppermute | solution.py:18
  84.9 2.6 %collective-permute-start.6 = (f32[257,128]{1,0:T(8,128)S(1)}, f32[257,128]{1,0:T(8,128)S(1)}, u32[]{:S(2)}, u32[]{:S(2)}) collective-permute-start(f32[257,128]{1,0:T(8,128)S(1)} %add.148), channel_id=1, source_target_pairs={{0,16},{4,20},{8,24},{12,28},{16,0},{20,4},{24,8},{28,12},{1,17},{... | collective-permute-start | bytes 394760 | tf_op jit(solution)/shard_map/ppermute | solution.py:18
  87.5 0.7 fusion.16
  88.2 4.1 %collective-permute-done.6 = f32[257,128]{1,0:T(8,128)S(1)} collective-permute-done((f32[257,128]{1,0:T(8,128)S(1)}, f32[257,128]{1,0:T(8,128)S(1)}, u32[]{:S(2)}, u32[]{:S(2)}) %collective-permute-start.6) | collective-permute-done | bytes 131616 | tf_op jit(solution)/shard_map/ppermute | solution.py:18
  96.9 0.7 multiply_reduce_fusion.2
  (72 shorter events, 9.2 us)
Async XLA Ops:
  0.6 28.0 %collective-permute-start = (f32[3,3]{1,0:T(4,128)}, f32[3,3]{1,0:T(4,128)S(1)}, u32[]{:S(2)}, u32[]{:S(2)}) collective-permute-start(f32[3,3]{1,0:T(4,128)} %bitcast.110), channel_id=1, source_target_pairs={{1,0},{2,1},{3,2},{4,3},{5,4},{6,5},{7,6},{8,7},{9,8},{10,9},{11,1... | collective-permute-start | bytes 116 | tf_op jit(solution)/shard_map/ppermute | solution.py:13
  21.2 7.1 %copy-start.1 = (f32[5,128,128]{2,1,0:T(8,128)S(1)}, f32[5,128,128]{2,1,0:T(8,128)}, u32[]{:S(2)}) copy-start(f32[5,128,128]{2,1,0:T(8,128)} %param.23) | copy-start | bytes 983044
  21.2 7.1 %copy-start.9 = (f32[5,128]{1,0:T(8,128)S(1)}, f32[5,128]{1,0:T(8,128)}, u32[]{:S(2)}) copy-start(f32[5,128]{1,0:T(8,128)} %param.35) | copy-start | bytes 7684
  21.2 7.4 %copy-start.4 = (s32[128,128]{1,0:T(8,128)S(1)}, s32[128,128]{1,0:T(8,128)}, u32[]{:S(2)}) copy-start(s32[128,128]{1,0:T(8,128)} %param.28) | copy-start | bytes 196612
  21.2 7.5 %copy-start.8 = (f32[3,128]{1,0:T(4,128)S(1)}, f32[3,128]{1,0:T(4,128)}, u32[]{:S(2)}) copy-start(f32[3,128]{1,0:T(4,128)} %param.36) | copy-start | bytes 4612
  28.4 3.3 %copy-start.2 = (f32[3,128,128]{2,1,0:T(8,128)S(1)}, f32[3,128,128]{2,1,0:T(8,128)}, u32[]{:S(2)}) copy-start(f32[3,128,128]{2,1,0:T(8,128)} %param.24) | copy-start | bytes 589828
  28.4 3.3 %copy-start.5 = (f32[128,128]{1,0:T(8,128)S(1)}, f32[128,128]{1,0:T(8,128)}, u32[]{:S(2)}) copy-start(f32[128,128]{1,0:T(8,128)} %param.26) | copy-start | bytes 196612
  28.4 3.3 %copy-start.6 = (f32[128,128]{1,0:T(8,128)S(1)}, f32[128,128]{1,0:T(8,128)}, u32[]{:S(2)}) copy-start(f32[128,128]{1,0:T(8,128)} %param.27) | copy-start | bytes 196612
  28.4 3.3 %copy-start.7 = (f32[128,128]{1,0:T(8,128)S(1)}, f32[128,128]{1,0:T(8,128)}, u32[]{:S(2)}) copy-start(f32[128,128]{1,0:T(8,128)} %param.25) | copy-start | bytes 196612
  28.4 3.3 %copy-start.12 = (s32[128]{0:T(128)S(1)}, s32[128]{0:T(128)}, u32[]{:S(2)}) copy-start(s32[128]{0:T(128)} %param.31) | copy-start | bytes 1540
  32.1 8.0 %copy-start.10 = (f32[5,128]{1,0:T(8,128)S(1)}, f32[5,128]{1,0:T(8,128)}, u32[]{:S(2)}) copy-start(f32[5,128]{1,0:T(8,128)} %param.32) | copy-start | bytes 7684
  32.1 8.6 %copy-start = (pred[256,16384]{1,0:T(32,128)(4,1)S(1)}, pred[256,16384]{1,0:T(32,128)(4,1)}, u32[]{:S(2)}) copy-start(pred[256,16384]{1,0:T(32,128)(4,1)} %iota_compare_fusion.14) | copy-start | bytes 12582916
  37.0 12.1 %collective-permute-start.1 = (f32[3,3]{1,0:T(4,128)S(1)}, f32[3,3]{1,0:T(4,128)S(1)}, u32[]{:S(2)}, u32[]{:S(2)}) collective-permute-start(f32[3,3]{1,0:T(4,128)S(1)} %slice.187), channel_id=1, source_target_pairs={{0,1},{1,2},{2,3},{3,4},{4,5},{5,6},{6,7},{7,8},{8,9},{9,10},{10,1... | collective-permute-start | bytes 116 | tf_op jit(solution)/shard_map/ppermute | solution.py:13
  40.7 8.4 %copy-start.11 = (f32[3,128]{1,0:T(4,128)S(1)}, f32[3,128]{1,0:T(4,128)}, u32[]{:S(2)}) copy-start(f32[3,128]{1,0:T(4,128)} %param.33) | copy-start | bytes 4612
  40.7 58.8 %copy-start.3 = (f32[2,4096]{1,0:T(2,128)S(1)}, f32[2,4096]{1,0:T(2,128)}, u32[]{:S(2)}) copy-start(f32[2,4096]{1,0:T(2,128)} %param.37) | copy-start | bytes 98308
  64.8 2.6 %collective-permute-start.2 = (f32[257,128]{1,0:T(8,128)S(1)}, f32[257,128]{1,0:T(8,128)S(1)}, u32[]{:S(2)}, u32[]{:S(2)}) collective-permute-start(f32[257,128]{1,0:T(8,128)S(1)} %pad_maximum_fusion.1), channel_id=1, source_target_pairs={{0,1},{1,0},{2,3},{3,2},{4,5},{5,4},{6,7},{7,6},{8,9},{9,8},{10,11... | collective-permute-start | bytes 394760 | tf_op jit(solution)/shard_map/ppermute | solution.py:18
  67.4 6.3 %collective-permute-start.3 = (f32[257,128]{1,0:T(8,128)S(1)}, f32[257,128]{1,0:T(8,128)S(1)}, u32[]{:S(2)}, u32[]{:S(2)}) collective-permute-start(f32[257,128]{1,0:T(8,128)S(1)} %fusion.32), channel_id=1, source_target_pairs={{0,2},{1,3},{2,0},{3,1},{4,6},{5,7},{6,4},{7,5},{8,10},{9,11},{10,... | collective-permute-start | bytes 394760 | tf_op jit(solution)/shard_map/ppermute | solution.py:18
  73.7 6.0 %collective-permute-start.4 = (f32[257,128]{1,0:T(8,128)S(1)}, f32[257,128]{1,0:T(8,128)S(1)}, u32[]{:S(2)}, u32[]{:S(2)}) collective-permute-start(f32[257,128]{1,0:T(8,128)S(1)} %add.146), channel_id=1, source_target_pairs={{0,4},{4,0},{8,12},{12,8},{16,20},{20,16},{24,28},{28,24},{1,5},{5... | collective-permute-start | bytes 394760 | tf_op jit(solution)/shard_map/ppermute | solution.py:18
  79.8 5.1 %collective-permute-start.5 = (f32[257,128]{1,0:T(8,128)S(1)}, f32[257,128]{1,0:T(8,128)S(1)}, u32[]{:S(2)}, u32[]{:S(2)}) collective-permute-start(f32[257,128]{1,0:T(8,128)S(1)} %add.147), channel_id=1, source_target_pairs={{0,8},{4,12},{8,0},{12,4},{16,24},{20,28},{24,16},{28,20},{1,9},{5... | collective-permute-start | bytes 394760 | tf_op jit(solution)/shard_map/ppermute | solution.py:18
  84.9 7.4 %collective-permute-start.6 = (f32[257,128]{1,0:T(8,128)S(1)}, f32[257,128]{1,0:T(8,128)S(1)}, u32[]{:S(2)}, u32[]{:S(2)}) collective-permute-start(f32[257,128]{1,0:T(8,128)S(1)} %add.148), channel_id=1, source_target_pairs={{0,16},{4,20},{8,24},{12,28},{16,0},{20,4},{24,8},{28,12},{1,17},{... | collective-permute-start | bytes 394760 | tf_op jit(solution)/shard_map/ppermute | solution.py:18

commit v5 on v4

--- a/solution.py
+++ b/solution.py
@@ -130,9 +130,8 @@
     res_sq = jnp.sum(src_res * src_res) + jnp.sum(att_res * att_res)
     res_q = jnp.sum(src_res * q_src) + jnp.sum(att_res * q_att)
     q_sq = jnp.sum(q_src * q_src) + jnp.sum(q_att * q_att)
-    scalars = jnp.zeros((1, lane), jnp.float32)
-    scalars = scalars.at[0, 0].set(res_sq).at[0, 1].set(curv_local)
-    scalars = scalars.at[0, 2].set(res_q).at[0, 3].set(q_sq)
+    scalars = jnp.stack([res_sq, curv_local, res_q, q_sq])
+    scalars = jnp.concatenate([scalars, jnp.zeros((lane - 4,), jnp.float32)]).reshape(1, lane)
     summed = doubling_sum(doubling_sum(jnp.concatenate([cal_term, scalars], axis=0), "cal"), "tm")
     res_sq, curvature, res_q, q_sq = (summed[rows, k] for k in range(4))
     q_cal_all = summed[:rows].reshape(all_blocks, col_width)

time: 101 us -> 86.5 us (0.86)
  other arithmetic: 19.2 us -> 11.1 us
  local copies, waits for them, and re-layouts: 10.3 us -> 4.93 us
    another operation x8 -> x0, other arithmetic: 8.02 us -> none
    scatter x4 -> x0, local copies, waits for them, and re-layouts: 4.19 us -> none  [the longest x2 2.75 us: local(): scalars = scalars.at[0, 2].set(res_q).at[0, 3].set(q_sq)]
    another operation x4 -> x0, local copies, waits for them, and re-layouts: 1.88 us -> none
where the time goes in v5:
time: 86.5 us; the launch traced here: 86 us
  matrix products  22.1 us (26%)
  waiting for transfers between devices  16.2 us (19%)
  starting transfers between devices  14.3 us (17%)
  other arithmetic  11.1 us (13%)
  between operations  9.51 us (11%)
  blocking collectives  7.84 us (9%)
  local copies, waits for them, and re-layouts  4.93 us (6%)
    ppermute x5, waiting for transfers between devices, exchanged(): return lax.ppermute(block, axis, [(i, i ^ distance) for i in devices])  16.2 us
    ppermute x5, starting transfers between devices, exchanged(): return lax.ppermute(block, axis, [(i, i ^ distance) for i in devices])  10.6 us
    dot_general x1, matrix products, local(): lax.dot_general(high_hot, cal_weighted, (((1,), (1,)), ((), ())), precisi...  8.4 us
    all_gather x1, blocking collectives, local(): lax.all_gather(jnp.stack([cal_dir, cal_res]), 'cal', axis=1, tiled=True)  7.84 us
    dot_general x1, matrix products, local(): lax.dot_general(cal_table, high_hot, (((0,), (0,)), ((), ())), precision=...  7.11 us
    dot_general x1, other arithmetic, local(): lax.dot_general(high_hot, cal_weighted, (((1,), (1,)), ((), ())), precisi...  4.09 us
    dot_general x1, matrix products, local(): lax.dot_general(spread, knot_hot, (((1,), (1,)), ((), ())), precision=EXACT)  3.92 us
    ppermute x2, starting transfers between devices, passed_along(): return lax.ppermute(block, axis, route)  3.75 us
  transfers between devices with their start and end apart: 7, of which 5 were waited for; matrix products, arithmetic and copies ran while one was open for 29% of the time, Pallas kernels for 0%

profile of v5, /device:TPU:0, one launch (start us, length us, event | category | flops | bytes accessed | tf_op | source)
XLA Modules:
  0.0 86.0 jit_solution(17792354262676630622)
XLA Ops:
  0.6 1.3 %collective-permute-start = (f32[3,3]{1,0:T(4,128)}, f32[3,3]{1,0:T(4,128)S(1)}, u32[]{:S(2)}, u32[]{:S(2)}) collective-permute-start(f32[3,3]{1,0:T(4,128)} %bitcast.105), channel_id=1, source_target_pairs={{1,0},{2,1},{3,2},{4,3},{5,4},{6,5},{7,6},{8,7},{9,8},{10,9},{11,1... | collective-permute-start | bytes 116 | tf_op jit(solution)/shard_map/ppermute | solution.py:13
  1.9 0.7 constant_dynamic-update-slice_fusion.1
  2.6 0.8 stack.57
  3.4 0.8 stack.56
  4.3 7.8 %all_gather.3 = f32[2,8,4096]{2,0,1:T(2,128)S(1)} all-gather(f32[2,2,4096]{2,0,1:T(2,128)S(1)} %pad_maximum_fusion.2), channel_id=1, replica_groups=mesh['tm'=8,'cal'=4] {'cal'}, dimensions={1}, use_global_device_ids=true | all-gather | bytes 327680 | tf_op jit(solution)/shard_map/all_gather | solution.py:82
  12.4 0.9 %add_select_fusion = (s32[16384]{0:T(1024)S(1)}, s32[16384]{0:T(1024)S(1)}) fusion(s32[128,128]{1,0:T(8,128)} %param.22, s32[128,128]{1,0:T(8,128)} %param.21), kind=kLoop, calls=%fused_computation.42 | loop fusion | flops 344064 | bytes 262144 | tf_op jit(solution)/shard_map/jit(remainder)/select_n | solution.py:107
  13.3 4.1 %iota_compare_fusion.14 = pred[256,16384]{1,0:T(32,128)(4,1)} fusion(s32[16384]{0:T(1024)S(1)} %get-tuple-element.42), kind=kLoop, calls=%fused_computation.1.clone.clone.2 | loop fusion | flops 4194304 | bytes 4259840 | tf_op jit(solution)/shard_map/dot_general | solution.py:129
  17.4 7.1 %fusion.11 = f32[16384]{0:T(1024)S(1)} fusion(f32[256,128]{1,0:T(8,128)S(1)} %bitcast.104, s32[16384]{0:T(1024)S(1)} %get-tuple-element.42, s32[16384]{0:T(1024)S(1)} %get-tuple-element.41), kind=kOutput, calls=%fused_computation.15 | convolution fusion | flops 6452920320 | bytes 327680 | tf_op jit(solution)/shard_map/dot_general | solution.py:109
  24.9 2.7 %fusion.3 = f32[12,16384]{1,0:T(8,128)S(1)} fusion(f32[12,128]{1,0:T(8,128)S(1)} %reshape.149, s32[16384]{0:T(1024)S(1)} %subtract_bitcast_fusion), kind=kOutput, calls=%fused_computation.6 | convolution fusion | flops 304087040 | bytes 858112 | tf_op jit(solution)/shard_map/dot_general | solution.py:100
  28.4 0.6 copy.26
  29.1 3.9 %fusion.2 = f32[12,128]{1,0:T(8,128)S(1)} fusion(f32[12,16384]{1,0:T(8,128)S(1)} %bitcast.103, s32[16384]{0:T(1024)S(1)} %subtract_bitcast_fusion), kind=kOutput, calls=%fused_computation.5 | convolution fusion | flops 304087040 | bytes 858112 | tf_op jit(solution)/shard_map/dot_general | solution.py:120
  33.2 2.5 %collective-permute-start.1 = (f32[3,3]{1,0:T(4,128)S(1)}, f32[3,3]{1,0:T(4,128)S(1)}, u32[]{:S(2)}, u32[]{:S(2)}) collective-permute-start(f32[3,3]{1,0:T(4,128)S(1)} %slice.109), channel_id=1, source_target_pairs={{0,1},{1,2},{2,3},{3,4},{4,5},{5,6},{6,7},{7,8},{8,9},{9,10},{10,1... | collective-permute-start | bytes 116 | tf_op jit(solution)/shard_map/ppermute | solution.py:13
  35.6 0.6 multiply_reduce_fusion.3
  36.3 0.6 multiply_reduce_fusion.4
  36.9 8.4 %fusion = f32[256,128]{1,0:T(8,128)S(1)} fusion(f32[16384]{0:T(1024)S(1)} %get-tuple-element.24, s32[16384]{0:T(1024)S(1)} %get-tuple-element.41, pred[256,16384]{1,0:T(32,128)(4,1)S(1)} %copy-done), kind=kOutput, calls=%fused_computation.2 | convolution fusion | flops 6446645248 | bytes 4456448 | tf_op jit(solution)/shard_map/dot_general | solution.py:129
  45.3 0.7 multiply_reduce_fusion.7
  49.9 0.7 concatenate.14
  50.6 1.6 %collective-permute-start.2 = (f32[257,128]{1,0:T(8,128)S(1)}, f32[257,128]{1,0:T(8,128)S(1)}, u32[]{:S(2)}, u32[]{:S(2)}) collective-permute-start(f32[257,128]{1,0:T(8,128)S(1)} %pad_maximum_fusion.1), channel_id=1, source_target_pairs={{0,1},{1,0},{2,3},{3,2},{4,5},{5,4},{6,7},{7,6},{8,9},{9,8},{10,11... | collective-permute-start | bytes 394760 | tf_op jit(solution)/shard_map/ppermute | solution.py:18
  52.2 1.0 %collective-permute-done.2 = f32[257,128]{1,0:T(8,128)S(1)} collective-permute-done((f32[257,128]{1,0:T(8,128)S(1)}, f32[257,128]{1,0:T(8,128)S(1)}, u32[]{:S(2)}, u32[]{:S(2)}) %collective-permute-start.2) | collective-permute-done | bytes 131616 | tf_op jit(solution)/shard_map/ppermute | solution.py:18
  53.2 2.2 %collective-permute-start.3 = (f32[257,128]{1,0:T(8,128)S(1)}, f32[257,128]{1,0:T(8,128)S(1)}, u32[]{:S(2)}, u32[]{:S(2)}) collective-permute-start(f32[257,128]{1,0:T(8,128)S(1)} %fusion.32), channel_id=1, source_target_pairs={{0,2},{1,3},{2,0},{3,1},{4,6},{5,7},{6,4},{7,5},{8,10},{9,11},{10,... | collective-permute-start | bytes 394760 | tf_op jit(solution)/shard_map/ppermute | solution.py:18
  55.4 4.1 %collective-permute-done.3 = f32[257,128]{1,0:T(8,128)S(1)} collective-permute-done((f32[257,128]{1,0:T(8,128)S(1)}, f32[257,128]{1,0:T(8,128)S(1)}, u32[]{:S(2)}, u32[]{:S(2)}) %collective-permute-start.3) | collective-permute-done | bytes 131616 | tf_op jit(solution)/shard_map/ppermute | solution.py:18
  59.5 2.5 %collective-permute-start.4 = (f32[257,128]{1,0:T(8,128)S(1)}, f32[257,128]{1,0:T(8,128)S(1)}, u32[]{:S(2)}, u32[]{:S(2)}) collective-permute-start(f32[257,128]{1,0:T(8,128)S(1)} %add.136), channel_id=1, source_target_pairs={{0,4},{4,0},{8,12},{12,8},{16,20},{20,16},{24,28},{28,24},{1,5},{5... | collective-permute-start | bytes 394760 | tf_op jit(solution)/shard_map/ppermute | solution.py:18
  62.0 3.5 %collective-permute-done.4 = f32[257,128]{1,0:T(8,128)S(1)} collective-permute-done((f32[257,128]{1,0:T(8,128)S(1)}, f32[257,128]{1,0:T(8,128)S(1)}, u32[]{:S(2)}, u32[]{:S(2)}) %collective-permute-start.4) | collective-permute-done | bytes 131616 | tf_op jit(solution)/shard_map/ppermute | solution.py:18
  65.6 1.6 %collective-permute-start.5 = (f32[257,128]{1,0:T(8,128)S(1)}, f32[257,128]{1,0:T(8,128)S(1)}, u32[]{:S(2)}, u32[]{:S(2)}) collective-permute-start(f32[257,128]{1,0:T(8,128)S(1)} %add.137), channel_id=1, source_target_pairs={{0,8},{4,12},{8,0},{12,4},{16,24},{20,28},{24,16},{28,20},{1,9},{5... | collective-permute-start | bytes 394760 | tf_op jit(solution)/shard_map/ppermute | solution.py:18
  67.2 3.4 %collective-permute-done.5 = f32[257,128]{1,0:T(8,128)S(1)} collective-permute-done((f32[257,128]{1,0:T(8,128)S(1)}, f32[257,128]{1,0:T(8,128)S(1)}, u32[]{:S(2)}, u32[]{:S(2)}) %collective-permute-start.5) | collective-permute-done | bytes 131616 | tf_op jit(solution)/shard_map/ppermute | solution.py:18
  70.7 2.7 %collective-permute-start.6 = (f32[257,128]{1,0:T(8,128)S(1)}, f32[257,128]{1,0:T(8,128)S(1)}, u32[]{:S(2)}, u32[]{:S(2)}) collective-permute-start(f32[257,128]{1,0:T(8,128)S(1)} %add.138), channel_id=1, source_target_pairs={{0,16},{4,20},{8,24},{12,28},{16,0},{20,4},{24,8},{28,12},{1,17},{... | collective-permute-start | bytes 394760 | tf_op jit(solution)/shard_map/ppermute | solution.py:18
  73.3 0.7 fusion.16
  74.0 4.1 %collective-permute-done.6 = f32[257,128]{1,0:T(8,128)S(1)} collective-permute-done((f32[257,128]{1,0:T(8,128)S(1)}, f32[257,128]{1,0:T(8,128)S(1)}, u32[]{:S(2)}, u32[]{:S(2)}) %collective-permute-start.6) | collective-permute-done | bytes 131616 | tf_op jit(solution)/shard_map/ppermute | solution.py:18
  82.7 0.7 multiply_reduce_fusion.2
  84.1 0.6 multiply_add_fusion.2
  84.7 0.7 multiply_add_fusion.3
  85.3 0.7 multiply_add_fusion.1
  (58 shorter events, 2.3 us)
Async XLA Ops:
  0.6 24.2 %collective-permute-start = (f32[3,3]{1,0:T(4,128)}, f32[3,3]{1,0:T(4,128)S(1)}, u32[]{:S(2)}, u32[]{:S(2)}) collective-permute-start(f32[3,3]{1,0:T(4,128)} %bitcast.105), channel_id=1, source_target_pairs={{1,0},{2,1},{3,2},{4,3},{5,4},{6,5},{7,6},{8,7},{9,8},{10,9},{11,1... | collective-permute-start | bytes 116 | tf_op jit(solution)/shard_map/ppermute | solution.py:13
  17.4 7.1 %copy-start.1 = (f32[5,128,128]{2,1,0:T(8,128)S(1)}, f32[5,128,128]{2,1,0:T(8,128)}, u32[]{:S(2)}) copy-start(f32[5,128,128]{2,1,0:T(8,128)} %param.15) | copy-start | bytes 983044
  17.4 7.1 %copy-start.9 = (f32[5,128]{1,0:T(8,128)S(1)}, f32[5,128]{1,0:T(8,128)}, u32[]{:S(2)}) copy-start(f32[5,128]{1,0:T(8,128)} %param.27) | copy-start | bytes 7684
  17.4 7.4 %copy-start.4 = (s32[128,128]{1,0:T(8,128)S(1)}, s32[128,128]{1,0:T(8,128)}, u32[]{:S(2)}) copy-start(s32[128,128]{1,0:T(8,128)} %param.20) | copy-start | bytes 196612
  17.4 7.5 %copy-start.8 = (f32[3,128]{1,0:T(4,128)S(1)}, f32[3,128]{1,0:T(4,128)}, u32[]{:S(2)}) copy-start(f32[3,128]{1,0:T(4,128)} %param.28) | copy-start | bytes 4612
  24.5 3.3 %copy-start.2 = (f32[3,128,128]{2,1,0:T(8,128)S(1)}, f32[3,128,128]{2,1,0:T(8,128)}, u32[]{:S(2)}) copy-start(f32[3,128,128]{2,1,0:T(8,128)} %param.16) | copy-start | bytes 589828
  24.5 3.3 %copy-start.5 = (f32[128,128]{1,0:T(8,128)S(1)}, f32[128,128]{1,0:T(8,128)}, u32[]{:S(2)}) copy-start(f32[128,128]{1,0:T(8,128)} %param.18) | copy-start | bytes 196612
  24.6 3.3 %copy-start.6 = (f32[128,128]{1,0:T(8,128)S(1)}, f32[128,128]{1,0:T(8,128)}, u32[]{:S(2)}) copy-start(f32[128,128]{1,0:T(8,128)} %param.19) | copy-start | bytes 196612
  24.6 3.3 %copy-start.7 = (f32[128,128]{1,0:T(8,128)S(1)}, f32[128,128]{1,0:T(8,128)}, u32[]{:S(2)}) copy-start(f32[128,128]{1,0:T(8,128)} %param.17) | copy-start | bytes 196612
  24.6 3.3 %copy-start.12 = (s32[128]{0:T(128)S(1)}, s32[128]{0:T(128)}, u32[]{:S(2)}) copy-start(s32[128]{0:T(128)} %param.23) | copy-start | bytes 1540
  28.3 8.0 %copy-start.10 = (f32[5,128]{1,0:T(8,128)S(1)}, f32[5,128]{1,0:T(8,128)}, u32[]{:S(2)}) copy-start(f32[5,128]{1,0:T(8,128)} %param.24) | copy-start | bytes 7684
  28.3 8.6 %copy-start = (pred[256,16384]{1,0:T(32,128)(4,1)S(1)}, pred[256,16384]{1,0:T(32,128)(4,1)}, u32[]{:S(2)}) copy-start(pred[256,16384]{1,0:T(32,128)(4,1)} %iota_compare_fusion.14) | copy-start | bytes 12582916
  33.2 12.1 %collective-permute-start.1 = (f32[3,3]{1,0:T(4,128)S(1)}, f32[3,3]{1,0:T(4,128)S(1)}, u32[]{:S(2)}, u32[]{:S(2)}) collective-permute-start(f32[3,3]{1,0:T(4,128)S(1)} %slice.109), channel_id=1, source_target_pairs={{0,1},{1,2},{2,3},{3,4},{4,5},{5,6},{6,7},{7,8},{8,9},{9,10},{10,1... | collective-permute-start | bytes 116 | tf_op jit(solution)/shard_map/ppermute | solution.py:13
  36.9 8.4 %copy-start.11 = (f32[3,128]{1,0:T(4,128)S(1)}, f32[3,128]{1,0:T(4,128)}, u32[]{:S(2)}) copy-start(f32[3,128]{1,0:T(4,128)} %param.25) | copy-start | bytes 4612
  36.9 48.5 %copy-start.3 = (f32[2,4096]{1,0:T(2,128)S(1)}, f32[2,4096]{1,0:T(2,128)}, u32[]{:S(2)}) copy-start(f32[2,4096]{1,0:T(2,128)} %param.29) | copy-start | bytes 98308
  50.6 2.6 %collective-permute-start.2 = (f32[257,128]{1,0:T(8,128)S(1)}, f32[257,128]{1,0:T(8,128)S(1)}, u32[]{:S(2)}, u32[]{:S(2)}) collective-permute-start(f32[257,128]{1,0:T(8,128)S(1)} %pad_maximum_fusion.1), channel_id=1, source_target_pairs={{0,1},{1,0},{2,3},{3,2},{4,5},{5,4},{6,7},{7,6},{8,9},{9,8},{10,11... | collective-permute-start | bytes 394760 | tf_op jit(solution)/shard_map/ppermute | solution.py:18
  53.2 6.3 %collective-permute-start.3 = (f32[257,128]{1,0:T(8,128)S(1)}, f32[257,128]{1,0:T(8,128)S(1)}, u32[]{:S(2)}, u32[]{:S(2)}) collective-permute-start(f32[257,128]{1,0:T(8,128)S(1)} %fusion.32), channel_id=1, source_target_pairs={{0,2},{1,3},{2,0},{3,1},{4,6},{5,7},{6,4},{7,5},{8,10},{9,11},{10,... | collective-permute-start | bytes 394760 | tf_op jit(solution)/shard_map/ppermute | solution.py:18
  59.5 6.0 %collective-permute-start.4 = (f32[257,128]{1,0:T(8,128)S(1)}, f32[257,128]{1,0:T(8,128)S(1)}, u32[]{:S(2)}, u32[]{:S(2)}) collective-permute-start(f32[257,128]{1,0:T(8,128)S(1)} %add.136), channel_id=1, source_target_pairs={{0,4},{4,0},{8,12},{12,8},{16,20},{20,16},{24,28},{28,24},{1,5},{5... | collective-permute-start | bytes 394760 | tf_op jit(solution)/shard_map/ppermute | solution.py:18
  65.6 5.1 %collective-permute-start.5 = (f32[257,128]{1,0:T(8,128)S(1)}, f32[257,128]{1,0:T(8,128)S(1)}, u32[]{:S(2)}, u32[]{:S(2)}) collective-permute-start(f32[257,128]{1,0:T(8,128)S(1)} %add.137), channel_id=1, source_target_pairs={{0,8},{4,12},{8,0},{12,4},{16,24},{20,28},{24,16},{28,20},{1,9},{5... | collective-permute-start | bytes 394760 | tf_op jit(solution)/shard_map/ppermute | solution.py:18
  70.7 7.4 %collective-permute-start.6 = (f32[257,128]{1,0:T(8,128)S(1)}, f32[257,128]{1,0:T(8,128)S(1)}, u32[]{:S(2)}, u32[]{:S(2)}) collective-permute-start(f32[257,128]{1,0:T(8,128)S(1)} %add.138), channel_id=1, source_target_pairs={{0,16},{4,20},{8,24},{12,28},{16,0},{20,4},{24,8},{28,12},{1,17},{... | collective-permute-start | bytes 394760 | tf_op jit(solution)/shard_map/ppermute | solution.py:18

commit v6 on v5

--- a/solution.py
+++ b/solution.py
@@ -41,6 +41,22 @@
         rows = rows + exchanged(rows, axis, distance)
         distance *= 2
     return rows
+
+
+def doubling_gather(block, axis):
+    count = lax.axis_size(axis)
+    me = lax.axis_index(axis)
+    distance = 1
+    while distance < count:
+        other = exchanged(block, axis, distance)
+        mine_first = (me // distance) % 2 == 0
+        block = jnp.where(
+            mine_first,
+            jnp.concatenate([block, other], axis=1),
+            jnp.concatenate([other, block], axis=1),
+        )
+        distance *= 2
+    return block
 
 
 def spline(phase):
@@ -79,7 +95,7 @@
     rows = cal_size // lane
     src_rows, slots = obs_phase.shape
 
-    cal_both = lax.all_gather(jnp.stack([cal_dir, cal_res]), "cal", axis=1, tiled=True)
+    cal_both = doubling_gather(jnp.stack([cal_dir, cal_res]), "cal")
     cal_values = cal_both[0]
     cal_res_all = cal_both[1]
     edge_knots = passed_along(att_dir[:, :3], ("tm", "cal"), -1)

time: 86.5 us -> 85.5 us (0.988)
  blocking collectives: 7.84 us -> 0 us
  waiting for transfers between devices: 16.2 us -> 20.3 us
  starting transfers between devices: 14.3 us -> 18 us
  local copies, waits for them, and re-layouts: 4.93 us -> 3.18 us
  other arithmetic: 11.1 us -> 12 us
    all_gather x1 -> x0, blocking collectives: 7.84 us -> none  [local(): lax.all_gather(jnp.stack([cal_dir, cal_res]), 'cal', axis=1, tiled=True)]
    ppermute x5 -> x7, starting transfers between devices: 10.6 us -> 14.7 us  [exchanged(): return lax.ppermute(block, axis, [(i, i ^ distance) for i in devices])]
    ppermute x5 -> x7, waiting for transfers between devices: 16.2 us -> 20.3 us  [exchanged(): return lax.ppermute(block, axis, [(i, i ^ distance) for i in devices])]
    another operation x2 -> x1, local copies, waits for them, and re-layouts: 1.56 us -> 0.03 us  [local(): cal_table = cal_values.reshape(rows, lane)]
  transfers between devices with their start and end apart: 7 -> 9, of which waited for: 5 -> 6; matrix products, arithmetic and copies ran while one was open for 29% -> 22% of each run, Pallas kernels for 0% -> 0%
where the time goes in v6:
time: 85.5 us; the launch traced here: 85.2 us
  matrix products  22.1 us (26%)
  waiting for transfers between devices  20.3 us (24%)
  starting transfers between devices  18 us (21%)
  other arithmetic  12 us (14%)
  between operations  9.58 us (11%)
  local copies, waits for them, and re-layouts  3.18 us (4%)
    ppermute x7, waiting for transfers between devices, exchanged(): return lax.ppermute(block, axis, [(i, i ^ distance) for i in devices])  20.3 us
    ppermute x7, starting transfers between devices, exchanged(): return lax.ppermute(block, axis, [(i, i ^ distance) for i in devices])  14.7 us
    dot_general x1, matrix products, local(): lax.dot_general(high_hot, cal_weighted, (((1,), (1,)), ((), ())), precisi...  8.4 us
    dot_general x1, matrix products, local(): lax.dot_general(cal_table, high_hot, (((0,), (0,)), ((), ())), precision=...  7.11 us
    dot_general x1, other arithmetic, local(): lax.dot_general(high_hot, cal_weighted, (((1,), (1,)), ((), ())), precisi...  4.09 us
    dot_general x1, matrix products, local(): lax.dot_general(spread, knot_hot, (((1,), (1,)), ((), ())), precision=EXACT)  3.92 us
    ppermute x2, starting transfers between devices, passed_along(): return lax.ppermute(block, axis, route)  3.31 us
    dot_general x1, matrix products, local(): jnp.dot(table, knot_hot, precision=EXACT).reshape(4, 3, src_rows, slots)  2.71 us
  transfers between devices with their start and end apart: 9, of which 6 were waited for; matrix products, arithmetic and copies ran while one was open for 22% of the time, Pallas kernels for 0%

profile of v6, /device:TPU:0, one launch (start us, length us, event | category | flops | bytes accessed | tf_op | source)
XLA Modules:
  0.0 85.2 jit_solution(8055198422460495573)
XLA Ops:
  0.7 0.9 %pad_maximum_fusion.2 = f32[2,2,4096]{2,1,0:T(2,128)S(1)} fusion(f32[1,2,4096]{2,1,0:T(2,128)} %bitcast.108, f32[1,2,4096]{2,1,0:T(2,128)} %bitcast.106), kind=kLoop, calls=%fused_computation.60 | loop fusion | flops 16384 | bytes 131072 | tf_op jit(solution)/shard_map/stack | solution.py:98
  2.1 1.3 %collective-permute-start = (f32[3,3]{1,0:T(4,128)}, f32[3,3]{1,0:T(4,128)S(1)}, u32[]{:S(2)}, u32[]{:S(2)}) collective-permute-start(f32[3,3]{1,0:T(4,128)} %bitcast.110), channel_id=1, source_target_pairs={{1,0},{2,1},{3,2},{4,3},{5,4},{6,5},{7,6},{8,7},{9,8},{10,9},{11,1... | collective-permute-start | bytes 116 | tf_op jit(solution)/shard_map/ppermute | solution.py:13
  3.4 0.7 constant_dynamic-update-slice_fusion.1
  4.1 0.9 %add_select_fusion = (s32[16384]{0:T(1024)S(1)}, s32[16384]{0:T(1024)S(1)}) fusion(s32[128,128]{1,0:T(8,128)} %param.22, s32[128,128]{1,0:T(8,128)} %param.21), kind=kLoop, calls=%fused_computation.44 | loop fusion | flops 344064 | bytes 262144 | tf_op jit(solution)/shard_map/jit(remainder)/select_n | solution.py:123
  5.0 4.1 %iota_compare_fusion.14 = pred[256,16384]{1,0:T(32,128)(4,1)} fusion(s32[16384]{0:T(1024)S(1)} %get-tuple-element.40), kind=kLoop, calls=%fused_computation.1.clone.clone.2 | loop fusion | flops 4194304 | bytes 4259840 | tf_op jit(solution)/shard_map/dot_general | solution.py:145
  9.4 2.7 %fusion.3 = f32[12,16384]{1,0:T(8,128)S(1)} fusion(f32[12,128]{1,0:T(8,128)S(1)} %reshape.149, s32[16384]{0:T(1024)S(1)} %subtract_bitcast_fusion), kind=kOutput, calls=%fused_computation.6 | convolution fusion | flops 304087040 | bytes 858112 | tf_op jit(solution)/shard_map/dot_general | solution.py:116
  12.5 3.2 %collective-permute-start.2 = (f32[2,4,4096]{2,1,0:T(4,128)S(1)}, f32[2,4,4096]{2,1,0:T(4,128)S(1)}, u32[]{:S(2)}, u32[]{:S(2)}) collective-permute-start(f32[2,4,4096]{2,1,0:T(4,128)S(1)} %maximum_select_fusion.1), channel_id=1, source_target_pairs={{0,2},{1,3},{2,0},{3,1},{4,6},{5,7},{6,4},{7,5},{8,10},{9,11},{10,... | collective-permute-start | bytes 393224 | tf_op jit(solution)/shard_map/ppermute | solution.py:18
  15.7 4.1 %collective-permute-done.2 = f32[2,4,4096]{2,1,0:T(4,128)S(1)} collective-permute-done((f32[2,4,4096]{2,1,0:T(4,128)S(1)}, f32[2,4,4096]{2,1,0:T(4,128)S(1)}, u32[]{:S(2)}, u32[]{:S(2)}) %collective-permute-start.2) | collective-permute-done | bytes 131104 | tf_op jit(solution)/shard_map/ppermute | solution.py:18
  20.0 7.1 %fusion.11 = f32[16384]{0:T(1024)S(1)} fusion(f32[256,128]{1,0:T(8,128)S(1)} %reshape_squeeze.3, s32[16384]{0:T(1024)S(1)} %get-tuple-element.40, s32[16384]{0:T(1024)S(1)} %get-tuple-element.39), kind=kOutput, calls=%fused_computation.15 | convolution fusion | flops 6452920320 | bytes 327680 | tf_op jit(solution)/shard_map/dot_general | solution.py:125
  27.7 0.6 copy.25
  28.3 3.9 %fusion.2 = f32[12,128]{1,0:T(8,128)S(1)} fusion(f32[12,16384]{1,0:T(8,128)S(1)} %bitcast.105, s32[16384]{0:T(1024)S(1)} %subtract_bitcast_fusion), kind=kOutput, calls=%fused_computation.5 | convolution fusion | flops 304087040 | bytes 858112 | tf_op jit(solution)/shard_map/dot_general | solution.py:136
  32.4 2.0 %collective-permute-start.3 = (f32[3,3]{1,0:T(4,128)S(1)}, f32[3,3]{1,0:T(4,128)S(1)}, u32[]{:S(2)}, u32[]{:S(2)}) collective-permute-start(f32[3,3]{1,0:T(4,128)S(1)} %slice.109), channel_id=1, source_target_pairs={{0,1},{1,2},{2,3},{3,4},{4,5},{5,6},{6,7},{7,8},{8,9},{9,10},{10,1... | collective-permute-start | bytes 116 | tf_op jit(solution)/shard_map/ppermute | solution.py:13
  34.5 0.6 multiply_reduce_fusion.4
  35.1 0.6 multiply_reduce_fusion.5
  35.7 8.4 %fusion = f32[256,128]{1,0:T(8,128)S(1)} fusion(f32[16384]{0:T(1024)S(1)} %get-tuple-element.24, s32[16384]{0:T(1024)S(1)} %get-tuple-element.39, pred[256,16384]{1,0:T(32,128)(4,1)S(1)} %copy-done), kind=kOutput, calls=%fused_computation.2 | convolution fusion | flops 6446645248 | bytes 4456448 | tf_op jit(solution)/shard_map/dot_general | solution.py:145
  44.2 0.7 multiply_reduce_fusion.8
  48.7 0.7 concatenate.30
  49.5 2.0 %collective-permute-start.4 = (f32[257,128]{1,0:T(8,128)S(1)}, f32[257,128]{1,0:T(8,128)S(1)}, u32[]{:S(2)}, u32[]{:S(2)}) collective-permute-start(f32[257,128]{1,0:T(8,128)S(1)} %pad_maximum_fusion.1), channel_id=1, source_target_pairs={{0,1},{1,0},{2,3},{3,2},{4,5},{5,4},{6,7},{7,6},{8,9},{9,8},{10,11... | collective-permute-start | bytes 394760 | tf_op jit(solution)/shard_map/ppermute | solution.py:18
  51.5 1.0 %collective-permute-done.4 = f32[257,128]{1,0:T(8,128)S(1)} collective-permute-done((f32[257,128]{1,0:T(8,128)S(1)}, f32[257,128]{1,0:T(8,128)S(1)}, u32[]{:S(2)}, u32[]{:S(2)}) %collective-permute-start.4) | collective-permute-done | bytes 131616 | tf_op jit(solution)/shard_map/ppermute | solution.py:18
  52.5 2.2 %collective-permute-start.5 = (f32[257,128]{1,0:T(8,128)S(1)}, f32[257,128]{1,0:T(8,128)S(1)}, u32[]{:S(2)}, u32[]{:S(2)}) collective-permute-start(f32[257,128]{1,0:T(8,128)S(1)} %fusion.32), channel_id=1, source_target_pairs={{0,2},{1,3},{2,0},{3,1},{4,6},{5,7},{6,4},{7,5},{8,10},{9,11},{10,... | collective-permute-start | bytes 394760 | tf_op jit(solution)/shard_map/ppermute | solution.py:18
  54.6 4.1 %collective-permute-done.5 = f32[257,128]{1,0:T(8,128)S(1)} collective-permute-done((f32[257,128]{1,0:T(8,128)S(1)}, f32[257,128]{1,0:T(8,128)S(1)}, u32[]{:S(2)}, u32[]{:S(2)}) %collective-permute-start.5) | collective-permute-done | bytes 131616 | tf_op jit(solution)/shard_map/ppermute | solution.py:18
  58.8 2.5 %collective-permute-start.6 = (f32[257,128]{1,0:T(8,128)S(1)}, f32[257,128]{1,0:T(8,128)S(1)}, u32[]{:S(2)}, u32[]{:S(2)}) collective-permute-start(f32[257,128]{1,0:T(8,128)S(1)} %add.147), channel_id=1, source_target_pairs={{0,4},{4,0},{8,12},{12,8},{16,20},{20,16},{24,28},{28,24},{1,5},{5... | collective-permute-start | bytes 394760 | tf_op jit(solution)/shard_map/ppermute | solution.py:18
  61.2 3.5 %collective-permute-done.6 = f32[257,128]{1,0:T(8,128)S(1)} collective-permute-done((f32[257,128]{1,0:T(8,128)S(1)}, f32[257,128]{1,0:T(8,128)S(1)}, u32[]{:S(2)}, u32[]{:S(2)}) %collective-permute-start.6) | collective-permute-done | bytes 131616 | tf_op jit(solution)/shard_map/ppermute | solution.py:18
  64.8 1.6 %collective-permute-start.7 = (f32[257,128]{1,0:T(8,128)S(1)}, f32[257,128]{1,0:T(8,128)S(1)}, u32[]{:S(2)}, u32[]{:S(2)}) collective-permute-start(f32[257,128]{1,0:T(8,128)S(1)} %add.148), channel_id=1, source_target_pairs={{0,8},{4,12},{8,0},{12,4},{16,24},{20,28},{24,16},{28,20},{1,9},{5... | collective-permute-start | bytes 394760 | tf_op jit(solution)/shard_map/ppermute | solution.py:18
  66.4 3.4 %collective-permute-done.7 = f32[257,128]{1,0:T(8,128)S(1)} collective-permute-done((f32[257,128]{1,0:T(8,128)S(1)}, f32[257,128]{1,0:T(8,128)S(1)}, u32[]{:S(2)}, u32[]{:S(2)}) %collective-permute-start.7) | collective-permute-done | bytes 131616 | tf_op jit(solution)/shard_map/ppermute | solution.py:18
  69.9 2.7 %collective-permute-start.8 = (f32[257,128]{1,0:T(8,128)S(1)}, f32[257,128]{1,0:T(8,128)S(1)}, u32[]{:S(2)}, u32[]{:S(2)}) collective-permute-start(f32[257,128]{1,0:T(8,128)S(1)} %add.149), channel_id=1, source_target_pairs={{0,16},{4,20},{8,24},{12,28},{16,0},{20,4},{24,8},{28,12},{1,17},{... | collective-permute-start | bytes 394760 | tf_op jit(solution)/shard_map/ppermute | solution.py:18
  72.6 0.6 multiply_reduce_fusion.3
  73.2 4.1 %collective-permute-done.8 = f32[257,128]{1,0:T(8,128)S(1)} collective-permute-done((f32[257,128]{1,0:T(8,128)S(1)}, f32[257,128]{1,0:T(8,128)S(1)}, u32[]{:S(2)}, u32[]{:S(2)}) %collective-permute-start.8) | collective-permute-done | bytes 131616 | tf_op jit(solution)/shard_map/ppermute | solution.py:18
  81.9 0.6 multiply_reduce_fusion.2
  83.3 0.6 multiply_add_fusion.2
  83.9 0.7 multiply_add_fusion.3
  84.5 0.6 multiply_add_fusion.1
  (64 shorter events, 2.7 us)
Async XLA Ops:
  0.6 8.8 %copy-start.9 = (f32[3,128]{1,0:T(4,128)S(1)}, f32[3,128]{1,0:T(4,128)}, u32[]{:S(2)}) copy-start(f32[3,128]{1,0:T(4,128)} %param.28) | copy-start | bytes 4612
  0.6 8.5 %copy-start.10 = (f32[5,128]{1,0:T(8,128)S(1)}, f32[5,128]{1,0:T(8,128)}, u32[]{:S(2)}) copy-start(f32[5,128]{1,0:T(8,128)} %param.27) | copy-start | bytes 7684
  0.7 8.5 %copy-start.1 = (f32[5,128,128]{2,1,0:T(8,128)S(1)}, f32[5,128,128]{2,1,0:T(8,128)}, u32[]{:S(2)}) copy-start(f32[5,128,128]{2,1,0:T(8,128)} %param.15) | copy-start | bytes 983044
  0.7 8.6 %copy-start.5 = (s32[128,128]{1,0:T(8,128)S(1)}, s32[128,128]{1,0:T(8,128)}, u32[]{:S(2)}) copy-start(s32[128,128]{1,0:T(8,128)} %param.20) | copy-start | bytes 196612
  1.5 10.8 %collective-permute-start.1 = (f32[2,2,4096]{2,1,0:T(2,128)S(1)}, f32[2,2,4096]{2,1,0:T(2,128)S(1)}, u32[]{:S(2)}, u32[]{:S(2)}) collective-permute-start(f32[2,2,4096]{2,1,0:T(2,128)S(1)} %pad_maximum_fusion.2), channel_id=1, source_target_pairs={{0,1},{1,0},{2,3},{3,2},{4,5},{5,4},{6,7},{7,6},{8,9},{9,8},{10,11... | collective-permute-start | bytes 196616 | tf_op jit(solution)/shard_map/ppermute | solution.py:18
  2.1 7.3 %collective-permute-start = (f32[3,3]{1,0:T(4,128)}, f32[3,3]{1,0:T(4,128)S(1)}, u32[]{:S(2)}, u32[]{:S(2)}) collective-permute-start(f32[3,3]{1,0:T(4,128)} %bitcast.110), channel_id=1, source_target_pairs={{1,0},{2,1},{3,2},{4,3},{5,4},{6,5},{7,6},{8,7},{9,8},{10,9},{11,1... | collective-permute-start | bytes 116 | tf_op jit(solution)/shard_map/ppermute | solution.py:13
  5.0 7.3 %copy-start.3 = (f32[2,4096]{1,0:T(2,128)S(1)}, f32[2,4096]{1,0:T(2,128)}, u32[]{:S(2)}) copy-start(f32[2,4096]{1,0:T(2,128)} %param.29) | copy-start | bytes 98308
  5.0 7.3 %copy-start.4 = (f32[2,4096]{1,0:T(2,128)S(1)}, f32[2,4096]{1,0:T(2,128)}, u32[]{:S(2)}) copy-start(f32[2,4096]{1,0:T(2,128)} %param.26) | copy-start | bytes 98308
  5.0 10.7 %copy-start.2 = (f32[3,128,128]{2,1,0:T(8,128)S(1)}, f32[3,128,128]{2,1,0:T(8,128)}, u32[]{:S(2)}) copy-start(f32[3,128,128]{2,1,0:T(8,128)} %param.16) | copy-start | bytes 589828
  12.5 7.4 %collective-permute-start.2 = (f32[2,4,4096]{2,1,0:T(4,128)S(1)}, f32[2,4,4096]{2,1,0:T(4,128)S(1)}, u32[]{:S(2)}, u32[]{:S(2)}) collective-permute-start(f32[2,4,4096]{2,1,0:T(4,128)S(1)} %maximum_select_fusion.1), channel_id=1, source_target_pairs={{0,2},{1,3},{2,0},{3,1},{4,6},{5,7},{6,4},{7,5},{8,10},{9,11},{10,... | collective-permute-start | bytes 393224 | tf_op jit(solution)/shard_map/ppermute | solution.py:18
  20.0 7.2 %copy-start.6 = (f32[128,128]{1,0:T(8,128)S(1)}, f32[128,128]{1,0:T(8,128)}, u32[]{:S(2)}) copy-start(f32[128,128]{1,0:T(8,128)} %param.18) | copy-start | bytes 196612
  20.0 7.2 %copy-start.7 = (f32[128,128]{1,0:T(8,128)S(1)}, f32[128,128]{1,0:T(8,128)}, u32[]{:S(2)}) copy-start(f32[128,128]{1,0:T(8,128)} %param.19) | copy-start | bytes 196612
  20.0 7.2 %copy-start.8 = (f32[128,128]{1,0:T(8,128)S(1)}, f32[128,128]{1,0:T(8,128)}, u32[]{:S(2)}) copy-start(f32[128,128]{1,0:T(8,128)} %param.17) | copy-start | bytes 196612
  20.0 7.2 %copy-start.13 = (s32[128]{0:T(128)S(1)}, s32[128]{0:T(128)}, u32[]{:S(2)}) copy-start(s32[128]{0:T(128)} %param.23) | copy-start | bytes 1540
  27.6 7.6 %copy-start.11 = (f32[5,128]{1,0:T(8,128)S(1)}, f32[5,128]{1,0:T(8,128)}, u32[]{:S(2)}) copy-start(f32[5,128]{1,0:T(8,128)} %param.24) | copy-start | bytes 7684
  27.6 8.2 %copy-start = (pred[256,16384]{1,0:T(32,128)(4,1)S(1)}, pred[256,16384]{1,0:T(32,128)(4,1)}, u32[]{:S(2)}) copy-start(pred[256,16384]{1,0:T(32,128)(4,1)} %iota_compare_fusion.14) | copy-start | bytes 12582916
  32.4 11.7 %collective-permute-start.3 = (f32[3,3]{1,0:T(4,128)S(1)}, f32[3,3]{1,0:T(4,128)S(1)}, u32[]{:S(2)}, u32[]{:S(2)}) collective-permute-start(f32[3,3]{1,0:T(4,128)S(1)} %slice.109), channel_id=1, source_target_pairs={{0,1},{1,2},{2,3},{3,4},{4,5},{5,6},{6,7},{7,8},{8,9},{9,10},{10,1... | collective-permute-start | bytes 116 | tf_op jit(solution)/shard_map/ppermute | solution.py:13
  35.7 8.4 %copy-start.12 = (f32[3,128]{1,0:T(4,128)S(1)}, f32[3,128]{1,0:T(4,128)}, u32[]{:S(2)}) copy-start(f32[3,128]{1,0:T(4,128)} %param.25) | copy-start | bytes 4612
  49.5 3.0 %collective-permute-start.4 = (f32[257,128]{1,0:T(8,128)S(1)}, f32[257,128]{1,0:T(8,128)S(1)}, u32[]{:S(2)}, u32[]{:S(2)}) collective-permute-start(f32[257,128]{1,0:T(8,128)S(1)} %pad_maximum_fusion.1), channel_id=1, source_target_pairs={{0,1},{1,0},{2,3},{3,2},{4,5},{5,4},{6,7},{7,6},{8,9},{9,8},{10,11... | collective-permute-start | bytes 394760 | tf_op jit(solution)/shard_map/ppermute | solution.py:18
  52.5 6.3 %collective-permute-start.5 = (f32[257,128]{1,0:T(8,128)S(1)}, f32[257,128]{1,0:T(8,128)S(1)}, u32[]{:S(2)}, u32[]{:S(2)}) collective-permute-start(f32[257,128]{1,0:T(8,128)S(1)} %fusion.32), channel_id=1, source_target_pairs={{0,2},{1,3},{2,0},{3,1},{4,6},{5,7},{6,4},{7,5},{8,10},{9,11},{10,... | collective-permute-start | bytes 394760 | tf_op jit(solution)/shard_map/ppermute | solution.py:18
  58.8 6.0 %collective-permute-start.6 = (f32[257,128]{1,0:T(8,128)S(1)}, f32[257,128]{1,0:T(8,128)S(1)}, u32[]{:S(2)}, u32[]{:S(2)}) collective-permute-start(f32[257,128]{1,0:T(8,128)S(1)} %add.147), channel_id=1, source_target_pairs={{0,4},{4,0},{8,12},{12,8},{16,20},{20,16},{24,28},{28,24},{1,5},{5... | collective-permute-start | bytes 394760 | tf_op jit(solution)/shard_map/ppermute | solution.py:18
  64.8 5.1 %collective-permute-start.7 = (f32[257,128]{1,0:T(8,128)S(1)}, f32[257,128]{1,0:T(8,128)S(1)}, u32[]{:S(2)}, u32[]{:S(2)}) collective-permute-start(f32[257,128]{1,0:T(8,128)S(1)} %add.148), channel_id=1, source_target_pairs={{0,8},{4,12},{8,0},{12,4},{16,24},{20,28},{24,16},{28,20},{1,9},{5... | collective-permute-start | bytes 394760 | tf_op jit(solution)/shard_map/ppermute | solution.py:18
  69.9 7.4 %collective-permute-start.8 = (f32[257,128]{1,0:T(8,128)S(1)}, f32[257,128]{1,0:T(8,128)S(1)}, u32[]{:S(2)}, u32[]{:S(2)}) collective-permute-start(f32[257,128]{1,0:T(8,128)S(1)} %add.149), channel_id=1, source_target_pairs={{0,16},{4,20},{8,24},{12,28},{16,0},{20,4},{24,8},{28,12},{1,17},{... | collective-permute-start | bytes 394760 | tf_op jit(solution)/shard_map/ppermute | solution.py:18

commit v7 on v6

--- a/solution.py
+++ b/solution.py
@@ -57,6 +57,16 @@
         )
         distance *= 2
     return block
+
+
+def in_thirds(values):
+    parts = []
+    rest = values
+    for _ in range(3):
+        head = lax.reduce_precision(rest, exponent_bits=8, mantissa_bits=7)
+        parts.append(head.astype(jnp.bfloat16))
+        rest = rest - head
+    return parts
 
 
 def spline(phase):
@@ -119,11 +129,13 @@
         y_att = y_att + basis[m] * jnp.sum(att_design * picked[m], axis=0)
 
     flat_index = flat(cal_block * col_width + cal_column)
-    high_hot = (flat_index // lane == lax.broadcasted_iota(jnp.int32, (rows, 1), 0)).astype(jnp.float32)
-    low_hot = (flat_index % lane == lax.broadcasted_iota(jnp.int32, (lane, 1), 0)).astype(jnp.float32)
+    high_hot = (flat_index // lane == lax.broadcasted_iota(jnp.int32, (rows, 1), 0)).astype(jnp.bfloat16)
+    low_hot = (flat_index % lane == lax.broadcasted_iota(jnp.int32, (lane, 1), 0)).astype(jnp.bfloat16)
     cal_table = cal_values.reshape(rows, lane)
-    row_vals = lax.dot_general(cal_table, high_hot, (((0,), (0,)), ((), ())), precision=EXACT)
-    y_cal = cal_design * jnp.sum(row_vals * low_hot, axis=0).reshape(src_rows, slots)
+    table_parts = jnp.concatenate([part.T for part in in_thirds(cal_table)], axis=0)
+    row_vals = jnp.dot(table_parts, high_hot, preferred_element_type=jnp.float32)
+    row_vals = row_vals.reshape(3, lane, n_obs) * low_hot.astype(jnp.float32)[None]
+    y_cal = cal_design * jnp.sum(row_vals, axis=(0, 1)).reshape(src_rows, slots)
 
     y_src = jnp.sum(src_design * src_dir[:, :, None], axis=0)
     response = live_mask * (y_src + y_att + y_cal)
@@ -141,8 +153,11 @@
     incoming = passed_along(grad_ext[:, knot_count:], ("tm", "cal"), 1)
     q_att = jnp.concatenate([grad_ext[:, :3] + incoming, grad_ext[:, 3:knot_count]], axis=1)
 
-    cal_weighted = flat(cal_design * weighted) * low_hot
-    cal_term = lax.dot_general(high_hot, cal_weighted, (((1,), (1,)), ((), ())), precision=EXACT)
+    cal_weighted = jnp.concatenate([low_hot * part for part in in_thirds(flat(cal_design * weighted))], axis=0)
+    cal_term = lax.dot_general(
+        high_hot, cal_weighted, (((1,), (1,)), ((), ())), preferred_element_type=jnp.float32
+    )
+    cal_term = cal_term[:, :lane] + cal_term[:, lane : 2 * lane] + cal_term[:, 2 * lane :]
     res_sq = jnp.sum(src_res * src_res) + jnp.sum(att_res * att_res)
     res_q = jnp.sum(src_res * q_src) + jnp.sum(att_res * q_att)
     q_sq = jnp.sum(q_src * q_src) + jnp.sum(q_att * q_att)

time: 85.5 us -> 97.5 us (1.14)
  matrix products: 22.1 us -> 31.5 us
  other arithmetic: 12 us -> 14.5 us
    dot_general x2, matrix products: 15.5 us -> 24.8 us  [the longest x1 17 us: local(): lax.dot_general(high_hot, cal_weighted, (((1,), (1,)), ((), ())), preferr...]
    convert_element_type x0 -> x3, other arithmetic: none -> 4.22 us  [the longest x1 4.1 us: local(): low_hot.astype(jnp.float32)[None]]
    dot_general x1 -> x0, other arithmetic: 4.09 us -> none  [local(): lax.dot_general(high_hot, cal_weighted, (((1,), (1,)), ((), ())), precisi...]
    mul x1, other arithmetic: 0.1 us -> 2.32 us  [local(): low_hot * part]
  transfers between devices with their start and end apart: 9 -> 9, of which waited for: 6 -> 6; matrix products, arithmetic and copies ran while one was open for 22% -> 31% of each run, Pallas kernels for 0% -> 0%
where the time goes in v7:
time: 97.5 us; the launch traced here: 97.1 us
  matrix products  31.5 us (32%)
  waiting for transfers between devices  20.3 us (21%)
  starting transfers between devices  18 us (18%)
  other arithmetic  14.5 us (15%)
  between operations  9.61 us (10%)
  local copies, waits for them, and re-layouts  3.24 us (3%)
    ppermute x7, waiting for transfers between devices, exchanged(): return lax.ppermute(block, axis, [(i, i ^ distance) for i in devices])  20.3 us
    dot_general x1, matrix products, local(): lax.dot_general(high_hot, cal_weighted, (((1,), (1,)), ((), ())), preferr...  17 us
    ppermute x7, starting transfers between devices, exchanged(): return lax.ppermute(block, axis, [(i, i ^ distance) for i in devices])  14.7 us
    dot_general x1, matrix products, local(): jnp.dot(table_parts, high_hot, preferred_element_type=jnp.float32)  7.8 us
    convert_element_type x1, other arithmetic, local(): low_hot.astype(jnp.float32)[None]  4.1 us
    dot_general x1, matrix products, local(): lax.dot_general(spread, knot_hot, (((1,), (1,)), ((), ())), precision=EXACT)  3.92 us
    ppermute x2, starting transfers between devices, passed_along(): return lax.ppermute(block, axis, route)  3.27 us
    dot_general x1, matrix products, local(): jnp.dot(table, knot_hot, precision=EXACT).reshape(4, 3, src_rows, slots)  2.71 us
  transfers between devices with their start and end apart: 9, of which 6 were waited for; matrix products, arithmetic and copies ran while one was open for 31% of the time, Pallas kernels for 0%

profile of v7, /device:TPU:0, one launch (start us, length us, event | category | flops | bytes accessed | tf_op | source)
XLA Modules:
  0.0 97.1 jit_solution(16078565056652931346)
XLA Ops:
  0.7 0.9 pad_maximum_fusion.2
  2.1 1.3 %collective-permute-start = (f32[3,3]{1,0:T(4,128)}, f32[3,3]{1,0:T(4,128)S(1)}, u32[]{:S(2)}, u32[]{:S(2)}) collective-permute-start(f32[3,3]{1,0:T(4,128)} %bitcast.123), channel_id=1, source_target_pairs={{1,0},{2,1},{3,2},{4,3},{5,4},{6,5},{7,6},{8,7},{9,8},{10,9},{11,1... | collective-permute-start | bytes 116 | tf_op jit(solution)/shard_map/ppermute | solution.py:13
  3.4 0.7 constant_dynamic-update-slice_fusion.1
  4.1 0.9 add_select_fusion.1
  5.0 4.1 %fusion.15 = f32[128,16384]{1,0:T(8,128)} fusion(s32[16384]{0:T(1024)S(1)} %get-tuple-element.45), kind=kLoop, calls=%fused_computation.19 | loop fusion | flops 6291456 | bytes 8454144 | tf_op jit(solution)/shard_map/convert_element_type | solution.py:137
  9.5 2.7 %fusion.8 = f32[12,16384]{1,0:T(8,128)S(1)} fusion(f32[12,128]{1,0:T(8,128)S(1)} %reshape.209, s32[16384]{0:T(1024)S(1)} %subtract_bitcast_fusion), kind=kOutput, calls=%fused_computation.11 | convolution fusion | flops 304087040 | bytes 858112 | tf_op jit(solution)/shard_map/dot_general | solution.py:126
  12.6 3.2 %collective-permute-start.2 = (f32[2,4,4096]{2,1,0:T(4,128)S(1)}, f32[2,4,4096]{2,1,0:T(4,128)S(1)}, u32[]{:S(2)}, u32[]{:S(2)}) collective-permute-start(f32[2,4,4096]{2,1,0:T(4,128)S(1)} %maximum_select_fusion.1), channel_id=1, source_target_pairs={{0,2},{1,3},{2,0},{3,1},{4,6},{5,7},{6,4},{7,5},{8,10},{9,11},{10,... | collective-permute-start | bytes 393224 | tf_op jit(solution)/shard_map/ppermute | solution.py:18
  15.9 4.1 %collective-permute-done.2 = f32[2,4,4096]{2,1,0:T(4,128)S(1)} collective-permute-done((f32[2,4,4096]{2,1,0:T(4,128)S(1)}, f32[2,4,4096]{2,1,0:T(4,128)S(1)}, u32[]{:S(2)}, u32[]{:S(2)}) %collective-permute-start.2) | collective-permute-done | bytes 131104 | tf_op jit(solution)/shard_map/ppermute | solution.py:18
  20.2 7.8 %fusion = f32[16384]{0:T(1024)S(1)} fusion(f32[128,16384]{1,0:T(8,128)} %fusion.15, s32[16384]{0:T(1024)S(1)} %get-tuple-element.44, bf16[128,256]{0,1:T(8,128)(2,1)S(1)} %get-tuple-element.42, bf16[128,256]{0,1:T(8,128)(2,1)S(1)} %get-tuple-element.43, bf16[128,256]{0,1:T(8,128)(2,1)S(1)} %get-tuple-element.41), kind=kOutput, calls=%fused_computation.1 | convolution fusion | flops 3238576128 | bytes 8716288 | tf_op jit(solution)/shard_map/dot_general | solution.py:136
  28.5 0.6 copy.25
  29.1 3.9 %fusion.7 = f32[12,128]{1,0:T(8,128)S(1)} fusion(f32[12,16384]{1,0:T(8,128)S(1)} %bitcast.118, s32[16384]{0:T(1024)S(1)} %subtract_bitcast_fusion), kind=kOutput, calls=%fused_computation.10 | convolution fusion | flops 304087040 | bytes 858112 | tf_op jit(solution)/shard_map/dot_general | solution.py:148
  33.2 2.0 %collective-permute-start.3 = (f32[3,3]{1,0:T(4,128)S(1)}, f32[3,3]{1,0:T(4,128)S(1)}, u32[]{:S(2)}, u32[]{:S(2)}) collective-permute-start(f32[3,3]{1,0:T(4,128)S(1)} %slice.124), channel_id=1, source_target_pairs={{0,1},{1,2},{2,3},{3,4},{4,5},{5,6},{6,7},{7,8},{8,9},{9,10},{10,1... | collective-permute-start | bytes 116 | tf_op jit(solution)/shard_map/ppermute | solution.py:13
  35.2 0.7 multiply_reduce_fusion.4
  35.9 2.3 %fusion.11 = (bf16[128,16384]{1,0:T(8,128)(2,1)S(1)}, bf16[128,16384]{1,0:T(8,128)(2,1)S(1)}, bf16[128,16384]{1,0:T(8,128)(2,1)S(1)}) fusion(s32[16384]{0:T(1024)S(1)} %get-tuple-element.45, bf16[16384]{0:T(1024)(128)(2,1)S(1)} %get-tuple-element.24, bf16[16384]{0:T(1024)(128)(2,1)S(1)} %get-tuple-element.40, bf16[16384]{0:T(1024)(128)(2,1)S(1)} %get-tuple-element.39), kind=kLoop, calls=%fused_computation.15 | loop fusion | flops 8388608 | bytes 12746752 | tf_op jit(solution)/shard_map/mul | solution.py:156
  38.3 17.0 %fusion.1 = f32[256,384]{1,0:T(8,128)S(1)} fusion(bf16[128,16384]{1,0:T(8,128)(2,1)S(1)} %get-tuple-element.47, bf16[128,16384]{1,0:T(8,128)(2,1)S(1)} %get-tuple-element.48, bf16[128,16384]{1,0:T(8,128)(2,1)S(1)} %get-tuple-element.46, s32[16384]{0:T(1024)S(1)} %get-tuple-element.44), kind=kOutput, calls=%fused_computation.3 | convolution fusion | flops 3263168512 | bytes 13041664 | tf_op jit(solution)/shard_map/dot_general | solution.py:157
  55.4 0.6 multiply_reduce_fusion.5
  56.0 0.7 multiply_reduce_fusion.8
  60.6 0.8 concatenate.38
  61.4 2.0 %collective-permute-start.4 = (f32[257,128]{1,0:T(8,128)S(1)}, f32[257,128]{1,0:T(8,128)S(1)}, u32[]{:S(2)}, u32[]{:S(2)}) collective-permute-start(f32[257,128]{1,0:T(8,128)S(1)} %pad_maximum_fusion.1), channel_id=1, source_target_pairs={{0,1},{1,0},{2,3},{3,2},{4,5},{5,4},{6,7},{7,6},{8,9},{9,8},{10,11... | collective-permute-start | bytes 394760 | tf_op jit(solution)/shard_map/ppermute | solution.py:18
  63.4 1.0 %collective-permute-done.4 = f32[257,128]{1,0:T(8,128)S(1)} collective-permute-done((f32[257,128]{1,0:T(8,128)S(1)}, f32[257,128]{1,0:T(8,128)S(1)}, u32[]{:S(2)}, u32[]{:S(2)}) %collective-permute-start.4) | collective-permute-done | bytes 131616 | tf_op jit(solution)/shard_map/ppermute | solution.py:18
  64.4 2.2 %collective-permute-start.5 = (f32[257,128]{1,0:T(8,128)S(1)}, f32[257,128]{1,0:T(8,128)S(1)}, u32[]{:S(2)}, u32[]{:S(2)}) collective-permute-start(f32[257,128]{1,0:T(8,128)S(1)} %fusion.51), channel_id=1, source_target_pairs={{0,2},{1,3},{2,0},{3,1},{4,6},{5,7},{6,4},{7,5},{8,10},{9,11},{10,... | collective-permute-start | bytes 394760 | tf_op jit(solution)/shard_map/ppermute | solution.py:18
  66.6 4.1 %collective-permute-done.5 = f32[257,128]{1,0:T(8,128)S(1)} collective-permute-done((f32[257,128]{1,0:T(8,128)S(1)}, f32[257,128]{1,0:T(8,128)S(1)}, u32[]{:S(2)}, u32[]{:S(2)}) %collective-permute-start.5) | collective-permute-done | bytes 131616 | tf_op jit(solution)/shard_map/ppermute | solution.py:18
  70.7 2.5 %collective-permute-start.6 = (f32[257,128]{1,0:T(8,128)S(1)}, f32[257,128]{1,0:T(8,128)S(1)}, u32[]{:S(2)}, u32[]{:S(2)}) collective-permute-start(f32[257,128]{1,0:T(8,128)S(1)} %add.155), channel_id=1, source_target_pairs={{0,4},{4,0},{8,12},{12,8},{16,20},{20,16},{24,28},{28,24},{1,5},{5... | collective-permute-start | bytes 394760 | tf_op jit(solution)/shard_map/ppermute | solution.py:18
  73.2 3.5 %collective-permute-done.6 = f32[257,128]{1,0:T(8,128)S(1)} collective-permute-done((f32[257,128]{1,0:T(8,128)S(1)}, f32[257,128]{1,0:T(8,128)S(1)}, u32[]{:S(2)}, u32[]{:S(2)}) %collective-permute-start.6) | collective-permute-done | bytes 131616 | tf_op jit(solution)/shard_map/ppermute | solution.py:18
  76.7 1.6 %collective-permute-start.7 = (f32[257,128]{1,0:T(8,128)S(1)}, f32[257,128]{1,0:T(8,128)S(1)}, u32[]{:S(2)}, u32[]{:S(2)}) collective-permute-start(f32[257,128]{1,0:T(8,128)S(1)} %add.156), channel_id=1, source_target_pairs={{0,8},{4,12},{8,0},{12,4},{16,24},{20,28},{24,16},{28,20},{1,9},{5... | collective-permute-start | bytes 394760 | tf_op jit(solution)/shard_map/ppermute | solution.py:18
  78.4 3.4 %collective-permute-done.7 = f32[257,128]{1,0:T(8,128)S(1)} collective-permute-done((f32[257,128]{1,0:T(8,128)S(1)}, f32[257,128]{1,0:T(8,128)S(1)}, u32[]{:S(2)}, u32[]{:S(2)}) %collective-permute-start.7) | collective-permute-done | bytes 131616 | tf_op jit(solution)/shard_map/ppermute | solution.py:18
  81.8 2.7 %collective-permute-start.8 = (f32[257,128]{1,0:T(8,128)S(1)}, f32[257,128]{1,0:T(8,128)S(1)}, u32[]{:S(2)}, u32[]{:S(2)}) collective-permute-start(f32[257,128]{1,0:T(8,128)S(1)} %add.157), channel_id=1, source_target_pairs={{0,16},{4,20},{8,24},{12,28},{16,0},{20,4},{24,8},{28,12},{1,17},{... | collective-permute-start | bytes 394760 | tf_op jit(solution)/shard_map/ppermute | solution.py:18
  84.5 0.6 multiply_reduce_fusion.3
  85.1 4.1 %collective-permute-done.8 = f32[257,128]{1,0:T(8,128)S(1)} collective-permute-done((f32[257,128]{1,0:T(8,128)S(1)}, f32[257,128]{1,0:T(8,128)S(1)}, u32[]{:S(2)}, u32[]{:S(2)}) %collective-permute-start.8) | collective-permute-done | bytes 131616 | tf_op jit(solution)/shard_map/ppermute | solution.py:18
  93.9 0.6 multiply_reduce_fusion.2
  95.8 0.7 multiply_add_fusion.3
  96.4 0.6 multiply_add_fusion.1
  (67 shorter events, 3.4 us)
Async XLA Ops:
  0.6 11.8 %copy-start.5 = (f32[2,4096]{1,0:T(2,128)S(1)}, f32[2,4096]{1,0:T(2,128)}, u32[]{:S(2)}) copy-start(f32[2,4096]{1,0:T(2,128)} %param.26) | copy-start | bytes 98308
  0.6 11.8 %copy-start.2 = (f32[2,4096]{1,0:T(2,128)S(1)}, f32[2,4096]{1,0:T(2,128)}, u32[]{:S(2)}) copy-start(f32[2,4096]{1,0:T(2,128)} %param.29) | copy-start | bytes 98308
  0.7 8.9 %copy-start.8 = (f32[3,128]{1,0:T(4,128)S(1)}, f32[3,128]{1,0:T(4,128)}, u32[]{:S(2)}) copy-start(f32[3,128]{1,0:T(4,128)} %param.28) | copy-start | bytes 4612
  0.7 8.5 %copy-start.3 = (f32[128,128]{1,0:T(8,128)S(1)}, f32[128,128]{1,0:T(8,128)}, u32[]{:S(2)}) copy-start(f32[128,128]{1,0:T(8,128)} %param.17) | copy-start | bytes 196612
  0.7 8.5 %copy-start.9 = (f32[5,128]{1,0:T(8,128)S(1)}, f32[5,128]{1,0:T(8,128)}, u32[]{:S(2)}) copy-start(f32[5,128]{1,0:T(8,128)} %param.27) | copy-start | bytes 7684
  0.7 8.5 %copy-start = (f32[5,128,128]{2,1,0:T(8,128)S(1)}, f32[5,128,128]{2,1,0:T(8,128)}, u32[]{:S(2)}) copy-start(f32[5,128,128]{2,1,0:T(8,128)} %param.15) | copy-start | bytes 983044
  0.7 8.7 %copy-start.7 = (s32[128,128]{1,0:T(8,128)S(1)}, s32[128,128]{1,0:T(8,128)}, u32[]{:S(2)}) copy-start(s32[128,128]{1,0:T(8,128)} %param.20) | copy-start | bytes 196612
  0.7 15.1 %copy-start.1 = (f32[3,128,128]{2,1,0:T(8,128)S(1)}, f32[3,128,128]{2,1,0:T(8,128)}, u32[]{:S(2)}) copy-start(f32[3,128,128]{2,1,0:T(8,128)} %param.16) | copy-start | bytes 589828
  1.6 10.9 %collective-permute-start.1 = (f32[2,2,4096]{2,1,0:T(2,128)S(1)}, f32[2,2,4096]{2,1,0:T(2,128)S(1)}, u32[]{:S(2)}, u32[]{:S(2)}) collective-permute-start(f32[2,2,4096]{2,1,0:T(2,128)S(1)} %pad_maximum_fusion.2), channel_id=1, source_target_pairs={{0,1},{1,0},{2,3},{3,2},{4,5},{5,4},{6,7},{7,6},{8,9},{9,8},{10,11... | collective-permute-start | bytes 196616 | tf_op jit(solution)/shard_map/ppermute | solution.py:18
  2.1 7.3 %collective-permute-start = (f32[3,3]{1,0:T(4,128)}, f32[3,3]{1,0:T(4,128)S(1)}, u32[]{:S(2)}, u32[]{:S(2)}) collective-permute-start(f32[3,3]{1,0:T(4,128)} %bitcast.123), channel_id=1, source_target_pairs={{1,0},{2,1},{3,2},{4,3},{5,4},{6,5},{7,6},{8,7},{9,8},{10,9},{11,1... | collective-permute-start | bytes 116 | tf_op jit(solution)/shard_map/ppermute | solution.py:13
  12.2 15.7 %copy-start.4 = (f32[128,128]{1,0:T(8,128)S(1)}, f32[128,128]{1,0:T(8,128)}, u32[]{:S(2)}) copy-start(f32[128,128]{1,0:T(8,128)} %param.18) | copy-start | bytes 196612
  12.2 15.7 %copy-start.6 = (f32[128,128]{1,0:T(8,128)S(1)}, f32[128,128]{1,0:T(8,128)}, u32[]{:S(2)}) copy-start(f32[128,128]{1,0:T(8,128)} %param.19) | copy-start | bytes 196612
  12.3 15.7 %copy-start.12 = (s32[128]{0:T(128)S(1)}, s32[128]{0:T(128)}, u32[]{:S(2)}) copy-start(s32[128]{0:T(128)} %param.23) | copy-start | bytes 1540
  12.6 7.4 %collective-permute-start.2 = (f32[2,4,4096]{2,1,0:T(4,128)S(1)}, f32[2,4,4096]{2,1,0:T(4,128)S(1)}, u32[]{:S(2)}, u32[]{:S(2)}) collective-permute-start(f32[2,4,4096]{2,1,0:T(4,128)S(1)} %maximum_select_fusion.1), channel_id=1, source_target_pairs={{0,2},{1,3},{2,0},{3,1},{4,6},{5,7},{6,4},{7,5},{8,10},{9,11},{10,... | collective-permute-start | bytes 393224 | tf_op jit(solution)/shard_map/ppermute | solution.py:18
  33.2 22.7 %collective-permute-start.3 = (f32[3,3]{1,0:T(4,128)S(1)}, f32[3,3]{1,0:T(4,128)S(1)}, u32[]{:S(2)}, u32[]{:S(2)}) collective-permute-start(f32[3,3]{1,0:T(4,128)S(1)} %slice.124), channel_id=1, source_target_pairs={{0,1},{1,2},{2,3},{3,4},{4,5},{5,6},{6,7},{7,8},{8,9},{9,10},{10,1... | collective-permute-start | bytes 116 | tf_op jit(solution)/shard_map/ppermute | solution.py:13
  38.3 17.1 %copy-start.10 = (f32[5,128]{1,0:T(8,128)S(1)}, f32[5,128]{1,0:T(8,128)}, u32[]{:S(2)}) copy-start(f32[5,128]{1,0:T(8,128)} %param.24) | copy-start | bytes 7684
  38.3 17.7 %copy-start.11 = (f32[3,128]{1,0:T(4,128)S(1)}, f32[3,128]{1,0:T(4,128)}, u32[]{:S(2)}) copy-start(f32[3,128]{1,0:T(4,128)} %param.25) | copy-start | bytes 4612
  61.4 3.0 %collective-permute-start.4 = (f32[257,128]{1,0:T(8,128)S(1)}, f32[257,128]{1,0:T(8,128)S(1)}, u32[]{:S(2)}, u32[]{:S(2)}) collective-permute-start(f32[257,128]{1,0:T(8,128)S(1)} %pad_maximum_fusion.1), channel_id=1, source_target_pairs={{0,1},{1,0},{2,3},{3,2},{4,5},{5,4},{6,7},{7,6},{8,9},{9,8},{10,11... | collective-permute-start | bytes 394760 | tf_op jit(solution)/shard_map/ppermute | solution.py:18
  64.4 6.3 %collective-permute-start.5 = (f32[257,128]{1,0:T(8,128)S(1)}, f32[257,128]{1,0:T(8,128)S(1)}, u32[]{:S(2)}, u32[]{:S(2)}) collective-permute-start(f32[257,128]{1,0:T(8,128)S(1)} %fusion.51), channel_id=1, source_target_pairs={{0,2},{1,3},{2,0},{3,1},{4,6},{5,7},{6,4},{7,5},{8,10},{9,11},{10,... | collective-permute-start | bytes 394760 | tf_op jit(solution)/shard_map/ppermute | solution.py:18
  70.7 6.0 %collective-permute-start.6 = (f32[257,128]{1,0:T(8,128)S(1)}, f32[257,128]{1,0:T(8,128)S(1)}, u32[]{:S(2)}, u32[]{:S(2)}) collective-permute-start(f32[257,128]{1,0:T(8,128)S(1)} %add.155), channel_id=1, source_target_pairs={{0,4},{4,0},{8,12},{12,8},{16,20},{20,16},{24,28},{28,24},{1,5},{5... | collective-permute-start | bytes 394760 | tf_op jit(solution)/shard_map/ppermute | solution.py:18
  76.7 5.1 %collective-permute-start.7 = (f32[257,128]{1,0:T(8,128)S(1)}, f32[257,128]{1,0:T(8,128)S(1)}, u32[]{:S(2)}, u32[]{:S(2)}) collective-permute-start(f32[257,128]{1,0:T(8,128)S(1)} %add.156), channel_id=1, source_target_pairs={{0,8},{4,12},{8,0},{12,4},{16,24},{20,28},{24,16},{28,20},{1,9},{5... | collective-permute-start | bytes 394760 | tf_op jit(solution)/shard_map/ppermute | solution.py:18
  81.8 7.4 %collective-permute-start.8 = (f32[257,128]{1,0:T(8,128)S(1)}, f32[257,128]{1,0:T(8,128)S(1)}, u32[]{:S(2)}, u32[]{:S(2)}) collective-permute-start(f32[257,128]{1,0:T(8,128)S(1)} %add.157), channel_id=1, source_target_pairs={{0,16},{4,20},{8,24},{12,28},{16,0},{20,4},{24,8},{28,12},{1,17},{... | collective-permute-start | bytes 394760 | tf_op jit(solution)/shard_map/ppermute | solution.py:18

commit v8 on v6

--- a/solution.py
+++ b/solution.py
@@ -21,8 +21,12 @@
 def halving_sum(rows, extra, axis):
     count = lax.axis_size(axis)
     me = lax.axis_index(axis)
-    distance = count // 2
-    while distance >= 1:
+    bits = count.bit_length() - 1
+    order = [int(format(i, "0%db" % bits)[::-1], 2) if bits else 0 for i in range(count)]
+    chunks = rows.reshape(count, rows.shape[0] // count, *rows.shape[1:])
+    rows = jnp.concatenate([chunks[k] for k in order], axis=0)
+    distance = 1
+    while distance < count:
         half = rows.shape[0] // 2
         upper = (me // distance) % 2
         keep = lax.dynamic_slice_in_dim(rows, upper * half, half, 0)
@@ -30,7 +34,7 @@
         got = exchanged(jnp.concatenate([send, extra], axis=0), axis, distance)
         rows = keep + got[:half]
         extra = extra + got[half:]
-        distance //= 2
+        distance *= 2
     return rows, extra
 
 
@@ -148,19 +152,20 @@
     q_sq = jnp.sum(q_src * q_src) + jnp.sum(q_att * q_att)
     scalars = jnp.stack([res_sq, curv_local, res_q, q_sq])
     scalars = jnp.concatenate([scalars, jnp.zeros((lane - 4,), jnp.float32)]).reshape(1, lane)
-    summed = doubling_sum(doubling_sum(jnp.concatenate([cal_term, scalars], axis=0), "cal"), "tm")
-    res_sq, curvature, res_q, q_sq = (summed[rows, k] for k in range(4))
-    q_cal_all = summed[:rows].reshape(all_blocks, col_width)
+    own_rows, scalars = halving_sum(cal_term, scalars, "cal")
+    summed = doubling_sum(jnp.concatenate([own_rows, scalars], axis=0), "tm")
+    res_sq, curvature, res_q, q_sq = (summed[-1, k] for k in range(4))
+    q_cal = summed[:-1].reshape(blocks, col_width)
 
     norm_now = res_sq + jnp.sum(cal_res_all * cal_res_all)
     step_len = norm_now / curvature
     new_src_res = src_res - step_len * q_src
     new_att_res = att_res - step_len * q_att
-    new_cal_all = cal_res_all - step_len * q_cal_all
+    new_cal_res = cal_res - step_len * q_cal
     kept = res_sq - step_len * (2.0 * res_q - step_len * q_sq)
-    norm_next = kept + jnp.sum(new_cal_all * new_cal_all)
+    cal_next = jnp.broadcast_to(jnp.sum(new_cal_res * new_cal_res), (1, lane))
+    norm_next = kept + doubling_sum(cal_next, "cal")[0, 0]
     ratio = norm_next / norm_now
-    new_cal_res = lax.dynamic_slice_in_dim(new_cal_all, lax.axis_index("cal") * blocks, blocks, 0)
     return (
         new_src_res,
         new_att_res,

time: 85.5 us -> 83.4 us (0.975)
  waiting for transfers between devices: 20.3 us -> 14.7 us
  starting transfers between devices: 18 us -> 20 us
  other arithmetic: 12 us -> 13.3 us
    ppermute x7 -> x9, waiting for transfers between devices: 20.3 us -> 14.7 us  [exchanged(): return lax.ppermute(block, axis, [(i, i ^ distance) for i in devices])]
    ppermute x7 -> x9, starting transfers between devices: 14.7 us -> 16.7 us  [exchanged(): return lax.ppermute(block, axis, [(i, i ^ distance) for i in devices])]
    add x5, other arithmetic: 0.09 us -> 1.32 us  [doubling_sum(): rows = rows + exchanged(rows, axis, distance)]
  transfers between devices with their start and end apart: 9 -> 11, of which waited for: 6 -> 7; matrix products, arithmetic and copies ran while one was open for 22% -> 22% of each run, Pallas kernels for 0% -> 0%
where the time goes in v8:
time: 83.4 us; the launch traced here: 83 us
  matrix products  22.1 us (26%)
  starting transfers between devices  20 us (24%)
  waiting for transfers between devices  14.7 us (18%)
  other arithmetic  13.3 us (16%)
  between operations  9.08 us (11%)
  local copies, waits for them, and re-layouts  3.86 us (5%)
    ppermute x9, starting transfers between devices, exchanged(): return lax.ppermute(block, axis, [(i, i ^ distance) for i in devices])  16.7 us
    ppermute x9, waiting for transfers between devices, exchanged(): return lax.ppermute(block, axis, [(i, i ^ distance) for i in devices])  14.7 us
    dot_general x1, matrix products, local(): lax.dot_general(high_hot, cal_weighted, (((1,), (1,)), ((), ())), precisi...  8.4 us
    dot_general x1, matrix products, local(): lax.dot_general(cal_table, high_hot, (((0,), (0,)), ((), ())), precision=...  7.11 us
    dot_general x1, other arithmetic, local(): lax.dot_general(high_hot, cal_weighted, (((1,), (1,)), ((), ())), precisi...  4.09 us
    dot_general x1, matrix products, local(): lax.dot_general(spread, knot_hot, (((1,), (1,)), ((), ())), precision=EXACT)  3.92 us
    ppermute x2, starting transfers between devices, passed_along(): return lax.ppermute(block, axis, route)  3.31 us
    dot_general x1, matrix products, local(): jnp.dot(table, knot_hot, precision=EXACT).reshape(4, 3, src_rows, slots)  2.71 us
  transfers between devices with their start and end apart: 11, of which 7 were waited for; matrix products, arithmetic and copies ran while one was open for 22% of the time, Pallas kernels for 0%

profile of v8, /device:TPU:0, one launch (start us, length us, event | category | flops | bytes accessed | tf_op | source)
XLA Modules:
  0.0 83.0 jit_solution(16532783104519303876)
XLA Ops:
  0.7 0.9 %pad_maximum_fusion.3 = f32[2,2,4096]{2,1,0:T(2,128)S(1)} fusion(f32[1,2,4096]{2,1,0:T(2,128)} %bitcast.102, f32[1,2,4096]{2,1,0:T(2,128)} %bitcast.104), kind=kLoop, calls=%fused_computation.59 | loop fusion | flops 16384 | bytes 131072 | tf_op jit(solution)/shard_map/stack | solution.py:102
  2.1 1.3 %collective-permute-start = (f32[3,3]{1,0:T(4,128)}, f32[3,3]{1,0:T(4,128)S(1)}, u32[]{:S(2)}, u32[]{:S(2)}) collective-permute-start(f32[3,3]{1,0:T(4,128)} %bitcast.106), channel_id=1, source_target_pairs={{1,0},{2,1},{3,2},{4,3},{5,4},{6,5},{7,6},{8,7},{9,8},{10,9},{11,1... | collective-permute-start | bytes 116 | tf_op jit(solution)/shard_map/ppermute | solution.py:13
  3.4 0.7 constant_dynamic-update-slice_fusion.1
  4.1 0.9 %add_select_fusion = (s32[16384]{0:T(1024)S(1)}, s32[16384]{0:T(1024)S(1)}) fusion(s32[128,128]{1,0:T(8,128)} %param.22, s32[128,128]{1,0:T(8,128)} %param.21), kind=kLoop, calls=%fused_computation.41 | loop fusion | flops 344064 | bytes 262144 | tf_op jit(solution)/shard_map/jit(remainder)/select_n | solution.py:127
  5.0 4.1 %iota_compare_fusion.14 = pred[256,16384]{1,0:T(32,128)(4,1)} fusion(s32[16384]{0:T(1024)S(1)} %get-tuple-element.40), kind=kLoop, calls=%fused_computation.1.clone.clone.2 | loop fusion | flops 4194304 | bytes 4259840 | tf_op jit(solution)/shard_map/dot_general | solution.py:149
  9.4 2.7 %fusion.3 = f32[12,16384]{1,0:T(8,128)S(1)} fusion(f32[12,128]{1,0:T(8,128)S(1)} %reshape.159, s32[16384]{0:T(1024)S(1)} %subtract_bitcast_fusion), kind=kOutput, calls=%fused_computation.6 | convolution fusion | flops 304087040 | bytes 858112 | tf_op jit(solution)/shard_map/dot_general | solution.py:120
  12.5 3.2 %collective-permute-start.2 = (f32[2,4,4096]{2,1,0:T(4,128)S(1)}, f32[2,4,4096]{2,1,0:T(4,128)S(1)}, u32[]{:S(2)}, u32[]{:S(2)}) collective-permute-start(f32[2,4,4096]{2,1,0:T(4,128)S(1)} %maximum_select_fusion.1), channel_id=1, source_target_pairs={{0,2},{1,3},{2,0},{3,1},{4,6},{5,7},{6,4},{7,5},{8,10},{9,11},{10,... | collective-permute-start | bytes 393224 | tf_op jit(solution)/shard_map/ppermute | solution.py:18
  15.7 4.1 %collective-permute-done.2 = f32[2,4,4096]{2,1,0:T(4,128)S(1)} collective-permute-done((f32[2,4,4096]{2,1,0:T(4,128)S(1)}, f32[2,4,4096]{2,1,0:T(4,128)S(1)}, u32[]{:S(2)}, u32[]{:S(2)}) %collective-permute-start.2) | collective-permute-done | bytes 131104 | tf_op jit(solution)/shard_map/ppermute | solution.py:18
  19.9 0.6 fusion.16
  20.6 7.1 %fusion.11 = f32[16384]{0:T(1024)S(1)} fusion(f32[256,128]{1,0:T(8,128)S(1)} %reshape_squeeze.3, s32[16384]{0:T(1024)S(1)} %get-tuple-element.40, s32[16384]{0:T(1024)S(1)} %get-tuple-element.39), kind=kOutput, calls=%fused_computation.15 | convolution fusion | flops 6452920320 | bytes 327680 | tf_op jit(solution)/shard_map/dot_general | solution.py:129
  28.9 3.9 %fusion.2 = f32[12,128]{1,0:T(8,128)S(1)} fusion(f32[12,16384]{1,0:T(8,128)S(1)} %bitcast.101, s32[16384]{0:T(1024)S(1)} %subtract_bitcast_fusion), kind=kOutput, calls=%fused_computation.5 | convolution fusion | flops 304087040 | bytes 858112 | tf_op jit(solution)/shard_map/dot_general | solution.py:140
  33.0 2.0 %collective-permute-start.3 = (f32[3,3]{1,0:T(4,128)S(1)}, f32[3,3]{1,0:T(4,128)S(1)}, u32[]{:S(2)}, u32[]{:S(2)}) collective-permute-start(f32[3,3]{1,0:T(4,128)S(1)} %slice.153), channel_id=1, source_target_pairs={{0,1},{1,2},{2,3},{3,4},{4,5},{5,6},{6,7},{7,8},{8,9},{9,10},{10,1... | collective-permute-start | bytes 116 | tf_op jit(solution)/shard_map/ppermute | solution.py:13
  35.7 8.4 %fusion = f32[256,128]{1,0:T(8,128)S(1)} fusion(f32[16384]{0:T(1024)S(1)} %get-tuple-element.22, s32[16384]{0:T(1024)S(1)} %get-tuple-element.39, pred[256,16384]{1,0:T(32,128)(4,1)S(1)} %copy-done), kind=kOutput, calls=%fused_computation.2 | convolution fusion | flops 6446645248 | bytes 4456448 | tf_op jit(solution)/shard_map/dot_general | solution.py:149
  44.8 0.8 multiply_reduce_fusion.7
  49.5 0.7 concatenate.40
  50.2 2.0 %collective-permute-start.4 = (f32[129,128]{1,0:T(8,128)S(1)}, f32[129,128]{1,0:T(8,128)S(1)}, u32[]{:S(2)}, u32[]{:S(2)}) collective-permute-start(f32[129,128]{1,0:T(8,128)S(1)} %pad_maximum_fusion.2), channel_id=1, source_target_pairs={{0,1},{1,0},{2,3},{3,2},{4,5},{5,4},{6,7},{7,6},{8,9},{9,8},{10,11... | collective-permute-start | bytes 198152 | tf_op jit(solution)/shard_map/ppermute | solution.py:18
  52.3 0.9 %collective-permute-done.4 = f32[129,128]{1,0:T(8,128)S(1)} collective-permute-done((f32[129,128]{1,0:T(8,128)S(1)}, f32[129,128]{1,0:T(8,128)S(1)}, u32[]{:S(2)}, u32[]{:S(2)}) %collective-permute-start.4) | collective-permute-done | bytes 66080 | tf_op jit(solution)/shard_map/ppermute | solution.py:18
  53.2 2.2 %collective-permute-start.5 = (f32[65,128]{1,0:T(8,128)S(1)}, f32[65,128]{1,0:T(8,128)S(1)}, u32[]{:S(2)}, u32[]{:S(2)}) collective-permute-start(f32[65,128]{1,0:T(8,128)S(1)} %pad_maximum_fusion.4), channel_id=1, source_target_pairs={{0,2},{1,3},{2,0},{3,1},{4,6},{5,7},{6,4},{7,5},{8,10},{9,11},{10,... | collective-permute-start | bytes 99848 | tf_op jit(solution)/shard_map/ppermute | solution.py:18
  55.4 2.0 %collective-permute-done.5 = f32[65,128]{1,0:T(8,128)S(1)} collective-permute-done((f32[65,128]{1,0:T(8,128)S(1)}, f32[65,128]{1,0:T(8,128)S(1)}, u32[]{:S(2)}, u32[]{:S(2)}) %collective-permute-start.5) | collective-permute-done | bytes 33312 | tf_op jit(solution)/shard_map/ppermute | solution.py:18
  57.4 2.5 %collective-permute-start.6 = (f32[65,128]{1,0:T(8,128)S(1)}, f32[65,128]{1,0:T(8,128)S(1)}, u32[]{:S(2)}, u32[]{:S(2)}) collective-permute-start(f32[65,128]{1,0:T(8,128)S(1)} %pad_maximum_fusion.5), channel_id=1, source_target_pairs={{0,4},{4,0},{8,12},{12,8},{16,20},{20,16},{24,28},{28,24},{1,5},{5... | collective-permute-start | bytes 99848 | tf_op jit(solution)/shard_map/ppermute | solution.py:18
  59.9 1.9 %collective-permute-done.6 = f32[65,128]{1,0:T(8,128)S(1)} collective-permute-done((f32[65,128]{1,0:T(8,128)S(1)}, f32[65,128]{1,0:T(8,128)S(1)}, u32[]{:S(2)}, u32[]{:S(2)}) %collective-permute-start.6) | collective-permute-done | bytes 33312 | tf_op jit(solution)/shard_map/ppermute | solution.py:18
  61.8 1.6 %collective-permute-start.7 = (f32[65,128]{1,0:T(8,128)S(1)}, f32[65,128]{1,0:T(8,128)S(1)}, u32[]{:S(2)}, u32[]{:S(2)}) collective-permute-start(f32[65,128]{1,0:T(8,128)S(1)} %fusion.32), channel_id=1, source_target_pairs={{0,8},{4,12},{8,0},{12,4},{16,24},{20,28},{24,16},{28,20},{1,9},{5... | collective-permute-start | bytes 99848 | tf_op jit(solution)/shard_map/ppermute | solution.py:18
  63.4 2.4 %collective-permute-done.7 = f32[65,128]{1,0:T(8,128)S(1)} collective-permute-done((f32[65,128]{1,0:T(8,128)S(1)}, f32[65,128]{1,0:T(8,128)S(1)}, u32[]{:S(2)}, u32[]{:S(2)}) %collective-permute-start.7) | collective-permute-done | bytes 33312 | tf_op jit(solution)/shard_map/ppermute | solution.py:18
  65.8 2.6 %collective-permute-start.8 = (f32[65,128]{1,0:T(8,128)S(1)}, f32[65,128]{1,0:T(8,128)S(1)}, u32[]{:S(2)}, u32[]{:S(2)}) collective-permute-start(f32[65,128]{1,0:T(8,128)S(1)} %add.178), channel_id=1, source_target_pairs={{0,16},{4,20},{8,24},{12,28},{16,0},{20,4},{24,8},{28,12},{1,17},{... | collective-permute-start | bytes 99848 | tf_op jit(solution)/shard_map/ppermute | solution.py:18
  68.4 2.3 %collective-permute-done.8 = f32[65,128]{1,0:T(8,128)S(1)} collective-permute-done((f32[65,128]{1,0:T(8,128)S(1)}, f32[65,128]{1,0:T(8,128)S(1)}, u32[]{:S(2)}, u32[]{:S(2)}) %collective-permute-start.8) | collective-permute-done | bytes 33312 | tf_op jit(solution)/shard_map/ppermute | solution.py:18
  73.3 0.6 multiply_reduce_fusion.3
  73.9 0.7 broadcast_in_dim.5
  74.7 1.1 %collective-permute-done.9 = f32[1,128]{1,0:T(1,128)S(1)} collective-permute-done((f32[1,128]{1,0:T(1,128)S(1)}, f32[1,128]{1,0:T(1,128)S(1)}, u32[]{:S(2)}, u32[]{:S(2)}) %collective-permute-start.9) | collective-permute-done | bytes 544 | tf_op jit(solution)/shard_map/ppermute | solution.py:18
  75.8 0.6 broadcast_add_fusion
  76.4 2.0 %collective-permute-start.10 = (f32[1,128]{1,0:T(1,128)S(1)}, f32[1,128]{1,0:T(1,128)S(1)}, u32[]{:S(2)}, u32[]{:S(2)}) collective-permute-start(f32[1,128]{1,0:T(1,128)S(1)} %broadcast_add_fusion), channel_id=1, source_target_pairs={{0,2},{1,3},{2,0},{3,1},{4,6},{5,7},{6,4},{7,5},{8,10},{9,11},{10,... | collective-permute-start | bytes 1544 | tf_op jit(solution)/shard_map/ppermute | solution.py:18
  80.4 0.7 fusion.40
  81.8 0.7 multiply_add_fusion.3
  (80 shorter events, 5.9 us)
Async XLA Ops:
  0.6 8.8 %copy-start.10 = (f32[3,128]{1,0:T(4,128)S(1)}, f32[3,128]{1,0:T(4,128)}, u32[]{:S(2)}) copy-start(f32[3,128]{1,0:T(4,128)} %param.28) | copy-start | bytes 4612
  0.6 8.5 %copy-start.11 = (f32[5,128]{1,0:T(8,128)S(1)}, f32[5,128]{1,0:T(8,128)}, u32[]{:S(2)}) copy-start(f32[5,128]{1,0:T(8,128)} %param.27) | copy-start | bytes 7684
  0.7 8.5 %copy-start.1 = (f32[5,128,128]{2,1,0:T(8,128)S(1)}, f32[5,128,128]{2,1,0:T(8,128)}, u32[]{:S(2)}) copy-start(f32[5,128,128]{2,1,0:T(8,128)} %param.15) | copy-start | bytes 983044
  0.7 8.6 %copy-start.6 = (s32[128,128]{1,0:T(8,128)S(1)}, s32[128,128]{1,0:T(8,128)}, u32[]{:S(2)}) copy-start(s32[128,128]{1,0:T(8,128)} %param.20) | copy-start | bytes 196612
  1.5 10.8 %collective-permute-start.1 = (f32[2,2,4096]{2,1,0:T(2,128)S(1)}, f32[2,2,4096]{2,1,0:T(2,128)S(1)}, u32[]{:S(2)}, u32[]{:S(2)}) collective-permute-start(f32[2,2,4096]{2,1,0:T(2,128)S(1)} %pad_maximum_fusion.3), channel_id=1, source_target_pairs={{0,1},{1,0},{2,3},{3,2},{4,5},{5,4},{6,7},{7,6},{8,9},{9,8},{10,11... | collective-permute-start | bytes 196616 | tf_op jit(solution)/shard_map/ppermute | solution.py:18
  2.1 7.3 %collective-permute-start = (f32[3,3]{1,0:T(4,128)}, f32[3,3]{1,0:T(4,128)S(1)}, u32[]{:S(2)}, u32[]{:S(2)}) collective-permute-start(f32[3,3]{1,0:T(4,128)} %bitcast.106), channel_id=1, source_target_pairs={{1,0},{2,1},{3,2},{4,3},{5,4},{6,5},{7,6},{8,7},{9,8},{10,9},{11,1... | collective-permute-start | bytes 116 | tf_op jit(solution)/shard_map/ppermute | solution.py:13
  5.0 7.3 %copy-start.3 = (f32[2,4096]{1,0:T(2,128)S(1)}, f32[2,4096]{1,0:T(2,128)}, u32[]{:S(2)}) copy-start(f32[2,4096]{1,0:T(2,128)} %param.26) | copy-start | bytes 98308
  5.0 7.3 %copy-start.4 = (f32[2,4096]{1,0:T(2,128)S(1)}, f32[2,4096]{1,0:T(2,128)}, u32[]{:S(2)}) copy-start(f32[2,4096]{1,0:T(2,128)} %param.29) | copy-start | bytes 98308
  5.0 10.7 %copy-start.2 = (f32[3,128,128]{2,1,0:T(8,128)S(1)}, f32[3,128,128]{2,1,0:T(8,128)}, u32[]{:S(2)}) copy-start(f32[3,128,128]{2,1,0:T(8,128)} %param.16) | copy-start | bytes 589828
  12.5 7.4 %collective-permute-start.2 = (f32[2,4,4096]{2,1,0:T(4,128)S(1)}, f32[2,4,4096]{2,1,0:T(4,128)S(1)}, u32[]{:S(2)}, u32[]{:S(2)}) collective-permute-start(f32[2,4,4096]{2,1,0:T(4,128)S(1)} %maximum_select_fusion.1), channel_id=1, source_target_pairs={{0,2},{1,3},{2,0},{3,1},{4,6},{5,7},{6,4},{7,5},{8,10},{9,11},{10,... | collective-permute-start | bytes 393224 | tf_op jit(solution)/shard_map/ppermute | solution.py:18
  20.6 7.2 %copy-start.7 = (f32[128,128]{1,0:T(8,128)S(1)}, f32[128,128]{1,0:T(8,128)}, u32[]{:S(2)}) copy-start(f32[128,128]{1,0:T(8,128)} %param.18) | copy-start | bytes 196612
  20.6 7.2 %copy-start.8 = (f32[128,128]{1,0:T(8,128)S(1)}, f32[128,128]{1,0:T(8,128)}, u32[]{:S(2)}) copy-start(f32[128,128]{1,0:T(8,128)} %param.19) | copy-start | bytes 196612
  20.6 7.2 %copy-start.9 = (f32[128,128]{1,0:T(8,128)S(1)}, f32[128,128]{1,0:T(8,128)}, u32[]{:S(2)}) copy-start(f32[128,128]{1,0:T(8,128)} %param.17) | copy-start | bytes 196612
  20.6 7.2 %copy-start.14 = (s32[128]{0:T(128)S(1)}, s32[128]{0:T(128)}, u32[]{:S(2)}) copy-start(s32[128]{0:T(128)} %param.23) | copy-start | bytes 1540
  28.2 7.5 %copy-start = (pred[256,16384]{1,0:T(32,128)(4,1)S(1)}, pred[256,16384]{1,0:T(32,128)(4,1)}, u32[]{:S(2)}) copy-start(pred[256,16384]{1,0:T(32,128)(4,1)} %iota_compare_fusion.14) | copy-start | bytes 12582916
  33.0 11.8 %collective-permute-start.3 = (f32[3,3]{1,0:T(4,128)S(1)}, f32[3,3]{1,0:T(4,128)S(1)}, u32[]{:S(2)}, u32[]{:S(2)}) collective-permute-start(f32[3,3]{1,0:T(4,128)S(1)} %slice.153), channel_id=1, source_target_pairs={{0,1},{1,2},{2,3},{3,4},{4,5},{5,6},{6,7},{7,8},{8,9},{9,10},{10,1... | collective-permute-start | bytes 116 | tf_op jit(solution)/shard_map/ppermute | solution.py:13
  35.7 8.4 %copy-start.12 = (f32[5,128]{1,0:T(8,128)S(1)}, f32[5,128]{1,0:T(8,128)}, u32[]{:S(2)}) copy-start(f32[5,128]{1,0:T(8,128)} %param.24) | copy-start | bytes 7684
  35.7 9.1 %copy-start.13 = (f32[3,128]{1,0:T(4,128)S(1)}, f32[3,128]{1,0:T(4,128)}, u32[]{:S(2)}) copy-start(f32[3,128]{1,0:T(4,128)} %param.25) | copy-start | bytes 4612
  50.2 2.9 %collective-permute-start.4 = (f32[129,128]{1,0:T(8,128)S(1)}, f32[129,128]{1,0:T(8,128)S(1)}, u32[]{:S(2)}, u32[]{:S(2)}) collective-permute-start(f32[129,128]{1,0:T(8,128)S(1)} %pad_maximum_fusion.2), channel_id=1, source_target_pairs={{0,1},{1,0},{2,3},{3,2},{4,5},{5,4},{6,7},{7,6},{8,9},{9,8},{10,11... | collective-permute-start | bytes 198152 | tf_op jit(solution)/shard_map/ppermute | solution.py:18
  53.2 4.2 %collective-permute-start.5 = (f32[65,128]{1,0:T(8,128)S(1)}, f32[65,128]{1,0:T(8,128)S(1)}, u32[]{:S(2)}, u32[]{:S(2)}) collective-permute-start(f32[65,128]{1,0:T(8,128)S(1)} %pad_maximum_fusion.4), channel_id=1, source_target_pairs={{0,2},{1,3},{2,0},{3,1},{4,6},{5,7},{6,4},{7,5},{8,10},{9,11},{10,... | collective-permute-start | bytes 99848 | tf_op jit(solution)/shard_map/ppermute | solution.py:18
  57.4 4.4 %collective-permute-start.6 = (f32[65,128]{1,0:T(8,128)S(1)}, f32[65,128]{1,0:T(8,128)S(1)}, u32[]{:S(2)}, u32[]{:S(2)}) collective-permute-start(f32[65,128]{1,0:T(8,128)S(1)} %pad_maximum_fusion.5), channel_id=1, source_target_pairs={{0,4},{4,0},{8,12},{12,8},{16,20},{20,16},{24,28},{28,24},{1,5},{5... | collective-permute-start | bytes 99848 | tf_op jit(solution)/shard_map/ppermute | solution.py:18
  61.8 4.0 %collective-permute-start.7 = (f32[65,128]{1,0:T(8,128)S(1)}, f32[65,128]{1,0:T(8,128)S(1)}, u32[]{:S(2)}, u32[]{:S(2)}) collective-permute-start(f32[65,128]{1,0:T(8,128)S(1)} %fusion.32), channel_id=1, source_target_pairs={{0,8},{4,12},{8,0},{12,4},{16,24},{20,28},{24,16},{28,20},{1,9},{5... | collective-permute-start | bytes 99848 | tf_op jit(solution)/shard_map/ppermute | solution.py:18
  65.8 4.9 %collective-permute-start.8 = (f32[65,128]{1,0:T(8,128)S(1)}, f32[65,128]{1,0:T(8,128)S(1)}, u32[]{:S(2)}, u32[]{:S(2)}) collective-permute-start(f32[65,128]{1,0:T(8,128)S(1)} %add.178), channel_id=1, source_target_pairs={{0,16},{4,20},{8,24},{12,28},{16,0},{20,4},{24,8},{28,12},{1,17},{... | collective-permute-start | bytes 99848 | tf_op jit(solution)/shard_map/ppermute | solution.py:18
  73.9 9.1 %copy-start.5 = (f32[2,4096]{1,0:T(2,128)}, f32[2,4096]{1,0:T(2,128)S(1)}, u32[]{:S(2)}) copy-start(f32[2,4096]{1,0:T(2,128)S(1)} %get-tuple-element.21) | copy-start | bytes 98308
  74.6 1.2 %collective-permute-start.9 = (f32[1,128]{1,0:T(1,128)S(1)}, f32[1,128]{1,0:T(1,128)S(1)}, u32[]{:S(2)}, u32[]{:S(2)}) collective-permute-start(f32[1,128]{1,0:T(1,128)S(1)} %broadcast_in_dim.5), channel_id=1, source_target_pairs={{0,1},{1,0},{2,3},{3,2},{4,5},{5,4},{6,7},{7,6},{8,9},{9,8},{10,11... | collective-permute-start | bytes 1544 | tf_op jit(solution)/shard_map/ppermute | solution.py:18
  76.4 4.0 %collective-permute-start.10 = (f32[1,128]{1,0:T(1,128)S(1)}, f32[1,128]{1,0:T(1,128)S(1)}, u32[]{:S(2)}, u32[]{:S(2)}) collective-permute-start(f32[1,128]{1,0:T(1,128)S(1)} %broadcast_add_fusion), channel_id=1, source_target_pairs={{0,2},{1,3},{2,0},{3,1},{4,6},{5,7},{6,4},{7,5},{8,10},{9,11},{10,... | collective-permute-start | bytes 1544 | tf_op jit(solution)/shard_map/ppermute | solution.py:18

commit v9 on v8

--- a/solution.py
+++ b/solution.py
@@ -99,9 +99,8 @@
     rows = cal_size // lane
     src_rows, slots = obs_phase.shape
 
-    cal_both = doubling_gather(jnp.stack([cal_dir, cal_res]), "cal")
-    cal_values = cal_both[0]
-    cal_res_all = cal_both[1]
+    cal_values = doubling_gather(cal_dir[None], "cal")[0]
+    first_row = (lax.axis_index("tm") == 0).astype(jnp.float32)
     edge_knots = passed_along(att_dir[:, :3], ("tm", "cal"), -1)
     att_ext = jnp.concatenate([att_dir, edge_knots], axis=1)
 
@@ -148,16 +147,17 @@
     cal_weighted = flat(cal_design * weighted) * low_hot
     cal_term = lax.dot_general(high_hot, cal_weighted, (((1,), (1,)), ((), ())), precision=EXACT)
     res_sq = jnp.sum(src_res * src_res) + jnp.sum(att_res * att_res)
+    cal_sq = first_row * jnp.sum(cal_res * cal_res)
     res_q = jnp.sum(src_res * q_src) + jnp.sum(att_res * q_att)
     q_sq = jnp.sum(q_src * q_src) + jnp.sum(q_att * q_att)
-    scalars = jnp.stack([res_sq, curv_local, res_q, q_sq])
-    scalars = jnp.concatenate([scalars, jnp.zeros((lane - 4,), jnp.float32)]).reshape(1, lane)
+    scalars = jnp.stack([res_sq, curv_local, res_q, q_sq, cal_sq])
+    scalars = jnp.concatenate([scalars, jnp.zeros((lane - 5,), jnp.float32)]).reshape(1, lane)
     own_rows, scalars = halving_sum(cal_term, scalars, "cal")
     summed = doubling_sum(jnp.concatenate([own_rows, scalars], axis=0), "tm")
-    res_sq, curvature, res_q, q_sq = (summed[-1, k] for k in range(4))
+    res_sq, curvature, res_q, q_sq, cal_sq = (summed[-1, k] for k in range(5))
     q_cal = summed[:-1].reshape(blocks, col_width)
 
-    norm_now = res_sq + jnp.sum(cal_res_all * cal_res_all)
+    norm_now = res_sq + cal_sq
     step_len = norm_now / curvature
     new_src_res = src_res - step_len * q_src
     new_att_res = att_res - step_len * q_att

time: 83.4 us -> 83.1 us (level)
  waiting for transfers between devices: 14.7 us -> 13.3 us
    ppermute x9, waiting for transfers between devices: 14.7 us -> 13.3 us  [exchanged(): return lax.ppermute(block, axis, [(i, i ^ distance) for i in devices])]
    another operation x1 -> x0, other arithmetic: 0.86 us -> none  [local(): cal_both = doubling_gather(jnp.stack([cal_dir, cal_res]), 'cal')]
  transfers between devices with their start and end apart: 11 -> 11, of which waited for: 7 -> 7; matrix products, arithmetic and copies ran while one was open for 22% -> 24% of each run, Pallas kernels for 0% -> 0%
where the time goes in v9:
time: 83.1 us; the launch traced here: 82.7 us
  matrix products  22.1 us (27%)
  starting transfers between devices  20.7 us (25%)
  waiting for transfers between devices  13.3 us (16%)
  other arithmetic  13.1 us (16%)
  between operations  9.68 us (12%)
  local copies, waits for them, and re-layouts  3.86 us (5%)
    ppermute x9, starting transfers between devices, exchanged(): return lax.ppermute(block, axis, [(i, i ^ distance) for i in devices])  17.4 us
    ppermute x9, waiting for transfers between devices, exchanged(): return lax.ppermute(block, axis, [(i, i ^ distance) for i in devices])  13.3 us
    dot_general x1, matrix products, local(): lax.dot_general(high_hot, cal_weighted, (((1,), (1,)), ((), ())), precisi...  8.4 us
    dot_general x1, matrix products, local(): lax.dot_general(cal_table, high_hot, (((0,), (0,)), ((), ())), precision=...  7.12 us
    dot_general x1, other arithmetic, local(): lax.dot_general(high_hot, cal_weighted, (((1,), (1,)), ((), ())), precisi...  4.09 us
    dot_general x1, matrix products, local(): lax.dot_general(spread, knot_hot, (((1,), (1,)), ((), ())), precision=EXACT)  3.92 us
    ppermute x2, starting transfers between devices, passed_along(): return lax.ppermute(block, axis, route)  3.3 us
    dot_general x1, matrix products, local(): jnp.dot(table, knot_hot, precision=EXACT).reshape(4, 3, src_rows, slots)  2.71 us
  transfers between devices with their start and end apart: 11, of which 7 were waited for; matrix products, arithmetic and copies ran while one was open for 24% of the time, Pallas kernels for 0%

profile of v9, /device:TPU:0, one launch (start us, length us, event | category | flops | bytes accessed | tf_op | source)
XLA Modules:
  0.0 82.7 jit_solution(14448701598080243179)
XLA Ops:
  1.2 1.3 %collective-permute-start = (f32[3,3]{1,0:T(4,128)}, f32[3,3]{1,0:T(4,128)S(1)}, u32[]{:S(2)}, u32[]{:S(2)}) collective-permute-start(f32[3,3]{1,0:T(4,128)} %bitcast.105), channel_id=1, source_target_pairs={{1,0},{2,1},{3,2},{4,3},{5,4},{6,5},{7,6},{8,7},{9,8},{10,9},{11,1... | collective-permute-start | bytes 116 | tf_op jit(solution)/shard_map/ppermute | solution.py:13
  2.5 0.7 constant_dynamic-update-slice_fusion.1
  3.2 1.4 %multiply_reduce_fusion.4 = f32[]{:T(128)} fusion(f32[2,4096]{1,0:T(2,128)} %param.26), kind=kLoop, calls=%fused_computation.77 | loop fusion | flops 16383 | bytes 32772 | tf_op jit(solution)/shard_map/reduce_sum | solution.py:150
  4.6 0.9 %add_select_fusion = (s32[16384]{0:T(1024)S(1)}, s32[16384]{0:T(1024)S(1)}) fusion(s32[128,128]{1,0:T(8,128)} %param.22, s32[128,128]{1,0:T(8,128)} %param.21), kind=kLoop, calls=%fused_computation.38 | loop fusion | flops 344064 | bytes 262144 | tf_op jit(solution)/shard_map/jit(remainder)/select_n | solution.py:126
  5.6 4.1 %iota_compare_fusion.14 = pred[256,16384]{1,0:T(32,128)(4,1)} fusion(s32[16384]{0:T(1024)S(1)} %get-tuple-element.38), kind=kLoop, calls=%fused_computation.1.clone.clone.2 | loop fusion | flops 4194304 | bytes 4259840 | tf_op jit(solution)/shard_map/dot_general | solution.py:148
  10.6 2.7 %fusion.3 = f32[12,16384]{1,0:T(8,128)S(1)} fusion(f32[12,128]{1,0:T(8,128)S(1)} %reshape.253, s32[16384]{0:T(1024)S(1)} %subtract_bitcast_fusion), kind=kOutput, calls=%fused_computation.6 | convolution fusion | flops 304087040 | bytes 858112 | tf_op jit(solution)/shard_map/dot_general | solution.py:119
  13.6 3.4 %collective-permute-start.2 = (f32[1,4,4096]{2,1,0:T(4,128)S(1)}, f32[1,4,4096]{2,1,0:T(4,128)S(1)}, u32[]{:S(2)}, u32[]{:S(2)}) collective-permute-start(f32[1,4,4096]{2,1,0:T(4,128)S(1)} %maximum_select_fusion.1), channel_id=1, source_target_pairs={{0,2},{1,3},{2,0},{3,1},{4,6},{5,7},{6,4},{7,5},{8,10},{9,11},{10,... | collective-permute-start | bytes 196616 | tf_op jit(solution)/shard_map/ppermute | solution.py:18
  17.0 2.7 %collective-permute-done.2 = f32[1,4,4096]{2,1,0:T(4,128)S(1)} collective-permute-done((f32[1,4,4096]{2,1,0:T(4,128)S(1)}, f32[1,4,4096]{2,1,0:T(4,128)S(1)}, u32[]{:S(2)}, u32[]{:S(2)}) %collective-permute-start.2) | collective-permute-done | bytes 65568 | tf_op jit(solution)/shard_map/ppermute | solution.py:18
  19.8 7.1 %fusion.11 = f32[16384]{0:T(1024)S(1)} fusion(f32[256,128]{1,0:T(8,128)S(1)} %select_n.97, s32[16384]{0:T(1024)S(1)} %get-tuple-element.38, s32[16384]{0:T(1024)S(1)} %get-tuple-element.37), kind=kOutput, calls=%fused_computation.15 | convolution fusion | flops 6452920320 | bytes 327680 | tf_op jit(solution)/shard_map/dot_general | solution.py:128
  28.1 3.9 %fusion.2 = f32[12,128]{1,0:T(8,128)S(1)} fusion(f32[12,16384]{1,0:T(8,128)S(1)} %bitcast.102, s32[16384]{0:T(1024)S(1)} %subtract_bitcast_fusion), kind=kOutput, calls=%fused_computation.5 | convolution fusion | flops 304087040 | bytes 858112 | tf_op jit(solution)/shard_map/dot_general | solution.py:139
  32.2 2.0 %collective-permute-start.3 = (f32[3,3]{1,0:T(4,128)S(1)}, f32[3,3]{1,0:T(4,128)S(1)}, u32[]{:S(2)}, u32[]{:S(2)}) collective-permute-start(f32[3,3]{1,0:T(4,128)S(1)} %slice.148), channel_id=1, source_target_pairs={{0,1},{1,2},{2,3},{3,4},{4,5},{5,6},{6,7},{7,8},{8,9},{9,10},{10,1... | collective-permute-start | bytes 116 | tf_op jit(solution)/shard_map/ppermute | solution.py:13
  34.9 8.4 %fusion = f32[256,128]{1,0:T(8,128)S(1)} fusion(f32[16384]{0:T(1024)S(1)} %get-tuple-element.22, s32[16384]{0:T(1024)S(1)} %get-tuple-element.37, pred[256,16384]{1,0:T(32,128)(4,1)S(1)} %copy-done), kind=kOutput, calls=%fused_computation.2 | convolution fusion | flops 6446645248 | bytes 4456448 | tf_op jit(solution)/shard_map/dot_general | solution.py:148
  44.0 0.7 multiply_reduce_fusion.8
  48.6 0.7 concatenate.69
  49.3 2.0 %collective-permute-start.4 = (f32[129,128]{1,0:T(8,128)S(1)}, f32[129,128]{1,0:T(8,128)S(1)}, u32[]{:S(2)}, u32[]{:S(2)}) collective-permute-start(f32[129,128]{1,0:T(8,128)S(1)} %pad_maximum_fusion.2), channel_id=1, source_target_pairs={{0,1},{1,0},{2,3},{3,2},{4,5},{5,4},{6,7},{7,6},{8,9},{9,8},{10,11... | collective-permute-start | bytes 198152 | tf_op jit(solution)/shard_map/ppermute | solution.py:18
  51.3 0.9 %collective-permute-done.4 = f32[129,128]{1,0:T(8,128)S(1)} collective-permute-done((f32[129,128]{1,0:T(8,128)S(1)}, f32[129,128]{1,0:T(8,128)S(1)}, u32[]{:S(2)}, u32[]{:S(2)}) %collective-permute-start.4) | collective-permute-done | bytes 66080 | tf_op jit(solution)/shard_map/ppermute | solution.py:18
  52.3 2.7 %collective-permute-start.5 = (f32[65,128]{1,0:T(8,128)S(1)}, f32[65,128]{1,0:T(8,128)S(1)}, u32[]{:S(2)}, u32[]{:S(2)}) collective-permute-start(f32[65,128]{1,0:T(8,128)S(1)} %pad_maximum_fusion.3), channel_id=1, source_target_pairs={{0,2},{1,3},{2,0},{3,1},{4,6},{5,7},{6,4},{7,5},{8,10},{9,11},{10,... | collective-permute-start | bytes 99848 | tf_op jit(solution)/shard_map/ppermute | solution.py:18
  55.0 2.0 %collective-permute-done.5 = f32[65,128]{1,0:T(8,128)S(1)} collective-permute-done((f32[65,128]{1,0:T(8,128)S(1)}, f32[65,128]{1,0:T(8,128)S(1)}, u32[]{:S(2)}, u32[]{:S(2)}) %collective-permute-start.5) | collective-permute-done | bytes 33312 | tf_op jit(solution)/shard_map/ppermute | solution.py:18
  57.0 2.5 %collective-permute-start.6 = (f32[65,128]{1,0:T(8,128)S(1)}, f32[65,128]{1,0:T(8,128)S(1)}, u32[]{:S(2)}, u32[]{:S(2)}) collective-permute-start(f32[65,128]{1,0:T(8,128)S(1)} %pad_maximum_fusion.4), channel_id=1, source_target_pairs={{0,4},{4,0},{8,12},{12,8},{16,20},{20,16},{24,28},{28,24},{1,5},{5... | collective-permute-start | bytes 99848 | tf_op jit(solution)/shard_map/ppermute | solution.py:18
  59.5 1.9 %collective-permute-done.6 = f32[65,128]{1,0:T(8,128)S(1)} collective-permute-done((f32[65,128]{1,0:T(8,128)S(1)}, f32[65,128]{1,0:T(8,128)S(1)}, u32[]{:S(2)}, u32[]{:S(2)}) %collective-permute-start.6) | collective-permute-done | bytes 33312 | tf_op jit(solution)/shard_map/ppermute | solution.py:18
  61.4 1.6 %collective-permute-start.7 = (f32[65,128]{1,0:T(8,128)S(1)}, f32[65,128]{1,0:T(8,128)S(1)}, u32[]{:S(2)}, u32[]{:S(2)}) collective-permute-start(f32[65,128]{1,0:T(8,128)S(1)} %fusion.31), channel_id=1, source_target_pairs={{0,8},{4,12},{8,0},{12,4},{16,24},{20,28},{24,16},{28,20},{1,9},{5... | collective-permute-start | bytes 99848 | tf_op jit(solution)/shard_map/ppermute | solution.py:18
  63.0 2.4 %collective-permute-done.7 = f32[65,128]{1,0:T(8,128)S(1)} collective-permute-done((f32[65,128]{1,0:T(8,128)S(1)}, f32[65,128]{1,0:T(8,128)S(1)}, u32[]{:S(2)}, u32[]{:S(2)}) %collective-permute-start.7) | collective-permute-done | bytes 33312 | tf_op jit(solution)/shard_map/ppermute | solution.py:18
  65.4 2.6 %collective-permute-start.8 = (f32[65,128]{1,0:T(8,128)S(1)}, f32[65,128]{1,0:T(8,128)S(1)}, u32[]{:S(2)}, u32[]{:S(2)}) collective-permute-start(f32[65,128]{1,0:T(8,128)S(1)} %add.178), channel_id=1, source_target_pairs={{0,16},{4,20},{8,24},{12,28},{16,0},{20,4},{24,8},{28,12},{1,17},{... | collective-permute-start | bytes 99848 | tf_op jit(solution)/shard_map/ppermute | solution.py:18
  68.0 2.3 %collective-permute-done.8 = f32[65,128]{1,0:T(8,128)S(1)} collective-permute-done((f32[65,128]{1,0:T(8,128)S(1)}, f32[65,128]{1,0:T(8,128)S(1)}, u32[]{:S(2)}, u32[]{:S(2)}) %collective-permute-start.8) | collective-permute-done | bytes 33312 | tf_op jit(solution)/shard_map/ppermute | solution.py:18
  72.9 0.6 multiply_reduce_fusion.3
  73.5 0.7 broadcast_in_dim.5
  74.3 1.1 %collective-permute-done.9 = f32[1,128]{1,0:T(1,128)S(1)} collective-permute-done((f32[1,128]{1,0:T(1,128)S(1)}, f32[1,128]{1,0:T(1,128)S(1)}, u32[]{:S(2)}, u32[]{:S(2)}) %collective-permute-start.9) | collective-permute-done | bytes 544 | tf_op jit(solution)/shard_map/ppermute | solution.py:18
  75.4 0.6 broadcast_add_fusion
  76.1 2.0 %collective-permute-start.10 = (f32[1,128]{1,0:T(1,128)S(1)}, f32[1,128]{1,0:T(1,128)S(1)}, u32[]{:S(2)}, u32[]{:S(2)}) collective-permute-start(f32[1,128]{1,0:T(1,128)S(1)} %broadcast_add_fusion), channel_id=1, source_target_pairs={{0,2},{1,3},{2,0},{3,1},{4,6},{5,7},{6,4},{7,5},{8,10},{9,11},{10,... | collective-permute-start | bytes 1544 | tf_op jit(solution)/shard_map/ppermute | solution.py:18
  80.0 0.7 fusion.39
  81.4 0.7 multiply_add_fusion.3
  82.0 0.6 multiply_add_fusion.1
  (79 shorter events, 5.1 us)
Async XLA Ops:
  0.6 10.0 %copy-start.10 = (f32[3,128]{1,0:T(4,128)S(1)}, f32[3,128]{1,0:T(4,128)}, u32[]{:S(2)}) copy-start(f32[3,128]{1,0:T(4,128)} %param.28) | copy-start | bytes 4612
  0.6 9.0 %copy-start.11 = (f32[5,128]{1,0:T(8,128)S(1)}, f32[5,128]{1,0:T(8,128)}, u32[]{:S(2)}) copy-start(f32[5,128]{1,0:T(8,128)} %param.27) | copy-start | bytes 7684
  0.7 9.0 %copy-start.1 = (f32[5,128,128]{2,1,0:T(8,128)S(1)}, f32[5,128,128]{2,1,0:T(8,128)}, u32[]{:S(2)}) copy-start(f32[5,128,128]{2,1,0:T(8,128)} %param.15) | copy-start | bytes 983044
  0.7 9.1 %copy-start.6 = (s32[128,128]{1,0:T(8,128)S(1)}, s32[128,128]{1,0:T(8,128)}, u32[]{:S(2)}) copy-start(s32[128,128]{1,0:T(8,128)} %param.20) | copy-start | bytes 196612
  0.7 12.8 %collective-permute-start.1 = (f32[1,2,4096]{2,1,0:T(2,128)}, f32[1,2,4096]{2,1,0:T(2,128)S(1)}, u32[]{:S(2)}, u32[]{:S(2)}) collective-permute-start(f32[1,2,4096]{2,1,0:T(2,128)} %bitcast.103), channel_id=1, source_target_pairs={{0,1},{1,0},{2,3},{3,2},{4,5},{5,4},{6,7},{7,6},{8,9},{9,8},{10,11... | collective-permute-start | bytes 98312 | tf_op jit(solution)/shard_map/ppermute | solution.py:18
  1.2 9.3 %collective-permute-start = (f32[3,3]{1,0:T(4,128)}, f32[3,3]{1,0:T(4,128)S(1)}, u32[]{:S(2)}, u32[]{:S(2)}) collective-permute-start(f32[3,3]{1,0:T(4,128)} %bitcast.105), channel_id=1, source_target_pairs={{1,0},{2,1},{3,2},{4,3},{5,4},{6,5},{7,6},{8,7},{9,8},{10,9},{11,1... | collective-permute-start | bytes 116 | tf_op jit(solution)/shard_map/ppermute | solution.py:13
  5.5 8.0 %copy-start.5 = (f32[2,4096]{1,0:T(2,128)S(1)}, f32[2,4096]{1,0:T(2,128)}, u32[]{:S(2)}) copy-start(f32[2,4096]{1,0:T(2,128)} %param.29) | copy-start | bytes 98308
  5.5 11.4 %copy-start.2 = (f32[3,128,128]{2,1,0:T(8,128)S(1)}, f32[3,128,128]{2,1,0:T(8,128)}, u32[]{:S(2)}) copy-start(f32[3,128,128]{2,1,0:T(8,128)} %param.16) | copy-start | bytes 589828
  13.6 6.1 %collective-permute-start.2 = (f32[1,4,4096]{2,1,0:T(4,128)S(1)}, f32[1,4,4096]{2,1,0:T(4,128)S(1)}, u32[]{:S(2)}, u32[]{:S(2)}) collective-permute-start(f32[1,4,4096]{2,1,0:T(4,128)S(1)} %maximum_select_fusion.1), channel_id=1, source_target_pairs={{0,2},{1,3},{2,0},{3,1},{4,6},{5,7},{6,4},{7,5},{8,10},{9,11},{10,... | collective-permute-start | bytes 196616 | tf_op jit(solution)/shard_map/ppermute | solution.py:18
  19.8 7.2 %copy-start.7 = (f32[128,128]{1,0:T(8,128)S(1)}, f32[128,128]{1,0:T(8,128)}, u32[]{:S(2)}) copy-start(f32[128,128]{1,0:T(8,128)} %param.18) | copy-start | bytes 196612
  19.8 7.2 %copy-start.8 = (f32[128,128]{1,0:T(8,128)S(1)}, f32[128,128]{1,0:T(8,128)}, u32[]{:S(2)}) copy-start(f32[128,128]{1,0:T(8,128)} %param.19) | copy-start | bytes 196612
  19.8 7.2 %copy-start.9 = (f32[128,128]{1,0:T(8,128)S(1)}, f32[128,128]{1,0:T(8,128)}, u32[]{:S(2)}) copy-start(f32[128,128]{1,0:T(8,128)} %param.17) | copy-start | bytes 196612
  19.8 7.2 %copy-start.14 = (s32[128]{0:T(128)S(1)}, s32[128]{0:T(128)}, u32[]{:S(2)}) copy-start(s32[128]{0:T(128)} %param.23) | copy-start | bytes 1540
  27.3 7.5 %copy-start = (pred[256,16384]{1,0:T(32,128)(4,1)S(1)}, pred[256,16384]{1,0:T(32,128)(4,1)}, u32[]{:S(2)}) copy-start(pred[256,16384]{1,0:T(32,128)(4,1)} %iota_compare_fusion.14) | copy-start | bytes 12582916
  32.2 11.8 %collective-permute-start.3 = (f32[3,3]{1,0:T(4,128)S(1)}, f32[3,3]{1,0:T(4,128)S(1)}, u32[]{:S(2)}, u32[]{:S(2)}) collective-permute-start(f32[3,3]{1,0:T(4,128)S(1)} %slice.148), channel_id=1, source_target_pairs={{0,1},{1,2},{2,3},{3,4},{4,5},{5,6},{6,7},{7,8},{8,9},{9,10},{10,1... | collective-permute-start | bytes 116 | tf_op jit(solution)/shard_map/ppermute | solution.py:13
  34.9 8.4 %copy-start.12 = (f32[5,128]{1,0:T(8,128)S(1)}, f32[5,128]{1,0:T(8,128)}, u32[]{:S(2)}) copy-start(f32[5,128]{1,0:T(8,128)} %param.24) | copy-start | bytes 7684
  34.9 9.1 %copy-start.13 = (f32[3,128]{1,0:T(4,128)S(1)}, f32[3,128]{1,0:T(4,128)}, u32[]{:S(2)}) copy-start(f32[3,128]{1,0:T(4,128)} %param.25) | copy-start | bytes 4612
  34.9 38.0 %copy-start.4 = (f32[2,4096]{1,0:T(2,128)S(1)}, f32[2,4096]{1,0:T(2,128)}, u32[]{:S(2)}) copy-start(f32[2,4096]{1,0:T(2,128)} %param.26) | copy-start | bytes 98308
  49.3 2.9 %collective-permute-start.4 = (f32[129,128]{1,0:T(8,128)S(1)}, f32[129,128]{1,0:T(8,128)S(1)}, u32[]{:S(2)}, u32[]{:S(2)}) collective-permute-start(f32[129,128]{1,0:T(8,128)S(1)} %pad_maximum_fusion.2), channel_id=1, source_target_pairs={{0,1},{1,0},{2,3},{3,2},{4,5},{5,4},{6,7},{7,6},{8,9},{9,8},{10,11... | collective-permute-start | bytes 198152 | tf_op jit(solution)/shard_map/ppermute | solution.py:18
  52.3 4.7 %collective-permute-start.5 = (f32[65,128]{1,0:T(8,128)S(1)}, f32[65,128]{1,0:T(8,128)S(1)}, u32[]{:S(2)}, u32[]{:S(2)}) collective-permute-start(f32[65,128]{1,0:T(8,128)S(1)} %pad_maximum_fusion.3), channel_id=1, source_target_pairs={{0,2},{1,3},{2,0},{3,1},{4,6},{5,7},{6,4},{7,5},{8,10},{9,11},{10,... | collective-permute-start | bytes 99848 | tf_op jit(solution)/shard_map/ppermute | solution.py:18
  57.0 4.4 %collective-permute-start.6 = (f32[65,128]{1,0:T(8,128)S(1)}, f32[65,128]{1,0:T(8,128)S(1)}, u32[]{:S(2)}, u32[]{:S(2)}) collective-permute-start(f32[65,128]{1,0:T(8,128)S(1)} %pad_maximum_fusion.4), channel_id=1, source_target_pairs={{0,4},{4,0},{8,12},{12,8},{16,20},{20,16},{24,28},{28,24},{1,5},{5... | collective-permute-start | bytes 99848 | tf_op jit(solution)/shard_map/ppermute | solution.py:18
  61.4 4.0 %collective-permute-start.7 = (f32[65,128]{1,0:T(8,128)S(1)}, f32[65,128]{1,0:T(8,128)S(1)}, u32[]{:S(2)}, u32[]{:S(2)}) collective-permute-start(f32[65,128]{1,0:T(8,128)S(1)} %fusion.31), channel_id=1, source_target_pairs={{0,8},{4,12},{8,0},{12,4},{16,24},{20,28},{24,16},{28,20},{1,9},{5... | collective-permute-start | bytes 99848 | tf_op jit(solution)/shard_map/ppermute | solution.py:18
  65.4 4.9 %collective-permute-start.8 = (f32[65,128]{1,0:T(8,128)S(1)}, f32[65,128]{1,0:T(8,128)S(1)}, u32[]{:S(2)}, u32[]{:S(2)}) collective-permute-start(f32[65,128]{1,0:T(8,128)S(1)} %add.178), channel_id=1, source_target_pairs={{0,16},{4,20},{8,24},{12,28},{16,0},{20,4},{24,8},{28,12},{1,17},{... | collective-permute-start | bytes 99848 | tf_op jit(solution)/shard_map/ppermute | solution.py:18
  73.5 9.1 %copy-start.3 = (f32[2,4096]{1,0:T(2,128)}, f32[2,4096]{1,0:T(2,128)S(1)}, u32[]{:S(2)}) copy-start(f32[2,4096]{1,0:T(2,128)S(1)} %get-tuple-element.21) | copy-start | bytes 98308
  74.2 1.2 %collective-permute-start.9 = (f32[1,128]{1,0:T(1,128)S(1)}, f32[1,128]{1,0:T(1,128)S(1)}, u32[]{:S(2)}, u32[]{:S(2)}) collective-permute-start(f32[1,128]{1,0:T(1,128)S(1)} %broadcast_in_dim.5), channel_id=1, source_target_pairs={{0,1},{1,0},{2,3},{3,2},{4,5},{5,4},{6,7},{7,6},{8,9},{9,8},{10,11... | collective-permute-start | bytes 1544 | tf_op jit(solution)/shard_map/ppermute | solution.py:18
  76.1 4.0 %collective-permute-start.10 = (f32[1,128]{1,0:T(1,128)S(1)}, f32[1,128]{1,0:T(1,128)S(1)}, u32[]{:S(2)}, u32[]{:S(2)}) collective-permute-start(f32[1,128]{1,0:T(1,128)S(1)} %broadcast_add_fusion), channel_id=1, source_target_pairs={{0,2},{1,3},{2,0},{3,1},{4,6},{5,7},{6,4},{7,5},{8,10},{9,11},{10,... | collective-permute-start | bytes 1544 | tf_op jit(solution)/shard_map/ppermute | solution.py:18

commit v10 on v9

--- a/solution.py
+++ b/solution.py
@@ -4,7 +4,7 @@
 from jax.sharding import PartitionSpec as P
 
 
-EXACT = lax.Precision.HIGHEST
+ONE_HOT_PRECISION = lax.Precision.HIGH
 
 
 def passed_along(block, axis, distance):
@@ -116,7 +116,7 @@
     knot_hot = (flat(local_knot) == lax.broadcasted_iota(jnp.int32, (knot_count, 1), 0)).astype(jnp.float32)
 
     table = jnp.stack([att_ext[:, m : m + knot_count] for m in range(4)], axis=0).reshape(12, knot_count)
-    picked = jnp.dot(table, knot_hot, precision=EXACT).reshape(4, 3, src_rows, slots)
+    picked = jnp.dot(table, knot_hot, precision=ONE_HOT_PRECISION).reshape(4, 3, src_rows, slots)
     y_att = jnp.zeros_like(obs_phase)
     for m in range(4):
         y_att = y_att + basis[m] * jnp.sum(att_design * picked[m], axis=0)
@@ -125,7 +125,7 @@
     high_hot = (flat_index // lane == lax.broadcasted_iota(jnp.int32, (rows, 1), 0)).astype(jnp.float32)
     low_hot = (flat_index % lane == lax.broadcasted_iota(jnp.int32, (lane, 1), 0)).astype(jnp.float32)
     cal_table = cal_values.reshape(rows, lane)
-    row_vals = lax.dot_general(cal_table, high_hot, (((0,), (0,)), ((), ())), precision=EXACT)
+    row_vals = lax.dot_general(cal_table, high_hot, (((0,), (0,)), ((), ())), precision=ONE_HOT_PRECISION)
     y_cal = cal_design * jnp.sum(row_vals * low_hot, axis=0).reshape(src_rows, slots)
 
     y_src = jnp.sum(src_design * src_dir[:, :, None], axis=0)
@@ -136,7 +136,7 @@
 
     scaled = att_design * weighted[None]
     spread = jnp.stack([basis[m][None] * scaled for m in range(4)], axis=0).reshape(12, n_obs)
-    gathered = lax.dot_general(spread, knot_hot, (((1,), (1,)), ((), ())), precision=EXACT)
+    gathered = lax.dot_general(spread, knot_hot, (((1,), (1,)), ((), ())), precision=ONE_HOT_PRECISION)
     gathered = gathered.reshape(4, 3, knot_count)
     grad_ext = jnp.zeros((3, knot_count + 3), jnp.float32)
     for m in range(4):
@@ -145,7 +145,7 @@
     q_att = jnp.concatenate([grad_ext[:, :3] + incoming, grad_ext[:, 3:knot_count]], axis=1)
 
     cal_weighted = flat(cal_design * weighted) * low_hot
-    cal_term = lax.dot_general(high_hot, cal_weighted, (((1,), (1,)), ((), ())), precision=EXACT)
+    cal_term = lax.dot_general(high_hot, cal_weighted, (((1,), (1,)), ((), ())), precision=ONE_HOT_PRECISION)
     res_sq = jnp.sum(src_res * src_res) + jnp.sum(att_res * att_res)
     cal_sq = first_row * jnp.sum(cal_res * cal_res)
     res_q = jnp.sum(src_res * q_src) + jnp.sum(att_res * q_att)

time: 83.1 us -> 75.4 us (0.907)
  matrix products: 22.1 us -> 14.7 us
    dot_general x1, matrix products: 8.4 us -> 4.49 us  [local(): lax.dot_general(high_hot, cal_weighted, (((1,), (1,)), ((), ())), precisi...]
    dot_general x2, matrix products: 6.63 us -> 4.59 us  [the longest x1 2.43 us: local(): lax.dot_general(spread, knot_hot, (((1,), (1,)), ((), ())), precision=ONE...]
    dot_general x1, matrix products: 7.12 us -> 5.58 us  [local(): lax.dot_general(cal_table, high_hot, (((0,), (0,)), ((), ())), precision=...]
  transfers between devices with their start and end apart: 11 -> 11, of which waited for: 7 -> 7; matrix products, arithmetic and copies ran while one was open for 24% -> 21% of each run, Pallas kernels for 0% -> 0%
where the time goes in v10:
time: 75.4 us; the launch traced here: 75 us
  starting transfers between devices  20.5 us (27%)
  matrix products  14.7 us (19%)
  waiting for transfers between devices  13.3 us (18%)
  other arithmetic  13.1 us (17%)
  between operations  9.67 us (13%)
  local copies, waits for them, and re-layouts  3.85 us (5%)
    ppermute x9, starting transfers between devices, exchanged(): return lax.ppermute(block, axis, [(i, i ^ distance) for i in devices])  17.4 us
    ppermute x9, waiting for transfers between devices, exchanged(): return lax.ppermute(block, axis, [(i, i ^ distance) for i in devices])  13.3 us
    dot_general x1, matrix products, local(): lax.dot_general(cal_table, high_hot, (((0,), (0,)), ((), ())), precision=...  5.58 us
    dot_general x1, matrix products, local(): lax.dot_general(high_hot, cal_weighted, (((1,), (1,)), ((), ())), precisi...  4.49 us
    dot_general x1, other arithmetic, local(): lax.dot_general(high_hot, cal_weighted, (((1,), (1,)), ((), ())), precisi...  4.09 us
    ppermute x2, starting transfers between devices, passed_along(): return lax.ppermute(block, axis, route)  3.1 us
    dot_general x1, matrix products, local(): lax.dot_general(spread, knot_hot, (((1,), (1,)), ((), ())), precision=ONE...  2.43 us
    dot_general x1, matrix products, local(): jnp.dot(table, knot_hot, precision=ONE_HOT_PRECISION)  2.16 us
  transfers between devices with their start and end apart: 11, of which 7 were waited for; matrix products, arithmetic and copies ran while one was open for 21% of the time, Pallas kernels for 0%

profile of v10, /device:TPU:0, one launch (start us, length us, event | category | flops | bytes accessed | tf_op | source)
XLA Modules:
  0.0 75.0 jit_solution(677265816439627453)
XLA Ops:
  1.2 1.3 %collective-permute-start = (f32[3,3]{1,0:T(4,128)}, f32[3,3]{1,0:T(4,128)S(1)}, u32[]{:S(2)}, u32[]{:S(2)}) collective-permute-start(f32[3,3]{1,0:T(4,128)} %bitcast.105), channel_id=1, source_target_pairs={{1,0},{2,1},{3,2},{4,3},{5,4},{6,5},{7,6},{8,7},{9,8},{10,9},{11,1... | collective-permute-start | bytes 116 | tf_op jit(solution)/shard_map/ppermute | solution.py:13
  2.5 0.7 constant_dynamic-update-slice_fusion.1
  3.2 1.4 %multiply_reduce_fusion.4 = f32[]{:T(128)} fusion(f32[2,4096]{1,0:T(2,128)} %param.26), kind=kLoop, calls=%fused_computation.77 | loop fusion | flops 16383 | bytes 32772 | tf_op jit(solution)/shard_map/reduce_sum | solution.py:150
  4.6 0.9 %add_select_fusion = (s32[16384]{0:T(1024)S(1)}, s32[16384]{0:T(1024)S(1)}) fusion(s32[128,128]{1,0:T(8,128)} %param.22, s32[128,128]{1,0:T(8,128)} %param.21), kind=kLoop, calls=%fused_computation.38 | loop fusion | flops 344064 | bytes 262144 | tf_op jit(solution)/shard_map/jit(remainder)/select_n | solution.py:126
  5.6 4.1 %iota_compare_fusion.14 = pred[256,16384]{1,0:T(32,128)(4,1)} fusion(s32[16384]{0:T(1024)S(1)} %get-tuple-element.38), kind=kLoop, calls=%fused_computation.1.clone.clone.2 | loop fusion | flops 4194304 | bytes 4259840 | tf_op jit(solution)/shard_map/dot_general | solution.py:148
  10.6 2.2 %fusion.3 = f32[12,16384]{1,0:T(8,128)S(1)} fusion(f32[12,128]{1,0:T(8,128)S(1)} %reshape.253, s32[16384]{0:T(1024)S(1)} %subtract_bitcast_fusion), kind=kOutput, calls=%fused_computation.6 | convolution fusion | flops 153092096 | bytes 858112 | tf_op jit(solution)/shard_map/dot_general | solution.py:119
  13.0 3.4 %collective-permute-start.2 = (f32[1,4,4096]{2,1,0:T(4,128)S(1)}, f32[1,4,4096]{2,1,0:T(4,128)S(1)}, u32[]{:S(2)}, u32[]{:S(2)}) collective-permute-start(f32[1,4,4096]{2,1,0:T(4,128)S(1)} %maximum_select_fusion.1), channel_id=1, source_target_pairs={{0,2},{1,3},{2,0},{3,1},{4,6},{5,7},{6,4},{7,5},{8,10},{9,11},{10,... | collective-permute-start | bytes 196616 | tf_op jit(solution)/shard_map/ppermute | solution.py:18
  16.4 2.7 %collective-permute-done.2 = f32[1,4,4096]{2,1,0:T(4,128)S(1)} collective-permute-done((f32[1,4,4096]{2,1,0:T(4,128)S(1)}, f32[1,4,4096]{2,1,0:T(4,128)S(1)}, u32[]{:S(2)}, u32[]{:S(2)}) %collective-permute-start.2) | collective-permute-done | bytes 65568 | tf_op jit(solution)/shard_map/ppermute | solution.py:18
  19.3 5.6 %fusion.11 = f32[16384]{0:T(1024)S(1)} fusion(f32[256,128]{1,0:T(8,128)S(1)} %select_n.97, s32[16384]{0:T(1024)S(1)} %get-tuple-element.38, s32[16384]{0:T(1024)S(1)} %get-tuple-element.37), kind=kOutput, calls=%fused_computation.15 | convolution fusion | flops 3231694848 | bytes 327680 | tf_op jit(solution)/shard_map/dot_general | solution.py:128
  26.0 2.4 %fusion.2 = f32[12,128]{1,0:T(8,128)S(1)} fusion(f32[12,16384]{1,0:T(8,128)S(1)} %bitcast.102, s32[16384]{0:T(1024)S(1)} %subtract_bitcast_fusion), kind=kOutput, calls=%fused_computation.5 | convolution fusion | flops 153092096 | bytes 858112 | tf_op jit(solution)/shard_map/dot_general | solution.py:139
  28.6 1.8 %collective-permute-start.3 = (f32[3,3]{1,0:T(4,128)S(1)}, f32[3,3]{1,0:T(4,128)S(1)}, u32[]{:S(2)}, u32[]{:S(2)}) collective-permute-start(f32[3,3]{1,0:T(4,128)S(1)} %slice.148), channel_id=1, source_target_pairs={{0,1},{1,2},{2,3},{3,4},{4,5},{5,6},{6,7},{7,8},{8,9},{9,10},{10,1... | collective-permute-start | bytes 116 | tf_op jit(solution)/shard_map/ppermute | solution.py:13
  31.1 4.5 %fusion = f32[256,128]{1,0:T(8,128)S(1)} fusion(f32[16384]{0:T(1024)S(1)} %get-tuple-element.22, s32[16384]{0:T(1024)S(1)} %get-tuple-element.37, pred[256,16384]{1,0:T(32,128)(4,1)S(1)} %copy-done), kind=kOutput, calls=%fused_computation.2 | convolution fusion | flops 3225419776 | bytes 4456448 | tf_op jit(solution)/shard_map/dot_general | solution.py:148
  36.3 0.7 multiply_reduce_fusion.8
  40.9 0.7 concatenate.69
  41.6 2.0 %collective-permute-start.4 = (f32[129,128]{1,0:T(8,128)S(1)}, f32[129,128]{1,0:T(8,128)S(1)}, u32[]{:S(2)}, u32[]{:S(2)}) collective-permute-start(f32[129,128]{1,0:T(8,128)S(1)} %pad_maximum_fusion.2), channel_id=1, source_target_pairs={{0,1},{1,0},{2,3},{3,2},{4,5},{5,4},{6,7},{7,6},{8,9},{9,8},{10,11... | collective-permute-start | bytes 198152 | tf_op jit(solution)/shard_map/ppermute | solution.py:18
  43.6 0.9 %collective-permute-done.4 = f32[129,128]{1,0:T(8,128)S(1)} collective-permute-done((f32[129,128]{1,0:T(8,128)S(1)}, f32[129,128]{1,0:T(8,128)S(1)}, u32[]{:S(2)}, u32[]{:S(2)}) %collective-permute-start.4) | collective-permute-done | bytes 66080 | tf_op jit(solution)/shard_map/ppermute | solution.py:18
  44.6 2.7 %collective-permute-start.5 = (f32[65,128]{1,0:T(8,128)S(1)}, f32[65,128]{1,0:T(8,128)S(1)}, u32[]{:S(2)}, u32[]{:S(2)}) collective-permute-start(f32[65,128]{1,0:T(8,128)S(1)} %pad_maximum_fusion.3), channel_id=1, source_target_pairs={{0,2},{1,3},{2,0},{3,1},{4,6},{5,7},{6,4},{7,5},{8,10},{9,11},{10,... | collective-permute-start | bytes 99848 | tf_op jit(solution)/shard_map/ppermute | solution.py:18
  47.3 2.0 %collective-permute-done.5 = f32[65,128]{1,0:T(8,128)S(1)} collective-permute-done((f32[65,128]{1,0:T(8,128)S(1)}, f32[65,128]{1,0:T(8,128)S(1)}, u32[]{:S(2)}, u32[]{:S(2)}) %collective-permute-start.5) | collective-permute-done | bytes 33312 | tf_op jit(solution)/shard_map/ppermute | solution.py:18
  49.3 2.5 %collective-permute-start.6 = (f32[65,128]{1,0:T(8,128)S(1)}, f32[65,128]{1,0:T(8,128)S(1)}, u32[]{:S(2)}, u32[]{:S(2)}) collective-permute-start(f32[65,128]{1,0:T(8,128)S(1)} %pad_maximum_fusion.4), channel_id=1, source_target_pairs={{0,4},{4,0},{8,12},{12,8},{16,20},{20,16},{24,28},{28,24},{1,5},{5... | collective-permute-start | bytes 99848 | tf_op jit(solution)/shard_map/ppermute | solution.py:18
  51.8 1.9 %collective-permute-done.6 = f32[65,128]{1,0:T(8,128)S(1)} collective-permute-done((f32[65,128]{1,0:T(8,128)S(1)}, f32[65,128]{1,0:T(8,128)S(1)}, u32[]{:S(2)}, u32[]{:S(2)}) %collective-permute-start.6) | collective-permute-done | bytes 33312 | tf_op jit(solution)/shard_map/ppermute | solution.py:18
  53.7 1.6 %collective-permute-start.7 = (f32[65,128]{1,0:T(8,128)S(1)}, f32[65,128]{1,0:T(8,128)S(1)}, u32[]{:S(2)}, u32[]{:S(2)}) collective-permute-start(f32[65,128]{1,0:T(8,128)S(1)} %fusion.31), channel_id=1, source_target_pairs={{0,8},{4,12},{8,0},{12,4},{16,24},{20,28},{24,16},{28,20},{1,9},{5... | collective-permute-start | bytes 99848 | tf_op jit(solution)/shard_map/ppermute | solution.py:18
  55.3 2.4 %collective-permute-done.7 = f32[65,128]{1,0:T(8,128)S(1)} collective-permute-done((f32[65,128]{1,0:T(8,128)S(1)}, f32[65,128]{1,0:T(8,128)S(1)}, u32[]{:S(2)}, u32[]{:S(2)}) %collective-permute-start.7) | collective-permute-done | bytes 33312 | tf_op jit(solution)/shard_map/ppermute | solution.py:18
  57.7 2.6 %collective-permute-start.8 = (f32[65,128]{1,0:T(8,128)S(1)}, f32[65,128]{1,0:T(8,128)S(1)}, u32[]{:S(2)}, u32[]{:S(2)}) collective-permute-start(f32[65,128]{1,0:T(8,128)S(1)} %add.178), channel_id=1, source_target_pairs={{0,16},{4,20},{8,24},{12,28},{16,0},{20,4},{24,8},{28,12},{1,17},{... | collective-permute-start | bytes 99848 | tf_op jit(solution)/shard_map/ppermute | solution.py:18
  60.3 2.3 %collective-permute-done.8 = f32[65,128]{1,0:T(8,128)S(1)} collective-permute-done((f32[65,128]{1,0:T(8,128)S(1)}, f32[65,128]{1,0:T(8,128)S(1)}, u32[]{:S(2)}, u32[]{:S(2)}) %collective-permute-start.8) | collective-permute-done | bytes 33312 | tf_op jit(solution)/shard_map/ppermute | solution.py:18
  65.2 0.6 multiply_reduce_fusion.3
  65.9 0.7 broadcast_in_dim.5
  66.6 1.1 %collective-permute-done.9 = f32[1,128]{1,0:T(1,128)S(1)} collective-permute-done((f32[1,128]{1,0:T(1,128)S(1)}, f32[1,128]{1,0:T(1,128)S(1)}, u32[]{:S(2)}, u32[]{:S(2)}) %collective-permute-start.9) | collective-permute-done | bytes 544 | tf_op jit(solution)/shard_map/ppermute | solution.py:18
  67.7 0.6 broadcast_add_fusion
  68.4 2.0 %collective-permute-start.10 = (f32[1,128]{1,0:T(1,128)S(1)}, f32[1,128]{1,0:T(1,128)S(1)}, u32[]{:S(2)}, u32[]{:S(2)}) collective-permute-start(f32[1,128]{1,0:T(1,128)S(1)} %broadcast_add_fusion), channel_id=1, source_target_pairs={{0,2},{1,3},{2,0},{3,1},{4,6},{5,7},{6,4},{7,5},{8,10},{9,11},{10,... | collective-permute-start | bytes 1544 | tf_op jit(solution)/shard_map/ppermute | solution.py:18
  72.3 0.7 fusion.39
  73.7 0.7 multiply_add_fusion.3
  74.3 0.6 multiply_add_fusion.1
  (79 shorter events, 5.1 us)
Async XLA Ops:
  0.6 10.0 %copy-start.10 = (f32[3,128]{1,0:T(4,128)S(1)}, f32[3,128]{1,0:T(4,128)}, u32[]{:S(2)}) copy-start(f32[3,128]{1,0:T(4,128)} %param.28) | copy-start | bytes 4612
  0.6 9.0 %copy-start.11 = (f32[5,128]{1,0:T(8,128)S(1)}, f32[5,128]{1,0:T(8,128)}, u32[]{:S(2)}) copy-start(f32[5,128]{1,0:T(8,128)} %param.27) | copy-start | bytes 7684
  0.7 9.0 %copy-start.1 = (f32[5,128,128]{2,1,0:T(8,128)S(1)}, f32[5,128,128]{2,1,0:T(8,128)}, u32[]{:S(2)}) copy-start(f32[5,128,128]{2,1,0:T(8,128)} %param.15) | copy-start | bytes 983044
  0.7 9.1 %copy-start.6 = (s32[128,128]{1,0:T(8,128)S(1)}, s32[128,128]{1,0:T(8,128)}, u32[]{:S(2)}) copy-start(s32[128,128]{1,0:T(8,128)} %param.20) | copy-start | bytes 196612
  0.7 12.3 %collective-permute-start.1 = (f32[1,2,4096]{2,1,0:T(2,128)}, f32[1,2,4096]{2,1,0:T(2,128)S(1)}, u32[]{:S(2)}, u32[]{:S(2)}) collective-permute-start(f32[1,2,4096]{2,1,0:T(2,128)} %bitcast.103), channel_id=1, source_target_pairs={{0,1},{1,0},{2,3},{3,2},{4,5},{5,4},{6,7},{7,6},{8,9},{9,8},{10,11... | collective-permute-start | bytes 98312 | tf_op jit(solution)/shard_map/ppermute | solution.py:18
  1.2 9.3 %collective-permute-start = (f32[3,3]{1,0:T(4,128)}, f32[3,3]{1,0:T(4,128)S(1)}, u32[]{:S(2)}, u32[]{:S(2)}) collective-permute-start(f32[3,3]{1,0:T(4,128)} %bitcast.105), channel_id=1, source_target_pairs={{1,0},{2,1},{3,2},{4,3},{5,4},{6,5},{7,6},{8,7},{9,8},{10,9},{11,1... | collective-permute-start | bytes 116 | tf_op jit(solution)/shard_map/ppermute | solution.py:13
  5.5 7.4 %copy-start.5 = (f32[2,4096]{1,0:T(2,128)S(1)}, f32[2,4096]{1,0:T(2,128)}, u32[]{:S(2)}) copy-start(f32[2,4096]{1,0:T(2,128)} %param.29) | copy-start | bytes 98308
  5.5 10.8 %copy-start.2 = (f32[3,128,128]{2,1,0:T(8,128)S(1)}, f32[3,128,128]{2,1,0:T(8,128)}, u32[]{:S(2)}) copy-start(f32[3,128,128]{2,1,0:T(8,128)} %param.16) | copy-start | bytes 589828
  13.0 6.1 %collective-permute-start.2 = (f32[1,4,4096]{2,1,0:T(4,128)S(1)}, f32[1,4,4096]{2,1,0:T(4,128)S(1)}, u32[]{:S(2)}, u32[]{:S(2)}) collective-permute-start(f32[1,4,4096]{2,1,0:T(4,128)S(1)} %maximum_select_fusion.1), channel_id=1, source_target_pairs={{0,2},{1,3},{2,0},{3,1},{4,6},{5,7},{6,4},{7,5},{8,10},{9,11},{10,... | collective-permute-start | bytes 196616 | tf_op jit(solution)/shard_map/ppermute | solution.py:18
  19.2 5.6 %copy-start.7 = (f32[128,128]{1,0:T(8,128)S(1)}, f32[128,128]{1,0:T(8,128)}, u32[]{:S(2)}) copy-start(f32[128,128]{1,0:T(8,128)} %param.18) | copy-start | bytes 196612
  19.2 5.6 %copy-start.8 = (f32[128,128]{1,0:T(8,128)S(1)}, f32[128,128]{1,0:T(8,128)}, u32[]{:S(2)}) copy-start(f32[128,128]{1,0:T(8,128)} %param.19) | copy-start | bytes 196612
  19.2 5.6 %copy-start.9 = (f32[128,128]{1,0:T(8,128)S(1)}, f32[128,128]{1,0:T(8,128)}, u32[]{:S(2)}) copy-start(f32[128,128]{1,0:T(8,128)} %param.17) | copy-start | bytes 196612
  19.2 5.6 %copy-start.14 = (s32[128]{0:T(128)S(1)}, s32[128]{0:T(128)}, u32[]{:S(2)}) copy-start(s32[128]{0:T(128)} %param.23) | copy-start | bytes 1540
  25.2 5.8 %copy-start = (pred[256,16384]{1,0:T(32,128)(4,1)S(1)}, pred[256,16384]{1,0:T(32,128)(4,1)}, u32[]{:S(2)}) copy-start(pred[256,16384]{1,0:T(32,128)(4,1)} %iota_compare_fusion.14) | copy-start | bytes 12582916
  28.6 7.6 %collective-permute-start.3 = (f32[3,3]{1,0:T(4,128)S(1)}, f32[3,3]{1,0:T(4,128)S(1)}, u32[]{:S(2)}, u32[]{:S(2)}) collective-permute-start(f32[3,3]{1,0:T(4,128)S(1)} %slice.148), channel_id=1, source_target_pairs={{0,1},{1,2},{2,3},{3,4},{4,5},{5,6},{6,7},{7,8},{8,9},{9,10},{10,1... | collective-permute-start | bytes 116 | tf_op jit(solution)/shard_map/ppermute | solution.py:13
  31.1 4.5 %copy-start.12 = (f32[5,128]{1,0:T(8,128)S(1)}, f32[5,128]{1,0:T(8,128)}, u32[]{:S(2)}) copy-start(f32[5,128]{1,0:T(8,128)} %param.24) | copy-start | bytes 7684
  31.1 5.2 %copy-start.13 = (f32[3,128]{1,0:T(4,128)S(1)}, f32[3,128]{1,0:T(4,128)}, u32[]{:S(2)}) copy-start(f32[3,128]{1,0:T(4,128)} %param.25) | copy-start | bytes 4612
  31.1 34.1 %copy-start.4 = (f32[2,4096]{1,0:T(2,128)S(1)}, f32[2,4096]{1,0:T(2,128)}, u32[]{:S(2)}) copy-start(f32[2,4096]{1,0:T(2,128)} %param.26) | copy-start | bytes 98308
  41.6 2.9 %collective-permute-start.4 = (f32[129,128]{1,0:T(8,128)S(1)}, f32[129,128]{1,0:T(8,128)S(1)}, u32[]{:S(2)}, u32[]{:S(2)}) collective-permute-start(f32[129,128]{1,0:T(8,128)S(1)} %pad_maximum_fusion.2), channel_id=1, source_target_pairs={{0,1},{1,0},{2,3},{3,2},{4,5},{5,4},{6,7},{7,6},{8,9},{9,8},{10,11... | collective-permute-start | bytes 198152 | tf_op jit(solution)/shard_map/ppermute | solution.py:18
  44.6 4.7 %collective-permute-start.5 = (f32[65,128]{1,0:T(8,128)S(1)}, f32[65,128]{1,0:T(8,128)S(1)}, u32[]{:S(2)}, u32[]{:S(2)}) collective-permute-start(f32[65,128]{1,0:T(8,128)S(1)} %pad_maximum_fusion.3), channel_id=1, source_target_pairs={{0,2},{1,3},{2,0},{3,1},{4,6},{5,7},{6,4},{7,5},{8,10},{9,11},{10,... | collective-permute-start | bytes 99848 | tf_op jit(solution)/shard_map/ppermute | solution.py:18
  49.3 4.4 %collective-permute-start.6 = (f32[65,128]{1,0:T(8,128)S(1)}, f32[65,128]{1,0:T(8,128)S(1)}, u32[]{:S(2)}, u32[]{:S(2)}) collective-permute-start(f32[65,128]{1,0:T(8,128)S(1)} %pad_maximum_fusion.4), channel_id=1, source_target_pairs={{0,4},{4,0},{8,12},{12,8},{16,20},{20,16},{24,28},{28,24},{1,5},{5... | collective-permute-start | bytes 99848 | tf_op jit(solution)/shard_map/ppermute | solution.py:18
  53.7 4.0 %collective-permute-start.7 = (f32[65,128]{1,0:T(8,128)S(1)}, f32[65,128]{1,0:T(8,128)S(1)}, u32[]{:S(2)}, u32[]{:S(2)}) collective-permute-start(f32[65,128]{1,0:T(8,128)S(1)} %fusion.31), channel_id=1, source_target_pairs={{0,8},{4,12},{8,0},{12,4},{16,24},{20,28},{24,16},{28,20},{1,9},{5... | collective-permute-start | bytes 99848 | tf_op jit(solution)/shard_map/ppermute | solution.py:18
  57.7 4.9 %collective-permute-start.8 = (f32[65,128]{1,0:T(8,128)S(1)}, f32[65,128]{1,0:T(8,128)S(1)}, u32[]{:S(2)}, u32[]{:S(2)}) collective-permute-start(f32[65,128]{1,0:T(8,128)S(1)} %add.178), channel_id=1, source_target_pairs={{0,16},{4,20},{8,24},{12,28},{16,0},{20,4},{24,8},{28,12},{1,17},{... | collective-permute-start | bytes 99848 | tf_op jit(solution)/shard_map/ppermute | solution.py:18
  65.8 9.1 %copy-start.3 = (f32[2,4096]{1,0:T(2,128)}, f32[2,4096]{1,0:T(2,128)S(1)}, u32[]{:S(2)}) copy-start(f32[2,4096]{1,0:T(2,128)S(1)} %get-tuple-element.21) | copy-start | bytes 98308
  66.5 1.2 %collective-permute-start.9 = (f32[1,128]{1,0:T(1,128)S(1)}, f32[1,128]{1,0:T(1,128)S(1)}, u32[]{:S(2)}, u32[]{:S(2)}) collective-permute-start(f32[1,128]{1,0:T(1,128)S(1)} %broadcast_in_dim.5), channel_id=1, source_target_pairs={{0,1},{1,0},{2,3},{3,2},{4,5},{5,4},{6,7},{7,6},{8,9},{9,8},{10,11... | collective-permute-start | bytes 1544 | tf_op jit(solution)/shard_map/ppermute | solution.py:18
  68.4 4.0 %collective-permute-start.10 = (f32[1,128]{1,0:T(1,128)S(1)}, f32[1,128]{1,0:T(1,128)S(1)}, u32[]{:S(2)}, u32[]{:S(2)}) collective-permute-start(f32[1,128]{1,0:T(1,128)S(1)} %broadcast_add_fusion), channel_id=1, source_target_pairs={{0,2},{1,3},{2,0},{3,1},{4,6},{5,7},{6,4},{7,5},{8,10},{9,11},{10,... | collective-permute-start | bytes 1544 | tf_op jit(solution)/shard_map/ppermute | solution.py:18

commit v11 on v10

--- a/solution.py
+++ b/solution.py
@@ -145,7 +145,9 @@
     q_att = jnp.concatenate([grad_ext[:, :3] + incoming, grad_ext[:, 3:knot_count]], axis=1)
 
     cal_weighted = flat(cal_design * weighted) * low_hot
-    cal_term = lax.dot_general(high_hot, cal_weighted, (((1,), (1,)), ((), ())), precision=ONE_HOT_PRECISION)
+    row_start = lax.broadcasted_iota(jnp.int32, (rows, 1), 0) * lane
+    high_range = ((flat_index >= row_start) & (flat_index < row_start + lane)).astype(jnp.float32)
+    cal_term = lax.dot_general(high_range, cal_weighted, (((1,), (1,)), ((), ())), precision=ONE_HOT_PRECISION)
     res_sq = jnp.sum(src_res * src_res) + jnp.sum(att_res * att_res)
     cal_sq = first_row * jnp.sum(cal_res * cal_res)
     res_q = jnp.sum(src_res * q_src) + jnp.sum(att_res * q_att)

time: 75.4 us -> 76 us (level)
  other arithmetic: 13.1 us -> 14.3 us
  waiting for transfers between devices: 13.3 us -> 12.3 us
    dot_general x1, other arithmetic: 4.09 us -> 0.87 us  [local(): lax.dot_general(high_range, cal_weighted, (((1,), (1,)), ((), ())), preci...]
    reduce_sum x1, other arithmetic: 0.06 us -> 1.07 us  [local(): y_att = y_att + basis[m] * jnp.sum(att_design * picked[m], axis=0)]
    ppermute x9, waiting for transfers between devices: 13.3 us -> 12.3 us  [exchanged(): return lax.ppermute(block, axis, [(i, i ^ distance) for i in devices])]
    reduce_sum x1, other arithmetic: 0.15 us -> 1.13 us  [local(): y_src = jnp.sum(src_design * src_dir[:, :, None], axis=0)]
    eq x1, other arithmetic: 0.01 us -> 0.85 us  [local(): flat(local_knot) == lax.broadcasted_iota(jnp.int32, (knot_count, 1), 0)]
    select_n x2, other arithmetic: 0.11 us -> 0.94 us  [doubling_gather(): jnp.where(mine_first, jnp.concatenate([block, other], axis=1), jnp.concat...]
    unnamed x34 -> x30, local copies, waits for them, and re-layouts: 1.62 us -> 1.63 us
where the time goes in v11:
time: 76 us; the launch traced here: 75.3 us
  starting transfers between devices  20.6 us (27%)
  matrix products  14.6 us (19%)
  other arithmetic  14.3 us (19%)
  waiting for transfers between devices  12.3 us (16%)
  between operations  9.68 us (13%)
  local copies, waits for them, and re-layouts  3.92 us (5%)
    ppermute x9, starting transfers between devices, exchanged(): return lax.ppermute(block, axis, [(i, i ^ distance) for i in devices])  17.4 us
    ppermute x9, waiting for transfers between devices, exchanged(): return lax.ppermute(block, axis, [(i, i ^ distance) for i in devices])  12.3 us
    dot_general x1, matrix products, local(): lax.dot_general(cal_table, high_hot, (((0,), (0,)), ((), ())), precision=...  5.59 us
    dot_general x1, matrix products, local(): lax.dot_general(high_range, cal_weighted, (((1,), (1,)), ((), ())), preci...  4.56 us
    ppermute x2, starting transfers between devices, passed_along(): return lax.ppermute(block, axis, route)  3.27 us
    dot_general x1, matrix products, local(): lax.dot_general(spread, knot_hot, (((1,), (1,)), ((), ())), precision=ONE...  2.26 us
    dot_general x1, matrix products, local(): jnp.dot(table, knot_hot, precision=ONE_HOT_PRECISION)  2.16 us
    unnamed x30, local copies, waits for them, and re-layouts  1.63 us
  transfers between devices with their start and end apart: 11, of which 7 were waited for; matrix products, arithmetic and copies ran while one was open for 21% of the time, Pallas kernels for 0%

profile of v11, /device:TPU:0, one launch (start us, length us, event | category | flops | bytes accessed | tf_op | source)
XLA Modules:
  0.0 75.3 jit_solution(1845794005764850040)
XLA Ops:
  1.1 1.3 %collective-permute-start = (f32[3,3]{1,0:T(4,128)}, f32[3,3]{1,0:T(4,128)S(1)}, u32[]{:S(2)}, u32[]{:S(2)}) collective-permute-start(f32[3,3]{1,0:T(4,128)} %bitcast.82), channel_id=1, source_target_pairs={{1,0},{2,1},{3,2},{4,3},{5,4},{6,5},{7,6},{8,7},{9,8},{10,9},{11,1... | collective-permute-start | bytes 116 | tf_op jit(solution)/shard_map/ppermute | solution.py:13
  2.5 0.7 constant_dynamic-update-slice_fusion.1
  3.2 0.9 %add_select_fusion.1 = (s32[16384]{0:T(1024)S(1)}, s32[16384]{0:T(1024)S(1)}) fusion(s32[128,128]{1,0:T(8,128)} %param.22, s32[128,128]{1,0:T(8,128)} %param.21), kind=kLoop, calls=%fused_computation.45 | loop fusion | flops 212992 | bytes 262144 | tf_op jit(solution)/shard_map/jit(remainder)/select_n | solution.py:126
  4.1 1.4 %multiply_reduce_fusion.4 = f32[]{:T(128)} fusion(f32[2,4096]{1,0:T(2,128)} %param.26), kind=kLoop, calls=%fused_computation.80 | loop fusion | flops 16383 | bytes 32772 | tf_op jit(solution)/shard_map/reduce_sum | solution.py:152
  5.5 1.1 %multiply_reduce_fusion.1 = f32[128,128]{1,0:T(8,128)S(1)} fusion(f32[5,128,128]{2,1,0:T(8,128)} %param.15, f32[5,128]{1,0:T(8,128)} %param.27), kind=kLoop, calls=%fused_computation.23 | loop fusion | flops 147456 | bytes 395776 | tf_op jit(solution)/shard_map/reduce_sum | solution.py:131
  6.7 0.9 %subtract_bitcast_fusion = s32[16384]{0:T(1024)S(1)} fusion(s32[128,128]{1,0:T(8,128)} %param.20, s32[]{:T(128)S(6)} %mul.256), kind=kLoop, calls=%fused_computation.68 | loop fusion | flops 16384 | bytes 131076 | tf_op jit(solution)/shard_map/eq | solution.py:116
  8.3 0.7 pad_maximum_fusion.5
  9.0 2.2 %fusion.7 = f32[12,16384]{1,0:T(8,128)S(1)} fusion(f32[12,128]{1,0:T(8,128)S(1)} %reshape.259, s32[16384]{0:T(1024)S(1)} %subtract_bitcast_fusion), kind=kOutput, calls=%fused_computation.10 | convolution fusion | flops 153092096 | bytes 858112 | tf_op jit(solution)/shard_map/dot_general | solution.py:119
  11.3 0.9 %maximum_select_fusion.1 = f32[1,4,4096]{2,1,0:T(4,128)S(1)} fusion(f32[1,2,4096]{2,1,0:T(2,128)S(1)} %collective-permute-done.1, f32[1,2,4096]{2,1,0:T(2,128)} %bitcast.81, pred[]{:T(512)S(6)} %eq.65), kind=kLoop, calls=%fused_computation.61 | loop fusion | flops 49152 | bytes 131073 | tf_op jit(solution)/shard_map/jit(_where)/select_n | solution.py:57
  12.2 3.2 %collective-permute-start.2 = (f32[1,4,4096]{2,1,0:T(4,128)S(1)}, f32[1,4,4096]{2,1,0:T(4,128)S(1)}, u32[]{:S(2)}, u32[]{:S(2)}) collective-permute-start(f32[1,4,4096]{2,1,0:T(4,128)S(1)} %maximum_select_fusion.1), channel_id=1, source_target_pairs={{0,2},{1,3},{2,0},{3,1},{4,6},{5,7},{6,4},{7,5},{8,10},{9,11},{10,... | collective-permute-start | bytes 196616 | tf_op jit(solution)/shard_map/ppermute | solution.py:18
  15.5 1.1 %fusion.20 = (f32[128,128]{1,0:T(8,128)S(1)}, f32[128,128]{1,0:T(8,128)S(1)}, f32[128,128]{1,0:T(8,128)S(1)}, f32[128,128]{1,0:T(8,128)S(1)}) fusion(f32[3,128,128]{2,1,0:T(8,128)} %param.16, f32[1,3,128,128]{3,1,2,0:T(4,128)S(1)} %get-tuple-element.30, f32[1,3,128,128]{3,1,2,0:T(4,128)S(1)} %get-tuple-element.28, ...), kind=kLoop, calls=%fused_computation.35 | loop fusion | flops 327680 | bytes 1245184 | tf_op jit(solution)/shard_map/reduce_sum | solution.py:122
  16.5 1.7 %collective-permute-done.2 = f32[1,4,4096]{2,1,0:T(4,128)S(1)} collective-permute-done((f32[1,4,4096]{2,1,0:T(4,128)S(1)}, f32[1,4,4096]{2,1,0:T(4,128)S(1)}, u32[]{:S(2)}, u32[]{:S(2)}) %collective-permute-start.2) | collective-permute-done | bytes 65568 | tf_op jit(solution)/shard_map/ppermute | solution.py:18
  18.3 5.6 %fusion.16 = f32[16384]{0:T(1024)S(1)} fusion(f32[256,128]{1,0:T(8,128)S(1)} %select_n.96, s32[16384]{0:T(1024)S(1)} %add_select_fusion, s32[16384]{0:T(1024)S(1)} %get-tuple-element.25), kind=kOutput, calls=%fused_computation.20 | convolution fusion | flops 3231694848 | bytes 327680 | tf_op jit(solution)/shard_map/dot_general | solution.py:128
  25.1 2.3 %fusion.6 = f32[12,128]{1,0:T(8,128)S(1)} fusion(f32[12,16384]{1,0:T(8,128)S(1)} %bitcast.79, s32[16384]{0:T(1024)S(1)} %subtract_bitcast_fusion), kind=kOutput, calls=%fused_computation.9 | convolution fusion | flops 153092096 | bytes 858112 | tf_op jit(solution)/shard_map/dot_general | solution.py:139
  27.5 2.0 %collective-permute-start.3 = (f32[3,3]{1,0:T(4,128)S(1)}, f32[3,3]{1,0:T(4,128)S(1)}, u32[]{:S(2)}, u32[]{:S(2)}) collective-permute-start(f32[3,3]{1,0:T(4,128)S(1)} %slice.148), channel_id=1, source_target_pairs={{0,1},{1,2},{2,3},{3,4},{4,5},{5,6},{6,7},{7,8},{8,9},{9,10},{10,1... | collective-permute-start | bytes 116 | tf_op jit(solution)/shard_map/ppermute | solution.py:13
  29.5 0.7 multiply_reduce_fusion.2
  30.2 0.9 %fusion.50 = f32[128,16384]{1,0:T(8,128)S(1)} fusion(f32[16384]{0:T(1024)S(1)} %get-tuple-element.22, s32[16384]{0:T(1024)S(1)} %get-tuple-element.25), kind=kLoop, calls=%fused_computation.6.clone.2 | loop fusion | flops 4194304 | bytes 8519680 | tf_op jit(solution)/shard_map/dot_general | solution.py:150
  31.2 4.6 %fusion = f32[256,128]{1,0:T(8,128)S(1)} fusion(s32[16384]{0:T(1024)S(1)} %get-tuple-element.26, s32[256]{0:T(256)S(1)} %get-tuple-element.56, s32[256]{0:T(256)S(1)} %get-tuple-element.55, f32[128,16384]{1,0:T(8,128)S(1)} %fusion.50), kind=kOutput, calls=%fused_computation.2 | convolution fusion | flops 3233808384 | bytes 8587264 | tf_op jit(solution)/shard_map/dot_general | solution.py:150
  36.4 0.7 multiply_reduce_fusion.8
  41.0 0.8 %concatenate.69 = f32[128]{0:T(128)S(1)} concatenate(f32[1]{0:T(128)} %bitcast.9, f32[1]{0:T(128)} %bitcast.10, f32[1]{0:T(128)} %bitcast.15, f32[1]{0:T(128)} %bitcast.16, f32[1]{0:T(128)} %bitcast.17, f32[123]{0:T(128)S(1)} %broadcast_in_dim.4), dimensions={0} | concatenate | bytes 1024 | tf_op jit(solution)/shard_map/concatenate | solution.py:156
  41.8 2.0 %collective-permute-start.4 = (f32[129,128]{1,0:T(8,128)S(1)}, f32[129,128]{1,0:T(8,128)S(1)}, u32[]{:S(2)}, u32[]{:S(2)}) collective-permute-start(f32[129,128]{1,0:T(8,128)S(1)} %pad_maximum_fusion.2), channel_id=1, source_target_pairs={{0,1},{1,0},{2,3},{3,2},{4,5},{5,4},{6,7},{7,6},{8,9},{9,8},{10,11... | collective-permute-start | bytes 198152 | tf_op jit(solution)/shard_map/ppermute | solution.py:18
  43.8 0.9 %collective-permute-done.4 = f32[129,128]{1,0:T(8,128)S(1)} collective-permute-done((f32[129,128]{1,0:T(8,128)S(1)}, f32[129,128]{1,0:T(8,128)S(1)}, u32[]{:S(2)}, u32[]{:S(2)}) %collective-permute-start.4) | collective-permute-done | bytes 66080 | tf_op jit(solution)/shard_map/ppermute | solution.py:18
  44.8 2.8 %collective-permute-start.5 = (f32[65,128]{1,0:T(8,128)S(1)}, f32[65,128]{1,0:T(8,128)S(1)}, u32[]{:S(2)}, u32[]{:S(2)}) collective-permute-start(f32[65,128]{1,0:T(8,128)S(1)} %pad_maximum_fusion.3), channel_id=1, source_target_pairs={{0,2},{1,3},{2,0},{3,1},{4,6},{5,7},{6,4},{7,5},{8,10},{9,11},{10,... | collective-permute-start | bytes 99848 | tf_op jit(solution)/shard_map/ppermute | solution.py:18
  47.6 2.0 %collective-permute-done.5 = f32[65,128]{1,0:T(8,128)S(1)} collective-permute-done((f32[65,128]{1,0:T(8,128)S(1)}, f32[65,128]{1,0:T(8,128)S(1)}, u32[]{:S(2)}, u32[]{:S(2)}) %collective-permute-start.5) | collective-permute-done | bytes 33312 | tf_op jit(solution)/shard_map/ppermute | solution.py:18
  49.7 2.5 %collective-permute-start.6 = (f32[65,128]{1,0:T(8,128)S(1)}, f32[65,128]{1,0:T(8,128)S(1)}, u32[]{:S(2)}, u32[]{:S(2)}) collective-permute-start(f32[65,128]{1,0:T(8,128)S(1)} %pad_maximum_fusion.4), channel_id=1, source_target_pairs={{0,4},{4,0},{8,12},{12,8},{16,20},{20,16},{24,28},{28,24},{1,5},{5... | collective-permute-start | bytes 99848 | tf_op jit(solution)/shard_map/ppermute | solution.py:18
  52.1 1.9 %collective-permute-done.6 = f32[65,128]{1,0:T(8,128)S(1)} collective-permute-done((f32[65,128]{1,0:T(8,128)S(1)}, f32[65,128]{1,0:T(8,128)S(1)}, u32[]{:S(2)}, u32[]{:S(2)}) %collective-permute-start.6) | collective-permute-done | bytes 33312 | tf_op jit(solution)/shard_map/ppermute | solution.py:18
  54.1 1.6 %collective-permute-start.7 = (f32[65,128]{1,0:T(8,128)S(1)}, f32[65,128]{1,0:T(8,128)S(1)}, u32[]{:S(2)}, u32[]{:S(2)}) collective-permute-start(f32[65,128]{1,0:T(8,128)S(1)} %fusion.35), channel_id=1, source_target_pairs={{0,8},{4,12},{8,0},{12,4},{16,24},{20,28},{24,16},{28,20},{1,9},{5... | collective-permute-start | bytes 99848 | tf_op jit(solution)/shard_map/ppermute | solution.py:18
  55.7 2.4 %collective-permute-done.7 = f32[65,128]{1,0:T(8,128)S(1)} collective-permute-done((f32[65,128]{1,0:T(8,128)S(1)}, f32[65,128]{1,0:T(8,128)S(1)}, u32[]{:S(2)}, u32[]{:S(2)}) %collective-permute-start.7) | collective-permute-done | bytes 33312 | tf_op jit(solution)/shard_map/ppermute | solution.py:18
  58.1 2.6 %collective-permute-start.8 = (f32[65,128]{1,0:T(8,128)S(1)}, f32[65,128]{1,0:T(8,128)S(1)}, u32[]{:S(2)}, u32[]{:S(2)}) collective-permute-start(f32[65,128]{1,0:T(8,128)S(1)} %add.187), channel_id=1, source_target_pairs={{0,16},{4,20},{8,24},{12,28},{16,0},{20,4},{24,8},{28,12},{1,17},{... | collective-permute-start | bytes 99848 | tf_op jit(solution)/shard_map/ppermute | solution.py:18
  60.6 2.3 %collective-permute-done.8 = f32[65,128]{1,0:T(8,128)S(1)} collective-permute-done((f32[65,128]{1,0:T(8,128)S(1)}, f32[65,128]{1,0:T(8,128)S(1)}, u32[]{:S(2)}, u32[]{:S(2)}) %collective-permute-start.8) | collective-permute-done | bytes 33312 | tf_op jit(solution)/shard_map/ppermute | solution.py:18
  66.9 1.1 %collective-permute-done.9 = f32[1,128]{1,0:T(1,128)S(1)} collective-permute-done((f32[1,128]{1,0:T(1,128)S(1)}, f32[1,128]{1,0:T(1,128)S(1)}, u32[]{:S(2)}, u32[]{:S(2)}) %collective-permute-start.9) | collective-permute-done | bytes 544 | tf_op jit(solution)/shard_map/ppermute | solution.py:18
  68.7 2.0 %collective-permute-start.10 = (f32[1,128]{1,0:T(1,128)S(1)}, f32[1,128]{1,0:T(1,128)S(1)}, u32[]{:S(2)}, u32[]{:S(2)}) collective-permute-start(f32[1,128]{1,0:T(1,128)S(1)} %broadcast_add_fusion.1), channel_id=1, source_target_pairs={{0,2},{1,3},{2,0},{3,1},{4,6},{5,7},{6,4},{7,5},{8,10},{9,11},{10,... | collective-permute-start | bytes 1544 | tf_op jit(solution)/shard_map/ppermute | solution.py:18
  (77 shorter events, 8.2 us)
Async XLA Ops:
  0.6 10.7 %collective-permute-start.1 = (f32[1,2,4096]{2,1,0:T(2,128)}, f32[1,2,4096]{2,1,0:T(2,128)S(1)}, u32[]{:S(2)}, u32[]{:S(2)}) collective-permute-start(f32[1,2,4096]{2,1,0:T(2,128)} %bitcast.80), channel_id=1, source_target_pairs={{0,1},{1,0},{2,3},{3,2},{4,5},{5,4},{6,7},{7,6},{8,9},{9,8},{10,11... | collective-permute-start | bytes 98312 | tf_op jit(solution)/shard_map/ppermute | solution.py:18
  1.1 7.0 %collective-permute-start = (f32[3,3]{1,0:T(4,128)}, f32[3,3]{1,0:T(4,128)S(1)}, u32[]{:S(2)}, u32[]{:S(2)}) collective-permute-start(f32[3,3]{1,0:T(4,128)} %bitcast.82), channel_id=1, source_target_pairs={{1,0},{2,1},{3,2},{4,3},{5,4},{6,5},{7,6},{8,7},{9,8},{10,9},{11,1... | collective-permute-start | bytes 116 | tf_op jit(solution)/shard_map/ppermute | solution.py:13
  11.3 12.6 %copy-start.5 = (f32[128,128]{1,0:T(8,128)S(1)}, f32[128,128]{1,0:T(8,128)}, u32[]{:S(2)}) copy-start(f32[128,128]{1,0:T(8,128)} %param.18) | copy-start | bytes 196612
  11.3 12.6 %copy-start.6 = (f32[128,128]{1,0:T(8,128)S(1)}, f32[128,128]{1,0:T(8,128)}, u32[]{:S(2)}) copy-start(f32[128,128]{1,0:T(8,128)} %param.19) | copy-start | bytes 196612
  11.3 12.6 %copy-start.7 = (f32[128,128]{1,0:T(8,128)S(1)}, f32[128,128]{1,0:T(8,128)}, u32[]{:S(2)}) copy-start(f32[128,128]{1,0:T(8,128)} %param.17) | copy-start | bytes 196612
  11.3 12.6 %copy-start.12 = (s32[128]{0:T(128)S(1)}, s32[128]{0:T(128)}, u32[]{:S(2)}) copy-start(s32[128]{0:T(128)} %param.23) | copy-start | bytes 1540
  12.2 6.0 %collective-permute-start.2 = (f32[1,4,4096]{2,1,0:T(4,128)S(1)}, f32[1,4,4096]{2,1,0:T(4,128)S(1)}, u32[]{:S(2)}, u32[]{:S(2)}) collective-permute-start(f32[1,4,4096]{2,1,0:T(4,128)S(1)} %maximum_select_fusion.1), channel_id=1, source_target_pairs={{0,2},{1,3},{2,0},{3,1},{4,6},{5,7},{6,4},{7,5},{8,10},{9,11},{10,... | collective-permute-start | bytes 196616 | tf_op jit(solution)/shard_map/ppermute | solution.py:18
  15.5 8.6 %copy-start = (f32[5,128,128]{2,1,0:T(8,128)S(1)}, f32[5,128,128]{2,1,0:T(8,128)}, u32[]{:S(2)}) copy-start(f32[5,128,128]{2,1,0:T(8,128)} %param.15) | copy-start | bytes 983044
  15.5 8.8 %copy-start.1 = (f32[3,128,128]{2,1,0:T(8,128)S(1)}, f32[3,128,128]{2,1,0:T(8,128)}, u32[]{:S(2)}) copy-start(f32[3,128,128]{2,1,0:T(8,128)} %param.16) | copy-start | bytes 589828
  27.5 8.9 %collective-permute-start.3 = (f32[3,3]{1,0:T(4,128)S(1)}, f32[3,3]{1,0:T(4,128)S(1)}, u32[]{:S(2)}, u32[]{:S(2)}) collective-permute-start(f32[3,3]{1,0:T(4,128)S(1)} %slice.148), channel_id=1, source_target_pairs={{0,1},{1,2},{2,3},{3,4},{4,5},{5,6},{6,7},{7,8},{8,9},{9,10},{10,1... | collective-permute-start | bytes 116 | tf_op jit(solution)/shard_map/ppermute | solution.py:13
  31.1 4.7 %copy-start.10 = (f32[5,128]{1,0:T(8,128)S(1)}, f32[5,128]{1,0:T(8,128)}, u32[]{:S(2)}) copy-start(f32[5,128]{1,0:T(8,128)} %param.24) | copy-start | bytes 7684
  31.1 5.3 %copy-start.11 = (f32[3,128]{1,0:T(4,128)S(1)}, f32[3,128]{1,0:T(4,128)}, u32[]{:S(2)}) copy-start(f32[3,128]{1,0:T(4,128)} %param.25) | copy-start | bytes 4612
  31.1 34.4 %copy-start.3 = (f32[2,4096]{1,0:T(2,128)S(1)}, f32[2,4096]{1,0:T(2,128)}, u32[]{:S(2)}) copy-start(f32[2,4096]{1,0:T(2,128)} %param.26) | copy-start | bytes 98308
  31.1 42.3 %copy-start.9 = (f32[5,128]{1,0:T(8,128)S(1)}, f32[5,128]{1,0:T(8,128)}, u32[]{:S(2)}) copy-start(f32[5,128]{1,0:T(8,128)} %param.27) | copy-start | bytes 7684
  31.1 42.9 %copy-start.8 = (f32[3,128]{1,0:T(4,128)S(1)}, f32[3,128]{1,0:T(4,128)}, u32[]{:S(2)}) copy-start(f32[3,128]{1,0:T(4,128)} %param.28) | copy-start | bytes 4612
  31.2 43.6 %copy-start.4 = (f32[2,4096]{1,0:T(2,128)S(1)}, f32[2,4096]{1,0:T(2,128)}, u32[]{:S(2)}) copy-start(f32[2,4096]{1,0:T(2,128)} %param.29) | copy-start | bytes 98308
  41.8 2.9 %collective-permute-start.4 = (f32[129,128]{1,0:T(8,128)S(1)}, f32[129,128]{1,0:T(8,128)S(1)}, u32[]{:S(2)}, u32[]{:S(2)}) collective-permute-start(f32[129,128]{1,0:T(8,128)S(1)} %pad_maximum_fusion.2), channel_id=1, source_target_pairs={{0,1},{1,0},{2,3},{3,2},{4,5},{5,4},{6,7},{7,6},{8,9},{9,8},{10,11... | collective-permute-start | bytes 198152 | tf_op jit(solution)/shard_map/ppermute | solution.py:18
  44.8 4.8 %collective-permute-start.5 = (f32[65,128]{1,0:T(8,128)S(1)}, f32[65,128]{1,0:T(8,128)S(1)}, u32[]{:S(2)}, u32[]{:S(2)}) collective-permute-start(f32[65,128]{1,0:T(8,128)S(1)} %pad_maximum_fusion.3), channel_id=1, source_target_pairs={{0,2},{1,3},{2,0},{3,1},{4,6},{5,7},{6,4},{7,5},{8,10},{9,11},{10,... | collective-permute-start | bytes 99848 | tf_op jit(solution)/shard_map/ppermute | solution.py:18
  49.7 4.4 %collective-permute-start.6 = (f32[65,128]{1,0:T(8,128)S(1)}, f32[65,128]{1,0:T(8,128)S(1)}, u32[]{:S(2)}, u32[]{:S(2)}) collective-permute-start(f32[65,128]{1,0:T(8,128)S(1)} %pad_maximum_fusion.4), channel_id=1, source_target_pairs={{0,4},{4,0},{8,12},{12,8},{16,20},{20,16},{24,28},{28,24},{1,5},{5... | collective-permute-start | bytes 99848 | tf_op jit(solution)/shard_map/ppermute | solution.py:18
  54.1 4.0 %collective-permute-start.7 = (f32[65,128]{1,0:T(8,128)S(1)}, f32[65,128]{1,0:T(8,128)S(1)}, u32[]{:S(2)}, u32[]{:S(2)}) collective-permute-start(f32[65,128]{1,0:T(8,128)S(1)} %fusion.35), channel_id=1, source_target_pairs={{0,8},{4,12},{8,0},{12,4},{16,24},{20,28},{24,16},{28,20},{1,9},{5... | collective-permute-start | bytes 99848 | tf_op jit(solution)/shard_map/ppermute | solution.py:18
  58.1 4.9 %collective-permute-start.8 = (f32[65,128]{1,0:T(8,128)S(1)}, f32[65,128]{1,0:T(8,128)S(1)}, u32[]{:S(2)}, u32[]{:S(2)}) collective-permute-start(f32[65,128]{1,0:T(8,128)S(1)} %add.187), channel_id=1, source_target_pairs={{0,16},{4,20},{8,24},{12,28},{16,0},{20,4},{24,8},{28,12},{1,17},{... | collective-permute-start | bytes 99848 | tf_op jit(solution)/shard_map/ppermute | solution.py:18
  66.2 9.2 %copy-start.2 = (f32[2,4096]{1,0:T(2,128)}, f32[2,4096]{1,0:T(2,128)S(1)}, u32[]{:S(2)}) copy-start(f32[2,4096]{1,0:T(2,128)S(1)} %get-tuple-element.21) | copy-start | bytes 98308
  66.9 1.2 %collective-permute-start.9 = (f32[1,128]{1,0:T(1,128)S(1)}, f32[1,128]{1,0:T(1,128)S(1)}, u32[]{:S(2)}, u32[]{:S(2)}) collective-permute-start(f32[1,128]{1,0:T(1,128)S(1)} %broadcast_in_dim.5), channel_id=1, source_target_pairs={{0,1},{1,0},{2,3},{3,2},{4,5},{5,4},{6,7},{7,6},{8,9},{9,8},{10,11... | collective-permute-start | bytes 1544 | tf_op jit(solution)/shard_map/ppermute | solution.py:18
  68.7 4.0 %collective-permute-start.10 = (f32[1,128]{1,0:T(1,128)S(1)}, f32[1,128]{1,0:T(1,128)S(1)}, u32[]{:S(2)}, u32[]{:S(2)}) collective-permute-start(f32[1,128]{1,0:T(1,128)S(1)} %broadcast_add_fusion.1), channel_id=1, source_target_pairs={{0,2},{1,3},{2,0},{3,1},{4,6},{5,7},{6,4},{7,5},{8,10},{9,11},{10,... | collective-permute-start | bytes 1544 | tf_op jit(solution)/shard_map/ppermute | solution.py:18

commit v12 on v10

--- a/solution.py
+++ b/solution.py
@@ -99,7 +99,8 @@
     rows = cal_size // lane
     src_rows, slots = obs_phase.shape
 
-    cal_values = doubling_gather(cal_dir[None], "cal")[0]
+    cal_both = doubling_gather(jnp.stack([cal_dir, cal_res]), "cal")
+    cal_values = cal_both[0]
     first_row = (lax.axis_index("tm") == 0).astype(jnp.float32)
     edge_knots = passed_along(att_dir[:, :3], ("tm", "cal"), -1)
     att_ext = jnp.concatenate([att_dir, edge_knots], axis=1)
@@ -152,19 +153,35 @@
     q_sq = jnp.sum(q_src * q_src) + jnp.sum(q_att * q_att)
     scalars = jnp.stack([res_sq, curv_local, res_q, q_sq, cal_sq])
     scalars = jnp.concatenate([scalars, jnp.zeros((lane - 5,), jnp.float32)]).reshape(1, lane)
-    own_rows, scalars = halving_sum(cal_term, scalars, "cal")
-    summed = doubling_sum(jnp.concatenate([own_rows, scalars], axis=0), "tm")
+    cal_count = lax.axis_size("cal")
+    cal_me = lax.axis_index("cal")
+    parity = cal_me % 2
+    share = rows // cal_count
+    chunks = cal_term.reshape(cal_count // 2, 2, share, lane)
+    keep = lax.dynamic_index_in_dim(chunks, parity, axis=1, keepdims=False).reshape(-1, lane)
+    send = lax.dynamic_index_in_dim(chunks, 1 - parity, axis=1, keepdims=False).reshape(-1, lane)
+    got = exchanged(jnp.concatenate([send, scalars], axis=0), "cal", 1)
+    summed = jnp.concatenate([keep + got[:-1], scalars + got[-1:]], axis=0)
+    distance = 2
+    while distance < cal_count:
+        summed = summed + exchanged(summed, "cal", distance)
+        distance *= 2
+    summed = doubling_sum(summed, "tm")
     res_sq, curvature, res_q, q_sq, cal_sq = (summed[-1, k] for k in range(5))
-    q_cal = summed[:-1].reshape(blocks, col_width)
+    q_kept = summed[:-1].reshape(cal_count // 2, blocks * col_width)
 
     norm_now = res_sq + cal_sq
     step_len = norm_now / curvature
     new_src_res = src_res - step_len * q_src
     new_att_res = att_res - step_len * q_att
-    new_cal_res = cal_res - step_len * q_cal
+    res_kept = cal_both[1].reshape(cal_count // 2, 2, blocks * col_width)
+    res_kept = lax.dynamic_index_in_dim(res_kept, parity, axis=1, keepdims=False)
+    new_kept = res_kept - step_len * q_kept
+    new_cal_res = lax.dynamic_index_in_dim(new_kept, cal_me // 2, axis=0, keepdims=False)
+    new_cal_res = new_cal_res.reshape(blocks, col_width)
     kept = res_sq - step_len * (2.0 * res_q - step_len * q_sq)
-    cal_next = jnp.broadcast_to(jnp.sum(new_cal_res * new_cal_res), (1, lane))
-    norm_next = kept + doubling_sum(cal_next, "cal")[0, 0]
+    cal_next = jnp.broadcast_to(jnp.sum(new_kept * new_kept), (1, lane))
+    norm_next = kept + (cal_next + exchanged(cal_next, "cal", 1))[0, 0]
     ratio = norm_next / norm_now
     return (
         new_src_res,

time: 75.4 us -> 76 us (level)
  starting transfers between devices: 20.5 us -> 18.7 us
  waiting for transfers between devices: 13.3 us -> 14.7 us
    ppermute x9 -> x8, starting transfers between devices: 17.4 us -> 15.8 us  [exchanged(): return lax.ppermute(block, axis, [(i, i ^ distance) for i in devices])]
    ppermute x9 -> x8, waiting for transfers between devices: 13.3 us -> 14.7 us  [exchanged(): return lax.ppermute(block, axis, [(i, i ^ distance) for i in devices])]
    add x5 -> x3, other arithmetic: 1.32 us -> 0.03 us  [doubling_sum(): rows = rows + exchanged(rows, axis, distance)]
    another operation x0 -> x1, other arithmetic: none -> 0.81 us  [local(): cal_both = doubling_gather(jnp.stack([cal_dir, cal_res]), 'cal')]
  transfers between devices with their start and end apart: 11 -> 10, of which waited for: 7 -> 6; matrix products, arithmetic and copies ran while one was open for 21% -> 21% of each run, Pallas kernels for 0% -> 0%
where the time goes in v12:
time: 76 us; the launch traced here: 75.2 us
  starting transfers between devices  18.7 us (25%)
  waiting for transfers between devices  14.7 us (19%)
  matrix products  14.7 us (19%)
  other arithmetic  13.4 us (18%)
  between operations  9.65 us (13%)
  local copies, waits for them, and re-layouts  4.13 us (5%)
    ppermute x8, starting transfers between devices, exchanged(): return lax.ppermute(block, axis, [(i, i ^ distance) for i in devices])  15.8 us
    ppermute x8, waiting for transfers between devices, exchanged(): return lax.ppermute(block, axis, [(i, i ^ distance) for i in devices])  14.7 us
    dot_general x1, matrix products, local(): lax.dot_general(cal_table, high_hot, (((0,), (0,)), ((), ())), precision=...  5.59 us
    dot_general x1, matrix products, local(): lax.dot_general(high_hot, cal_weighted, (((1,), (1,)), ((), ())), precisi...  4.49 us
    dot_general x1, other arithmetic, local(): lax.dot_general(high_hot, cal_weighted, (((1,), (1,)), ((), ())), precisi...  4.09 us
    ppermute x2, starting transfers between devices, passed_along(): return lax.ppermute(block, axis, route)  2.85 us
    dot_general x1, matrix products, local(): lax.dot_general(spread, knot_hot, (((1,), (1,)), ((), ())), precision=ONE...  2.43 us
    dot_general x1, matrix products, local(): jnp.dot(table, knot_hot, precision=ONE_HOT_PRECISION)  2.16 us
  transfers between devices with their start and end apart: 10, of which 6 were waited for; matrix products, arithmetic and copies ran while one was open for 21% of the time, Pallas kernels for 0%

profile of v12, /device:TPU:0, one launch (start us, length us, event | category | flops | bytes accessed | tf_op | source)
XLA Modules:
  0.0 75.2 jit_solution(18272731278284079767)
XLA Ops:
  0.7 1.4 %collective-permute-start = (f32[3,3]{1,0:T(4,128)}, f32[3,3]{1,0:T(4,128)S(1)}, u32[]{:S(2)}, u32[]{:S(2)}) collective-permute-start(f32[3,3]{1,0:T(4,128)} %bitcast.117), channel_id=1, source_target_pairs={{1,0},{2,1},{3,2},{4,3},{5,4},{6,5},{7,6},{8,7},{9,8},{10,9},{11,1... | collective-permute-start | bytes 116 | tf_op jit(solution)/shard_map/ppermute | solution.py:13
  2.1 0.8 %pad_maximum_fusion.3 = f32[2,2,4096]{2,1,0:T(2,128)S(1)} fusion(f32[1,2,4096]{2,1,0:T(2,128)} %bitcast.113, f32[1,2,4096]{2,1,0:T(2,128)} %bitcast.111), kind=kLoop, calls=%fused_computation.58 | loop fusion | flops 16384 | bytes 131072 | tf_op jit(solution)/shard_map/stack | solution.py:102
  2.9 1.2 %collective-permute-start.1 = (f32[2,2,4096]{2,1,0:T(2,128)S(1)}, f32[2,2,4096]{2,1,0:T(2,128)S(1)}, u32[]{:S(2)}, u32[]{:S(2)}) collective-permute-start(f32[2,2,4096]{2,1,0:T(2,128)S(1)} %pad_maximum_fusion.3), channel_id=1, source_target_pairs={{0,1},{1,0},{2,3},{3,2},{4,5},{5,4},{6,7},{7,6},{8,9},{9,8},{10,11... | collective-permute-start | bytes 196616 | tf_op jit(solution)/shard_map/ppermute | solution.py:18
  4.1 1.4 %multiply_reduce_fusion.4 = f32[]{:T(128)} fusion(f32[2,4096]{1,0:T(2,128)} %param.26), kind=kLoop, calls=%fused_computation.77 | loop fusion | flops 16383 | bytes 32772 | tf_op jit(solution)/shard_map/reduce_sum | solution.py:151
  5.5 0.7 constant_dynamic-update-slice_fusion.1
  6.2 0.9 %add_select_fusion = (s32[16384]{0:T(1024)S(1)}, s32[16384]{0:T(1024)S(1)}) fusion(s32[128,128]{1,0:T(8,128)} %param.22, s32[128,128]{1,0:T(8,128)} %param.21), kind=kLoop, calls=%fused_computation.38 | loop fusion | flops 344064 | bytes 262144 | tf_op jit(solution)/shard_map/jit(remainder)/select_n | solution.py:127
  7.2 4.1 %iota_compare_fusion.14 = pred[256,16384]{1,0:T(32,128)(4,1)} fusion(s32[16384]{0:T(1024)S(1)} %get-tuple-element.38), kind=kLoop, calls=%fused_computation.1.clone.clone.2 | loop fusion | flops 4194304 | bytes 4259840 | tf_op jit(solution)/shard_map/dot_general | solution.py:149
  12.2 2.2 %fusion.3 = f32[12,16384]{1,0:T(8,128)S(1)} fusion(f32[12,128]{1,0:T(8,128)S(1)} %reshape.164, s32[16384]{0:T(1024)S(1)} %subtract_bitcast_fusion), kind=kOutput, calls=%fused_computation.6 | convolution fusion | flops 153092096 | bytes 858112 | tf_op jit(solution)/shard_map/dot_general | solution.py:120
  14.7 3.0 %collective-permute-start.2 = (f32[2,4,4096]{2,1,0:T(4,128)S(1)}, f32[2,4,4096]{2,1,0:T(4,128)S(1)}, u32[]{:S(2)}, u32[]{:S(2)}) collective-permute-start(f32[2,4,4096]{2,1,0:T(4,128)S(1)} %maximum_select_fusion.1), channel_id=1, source_target_pairs={{0,2},{1,3},{2,0},{3,1},{4,6},{5,7},{6,4},{7,5},{8,10},{9,11},{10,... | collective-permute-start | bytes 393224 | tf_op jit(solution)/shard_map/ppermute | solution.py:18
  17.8 3.7 %collective-permute-done.2 = f32[2,4,4096]{2,1,0:T(4,128)S(1)} collective-permute-done((f32[2,4,4096]{2,1,0:T(4,128)S(1)}, f32[2,4,4096]{2,1,0:T(4,128)S(1)}, u32[]{:S(2)}, u32[]{:S(2)}) %collective-permute-start.2) | collective-permute-done | bytes 131104 | tf_op jit(solution)/shard_map/ppermute | solution.py:18
  21.6 5.6 %fusion.11 = f32[16384]{0:T(1024)S(1)} fusion(f32[256,128]{1,0:T(8,128)S(1)} %reshape_squeeze.6, s32[16384]{0:T(1024)S(1)} %get-tuple-element.38, s32[16384]{0:T(1024)S(1)} %get-tuple-element.37), kind=kOutput, calls=%fused_computation.15 | convolution fusion | flops 3231694848 | bytes 327680 | tf_op jit(solution)/shard_map/dot_general | solution.py:129
  28.4 2.4 %fusion.2 = f32[12,128]{1,0:T(8,128)S(1)} fusion(f32[12,16384]{1,0:T(8,128)S(1)} %bitcast.110, s32[16384]{0:T(1024)S(1)} %subtract_bitcast_fusion), kind=kOutput, calls=%fused_computation.5 | convolution fusion | flops 153092096 | bytes 858112 | tf_op jit(solution)/shard_map/dot_general | solution.py:140
  31.0 0.6 multiply_reduce_fusion.3
  31.7 1.4 %collective-permute-start.3 = (f32[3,3]{1,0:T(4,128)S(1)}, f32[3,3]{1,0:T(4,128)S(1)}, u32[]{:S(2)}, u32[]{:S(2)}) collective-permute-start(f32[3,3]{1,0:T(4,128)S(1)} %slice.125), channel_id=1, source_target_pairs={{0,1},{1,2},{2,3},{3,4},{4,5},{5,6},{6,7},{7,8},{8,9},{9,10},{10,1... | collective-permute-start | bytes 116 | tf_op jit(solution)/shard_map/ppermute | solution.py:13
  33.7 4.5 %fusion = f32[256,128]{1,0:T(8,128)S(1)} fusion(f32[16384]{0:T(1024)S(1)} %get-tuple-element.22, s32[16384]{0:T(1024)S(1)} %get-tuple-element.37, pred[256,16384]{1,0:T(32,128)(4,1)S(1)} %copy-done), kind=kOutput, calls=%fused_computation.2 | convolution fusion | flops 3225419776 | bytes 4456448 | tf_op jit(solution)/shard_map/dot_general | solution.py:149
  38.3 0.7 multiply_reduce_fusion.8
  42.9 0.7 concatenate.33
  43.6 2.4 %collective-permute-start.4 = (f32[129,128]{1,0:T(8,128)S(1)}, f32[129,128]{1,0:T(8,128)S(1)}, u32[]{:S(2)}, u32[]{:S(2)}) collective-permute-start(f32[129,128]{1,0:T(8,128)S(1)} %pad_maximum_fusion.1), channel_id=1, source_target_pairs={{0,1},{1,0},{2,3},{3,2},{4,5},{5,4},{6,7},{7,6},{8,9},{9,8},{10,11... | collective-permute-start | bytes 198152 | tf_op jit(solution)/shard_map/ppermute | solution.py:18
  46.0 0.9 %collective-permute-done.4 = f32[129,128]{1,0:T(8,128)S(1)} collective-permute-done((f32[129,128]{1,0:T(8,128)S(1)}, f32[129,128]{1,0:T(8,128)S(1)}, u32[]{:S(2)}, u32[]{:S(2)}) %collective-permute-start.4) | collective-permute-done | bytes 66080 | tf_op jit(solution)/shard_map/ppermute | solution.py:18
  46.9 2.4 %collective-permute-start.5 = (f32[129,128]{1,0:T(8,128)S(1)}, f32[129,128]{1,0:T(8,128)S(1)}, u32[]{:S(2)}, u32[]{:S(2)}) collective-permute-start(f32[129,128]{1,0:T(8,128)S(1)} %pad_maximum_fusion.2), channel_id=1, source_target_pairs={{0,2},{1,3},{2,0},{3,1},{4,6},{5,7},{6,4},{7,5},{8,10},{9,11},{10,... | collective-permute-start | bytes 198152 | tf_op jit(solution)/shard_map/ppermute | solution.py:18
  49.3 2.7 %collective-permute-done.5 = f32[129,128]{1,0:T(8,128)S(1)} collective-permute-done((f32[129,128]{1,0:T(8,128)S(1)}, f32[129,128]{1,0:T(8,128)S(1)}, u32[]{:S(2)}, u32[]{:S(2)}) %collective-permute-start.5) | collective-permute-done | bytes 66080 | tf_op jit(solution)/shard_map/ppermute | solution.py:18
  52.0 2.5 %collective-permute-start.6 = (f32[129,128]{1,0:T(8,128)S(1)}, f32[129,128]{1,0:T(8,128)S(1)}, u32[]{:S(2)}, u32[]{:S(2)}) collective-permute-start(f32[129,128]{1,0:T(8,128)S(1)} %fusion.31), channel_id=1, source_target_pairs={{0,4},{4,0},{8,12},{12,8},{16,20},{20,16},{24,28},{28,24},{1,5},{5... | collective-permute-start | bytes 198152 | tf_op jit(solution)/shard_map/ppermute | solution.py:18
  54.5 2.3 %collective-permute-done.6 = f32[129,128]{1,0:T(8,128)S(1)} collective-permute-done((f32[129,128]{1,0:T(8,128)S(1)}, f32[129,128]{1,0:T(8,128)S(1)}, u32[]{:S(2)}, u32[]{:S(2)}) %collective-permute-start.6) | collective-permute-done | bytes 66080 | tf_op jit(solution)/shard_map/ppermute | solution.py:18
  56.8 1.6 %collective-permute-start.7 = (f32[129,128]{1,0:T(8,128)S(1)}, f32[129,128]{1,0:T(8,128)S(1)}, u32[]{:S(2)}, u32[]{:S(2)}) collective-permute-start(f32[129,128]{1,0:T(8,128)S(1)} %add.169), channel_id=1, source_target_pairs={{0,8},{4,12},{8,0},{12,4},{16,24},{20,28},{24,16},{28,20},{1,9},{5... | collective-permute-start | bytes 198152 | tf_op jit(solution)/shard_map/ppermute | solution.py:18
  58.5 2.6 %collective-permute-done.7 = f32[129,128]{1,0:T(8,128)S(1)} collective-permute-done((f32[129,128]{1,0:T(8,128)S(1)}, f32[129,128]{1,0:T(8,128)S(1)}, u32[]{:S(2)}, u32[]{:S(2)}) %collective-permute-start.7) | collective-permute-done | bytes 66080 | tf_op jit(solution)/shard_map/ppermute | solution.py:18
  61.1 2.7 %collective-permute-start.8 = (f32[129,128]{1,0:T(8,128)S(1)}, f32[129,128]{1,0:T(8,128)S(1)}, u32[]{:S(2)}, u32[]{:S(2)}) collective-permute-start(f32[129,128]{1,0:T(8,128)S(1)} %add.170), channel_id=1, source_target_pairs={{0,16},{4,20},{8,24},{12,28},{16,0},{20,4},{24,8},{28,12},{1,17},{... | collective-permute-start | bytes 198152 | tf_op jit(solution)/shard_map/ppermute | solution.py:18
  63.9 2.5 %collective-permute-done.8 = f32[129,128]{1,0:T(8,128)S(1)} collective-permute-done((f32[129,128]{1,0:T(8,128)S(1)}, f32[129,128]{1,0:T(8,128)S(1)}, u32[]{:S(2)}, u32[]{:S(2)}) %collective-permute-start.8) | collective-permute-done | bytes 66080 | tf_op jit(solution)/shard_map/ppermute | solution.py:18
  69.1 0.7 multiply_reduce_fusion.2
  69.8 0.6 broadcast_in_dim.5
  72.6 0.7 broadcast_add_fusion
  73.3 0.7 multiply_add_fusion.3
  74.6 0.6 multiply_add_fusion.1
  (77 shorter events, 4.4 us)
Async XLA Ops:
  0.6 11.6 %copy-start.10 = (f32[3,128]{1,0:T(4,128)S(1)}, f32[3,128]{1,0:T(4,128)}, u32[]{:S(2)}) copy-start(f32[3,128]{1,0:T(4,128)} %param.28) | copy-start | bytes 4612
  0.6 10.6 %copy-start.6 = (s32[128,128]{1,0:T(8,128)S(1)}, s32[128,128]{1,0:T(8,128)}, u32[]{:S(2)}) copy-start(s32[128,128]{1,0:T(8,128)} %param.20) | copy-start | bytes 196612
  0.7 10.6 %copy-start.11 = (f32[5,128]{1,0:T(8,128)S(1)}, f32[5,128]{1,0:T(8,128)}, u32[]{:S(2)}) copy-start(f32[5,128]{1,0:T(8,128)} %param.27) | copy-start | bytes 7684
  0.7 10.6 %copy-start.1 = (f32[5,128,128]{2,1,0:T(8,128)S(1)}, f32[5,128,128]{2,1,0:T(8,128)}, u32[]{:S(2)}) copy-start(f32[5,128,128]{2,1,0:T(8,128)} %param.15) | copy-start | bytes 983044
  0.7 11.4 %collective-permute-start = (f32[3,3]{1,0:T(4,128)}, f32[3,3]{1,0:T(4,128)S(1)}, u32[]{:S(2)}, u32[]{:S(2)}) collective-permute-start(f32[3,3]{1,0:T(4,128)} %bitcast.117), channel_id=1, source_target_pairs={{1,0},{2,1},{3,2},{4,3},{5,4},{6,5},{7,6},{8,7},{9,8},{10,9},{11,1... | collective-permute-start | bytes 116 | tf_op jit(solution)/shard_map/ppermute | solution.py:13
  2.9 11.6 %collective-permute-start.1 = (f32[2,2,4096]{2,1,0:T(2,128)S(1)}, f32[2,2,4096]{2,1,0:T(2,128)S(1)}, u32[]{:S(2)}, u32[]{:S(2)}) collective-permute-start(f32[2,2,4096]{2,1,0:T(2,128)S(1)} %pad_maximum_fusion.3), channel_id=1, source_target_pairs={{0,1},{1,0},{2,3},{3,2},{4,5},{5,4},{6,7},{7,6},{8,9},{9,8},{10,11... | collective-permute-start | bytes 196616 | tf_op jit(solution)/shard_map/ppermute | solution.py:18
  7.1 7.4 %copy-start.3 = (f32[2,4096]{1,0:T(2,128)S(1)}, f32[2,4096]{1,0:T(2,128)}, u32[]{:S(2)}) copy-start(f32[2,4096]{1,0:T(2,128)} %param.29) | copy-start | bytes 98308
  7.1 7.4 %copy-start.4 = (f32[2,4096]{1,0:T(2,128)S(1)}, f32[2,4096]{1,0:T(2,128)}, u32[]{:S(2)}) copy-start(f32[2,4096]{1,0:T(2,128)} %param.26) | copy-start | bytes 98308
  7.2 10.5 %copy-start.2 = (f32[3,128,128]{2,1,0:T(8,128)S(1)}, f32[3,128,128]{2,1,0:T(8,128)}, u32[]{:S(2)}) copy-start(f32[3,128,128]{2,1,0:T(8,128)} %param.16) | copy-start | bytes 589828
  14.7 6.7 %collective-permute-start.2 = (f32[2,4,4096]{2,1,0:T(4,128)S(1)}, f32[2,4,4096]{2,1,0:T(4,128)S(1)}, u32[]{:S(2)}, u32[]{:S(2)}) collective-permute-start(f32[2,4,4096]{2,1,0:T(4,128)S(1)} %maximum_select_fusion.1), channel_id=1, source_target_pairs={{0,2},{1,3},{2,0},{3,1},{4,6},{5,7},{6,4},{7,5},{8,10},{9,11},{10,... | collective-permute-start | bytes 393224 | tf_op jit(solution)/shard_map/ppermute | solution.py:18
  21.6 5.6 %copy-start.7 = (f32[128,128]{1,0:T(8,128)S(1)}, f32[128,128]{1,0:T(8,128)}, u32[]{:S(2)}) copy-start(f32[128,128]{1,0:T(8,128)} %param.18) | copy-start | bytes 196612
  21.6 5.6 %copy-start.8 = (f32[128,128]{1,0:T(8,128)S(1)}, f32[128,128]{1,0:T(8,128)}, u32[]{:S(2)}) copy-start(f32[128,128]{1,0:T(8,128)} %param.19) | copy-start | bytes 196612
  21.6 5.6 %copy-start.9 = (f32[128,128]{1,0:T(8,128)S(1)}, f32[128,128]{1,0:T(8,128)}, u32[]{:S(2)}) copy-start(f32[128,128]{1,0:T(8,128)} %param.17) | copy-start | bytes 196612
  21.6 5.6 %copy-start.14 = (s32[128]{0:T(128)S(1)}, s32[128]{0:T(128)}, u32[]{:S(2)}) copy-start(s32[128]{0:T(128)} %param.23) | copy-start | bytes 1540
  27.6 5.5 %copy-start.12 = (f32[5,128]{1,0:T(8,128)S(1)}, f32[5,128]{1,0:T(8,128)}, u32[]{:S(2)}) copy-start(f32[5,128]{1,0:T(8,128)} %param.24) | copy-start | bytes 7684
  27.6 6.1 %copy-start = (pred[256,16384]{1,0:T(32,128)(4,1)S(1)}, pred[256,16384]{1,0:T(32,128)(4,1)}, u32[]{:S(2)}) copy-start(pred[256,16384]{1,0:T(32,128)(4,1)} %iota_compare_fusion.14) | copy-start | bytes 12582916
  31.7 6.6 %collective-permute-start.3 = (f32[3,3]{1,0:T(4,128)S(1)}, f32[3,3]{1,0:T(4,128)S(1)}, u32[]{:S(2)}, u32[]{:S(2)}) collective-permute-start(f32[3,3]{1,0:T(4,128)S(1)} %slice.125), channel_id=1, source_target_pairs={{0,1},{1,2},{2,3},{3,4},{4,5},{5,6},{6,7},{7,8},{8,9},{9,10},{10,1... | collective-permute-start | bytes 116 | tf_op jit(solution)/shard_map/ppermute | solution.py:13
  33.7 4.5 %copy-start.13 = (f32[3,128]{1,0:T(4,128)S(1)}, f32[3,128]{1,0:T(4,128)}, u32[]{:S(2)}) copy-start(f32[3,128]{1,0:T(4,128)} %param.25) | copy-start | bytes 4612
  43.6 3.3 %collective-permute-start.4 = (f32[129,128]{1,0:T(8,128)S(1)}, f32[129,128]{1,0:T(8,128)S(1)}, u32[]{:S(2)}, u32[]{:S(2)}) collective-permute-start(f32[129,128]{1,0:T(8,128)S(1)} %pad_maximum_fusion.1), channel_id=1, source_target_pairs={{0,1},{1,0},{2,3},{3,2},{4,5},{5,4},{6,7},{7,6},{8,9},{9,8},{10,11... | collective-permute-start | bytes 198152 | tf_op jit(solution)/shard_map/ppermute | solution.py:18
  46.9 5.1 %collective-permute-start.5 = (f32[129,128]{1,0:T(8,128)S(1)}, f32[129,128]{1,0:T(8,128)S(1)}, u32[]{:S(2)}, u32[]{:S(2)}) collective-permute-start(f32[129,128]{1,0:T(8,128)S(1)} %pad_maximum_fusion.2), channel_id=1, source_target_pairs={{0,2},{1,3},{2,0},{3,1},{4,6},{5,7},{6,4},{7,5},{8,10},{9,11},{10,... | collective-permute-start | bytes 198152 | tf_op jit(solution)/shard_map/ppermute | solution.py:18
  52.0 4.8 %collective-permute-start.6 = (f32[129,128]{1,0:T(8,128)S(1)}, f32[129,128]{1,0:T(8,128)S(1)}, u32[]{:S(2)}, u32[]{:S(2)}) collective-permute-start(f32[129,128]{1,0:T(8,128)S(1)} %fusion.31), channel_id=1, source_target_pairs={{0,4},{4,0},{8,12},{12,8},{16,20},{20,16},{24,28},{28,24},{1,5},{5... | collective-permute-start | bytes 198152 | tf_op jit(solution)/shard_map/ppermute | solution.py:18
  56.8 4.4 %collective-permute-start.7 = (f32[129,128]{1,0:T(8,128)S(1)}, f32[129,128]{1,0:T(8,128)S(1)}, u32[]{:S(2)}, u32[]{:S(2)}) collective-permute-start(f32[129,128]{1,0:T(8,128)S(1)} %add.169), channel_id=1, source_target_pairs={{0,8},{4,12},{8,0},{12,4},{16,24},{20,28},{24,16},{28,20},{1,9},{5... | collective-permute-start | bytes 198152 | tf_op jit(solution)/shard_map/ppermute | solution.py:18
  61.1 5.3 %collective-permute-start.8 = (f32[129,128]{1,0:T(8,128)S(1)}, f32[129,128]{1,0:T(8,128)S(1)}, u32[]{:S(2)}, u32[]{:S(2)}) collective-permute-start(f32[129,128]{1,0:T(8,128)S(1)} %add.170), channel_id=1, source_target_pairs={{0,16},{4,20},{8,24},{12,28},{16,0},{20,4},{24,8},{28,12},{1,17},{... | collective-permute-start | bytes 198152 | tf_op jit(solution)/shard_map/ppermute | solution.py:18
  70.4 2.2 %collective-permute-start.9 = (f32[1,128]{1,0:T(1,128)S(1)}, f32[1,128]{1,0:T(1,128)S(1)}, u32[]{:S(2)}, u32[]{:S(2)}) collective-permute-start(f32[1,128]{1,0:T(1,128)S(1)} %broadcast_in_dim.5), channel_id=1, source_target_pairs={{0,1},{1,0},{2,3},{3,2},{4,5},{5,4},{6,7},{7,6},{8,9},{9,8},{10,11... | collective-permute-start | bytes 1544 | tf_op jit(solution)/shard_map/ppermute | solution.py:18
  72.6 2.7 %copy-start.5 = (f32[2,4096]{1,0:T(2,128)}, f32[2,4096]{1,0:T(2,128)S(1)}, u32[]{:S(2)}) copy-start(f32[2,4096]{1,0:T(2,128)S(1)} %reshape.171) | copy-start | bytes 98308

commit v13 on v10

--- a/solution.py
+++ b/solution.py
@@ -101,8 +101,9 @@
 
     cal_values = doubling_gather(cal_dir[None], "cal")[0]
     first_row = (lax.axis_index("tm") == 0).astype(jnp.float32)
-    edge_knots = passed_along(att_dir[:, :3], ("tm", "cal"), -1)
-    att_ext = jnp.concatenate([att_dir, edge_knots], axis=1)
+    edge_both = passed_along(jnp.stack([att_dir[:, :3], att_res[:, :3]]), ("tm", "cal"), -1)
+    att_ext = jnp.concatenate([att_dir, edge_both[0]], axis=1)
+    next_res = edge_both[1]
 
     live_mask = (lax.broadcasted_iota(jnp.int32, obs_phase.shape, 1) < obs_count[:, None]).astype(
         jnp.float32
@@ -141,21 +142,38 @@
     grad_ext = jnp.zeros((3, knot_count + 3), jnp.float32)
     for m in range(4):
         grad_ext = grad_ext + jnp.pad(gathered[m], ((0, 0), (m, 3 - m)))
-    incoming = passed_along(grad_ext[:, knot_count:], ("tm", "cal"), 1)
-    q_att = jnp.concatenate([grad_ext[:, :3] + incoming, grad_ext[:, 3:knot_count]], axis=1)
+    own_att = grad_ext[:, :knot_count]
+    edge_out = grad_ext[:, knot_count:]
 
     cal_weighted = flat(cal_design * weighted) * low_hot
     cal_term = lax.dot_general(high_hot, cal_weighted, (((1,), (1,)), ((), ())), precision=ONE_HOT_PRECISION)
     res_sq = jnp.sum(src_res * src_res) + jnp.sum(att_res * att_res)
     cal_sq = first_row * jnp.sum(cal_res * cal_res)
-    res_q = jnp.sum(src_res * q_src) + jnp.sum(att_res * q_att)
-    q_sq = jnp.sum(q_src * q_src) + jnp.sum(q_att * q_att)
+    res_q = jnp.sum(src_res * q_src) + jnp.sum(att_res * own_att) + jnp.sum(next_res * edge_out)
+    q_sq = jnp.sum(q_src * q_src) + jnp.sum(own_att * own_att)
     scalars = jnp.stack([res_sq, curv_local, res_q, q_sq, cal_sq])
     scalars = jnp.concatenate([scalars, jnp.zeros((lane - 5,), jnp.float32)]).reshape(1, lane)
-    own_rows, scalars = halving_sum(cal_term, scalars, "cal")
-    summed = doubling_sum(jnp.concatenate([own_rows, scalars], axis=0), "tm")
-    res_sq, curvature, res_q, q_sq, cal_sq = (summed[-1, k] for k in range(5))
-    q_cal = summed[:-1].reshape(blocks, col_width)
+    device_count = lax.axis_size(("tm", "cal"))
+    device = lax.axis_index(("tm", "cal"))
+    slot_rows = -(-device_count * 9 // lane)
+    mine = (lax.broadcasted_iota(jnp.int32, (device_count, 1), 0) == device).astype(jnp.float32)
+
+    def slotted(values):
+        table = (mine * values.reshape(1, 9)).reshape(-1)
+        return jnp.pad(table, (0, slot_rows * lane - device_count * 9)).reshape(slot_rows, lane)
+
+    extra = jnp.concatenate([scalars, slotted(edge_out), slotted(own_att[:, :3])], axis=0)
+    own_rows, extra = halving_sum(cal_term, extra, "cal")
+    summed = doubling_sum(jnp.concatenate([own_rows, extra], axis=0), "tm")
+    res_sq, curvature, res_q, q_sq, cal_sq = (summed[-2 * slot_rows - 1, k] for k in range(5))
+    q_cal = summed[: -2 * slot_rows - 1].reshape(blocks, col_width)
+    edges = summed[-2 * slot_rows :].reshape(2, -1)[:, : device_count * 9].reshape(2, device_count, 9)
+    sent, heads = edges[0, :-1], edges[1, 1:]
+    q_sq = q_sq + jnp.sum(sent * sent) + 2.0 * jnp.sum(sent * heads)
+    previous = jnp.maximum(device - 1, 0)
+    incoming = lax.dynamic_index_in_dim(edges[0], previous, axis=0, keepdims=False).reshape(3, 3)
+    incoming = incoming * (device > 0).astype(jnp.float32)
+    q_att = jnp.concatenate([own_att[:, :3] + incoming, own_att[:, 3:]], axis=1)
 
     norm_now = res_sq + cal_sq
     step_len = norm_now / curvature

time: 75.4 us -> 77 us (1.021)
  starting transfers between devices: 20.5 us -> 16.6 us
  between operations: 9.67 us -> 11.7 us
  matrix products: 14.7 us -> 16.5 us
  other arithmetic: 13.1 us -> 14.7 us
  waiting for transfers between devices: 13.3 us -> 12.5 us
    ppermute x9, starting transfers between devices: 17.4 us -> 15.4 us  [exchanged(): return lax.ppermute(block, axis, [(i, i ^ distance) for i in devices])]
    ppermute x2 -> x1, starting transfers between devices: 3.1 us -> 1.28 us  [passed_along(): return lax.ppermute(block, axis, route)]
    dot_general x1, matrix products: 4.49 us -> 6.31 us  [local(): lax.dot_general(high_hot, cal_weighted, (((1,), (1,)), ((), ())), precisi...]
    reduce_sum x2 -> x4, other arithmetic: 1.29 us -> 2.52 us  [the longest x2 1.31 us: local(): q_sq = jnp.sum(q_src * q_src) + jnp.sum(own_att * own_att)]
    unnamed x34 -> x31, local copies, waits for them, and re-layouts: 1.62 us -> 0.94 us
  transfers between devices with their start and end apart: 11 -> 10, of which waited for: 7 -> 7; matrix products, arithmetic and copies ran while one was open for 21% -> 13% of each run, Pallas kernels for 0% -> 0%
where the time goes in v13:
time: 77 us; the launch traced here: 76.6 us
  starting transfers between devices  16.6 us (22%)
  matrix products  16.5 us (21%)
  other arithmetic  14.7 us (19%)
  waiting for transfers between devices  12.5 us (16%)
  between operations  11.7 us (15%)
  local copies, waits for them, and re-layouts  4.56 us (6%)
    ppermute x9, starting transfers between devices, exchanged(): return lax.ppermute(block, axis, [(i, i ^ distance) for i in devices])  15.4 us
    ppermute x9, waiting for transfers between devices, exchanged(): return lax.ppermute(block, axis, [(i, i ^ distance) for i in devices])  12.5 us
    dot_general x1, matrix products, local(): lax.dot_general(high_hot, cal_weighted, (((1,), (1,)), ((), ())), precisi...  6.31 us
    dot_general x1, matrix products, local(): lax.dot_general(cal_table, high_hot, (((0,), (0,)), ((), ())), precision=...  5.59 us
    dot_general x1, other arithmetic, local(): lax.dot_general(high_hot, cal_weighted, (((1,), (1,)), ((), ())), precisi...  4.09 us
    dot_general x1, matrix products, local(): lax.dot_general(spread, knot_hot, (((1,), (1,)), ((), ())), precision=ONE...  2.43 us
    dot_general x1, matrix products, local(): jnp.dot(table, knot_hot, precision=ONE_HOT_PRECISION)  2.16 us
  transfers between devices with their start and end apart: 10, of which 7 were waited for; matrix products, arithmetic and copies ran while one was open for 13% of the time, Pallas kernels for 0%

profile of v13, /device:TPU:0, one launch (start us, length us, event | category | flops | bytes accessed | tf_op | source)
XLA Modules:
  0.0 76.6 jit_solution(11573430619470547789)
XLA Ops:
  0.7 0.8 slice_bitcast_fusion.6
  1.4 1.3 %collective-permute-start = (f32[2,3,3]{2,1,0:T(4,128)S(1)}, f32[2,3,3]{2,1,0:T(4,128)S(1)}, u32[]{:S(2)}, u32[]{:S(2)}) collective-permute-start(f32[2,3,3]{2,1,0:T(4,128)S(1)} %pad_maximum_fusion.6), channel_id=1, source_target_pairs={{1,0},{2,1},{3,2},{4,3},{5,4},{6,5},{7,6},{8,7},{9,8},{10,9},{11,1... | collective-permute-start | bytes 224 | tf_op jit(solution)/shard_map/ppermute | solution.py:13
  2.7 1.2 %collective-permute-start.1 = (f32[1,2,4096]{2,1,0:T(2,128)}, f32[1,2,4096]{2,1,0:T(2,128)S(1)}, u32[]{:S(2)}, u32[]{:S(2)}) collective-permute-start(f32[1,2,4096]{2,1,0:T(2,128)} %bitcast.118), channel_id=1, source_target_pairs={{0,1},{1,0},{2,3},{3,2},{4,5},{5,4},{6,7},{7,6},{8,9},{9,8},{10,11... | collective-permute-start | bytes 98312 | tf_op jit(solution)/shard_map/ppermute | solution.py:18
  3.9 1.4 %multiply_reduce_fusion.4 = f32[]{:T(128)} fusion(f32[2,4096]{1,0:T(2,128)} %param.26), kind=kLoop, calls=%fused_computation.77 | loop fusion | flops 16383 | bytes 32772 | tf_op jit(solution)/shard_map/reduce_sum | solution.py:151
  5.3 0.9 %add_select_fusion = (s32[16384]{0:T(1024)S(1)}, s32[16384]{0:T(1024)S(1)}) fusion(s32[128,128]{1,0:T(8,128)} %param.22, s32[128,128]{1,0:T(8,128)} %param.21), kind=kLoop, calls=%fused_computation.38 | loop fusion | flops 344064 | bytes 262144 | tf_op jit(solution)/shard_map/jit(remainder)/select_n | solution.py:127
  6.3 4.1 %iota_compare_fusion.14 = pred[256,16384]{1,0:T(32,128)(4,1)} fusion(s32[16384]{0:T(1024)S(1)} %get-tuple-element.40), kind=kLoop, calls=%fused_computation.1.clone.clone.2 | loop fusion | flops 4194304 | bytes 4259840 | tf_op jit(solution)/shard_map/dot_general | solution.py:149
  11.3 2.2 %fusion.3 = f32[12,16384]{1,0:T(8,128)S(1)} fusion(f32[12,128]{1,0:T(8,128)S(1)} %reshape.292, s32[16384]{0:T(1024)S(1)} %subtract_bitcast_fusion), kind=kOutput, calls=%fused_computation.6 | convolution fusion | flops 153092096 | bytes 858112 | tf_op jit(solution)/shard_map/dot_general | solution.py:120
  13.8 3.0 %collective-permute-start.2 = (f32[1,4,4096]{2,1,0:T(4,128)S(1)}, f32[1,4,4096]{2,1,0:T(4,128)S(1)}, u32[]{:S(2)}, u32[]{:S(2)}) collective-permute-start(f32[1,4,4096]{2,1,0:T(4,128)S(1)} %maximum_select_fusion.1), channel_id=1, source_target_pairs={{0,2},{1,3},{2,0},{3,1},{4,6},{5,7},{6,4},{7,5},{8,10},{9,11},{10,... | collective-permute-start | bytes 196616 | tf_op jit(solution)/shard_map/ppermute | solution.py:18
  16.8 2.3 %collective-permute-done.2 = f32[1,4,4096]{2,1,0:T(4,128)S(1)} collective-permute-done((f32[1,4,4096]{2,1,0:T(4,128)S(1)}, f32[1,4,4096]{2,1,0:T(4,128)S(1)}, u32[]{:S(2)}, u32[]{:S(2)}) %collective-permute-start.2) | collective-permute-done | bytes 65568 | tf_op jit(solution)/shard_map/ppermute | solution.py:18
  19.2 5.6 %fusion.11 = f32[16384]{0:T(1024)S(1)} fusion(f32[256,128]{1,0:T(8,128)S(1)} %select_n.99, s32[16384]{0:T(1024)S(1)} %get-tuple-element.40, s32[16384]{0:T(1024)S(1)} %get-tuple-element.39), kind=kOutput, calls=%fused_computation.15 | convolution fusion | flops 3231694848 | bytes 327680 | tf_op jit(solution)/shard_map/dot_general | solution.py:129
  26.0 2.4 %fusion.2 = f32[12,128]{1,0:T(8,128)S(1)} fusion(f32[12,16384]{1,0:T(8,128)S(1)} %bitcast.117, s32[16384]{0:T(1024)S(1)} %subtract_bitcast_fusion), kind=kOutput, calls=%fused_computation.5 | convolution fusion | flops 153092096 | bytes 858112 | tf_op jit(solution)/shard_map/dot_general | solution.py:140
  28.5 0.7 multiply_reduce_fusion.9
  30.3 0.6 multiply_reduce_fusion.2
  31.0 6.3 %fusion = f32[256,128]{1,0:T(8,128)S(1)} fusion(f32[16384]{0:T(1024)S(1)} %get-tuple-element.24, s32[16384]{0:T(1024)S(1)} %get-tuple-element.39, pred[256,16384]{1,0:T(32,128)(4,1)} %iota_compare_fusion.14), kind=kOutput, calls=%fused_computation.2 | convolution fusion | flops 3225419776 | bytes 4456448 | tf_op jit(solution)/shard_map/dot_general | solution.py:149
  42.5 0.7 concatenate.72
  43.3 1.2 %collective-permute-done.3 = f32[135,128]{1,0:T(8,128)S(1)} collective-permute-done((f32[135,128]{1,0:T(8,128)S(1)}, f32[135,128]{1,0:T(8,128)S(1)}, u32[]{:S(2)}, u32[]{:S(2)}) %collective-permute-start.3) | collective-permute-done | bytes 69152 | tf_op jit(solution)/shard_map/ppermute | solution.py:18
  44.6 2.0 %collective-permute-start.4 = (f32[71,128]{1,0:T(8,128)S(1)}, f32[71,128]{1,0:T(8,128)S(1)}, u32[]{:S(2)}, u32[]{:S(2)}) collective-permute-start(f32[71,128]{1,0:T(8,128)S(1)} %pad_maximum_fusion.3), channel_id=1, source_target_pairs={{0,2},{1,3},{2,0},{3,1},{4,6},{5,7},{6,4},{7,5},{8,10},{9,11},{10,... | collective-permute-start | bytes 109064 | tf_op jit(solution)/shard_map/ppermute | solution.py:18
  46.6 2.0 %collective-permute-done.4 = f32[71,128]{1,0:T(8,128)S(1)} collective-permute-done((f32[71,128]{1,0:T(8,128)S(1)}, f32[71,128]{1,0:T(8,128)S(1)}, u32[]{:S(2)}, u32[]{:S(2)}) %collective-permute-start.4) | collective-permute-done | bytes 36384 | tf_op jit(solution)/shard_map/ppermute | solution.py:18
  48.7 2.6 %collective-permute-start.5 = (f32[71,128]{1,0:T(8,128)S(1)}, f32[71,128]{1,0:T(8,128)S(1)}, u32[]{:S(2)}, u32[]{:S(2)}) collective-permute-start(f32[71,128]{1,0:T(8,128)S(1)} %pad_maximum_fusion.4), channel_id=1, source_target_pairs={{0,4},{4,0},{8,12},{12,8},{16,20},{20,16},{24,28},{28,24},{1,5},{5... | collective-permute-start | bytes 109064 | tf_op jit(solution)/shard_map/ppermute | solution.py:18
  51.3 1.9 %collective-permute-done.5 = f32[71,128]{1,0:T(8,128)S(1)} collective-permute-done((f32[71,128]{1,0:T(8,128)S(1)}, f32[71,128]{1,0:T(8,128)S(1)}, u32[]{:S(2)}, u32[]{:S(2)}) %collective-permute-start.5) | collective-permute-done | bytes 36384 | tf_op jit(solution)/shard_map/ppermute | solution.py:18
  53.3 3.0 %collective-permute-start.6 = (f32[71,128]{1,0:T(8,128)S(1)}, f32[71,128]{1,0:T(8,128)S(1)}, u32[]{:S(2)}, u32[]{:S(2)}) collective-permute-start(f32[71,128]{1,0:T(8,128)S(1)} %fusion.42), channel_id=1, source_target_pairs={{0,8},{4,12},{8,0},{12,4},{16,24},{20,28},{24,16},{28,20},{1,9},{5... | collective-permute-start | bytes 109064 | tf_op jit(solution)/shard_map/ppermute | solution.py:18
  56.2 1.9 %collective-permute-done.6 = f32[71,128]{1,0:T(8,128)S(1)} collective-permute-done((f32[71,128]{1,0:T(8,128)S(1)}, f32[71,128]{1,0:T(8,128)S(1)}, u32[]{:S(2)}, u32[]{:S(2)}) %collective-permute-start.6) | collective-permute-done | bytes 36384 | tf_op jit(solution)/shard_map/ppermute | solution.py:18
  58.2 3.0 %collective-permute-start.7 = (f32[71,128]{1,0:T(8,128)S(1)}, f32[71,128]{1,0:T(8,128)S(1)}, u32[]{:S(2)}, u32[]{:S(2)}) collective-permute-start(f32[71,128]{1,0:T(8,128)S(1)} %add.195), channel_id=1, source_target_pairs={{0,16},{4,20},{8,24},{12,28},{16,0},{20,4},{24,8},{28,12},{1,17},{... | collective-permute-start | bytes 109064 | tf_op jit(solution)/shard_map/ppermute | solution.py:18
  61.3 1.9 %collective-permute-done.7 = f32[71,128]{1,0:T(8,128)S(1)} collective-permute-done((f32[71,128]{1,0:T(8,128)S(1)}, f32[71,128]{1,0:T(8,128)S(1)}, u32[]{:S(2)}, u32[]{:S(2)}) %collective-permute-start.7) | collective-permute-done | bytes 36384 | tf_op jit(solution)/shard_map/ppermute | solution.py:18
  66.0 0.7 multiply_reduce_fusion.3
  66.7 0.7 broadcast_in_dim.5
  67.7 0.6 fusion.30
  69.6 0.7 broadcast_add_fusion
  72.6 1.3 %collective-permute-done.9 = f32[1,128]{1,0:T(1,128)S(1)} collective-permute-done((f32[1,128]{1,0:T(1,128)S(1)}, f32[1,128]{1,0:T(1,128)S(1)}, u32[]{:S(2)}, u32[]{:S(2)}) %collective-permute-start.9) | collective-permute-done | bytes 544 | tf_op jit(solution)/shard_map/ppermute | solution.py:18
  73.9 0.7 fusion.51
  75.3 0.6 multiply_add_fusion.1
  75.9 0.7 multiply_add_fusion.3
  (92 shorter events, 5.9 us)
Async XLA Ops:
  0.6 10.6 %copy-start.9 = (f32[3,128]{1,0:T(4,128)S(1)}, f32[3,128]{1,0:T(4,128)}, u32[]{:S(2)}) copy-start(f32[3,128]{1,0:T(4,128)} %param.28) | copy-start | bytes 4612
  0.6 9.7 %copy-start.11 = (f32[5,128]{1,0:T(8,128)S(1)}, f32[5,128]{1,0:T(8,128)}, u32[]{:S(2)}) copy-start(f32[5,128]{1,0:T(8,128)} %param.27) | copy-start | bytes 7684
  0.7 9.7 %copy-start = (f32[5,128,128]{2,1,0:T(8,128)S(1)}, f32[5,128,128]{2,1,0:T(8,128)}, u32[]{:S(2)}) copy-start(f32[5,128,128]{2,1,0:T(8,128)} %param.15) | copy-start | bytes 983044
  0.7 9.9 %copy-start.5 = (s32[128,128]{1,0:T(8,128)S(1)}, s32[128,128]{1,0:T(8,128)}, u32[]{:S(2)}) copy-start(s32[128,128]{1,0:T(8,128)} %param.20) | copy-start | bytes 196612
  1.4 9.8 %collective-permute-start = (f32[2,3,3]{2,1,0:T(4,128)S(1)}, f32[2,3,3]{2,1,0:T(4,128)S(1)}, u32[]{:S(2)}, u32[]{:S(2)}) collective-permute-start(f32[2,3,3]{2,1,0:T(4,128)S(1)} %pad_maximum_fusion.6), channel_id=1, source_target_pairs={{1,0},{2,1},{3,2},{4,3},{5,4},{6,5},{7,6},{8,7},{9,8},{10,9},{11,1... | collective-permute-start | bytes 224 | tf_op jit(solution)/shard_map/ppermute | solution.py:13
  2.7 11.0 %collective-permute-start.1 = (f32[1,2,4096]{2,1,0:T(2,128)}, f32[1,2,4096]{2,1,0:T(2,128)S(1)}, u32[]{:S(2)}, u32[]{:S(2)}) collective-permute-start(f32[1,2,4096]{2,1,0:T(2,128)} %bitcast.118), channel_id=1, source_target_pairs={{0,1},{1,0},{2,3},{3,2},{4,5},{5,4},{6,7},{7,6},{8,9},{9,8},{10,11... | collective-permute-start | bytes 98312 | tf_op jit(solution)/shard_map/ppermute | solution.py:18
  6.2 7.4 %copy-start.4 = (f32[2,4096]{1,0:T(2,128)S(1)}, f32[2,4096]{1,0:T(2,128)}, u32[]{:S(2)}) copy-start(f32[2,4096]{1,0:T(2,128)} %param.29) | copy-start | bytes 98308
  6.3 10.5 %copy-start.1 = (f32[3,128,128]{2,1,0:T(8,128)S(1)}, f32[3,128,128]{2,1,0:T(8,128)}, u32[]{:S(2)}) copy-start(f32[3,128,128]{2,1,0:T(8,128)} %param.16) | copy-start | bytes 589828
  13.8 5.3 %collective-permute-start.2 = (f32[1,4,4096]{2,1,0:T(4,128)S(1)}, f32[1,4,4096]{2,1,0:T(4,128)S(1)}, u32[]{:S(2)}, u32[]{:S(2)}) collective-permute-start(f32[1,4,4096]{2,1,0:T(4,128)S(1)} %maximum_select_fusion.1), channel_id=1, source_target_pairs={{0,2},{1,3},{2,0},{3,1},{4,6},{5,7},{6,4},{7,5},{8,10},{9,11},{10,... | collective-permute-start | bytes 196616 | tf_op jit(solution)/shard_map/ppermute | solution.py:18
  19.2 5.6 %copy-start.6 = (f32[128,128]{1,0:T(8,128)S(1)}, f32[128,128]{1,0:T(8,128)}, u32[]{:S(2)}) copy-start(f32[128,128]{1,0:T(8,128)} %param.18) | copy-start | bytes 196612
  19.2 5.6 %copy-start.7 = (f32[128,128]{1,0:T(8,128)S(1)}, f32[128,128]{1,0:T(8,128)}, u32[]{:S(2)}) copy-start(f32[128,128]{1,0:T(8,128)} %param.19) | copy-start | bytes 196612
  19.2 5.6 %copy-start.8 = (f32[128,128]{1,0:T(8,128)S(1)}, f32[128,128]{1,0:T(8,128)}, u32[]{:S(2)}) copy-start(f32[128,128]{1,0:T(8,128)} %param.17) | copy-start | bytes 196612
  19.2 5.6 %copy-start.13 = (s32[128]{0:T(128)S(1)}, s32[128]{0:T(128)}, u32[]{:S(2)}) copy-start(s32[128]{0:T(128)} %param.23) | copy-start | bytes 1540
  25.2 3.3 %copy-start.10 = (f32[3,128]{1,0:T(4,128)S(1)}, f32[3,128]{1,0:T(4,128)}, u32[]{:S(2)}) copy-start(f32[3,128]{1,0:T(4,128)} %param.25) | copy-start | bytes 4612
  31.0 6.3 %copy-start.12 = (f32[5,128]{1,0:T(8,128)S(1)}, f32[5,128]{1,0:T(8,128)}, u32[]{:S(2)}) copy-start(f32[5,128]{1,0:T(8,128)} %param.24) | copy-start | bytes 7684
  31.0 35.0 %copy-start.3 = (f32[2,4096]{1,0:T(2,128)S(1)}, f32[2,4096]{1,0:T(2,128)}, u32[]{:S(2)}) copy-start(f32[2,4096]{1,0:T(2,128)} %param.26) | copy-start | bytes 98308
  43.3 1.3 %collective-permute-start.3 = (f32[135,128]{1,0:T(8,128)S(1)}, f32[135,128]{1,0:T(8,128)S(1)}, u32[]{:S(2)}, u32[]{:S(2)}) collective-permute-start(f32[135,128]{1,0:T(8,128)S(1)} %pad_maximum_fusion.2), channel_id=1, source_target_pairs={{0,1},{1,0},{2,3},{3,2},{4,5},{5,4},{6,7},{7,6},{8,9},{9,8},{10,11... | collective-permute-start | bytes 207368 | tf_op jit(solution)/shard_map/ppermute | solution.py:18
  44.6 4.0 %collective-permute-start.4 = (f32[71,128]{1,0:T(8,128)S(1)}, f32[71,128]{1,0:T(8,128)S(1)}, u32[]{:S(2)}, u32[]{:S(2)}) collective-permute-start(f32[71,128]{1,0:T(8,128)S(1)} %pad_maximum_fusion.3), channel_id=1, source_target_pairs={{0,2},{1,3},{2,0},{3,1},{4,6},{5,7},{6,4},{7,5},{8,10},{9,11},{10,... | collective-permute-start | bytes 109064 | tf_op jit(solution)/shard_map/ppermute | solution.py:18
  48.7 4.6 %collective-permute-start.5 = (f32[71,128]{1,0:T(8,128)S(1)}, f32[71,128]{1,0:T(8,128)S(1)}, u32[]{:S(2)}, u32[]{:S(2)}) collective-permute-start(f32[71,128]{1,0:T(8,128)S(1)} %pad_maximum_fusion.4), channel_id=1, source_target_pairs={{0,4},{4,0},{8,12},{12,8},{16,20},{20,16},{24,28},{28,24},{1,5},{5... | collective-permute-start | bytes 109064 | tf_op jit(solution)/shard_map/ppermute | solution.py:18
  53.3 4.9 %collective-permute-start.6 = (f32[71,128]{1,0:T(8,128)S(1)}, f32[71,128]{1,0:T(8,128)S(1)}, u32[]{:S(2)}, u32[]{:S(2)}) collective-permute-start(f32[71,128]{1,0:T(8,128)S(1)} %fusion.42), channel_id=1, source_target_pairs={{0,8},{4,12},{8,0},{12,4},{16,24},{20,28},{24,16},{28,20},{1,9},{5... | collective-permute-start | bytes 109064 | tf_op jit(solution)/shard_map/ppermute | solution.py:18
  58.2 5.0 %collective-permute-start.7 = (f32[71,128]{1,0:T(8,128)S(1)}, f32[71,128]{1,0:T(8,128)S(1)}, u32[]{:S(2)}, u32[]{:S(2)}) collective-permute-start(f32[71,128]{1,0:T(8,128)S(1)} %add.195), channel_id=1, source_target_pairs={{0,16},{4,20},{8,24},{12,28},{16,0},{20,4},{24,8},{28,12},{1,17},{... | collective-permute-start | bytes 109064 | tf_op jit(solution)/shard_map/ppermute | solution.py:18
  66.7 9.9 %copy-start.2 = (f32[2,4096]{1,0:T(2,128)}, f32[2,4096]{1,0:T(2,128)S(1)}, u32[]{:S(2)}) copy-start(f32[2,4096]{1,0:T(2,128)S(1)} %get-tuple-element.23) | copy-start | bytes 98308
  67.4 2.2 %collective-permute-start.8 = (f32[1,128]{1,0:T(1,128)S(1)}, f32[1,128]{1,0:T(1,128)S(1)}, u32[]{:S(2)}, u32[]{:S(2)}) collective-permute-start(f32[1,128]{1,0:T(1,128)S(1)} %broadcast_in_dim.5), channel_id=1, source_target_pairs={{0,1},{1,0},{2,3},{3,2},{4,5},{5,4},{6,7},{7,6},{8,9},{9,8},{10,11... | collective-permute-start | bytes 1544 | tf_op jit(solution)/shard_map/ppermute | solution.py:18
  70.3 3.6 %collective-permute-start.9 = (f32[1,128]{1,0:T(1,128)S(1)}, f32[1,128]{1,0:T(1,128)S(1)}, u32[]{:S(2)}, u32[]{:S(2)}) collective-permute-start(f32[1,128]{1,0:T(1,128)S(1)} %broadcast_add_fusion), channel_id=1, source_target_pairs={{0,2},{1,3},{2,0},{3,1},{4,6},{5,7},{6,4},{7,5},{8,10},{9,11},{10,... | collective-permute-start | bytes 1544 | tf_op jit(solution)/shard_map/ppermute | solution.py:18

commit v14 on v10

--- a/solution.py
+++ b/solution.py
@@ -157,14 +157,18 @@
     res_sq, curvature, res_q, q_sq, cal_sq = (summed[-1, k] for k in range(5))
     q_cal = summed[:-1].reshape(blocks, col_width)
 
+    cal_dots = jnp.stack([jnp.sum(cal_res * q_cal), jnp.sum(q_cal * q_cal)])
+    cal_dots = jnp.concatenate([cal_dots, jnp.zeros((lane - 2,), jnp.float32)]).reshape(1, lane)
+    cal_dots = doubling_sum(cal_dots, "cal")
+    res_q = res_q + cal_dots[0, 0]
+    q_sq = q_sq + cal_dots[0, 1]
+
     norm_now = res_sq + cal_sq
     step_len = norm_now / curvature
     new_src_res = src_res - step_len * q_src
     new_att_res = att_res - step_len * q_att
     new_cal_res = cal_res - step_len * q_cal
-    kept = res_sq - step_len * (2.0 * res_q - step_len * q_sq)
-    cal_next = jnp.broadcast_to(jnp.sum(new_cal_res * new_cal_res), (1, lane))
-    norm_next = kept + doubling_sum(cal_next, "cal")[0, 0]
+    norm_next = norm_now - step_len * (2.0 * res_q - step_len * q_sq)
     ratio = norm_next / norm_now
     return (
         new_src_res,

time: 75.4 us -> 79.5 us (1.054)
  other arithmetic: 13.1 us -> 16.7 us
    add x5, other arithmetic: 1.32 us -> 2.84 us  [doubling_sum(): rows = rows + exchanged(rows, axis, distance)]
    reshape x0 -> x1, other arithmetic: none -> 1.41 us  [local(): jnp.concatenate([cal_dots, jnp.zeros((lane - 2,), jnp.float32)])]
    unnamed x34 -> x32, local copies, waits for them, and re-layouts: 1.62 us -> 1.62 us
  transfers between devices with their start and end apart: 11 -> 11, of which waited for: 7 -> 7; matrix products, arithmetic and copies ran while one was open for 21% -> 20% of each run, Pallas kernels for 0% -> 0%
where the time goes in v14:
time: 79.5 us; the launch traced here: 79 us
  starting transfers between devices  20.3 us (26%)
  other arithmetic  16.7 us (21%)
  matrix products  14.7 us (18%)
  waiting for transfers between devices  13.3 us (17%)
  between operations  10.3 us (13%)
  local copies, waits for them, and re-layouts  3.77 us (5%)
    ppermute x9, starting transfers between devices, exchanged(): return lax.ppermute(block, axis, [(i, i ^ distance) for i in devices])  17.2 us
    ppermute x9, waiting for transfers between devices, exchanged(): return lax.ppermute(block, axis, [(i, i ^ distance) for i in devices])  13.3 us
    dot_general x1, matrix products, local(): lax.dot_general(cal_table, high_hot, (((0,), (0,)), ((), ())), precision=...  5.58 us
    dot_general x1, matrix products, local(): lax.dot_general(high_hot, cal_weighted, (((1,), (1,)), ((), ())), precisi...  4.49 us
    dot_general x1, other arithmetic, local(): lax.dot_general(high_hot, cal_weighted, (((1,), (1,)), ((), ())), precisi...  4.09 us
    ppermute x2, starting transfers between devices, passed_along(): return lax.ppermute(block, axis, route)  3.1 us
    add x5, other arithmetic, doubling_sum(): rows = rows + exchanged(rows, axis, distance)  2.84 us
    dot_general x1, matrix products, local(): lax.dot_general(spread, knot_hot, (((1,), (1,)), ((), ())), precision=ONE...  2.43 us
  transfers between devices with their start and end apart: 11, of which 7 were waited for; matrix products, arithmetic and copies ran while one was open for 20% of the time, Pallas kernels for 0%

profile of v14, /device:TPU:0, one launch (start us, length us, event | category | flops | bytes accessed | tf_op | source)
XLA Modules:
  0.0 79.0 jit_solution(10330464189631997521)
XLA Ops:
  1.2 1.3 %collective-permute-start = (f32[3,3]{1,0:T(4,128)}, f32[3,3]{1,0:T(4,128)S(1)}, u32[]{:S(2)}, u32[]{:S(2)}) collective-permute-start(f32[3,3]{1,0:T(4,128)} %bitcast.110), channel_id=1, source_target_pairs={{1,0},{2,1},{3,2},{4,3},{5,4},{6,5},{7,6},{8,7},{9,8},{10,9},{11,1... | collective-permute-start | bytes 116 | tf_op jit(solution)/shard_map/ppermute | solution.py:13
  2.5 0.7 constant_dynamic-update-slice_fusion.1
  3.2 1.4 %multiply_reduce_fusion.5 = f32[]{:T(128)} fusion(f32[2,4096]{1,0:T(2,128)} %param.26), kind=kLoop, calls=%fused_computation.78 | loop fusion | flops 16383 | bytes 32772 | tf_op jit(solution)/shard_map/reduce_sum | solution.py:150
  4.6 0.9 %add_select_fusion = (s32[16384]{0:T(1024)S(1)}, s32[16384]{0:T(1024)S(1)}) fusion(s32[128,128]{1,0:T(8,128)} %param.22, s32[128,128]{1,0:T(8,128)} %param.21), kind=kLoop, calls=%fused_computation.38 | loop fusion | flops 344064 | bytes 262144 | tf_op jit(solution)/shard_map/jit(remainder)/select_n | solution.py:126
  5.6 4.1 %iota_compare_fusion.14 = pred[256,16384]{1,0:T(32,128)(4,1)} fusion(s32[16384]{0:T(1024)S(1)} %get-tuple-element.38), kind=kLoop, calls=%fused_computation.1.clone.clone.2 | loop fusion | flops 4194304 | bytes 4259840 | tf_op jit(solution)/shard_map/dot_general | solution.py:148
  10.6 2.2 %fusion.3 = f32[12,16384]{1,0:T(8,128)S(1)} fusion(f32[12,128]{1,0:T(8,128)S(1)} %reshape.259, s32[16384]{0:T(1024)S(1)} %subtract_bitcast_fusion), kind=kOutput, calls=%fused_computation.6 | convolution fusion | flops 153092096 | bytes 858112 | tf_op jit(solution)/shard_map/dot_general | solution.py:119
  13.0 3.4 %collective-permute-start.2 = (f32[1,4,4096]{2,1,0:T(4,128)S(1)}, f32[1,4,4096]{2,1,0:T(4,128)S(1)}, u32[]{:S(2)}, u32[]{:S(2)}) collective-permute-start(f32[1,4,4096]{2,1,0:T(4,128)S(1)} %maximum_select_fusion.1), channel_id=1, source_target_pairs={{0,2},{1,3},{2,0},{3,1},{4,6},{5,7},{6,4},{7,5},{8,10},{9,11},{10,... | collective-permute-start | bytes 196616 | tf_op jit(solution)/shard_map/ppermute | solution.py:18
  16.4 2.7 %collective-permute-done.2 = f32[1,4,4096]{2,1,0:T(4,128)S(1)} collective-permute-done((f32[1,4,4096]{2,1,0:T(4,128)S(1)}, f32[1,4,4096]{2,1,0:T(4,128)S(1)}, u32[]{:S(2)}, u32[]{:S(2)}) %collective-permute-start.2) | collective-permute-done | bytes 65568 | tf_op jit(solution)/shard_map/ppermute | solution.py:18
  19.3 5.6 %fusion.11 = f32[16384]{0:T(1024)S(1)} fusion(f32[256,128]{1,0:T(8,128)S(1)} %select_n.97, s32[16384]{0:T(1024)S(1)} %get-tuple-element.38, s32[16384]{0:T(1024)S(1)} %get-tuple-element.37), kind=kOutput, calls=%fused_computation.15 | convolution fusion | flops 3231694848 | bytes 327680 | tf_op jit(solution)/shard_map/dot_general | solution.py:128
  26.0 2.4 %fusion.2 = f32[12,128]{1,0:T(8,128)S(1)} fusion(f32[12,16384]{1,0:T(8,128)S(1)} %bitcast.107, s32[16384]{0:T(1024)S(1)} %subtract_bitcast_fusion), kind=kOutput, calls=%fused_computation.5 | convolution fusion | flops 153092096 | bytes 858112 | tf_op jit(solution)/shard_map/dot_general | solution.py:139
  28.6 1.8 %collective-permute-start.3 = (f32[3,3]{1,0:T(4,128)S(1)}, f32[3,3]{1,0:T(4,128)S(1)}, u32[]{:S(2)}, u32[]{:S(2)}) collective-permute-start(f32[3,3]{1,0:T(4,128)S(1)} %slice.152), channel_id=1, source_target_pairs={{0,1},{1,2},{2,3},{3,4},{4,5},{5,6},{6,7},{7,8},{8,9},{9,10},{10,1... | collective-permute-start | bytes 116 | tf_op jit(solution)/shard_map/ppermute | solution.py:13
  31.1 4.5 %fusion = f32[256,128]{1,0:T(8,128)S(1)} fusion(f32[16384]{0:T(1024)S(1)} %get-tuple-element.22, s32[16384]{0:T(1024)S(1)} %get-tuple-element.37, pred[256,16384]{1,0:T(32,128)(4,1)S(1)} %copy-done), kind=kOutput, calls=%fused_computation.2 | convolution fusion | flops 3225419776 | bytes 4456448 | tf_op jit(solution)/shard_map/dot_general | solution.py:148
  36.3 0.7 multiply_reduce_fusion.9
  40.9 0.7 concatenate.72
  41.6 2.0 %collective-permute-start.4 = (f32[129,128]{1,0:T(8,128)S(1)}, f32[129,128]{1,0:T(8,128)S(1)}, u32[]{:S(2)}, u32[]{:S(2)}) collective-permute-start(f32[129,128]{1,0:T(8,128)S(1)} %pad_maximum_fusion.2), channel_id=1, source_target_pairs={{0,1},{1,0},{2,3},{3,2},{4,5},{5,4},{6,7},{7,6},{8,9},{9,8},{10,11... | collective-permute-start | bytes 198152 | tf_op jit(solution)/shard_map/ppermute | solution.py:18
  43.6 0.9 %collective-permute-done.4 = f32[129,128]{1,0:T(8,128)S(1)} collective-permute-done((f32[129,128]{1,0:T(8,128)S(1)}, f32[129,128]{1,0:T(8,128)S(1)}, u32[]{:S(2)}, u32[]{:S(2)}) %collective-permute-start.4) | collective-permute-done | bytes 66080 | tf_op jit(solution)/shard_map/ppermute | solution.py:18
  44.6 2.7 %collective-permute-start.5 = (f32[65,128]{1,0:T(8,128)S(1)}, f32[65,128]{1,0:T(8,128)S(1)}, u32[]{:S(2)}, u32[]{:S(2)}) collective-permute-start(f32[65,128]{1,0:T(8,128)S(1)} %pad_maximum_fusion.3), channel_id=1, source_target_pairs={{0,2},{1,3},{2,0},{3,1},{4,6},{5,7},{6,4},{7,5},{8,10},{9,11},{10,... | collective-permute-start | bytes 99848 | tf_op jit(solution)/shard_map/ppermute | solution.py:18
  47.3 2.0 %collective-permute-done.5 = f32[65,128]{1,0:T(8,128)S(1)} collective-permute-done((f32[65,128]{1,0:T(8,128)S(1)}, f32[65,128]{1,0:T(8,128)S(1)}, u32[]{:S(2)}, u32[]{:S(2)}) %collective-permute-start.5) | collective-permute-done | bytes 33312 | tf_op jit(solution)/shard_map/ppermute | solution.py:18
  49.3 2.5 %collective-permute-start.6 = (f32[65,128]{1,0:T(8,128)S(1)}, f32[65,128]{1,0:T(8,128)S(1)}, u32[]{:S(2)}, u32[]{:S(2)}) collective-permute-start(f32[65,128]{1,0:T(8,128)S(1)} %pad_maximum_fusion.4), channel_id=1, source_target_pairs={{0,4},{4,0},{8,12},{12,8},{16,20},{20,16},{24,28},{28,24},{1,5},{5... | collective-permute-start | bytes 99848 | tf_op jit(solution)/shard_map/ppermute | solution.py:18
  51.8 1.9 %collective-permute-done.6 = f32[65,128]{1,0:T(8,128)S(1)} collective-permute-done((f32[65,128]{1,0:T(8,128)S(1)}, f32[65,128]{1,0:T(8,128)S(1)}, u32[]{:S(2)}, u32[]{:S(2)}) %collective-permute-start.6) | collective-permute-done | bytes 33312 | tf_op jit(solution)/shard_map/ppermute | solution.py:18
  53.7 1.6 %collective-permute-start.7 = (f32[65,128]{1,0:T(8,128)S(1)}, f32[65,128]{1,0:T(8,128)S(1)}, u32[]{:S(2)}, u32[]{:S(2)}) collective-permute-start(f32[65,128]{1,0:T(8,128)S(1)} %fusion.31), channel_id=1, source_target_pairs={{0,8},{4,12},{8,0},{12,4},{16,24},{20,28},{24,16},{28,20},{1,9},{5... | collective-permute-start | bytes 99848 | tf_op jit(solution)/shard_map/ppermute | solution.py:18
  55.3 2.4 %collective-permute-done.7 = f32[65,128]{1,0:T(8,128)S(1)} collective-permute-done((f32[65,128]{1,0:T(8,128)S(1)}, f32[65,128]{1,0:T(8,128)S(1)}, u32[]{:S(2)}, u32[]{:S(2)}) %collective-permute-start.7) | collective-permute-done | bytes 33312 | tf_op jit(solution)/shard_map/ppermute | solution.py:18
  57.7 2.6 %collective-permute-start.8 = (f32[65,128]{1,0:T(8,128)S(1)}, f32[65,128]{1,0:T(8,128)S(1)}, u32[]{:S(2)}, u32[]{:S(2)}) collective-permute-start(f32[65,128]{1,0:T(8,128)S(1)} %add.188), channel_id=1, source_target_pairs={{0,16},{4,20},{8,24},{12,28},{16,0},{20,4},{24,8},{28,12},{1,17},{... | collective-permute-start | bytes 99848 | tf_op jit(solution)/shard_map/ppermute | solution.py:18
  60.3 2.3 %collective-permute-done.8 = f32[65,128]{1,0:T(8,128)S(1)} collective-permute-done((f32[65,128]{1,0:T(8,128)S(1)}, f32[65,128]{1,0:T(8,128)S(1)}, u32[]{:S(2)}, u32[]{:S(2)}) %collective-permute-start.8) | collective-permute-done | bytes 33312 | tf_op jit(solution)/shard_map/ppermute | solution.py:18
  63.2 0.7 multiply_reduce_fusion.4
  63.9 1.4 %maximum_bitcast_fusion = f32[1,128]{1,0:T(1,128)S(1)} fusion(f32[126]{0:T(128)S(1)} %broadcast_in_dim.5, f32[1]{0:T(128)} %bitcast.22, f32[1]{0:T(128)} %bitcast.21), kind=kLoop, calls=%fused_computation.102 | loop fusion | flops 256 | bytes 1024 | tf_op jit(solution)/shard_map/reshape | solution.py:161
  65.4 1.1 %collective-permute-done.9 = f32[1,128]{1,0:T(1,128)S(1)} collective-permute-done((f32[1,128]{1,0:T(1,128)S(1)}, f32[1,128]{1,0:T(1,128)S(1)}, u32[]{:S(2)}, u32[]{:S(2)}) %collective-permute-start.9) | collective-permute-done | bytes 544 | tf_op jit(solution)/shard_map/ppermute | solution.py:18
  66.5 1.4 %fusion.41 = f32[1,128]{1,0:T(1,128)S(1)} fusion(f32[1,128]{1,0:T(1,128)S(1)} %collective-permute-done.9, f32[126]{0:T(128)S(1)} %broadcast_in_dim.5, f32[1]{0:T(128)} %bitcast.22, f32[1]{0:T(128)} %bitcast.21), kind=kLoop, calls=%fused_computation.110 | loop fusion | flops 384 | bytes 1536 | tf_op jit(solution)/shard_map/add | solution.py:45
  67.9 2.0 %collective-permute-start.10 = (f32[1,128]{1,0:T(1,128)S(1)}, f32[1,128]{1,0:T(1,128)S(1)}, u32[]{:S(2)}, u32[]{:S(2)}) collective-permute-start(f32[1,128]{1,0:T(1,128)S(1)} %fusion.41), channel_id=1, source_target_pairs={{0,2},{1,3},{2,0},{3,1},{4,6},{5,7},{6,4},{7,5},{8,10},{9,11},{10,... | collective-permute-start | bytes 1544 | tf_op jit(solution)/shard_map/ppermute | solution.py:18
  72.4 1.4 %fusion.42 = f32[1,128]{1,0:T(1,128)S(1)} fusion(f32[1,128]{1,0:T(1,128)S(1)} %collective-permute-done.10, f32[1,128]{1,0:T(1,128)S(1)} %collective-permute-done.9, f32[126]{0:T(128)S(1)} %broadcast_in_dim.5, f32[1]{0:T(128)} %bitcast.22, f32[1]{0:T(128)} %bitcast.21), kind=kLoop, calls=%fused_computation.111 | loop fusion | flops 512 | bytes 2048 | tf_op jit(solution)/shard_map/add | solution.py:45
  77.7 0.7 multiply_add_fusion.3
  78.3 0.7 multiply_add_fusion.1
  (79 shorter events, 6.3 us)
Async XLA Ops:
  0.6 10.0 %copy-start.9 = (f32[3,128]{1,0:T(4,128)S(1)}, f32[3,128]{1,0:T(4,128)}, u32[]{:S(2)}) copy-start(f32[3,128]{1,0:T(4,128)} %param.28) | copy-start | bytes 4612
  0.6 9.0 %copy-start.10 = (f32[5,128]{1,0:T(8,128)S(1)}, f32[5,128]{1,0:T(8,128)}, u32[]{:S(2)}) copy-start(f32[5,128]{1,0:T(8,128)} %param.27) | copy-start | bytes 7684
  0.7 9.0 %copy-start.1 = (f32[5,128,128]{2,1,0:T(8,128)S(1)}, f32[5,128,128]{2,1,0:T(8,128)}, u32[]{:S(2)}) copy-start(f32[5,128,128]{2,1,0:T(8,128)} %param.15) | copy-start | bytes 983044
  0.7 9.1 %copy-start.5 = (s32[128,128]{1,0:T(8,128)S(1)}, s32[128,128]{1,0:T(8,128)}, u32[]{:S(2)}) copy-start(s32[128,128]{1,0:T(8,128)} %param.20) | copy-start | bytes 196612
  0.7 12.3 %collective-permute-start.1 = (f32[1,2,4096]{2,1,0:T(2,128)}, f32[1,2,4096]{2,1,0:T(2,128)S(1)}, u32[]{:S(2)}, u32[]{:S(2)}) collective-permute-start(f32[1,2,4096]{2,1,0:T(2,128)} %bitcast.108), channel_id=1, source_target_pairs={{0,1},{1,0},{2,3},{3,2},{4,5},{5,4},{6,7},{7,6},{8,9},{9,8},{10,11... | collective-permute-start | bytes 98312 | tf_op jit(solution)/shard_map/ppermute | solution.py:18
  1.2 9.3 %collective-permute-start = (f32[3,3]{1,0:T(4,128)}, f32[3,3]{1,0:T(4,128)S(1)}, u32[]{:S(2)}, u32[]{:S(2)}) collective-permute-start(f32[3,3]{1,0:T(4,128)} %bitcast.110), channel_id=1, source_target_pairs={{1,0},{2,1},{3,2},{4,3},{5,4},{6,5},{7,6},{8,7},{9,8},{10,9},{11,1... | collective-permute-start | bytes 116 | tf_op jit(solution)/shard_map/ppermute | solution.py:13
  5.5 7.4 %copy-start.4 = (f32[2,4096]{1,0:T(2,128)S(1)}, f32[2,4096]{1,0:T(2,128)}, u32[]{:S(2)}) copy-start(f32[2,4096]{1,0:T(2,128)} %param.29) | copy-start | bytes 98308
  5.5 10.8 %copy-start.2 = (f32[3,128,128]{2,1,0:T(8,128)S(1)}, f32[3,128,128]{2,1,0:T(8,128)}, u32[]{:S(2)}) copy-start(f32[3,128,128]{2,1,0:T(8,128)} %param.16) | copy-start | bytes 589828
  13.0 6.1 %collective-permute-start.2 = (f32[1,4,4096]{2,1,0:T(4,128)S(1)}, f32[1,4,4096]{2,1,0:T(4,128)S(1)}, u32[]{:S(2)}, u32[]{:S(2)}) collective-permute-start(f32[1,4,4096]{2,1,0:T(4,128)S(1)} %maximum_select_fusion.1), channel_id=1, source_target_pairs={{0,2},{1,3},{2,0},{3,1},{4,6},{5,7},{6,4},{7,5},{8,10},{9,11},{10,... | collective-permute-start | bytes 196616 | tf_op jit(solution)/shard_map/ppermute | solution.py:18
  19.2 5.6 %copy-start.6 = (f32[128,128]{1,0:T(8,128)S(1)}, f32[128,128]{1,0:T(8,128)}, u32[]{:S(2)}) copy-start(f32[128,128]{1,0:T(8,128)} %param.18) | copy-start | bytes 196612
  19.2 5.6 %copy-start.7 = (f32[128,128]{1,0:T(8,128)S(1)}, f32[128,128]{1,0:T(8,128)}, u32[]{:S(2)}) copy-start(f32[128,128]{1,0:T(8,128)} %param.19) | copy-start | bytes 196612
  19.2 5.6 %copy-start.8 = (f32[128,128]{1,0:T(8,128)S(1)}, f32[128,128]{1,0:T(8,128)}, u32[]{:S(2)}) copy-start(f32[128,128]{1,0:T(8,128)} %param.17) | copy-start | bytes 196612
  19.2 5.6 %copy-start.13 = (s32[128]{0:T(128)S(1)}, s32[128]{0:T(128)}, u32[]{:S(2)}) copy-start(s32[128]{0:T(128)} %param.23) | copy-start | bytes 1540
  25.2 5.8 %copy-start = (pred[256,16384]{1,0:T(32,128)(4,1)S(1)}, pred[256,16384]{1,0:T(32,128)(4,1)}, u32[]{:S(2)}) copy-start(pred[256,16384]{1,0:T(32,128)(4,1)} %iota_compare_fusion.14) | copy-start | bytes 12582916
  28.6 7.6 %collective-permute-start.3 = (f32[3,3]{1,0:T(4,128)S(1)}, f32[3,3]{1,0:T(4,128)S(1)}, u32[]{:S(2)}, u32[]{:S(2)}) collective-permute-start(f32[3,3]{1,0:T(4,128)S(1)} %slice.152), channel_id=1, source_target_pairs={{0,1},{1,2},{2,3},{3,4},{4,5},{5,6},{6,7},{7,8},{8,9},{9,10},{10,1... | collective-permute-start | bytes 116 | tf_op jit(solution)/shard_map/ppermute | solution.py:13
  31.1 4.5 %copy-start.11 = (f32[5,128]{1,0:T(8,128)S(1)}, f32[5,128]{1,0:T(8,128)}, u32[]{:S(2)}) copy-start(f32[5,128]{1,0:T(8,128)} %param.24) | copy-start | bytes 7684
  31.1 5.2 %copy-start.12 = (f32[3,128]{1,0:T(4,128)S(1)}, f32[3,128]{1,0:T(4,128)}, u32[]{:S(2)}) copy-start(f32[3,128]{1,0:T(4,128)} %param.25) | copy-start | bytes 4612
  31.1 32.1 %copy-start.3 = (f32[2,4096]{1,0:T(2,128)S(1)}, f32[2,4096]{1,0:T(2,128)}, u32[]{:S(2)}) copy-start(f32[2,4096]{1,0:T(2,128)} %param.26) | copy-start | bytes 98308
  41.6 2.9 %collective-permute-start.4 = (f32[129,128]{1,0:T(8,128)S(1)}, f32[129,128]{1,0:T(8,128)S(1)}, u32[]{:S(2)}, u32[]{:S(2)}) collective-permute-start(f32[129,128]{1,0:T(8,128)S(1)} %pad_maximum_fusion.2), channel_id=1, source_target_pairs={{0,1},{1,0},{2,3},{3,2},{4,5},{5,4},{6,7},{7,6},{8,9},{9,8},{10,11... | collective-permute-start | bytes 198152 | tf_op jit(solution)/shard_map/ppermute | solution.py:18
  44.6 4.7 %collective-permute-start.5 = (f32[65,128]{1,0:T(8,128)S(1)}, f32[65,128]{1,0:T(8,128)S(1)}, u32[]{:S(2)}, u32[]{:S(2)}) collective-permute-start(f32[65,128]{1,0:T(8,128)S(1)} %pad_maximum_fusion.3), channel_id=1, source_target_pairs={{0,2},{1,3},{2,0},{3,1},{4,6},{5,7},{6,4},{7,5},{8,10},{9,11},{10,... | collective-permute-start | bytes 99848 | tf_op jit(solution)/shard_map/ppermute | solution.py:18
  49.3 4.4 %collective-permute-start.6 = (f32[65,128]{1,0:T(8,128)S(1)}, f32[65,128]{1,0:T(8,128)S(1)}, u32[]{:S(2)}, u32[]{:S(2)}) collective-permute-start(f32[65,128]{1,0:T(8,128)S(1)} %pad_maximum_fusion.4), channel_id=1, source_target_pairs={{0,4},{4,0},{8,12},{12,8},{16,20},{20,16},{24,28},{28,24},{1,5},{5... | collective-permute-start | bytes 99848 | tf_op jit(solution)/shard_map/ppermute | solution.py:18
  53.7 4.0 %collective-permute-start.7 = (f32[65,128]{1,0:T(8,128)S(1)}, f32[65,128]{1,0:T(8,128)S(1)}, u32[]{:S(2)}, u32[]{:S(2)}) collective-permute-start(f32[65,128]{1,0:T(8,128)S(1)} %fusion.31), channel_id=1, source_target_pairs={{0,8},{4,12},{8,0},{12,4},{16,24},{20,28},{24,16},{28,20},{1,9},{5... | collective-permute-start | bytes 99848 | tf_op jit(solution)/shard_map/ppermute | solution.py:18
  57.7 4.9 %collective-permute-start.8 = (f32[65,128]{1,0:T(8,128)S(1)}, f32[65,128]{1,0:T(8,128)S(1)}, u32[]{:S(2)}, u32[]{:S(2)}) collective-permute-start(f32[65,128]{1,0:T(8,128)S(1)} %add.188), channel_id=1, source_target_pairs={{0,16},{4,20},{8,24},{12,28},{16,0},{20,4},{24,8},{28,12},{1,17},{... | collective-permute-start | bytes 99848 | tf_op jit(solution)/shard_map/ppermute | solution.py:18
  65.3 1.1 %collective-permute-start.9 = (f32[1,128]{1,0:T(1,128)S(1)}, f32[1,128]{1,0:T(1,128)S(1)}, u32[]{:S(2)}, u32[]{:S(2)}) collective-permute-start(f32[1,128]{1,0:T(1,128)S(1)} %maximum_bitcast_fusion), channel_id=1, source_target_pairs={{0,1},{1,0},{2,3},{3,2},{4,5},{5,4},{6,7},{7,6},{8,9},{9,8},{10,11... | collective-permute-start | bytes 1544 | tf_op jit(solution)/shard_map/ppermute | solution.py:18
  67.9 4.6 %collective-permute-start.10 = (f32[1,128]{1,0:T(1,128)S(1)}, f32[1,128]{1,0:T(1,128)S(1)}, u32[]{:S(2)}, u32[]{:S(2)}) collective-permute-start(f32[1,128]{1,0:T(1,128)S(1)} %fusion.41), channel_id=1, source_target_pairs={{0,2},{1,3},{2,0},{3,1},{4,6},{5,7},{6,4},{7,5},{8,10},{9,11},{10,... | collective-permute-start | bytes 1544 | tf_op jit(solution)/shard_map/ppermute | solution.py:18

commit v15 on v10

--- a/solution.py
+++ b/solution.py
@@ -50,8 +50,9 @@
 def doubling_gather(block, axis):
     count = lax.axis_size(axis)
     me = lax.axis_index(axis)
-    distance = 1
-    while distance < count:
+    bits = count.bit_length() - 1
+    distance = count // 2
+    while distance >= 1:
         other = exchanged(block, axis, distance)
         mine_first = (me // distance) % 2 == 0
         block = jnp.where(
@@ -59,8 +60,10 @@
             jnp.concatenate([block, other], axis=1),
             jnp.concatenate([other, block], axis=1),
         )
-        distance *= 2
-    return block
+        distance //= 2
+    order = [int(format(i, "0%db" % bits)[::-1], 2) if bits else 0 for i in range(count)]
+    parts = block.reshape(block.shape[0], count, block.shape[1] // count, *block.shape[2:])
+    return jnp.concatenate([parts[:, k] for k in order], axis=1)
 
 
 def spline(phase):

time: 75.4 us -> 72.3 us (0.959)
  waiting for transfers between devices: 13.3 us -> 11.6 us
  starting transfers between devices: 20.5 us -> 18.8 us
    ppermute x9, starting transfers between devices: 17.4 us -> 15.3 us  [exchanged(): return lax.ppermute(block, axis, [(i, i ^ distance) for i in devices])]
    ppermute x9, waiting for transfers between devices: 13.3 us -> 11.6 us  [exchanged(): return lax.ppermute(block, axis, [(i, i ^ distance) for i in devices])]
  transfers between devices with their start and end apart: 11 -> 11, of which waited for: 7 -> 7; matrix products, arithmetic and copies ran while one was open for 21% -> 22% of each run, Pallas kernels for 0% -> 0%
where the time goes in v15:
time: 72.3 us; the launch traced here: 71.8 us
  starting transfers between devices  18.8 us (26%)
  matrix products  14.7 us (20%)
  other arithmetic  13.1 us (18%)
  waiting for transfers between devices  11.6 us (16%)
  between operations  9.69 us (13%)
  local copies, waits for them, and re-layouts  3.94 us (5%)
    ppermute x9, starting transfers between devices, exchanged(): return lax.ppermute(block, axis, [(i, i ^ distance) for i in devices])  15.3 us
    ppermute x9, waiting for transfers between devices, exchanged(): return lax.ppermute(block, axis, [(i, i ^ distance) for i in devices])  11.6 us
    dot_general x1, matrix products, local(): lax.dot_general(cal_table, high_hot, (((0,), (0,)), ((), ())), precision=...  5.59 us
    dot_general x1, matrix products, local(): lax.dot_general(high_hot, cal_weighted, (((1,), (1,)), ((), ())), precisi...  4.49 us
    dot_general x1, other arithmetic, local(): lax.dot_general(high_hot, cal_weighted, (((1,), (1,)), ((), ())), precisi...  4.09 us
    ppermute x2, starting transfers between devices, passed_along(): return lax.ppermute(block, axis, route)  3.54 us
    dot_general x1, matrix products, local(): lax.dot_general(spread, knot_hot, (((1,), (1,)), ((), ())), precision=ONE...  2.43 us
    dot_general x1, matrix products, local(): jnp.dot(table, knot_hot, precision=ONE_HOT_PRECISION)  2.16 us
  transfers between devices with their start and end apart: 11, of which 7 were waited for; matrix products, arithmetic and copies ran while one was open for 22% of the time, Pallas kernels for 0%

profile of v15, /device:TPU:0, one launch (start us, length us, event | category | flops | bytes accessed | tf_op | source)
XLA Modules:
  0.0 71.8 jit_solution(2395453085050769716)
XLA Ops:
  0.7 3.0 %collective-permute-start.1 = (f32[1,2,4096]{2,1,0:T(2,128)}, f32[1,2,4096]{2,1,0:T(2,128)S(1)}, u32[]{:S(2)}, u32[]{:S(2)}) collective-permute-start(f32[1,2,4096]{2,1,0:T(2,128)} %bitcast.111), channel_id=1, source_target_pairs={{0,2},{1,3},{2,0},{3,1},{4,6},{5,7},{6,4},{7,5},{8,10},{9,11},{10,... | collective-permute-start | bytes 98312 | tf_op jit(solution)/shard_map/ppermute | solution.py:18
  3.7 1.3 %collective-permute-start = (f32[3,3]{1,0:T(4,128)}, f32[3,3]{1,0:T(4,128)S(1)}, u32[]{:S(2)}, u32[]{:S(2)}) collective-permute-start(f32[3,3]{1,0:T(4,128)} %bitcast.113), channel_id=1, source_target_pairs={{1,0},{2,1},{3,2},{4,3},{5,4},{6,5},{7,6},{8,7},{9,8},{10,9},{11,1... | collective-permute-start | bytes 116 | tf_op jit(solution)/shard_map/ppermute | solution.py:13
  5.0 0.7 constant_dynamic-update-slice_fusion.1
  5.7 1.4 %multiply_reduce_fusion.4 = f32[]{:T(128)} fusion(f32[2,4096]{1,0:T(2,128)} %param.26), kind=kLoop, calls=%fused_computation.82 | loop fusion | flops 16383 | bytes 32772 | tf_op jit(solution)/shard_map/reduce_sum | solution.py:153
  7.1 0.9 %add_select_fusion = (s32[16384]{0:T(1024)S(1)}, s32[16384]{0:T(1024)S(1)}) fusion(s32[128,128]{1,0:T(8,128)} %param.22, s32[128,128]{1,0:T(8,128)} %param.21), kind=kLoop, calls=%fused_computation.39 | loop fusion | flops 344064 | bytes 262144 | tf_op jit(solution)/shard_map/jit(remainder)/select_n | solution.py:129
  8.0 4.1 %iota_compare_fusion.14 = pred[256,16384]{1,0:T(32,128)(4,1)} fusion(s32[16384]{0:T(1024)S(1)} %get-tuple-element.38), kind=kLoop, calls=%fused_computation.1.clone.clone.2 | loop fusion | flops 4194304 | bytes 4259840 | tf_op jit(solution)/shard_map/dot_general | solution.py:151
  13.1 2.2 %fusion.3 = f32[12,16384]{1,0:T(8,128)S(1)} fusion(f32[12,128]{1,0:T(8,128)S(1)} %reshape.269, s32[16384]{0:T(1024)S(1)} %subtract_bitcast_fusion), kind=kOutput, calls=%fused_computation.6 | convolution fusion | flops 153092096 | bytes 858112 | tf_op jit(solution)/shard_map/dot_general | solution.py:122
  15.5 1.2 %collective-permute-start.2 = (f32[1,4,4096]{2,1,0:T(4,128)S(1)}, f32[1,4,4096]{2,1,0:T(4,128)S(1)}, u32[]{:S(2)}, u32[]{:S(2)}) collective-permute-start(f32[1,4,4096]{2,1,0:T(4,128)S(1)} %maximum_select_fusion.1), channel_id=1, source_target_pairs={{0,1},{1,0},{2,3},{3,2},{4,5},{5,4},{6,7},{7,6},{8,9},{9,8},{10,11... | collective-permute-start | bytes 196616 | tf_op jit(solution)/shard_map/ppermute | solution.py:18
  16.8 0.8 %collective-permute-done.2 = f32[1,4,4096]{2,1,0:T(4,128)S(1)} collective-permute-done((f32[1,4,4096]{2,1,0:T(4,128)S(1)}, f32[1,4,4096]{2,1,0:T(4,128)S(1)}, u32[]{:S(2)}, u32[]{:S(2)}) %collective-permute-start.2) | collective-permute-done | bytes 65568 | tf_op jit(solution)/shard_map/ppermute | solution.py:18
  17.9 5.6 %fusion.11 = f32[16384]{0:T(1024)S(1)} fusion(f32[256,128]{1,0:T(8,128)S(1)} %reshape_squeeze.3, s32[16384]{0:T(1024)S(1)} %get-tuple-element.38, s32[16384]{0:T(1024)S(1)} %get-tuple-element.37), kind=kOutput, calls=%fused_computation.15 | convolution fusion | flops 3231694848 | bytes 327680 | tf_op jit(solution)/shard_map/dot_general | solution.py:131
  24.7 2.4 %fusion.2 = f32[12,128]{1,0:T(8,128)S(1)} fusion(f32[12,16384]{1,0:T(8,128)S(1)} %bitcast.110, s32[16384]{0:T(1024)S(1)} %subtract_bitcast_fusion), kind=kOutput, calls=%fused_computation.5 | convolution fusion | flops 153092096 | bytes 858112 | tf_op jit(solution)/shard_map/dot_general | solution.py:142
  27.3 2.3 %collective-permute-start.3 = (f32[3,3]{1,0:T(4,128)S(1)}, f32[3,3]{1,0:T(4,128)S(1)}, u32[]{:S(2)}, u32[]{:S(2)}) collective-permute-start(f32[3,3]{1,0:T(4,128)S(1)} %slice.168), channel_id=1, source_target_pairs={{0,1},{1,2},{2,3},{3,4},{4,5},{5,6},{6,7},{7,8},{8,9},{9,10},{10,1... | collective-permute-start | bytes 116 | tf_op jit(solution)/shard_map/ppermute | solution.py:13
  30.2 4.5 %fusion = f32[256,128]{1,0:T(8,128)S(1)} fusion(f32[16384]{0:T(1024)S(1)} %get-tuple-element.22, s32[16384]{0:T(1024)S(1)} %get-tuple-element.37, pred[256,16384]{1,0:T(32,128)(4,1)S(1)} %copy-done), kind=kOutput, calls=%fused_computation.2 | convolution fusion | flops 3225419776 | bytes 4456448 | tf_op jit(solution)/shard_map/dot_general | solution.py:151
  35.4 0.7 multiply_reduce_fusion.8
  40.0 0.7 concatenate.73
  40.7 0.9 %collective-permute-start.4 = (f32[129,128]{1,0:T(8,128)S(1)}, f32[129,128]{1,0:T(8,128)S(1)}, u32[]{:S(2)}, u32[]{:S(2)}) collective-permute-start(f32[129,128]{1,0:T(8,128)S(1)} %pad_maximum_fusion.3), channel_id=1, source_target_pairs={{0,1},{1,0},{2,3},{3,2},{4,5},{5,4},{6,7},{7,6},{8,9},{9,8},{10,11... | collective-permute-start | bytes 198152 | tf_op jit(solution)/shard_map/ppermute | solution.py:18
  41.6 0.9 %collective-permute-done.4 = f32[129,128]{1,0:T(8,128)S(1)} collective-permute-done((f32[129,128]{1,0:T(8,128)S(1)}, f32[129,128]{1,0:T(8,128)S(1)}, u32[]{:S(2)}, u32[]{:S(2)}) %collective-permute-start.4) | collective-permute-done | bytes 66080 | tf_op jit(solution)/shard_map/ppermute | solution.py:18
  42.5 2.0 %collective-permute-start.5 = (f32[65,128]{1,0:T(8,128)S(1)}, f32[65,128]{1,0:T(8,128)S(1)}, u32[]{:S(2)}, u32[]{:S(2)}) collective-permute-start(f32[65,128]{1,0:T(8,128)S(1)} %pad_maximum_fusion.4), channel_id=1, source_target_pairs={{0,2},{1,3},{2,0},{3,1},{4,6},{5,7},{6,4},{7,5},{8,10},{9,11},{10,... | collective-permute-start | bytes 99848 | tf_op jit(solution)/shard_map/ppermute | solution.py:18
  44.5 2.0 %collective-permute-done.5 = f32[65,128]{1,0:T(8,128)S(1)} collective-permute-done((f32[65,128]{1,0:T(8,128)S(1)}, f32[65,128]{1,0:T(8,128)S(1)}, u32[]{:S(2)}, u32[]{:S(2)}) %collective-permute-start.5) | collective-permute-done | bytes 33312 | tf_op jit(solution)/shard_map/ppermute | solution.py:18
  46.6 2.0 %collective-permute-start.6 = (f32[65,128]{1,0:T(8,128)S(1)}, f32[65,128]{1,0:T(8,128)S(1)}, u32[]{:S(2)}, u32[]{:S(2)}) collective-permute-start(f32[65,128]{1,0:T(8,128)S(1)} %pad_maximum_fusion.5), channel_id=1, source_target_pairs={{0,4},{4,0},{8,12},{12,8},{16,20},{20,16},{24,28},{28,24},{1,5},{5... | collective-permute-start | bytes 99848 | tf_op jit(solution)/shard_map/ppermute | solution.py:18
  48.5 2.1 %collective-permute-done.6 = f32[65,128]{1,0:T(8,128)S(1)} collective-permute-done((f32[65,128]{1,0:T(8,128)S(1)}, f32[65,128]{1,0:T(8,128)S(1)}, u32[]{:S(2)}, u32[]{:S(2)}) %collective-permute-start.6) | collective-permute-done | bytes 33312 | tf_op jit(solution)/shard_map/ppermute | solution.py:18
  50.6 1.6 %collective-permute-start.7 = (f32[65,128]{1,0:T(8,128)S(1)}, f32[65,128]{1,0:T(8,128)S(1)}, u32[]{:S(2)}, u32[]{:S(2)}) collective-permute-start(f32[65,128]{1,0:T(8,128)S(1)} %fusion.31), channel_id=1, source_target_pairs={{0,8},{4,12},{8,0},{12,4},{16,24},{20,28},{24,16},{28,20},{1,9},{5... | collective-permute-start | bytes 99848 | tf_op jit(solution)/shard_map/ppermute | solution.py:18
  52.2 2.4 %collective-permute-done.7 = f32[65,128]{1,0:T(8,128)S(1)} collective-permute-done((f32[65,128]{1,0:T(8,128)S(1)}, f32[65,128]{1,0:T(8,128)S(1)}, u32[]{:S(2)}, u32[]{:S(2)}) %collective-permute-start.7) | collective-permute-done | bytes 33312 | tf_op jit(solution)/shard_map/ppermute | solution.py:18
  54.6 2.6 %collective-permute-start.8 = (f32[65,128]{1,0:T(8,128)S(1)}, f32[65,128]{1,0:T(8,128)S(1)}, u32[]{:S(2)}, u32[]{:S(2)}) collective-permute-start(f32[65,128]{1,0:T(8,128)S(1)} %add.178), channel_id=1, source_target_pairs={{0,16},{4,20},{8,24},{12,28},{16,0},{20,4},{24,8},{28,12},{1,17},{... | collective-permute-start | bytes 99848 | tf_op jit(solution)/shard_map/ppermute | solution.py:18
  57.2 2.3 %collective-permute-done.8 = f32[65,128]{1,0:T(8,128)S(1)} collective-permute-done((f32[65,128]{1,0:T(8,128)S(1)}, f32[65,128]{1,0:T(8,128)S(1)}, u32[]{:S(2)}, u32[]{:S(2)}) %collective-permute-start.8) | collective-permute-done | bytes 33312 | tf_op jit(solution)/shard_map/ppermute | solution.py:18
  62.1 0.6 multiply_reduce_fusion.3
  62.7 0.7 broadcast_in_dim.5
  63.5 1.1 %collective-permute-done.9 = f32[1,128]{1,0:T(1,128)S(1)} collective-permute-done((f32[1,128]{1,0:T(1,128)S(1)}, f32[1,128]{1,0:T(1,128)S(1)}, u32[]{:S(2)}, u32[]{:S(2)}) %collective-permute-start.9) | collective-permute-done | bytes 544 | tf_op jit(solution)/shard_map/ppermute | solution.py:18
  64.6 0.6 broadcast_add_fusion
  65.2 2.0 %collective-permute-start.10 = (f32[1,128]{1,0:T(1,128)S(1)}, f32[1,128]{1,0:T(1,128)S(1)}, u32[]{:S(2)}, u32[]{:S(2)}) collective-permute-start(f32[1,128]{1,0:T(1,128)S(1)} %broadcast_add_fusion), channel_id=1, source_target_pairs={{0,2},{1,3},{2,0},{3,1},{4,6},{5,7},{6,4},{7,5},{8,10},{9,11},{10,... | collective-permute-start | bytes 1544 | tf_op jit(solution)/shard_map/ppermute | solution.py:18
  69.2 0.7 fusion.39
  70.6 0.7 multiply_add_fusion.3
  (82 shorter events, 5.4 us)
Async XLA Ops:
  0.6 12.4 %copy-start.10 = (f32[3,128]{1,0:T(4,128)S(1)}, f32[3,128]{1,0:T(4,128)}, u32[]{:S(2)}) copy-start(f32[3,128]{1,0:T(4,128)} %param.28) | copy-start | bytes 4612
  0.6 11.5 %copy-start.11 = (f32[5,128]{1,0:T(8,128)S(1)}, f32[5,128]{1,0:T(8,128)}, u32[]{:S(2)}) copy-start(f32[5,128]{1,0:T(8,128)} %param.27) | copy-start | bytes 7684
  0.7 11.5 %copy-start.1 = (f32[5,128,128]{2,1,0:T(8,128)S(1)}, f32[5,128,128]{2,1,0:T(8,128)}, u32[]{:S(2)}) copy-start(f32[5,128,128]{2,1,0:T(8,128)} %param.15) | copy-start | bytes 983044
  0.7 11.6 %copy-start.6 = (s32[128,128]{1,0:T(8,128)S(1)}, s32[128,128]{1,0:T(8,128)}, u32[]{:S(2)}) copy-start(s32[128,128]{1,0:T(8,128)} %param.20) | copy-start | bytes 196612
  0.7 14.8 %collective-permute-start.1 = (f32[1,2,4096]{2,1,0:T(2,128)}, f32[1,2,4096]{2,1,0:T(2,128)S(1)}, u32[]{:S(2)}, u32[]{:S(2)}) collective-permute-start(f32[1,2,4096]{2,1,0:T(2,128)} %bitcast.111), channel_id=1, source_target_pairs={{0,2},{1,3},{2,0},{3,1},{4,6},{5,7},{6,4},{7,5},{8,10},{9,11},{10,... | collective-permute-start | bytes 98312 | tf_op jit(solution)/shard_map/ppermute | solution.py:18
  3.7 9.3 %collective-permute-start = (f32[3,3]{1,0:T(4,128)}, f32[3,3]{1,0:T(4,128)S(1)}, u32[]{:S(2)}, u32[]{:S(2)}) collective-permute-start(f32[3,3]{1,0:T(4,128)} %bitcast.113), channel_id=1, source_target_pairs={{1,0},{2,1},{3,2},{4,3},{5,4},{6,5},{7,6},{8,7},{9,8},{10,9},{11,1... | collective-permute-start | bytes 116 | tf_op jit(solution)/shard_map/ppermute | solution.py:13
  8.0 7.4 %copy-start.5 = (f32[2,4096]{1,0:T(2,128)S(1)}, f32[2,4096]{1,0:T(2,128)}, u32[]{:S(2)}) copy-start(f32[2,4096]{1,0:T(2,128)} %param.29) | copy-start | bytes 98308
  8.0 8.7 %copy-start.2 = (f32[3,128,128]{2,1,0:T(8,128)S(1)}, f32[3,128,128]{2,1,0:T(8,128)}, u32[]{:S(2)}) copy-start(f32[3,128,128]{2,1,0:T(8,128)} %param.16) | copy-start | bytes 589828
  15.5 2.1 %collective-permute-start.2 = (f32[1,4,4096]{2,1,0:T(4,128)S(1)}, f32[1,4,4096]{2,1,0:T(4,128)S(1)}, u32[]{:S(2)}, u32[]{:S(2)}) collective-permute-start(f32[1,4,4096]{2,1,0:T(4,128)S(1)} %maximum_select_fusion.1), channel_id=1, source_target_pairs={{0,1},{1,0},{2,3},{3,2},{4,5},{5,4},{6,7},{7,6},{8,9},{9,8},{10,11... | collective-permute-start | bytes 196616 | tf_op jit(solution)/shard_map/ppermute | solution.py:18
  17.9 5.6 %copy-start.7 = (f32[128,128]{1,0:T(8,128)S(1)}, f32[128,128]{1,0:T(8,128)}, u32[]{:S(2)}) copy-start(f32[128,128]{1,0:T(8,128)} %param.18) | copy-start | bytes 196612
  17.9 5.6 %copy-start.8 = (f32[128,128]{1,0:T(8,128)S(1)}, f32[128,128]{1,0:T(8,128)}, u32[]{:S(2)}) copy-start(f32[128,128]{1,0:T(8,128)} %param.19) | copy-start | bytes 196612
  17.9 5.6 %copy-start.9 = (f32[128,128]{1,0:T(8,128)S(1)}, f32[128,128]{1,0:T(8,128)}, u32[]{:S(2)}) copy-start(f32[128,128]{1,0:T(8,128)} %param.17) | copy-start | bytes 196612
  17.9 5.6 %copy-start.14 = (s32[128]{0:T(128)S(1)}, s32[128]{0:T(128)}, u32[]{:S(2)}) copy-start(s32[128]{0:T(128)} %param.23) | copy-start | bytes 1540
  23.9 6.3 %copy-start = (pred[256,16384]{1,0:T(32,128)(4,1)S(1)}, pred[256,16384]{1,0:T(32,128)(4,1)}, u32[]{:S(2)}) copy-start(pred[256,16384]{1,0:T(32,128)(4,1)} %iota_compare_fusion.14) | copy-start | bytes 12582916
  27.3 8.1 %collective-permute-start.3 = (f32[3,3]{1,0:T(4,128)S(1)}, f32[3,3]{1,0:T(4,128)S(1)}, u32[]{:S(2)}, u32[]{:S(2)}) collective-permute-start(f32[3,3]{1,0:T(4,128)S(1)} %slice.168), channel_id=1, source_target_pairs={{0,1},{1,2},{2,3},{3,4},{4,5},{5,6},{6,7},{7,8},{8,9},{9,10},{10,1... | collective-permute-start | bytes 116 | tf_op jit(solution)/shard_map/ppermute | solution.py:13
  30.2 4.5 %copy-start.12 = (f32[5,128]{1,0:T(8,128)S(1)}, f32[5,128]{1,0:T(8,128)}, u32[]{:S(2)}) copy-start(f32[5,128]{1,0:T(8,128)} %param.24) | copy-start | bytes 7684
  30.2 5.2 %copy-start.13 = (f32[3,128]{1,0:T(4,128)S(1)}, f32[3,128]{1,0:T(4,128)}, u32[]{:S(2)}) copy-start(f32[3,128]{1,0:T(4,128)} %param.25) | copy-start | bytes 4612
  30.2 31.9 %copy-start.4 = (f32[2,4096]{1,0:T(2,128)S(1)}, f32[2,4096]{1,0:T(2,128)}, u32[]{:S(2)}) copy-start(f32[2,4096]{1,0:T(2,128)} %param.26) | copy-start | bytes 98308
  40.7 1.8 %collective-permute-start.4 = (f32[129,128]{1,0:T(8,128)S(1)}, f32[129,128]{1,0:T(8,128)S(1)}, u32[]{:S(2)}, u32[]{:S(2)}) collective-permute-start(f32[129,128]{1,0:T(8,128)S(1)} %pad_maximum_fusion.3), channel_id=1, source_target_pairs={{0,1},{1,0},{2,3},{3,2},{4,5},{5,4},{6,7},{7,6},{8,9},{9,8},{10,11... | collective-permute-start | bytes 198152 | tf_op jit(solution)/shard_map/ppermute | solution.py:18
  42.5 4.0 %collective-permute-start.5 = (f32[65,128]{1,0:T(8,128)S(1)}, f32[65,128]{1,0:T(8,128)S(1)}, u32[]{:S(2)}, u32[]{:S(2)}) collective-permute-start(f32[65,128]{1,0:T(8,128)S(1)} %pad_maximum_fusion.4), channel_id=1, source_target_pairs={{0,2},{1,3},{2,0},{3,1},{4,6},{5,7},{6,4},{7,5},{8,10},{9,11},{10,... | collective-permute-start | bytes 99848 | tf_op jit(solution)/shard_map/ppermute | solution.py:18
  46.6 4.0 %collective-permute-start.6 = (f32[65,128]{1,0:T(8,128)S(1)}, f32[65,128]{1,0:T(8,128)S(1)}, u32[]{:S(2)}, u32[]{:S(2)}) collective-permute-start(f32[65,128]{1,0:T(8,128)S(1)} %pad_maximum_fusion.5), channel_id=1, source_target_pairs={{0,4},{4,0},{8,12},{12,8},{16,20},{20,16},{24,28},{28,24},{1,5},{5... | collective-permute-start | bytes 99848 | tf_op jit(solution)/shard_map/ppermute | solution.py:18
  50.6 4.0 %collective-permute-start.7 = (f32[65,128]{1,0:T(8,128)S(1)}, f32[65,128]{1,0:T(8,128)S(1)}, u32[]{:S(2)}, u32[]{:S(2)}) collective-permute-start(f32[65,128]{1,0:T(8,128)S(1)} %fusion.31), channel_id=1, source_target_pairs={{0,8},{4,12},{8,0},{12,4},{16,24},{20,28},{24,16},{28,20},{1,9},{5... | collective-permute-start | bytes 99848 | tf_op jit(solution)/shard_map/ppermute | solution.py:18
  54.6 4.9 %collective-permute-start.8 = (f32[65,128]{1,0:T(8,128)S(1)}, f32[65,128]{1,0:T(8,128)S(1)}, u32[]{:S(2)}, u32[]{:S(2)}) collective-permute-start(f32[65,128]{1,0:T(8,128)S(1)} %add.178), channel_id=1, source_target_pairs={{0,16},{4,20},{8,24},{12,28},{16,0},{20,4},{24,8},{28,12},{1,17},{... | collective-permute-start | bytes 99848 | tf_op jit(solution)/shard_map/ppermute | solution.py:18
  62.7 9.1 %copy-start.3 = (f32[2,4096]{1,0:T(2,128)}, f32[2,4096]{1,0:T(2,128)S(1)}, u32[]{:S(2)}) copy-start(f32[2,4096]{1,0:T(2,128)S(1)} %get-tuple-element.21) | copy-start | bytes 98308
  63.4 1.2 %collective-permute-start.9 = (f32[1,128]{1,0:T(1,128)S(1)}, f32[1,128]{1,0:T(1,128)S(1)}, u32[]{:S(2)}, u32[]{:S(2)}) collective-permute-start(f32[1,128]{1,0:T(1,128)S(1)} %broadcast_in_dim.5), channel_id=1, source_target_pairs={{0,1},{1,0},{2,3},{3,2},{4,5},{5,4},{6,7},{7,6},{8,9},{9,8},{10,11... | collective-permute-start | bytes 1544 | tf_op jit(solution)/shard_map/ppermute | solution.py:18
  65.2 4.0 %collective-permute-start.10 = (f32[1,128]{1,0:T(1,128)S(1)}, f32[1,128]{1,0:T(1,128)S(1)}, u32[]{:S(2)}, u32[]{:S(2)}) collective-permute-start(f32[1,128]{1,0:T(1,128)S(1)} %broadcast_add_fusion), channel_id=1, source_target_pairs={{0,2},{1,3},{2,0},{3,1},{4,6},{5,7},{6,4},{7,5},{8,10},{9,11},{10,... | collective-permute-start | bytes 1544 | tf_op jit(solution)/shard_map/ppermute | solution.py:18

commit v16 on v15

--- a/solution.py
+++ b/solution.py
@@ -40,10 +40,10 @@
 
 def doubling_sum(rows, axis):
     count = lax.axis_size(axis)
-    distance = 1
-    while distance < count:
+    distance = count // 2
+    while distance >= 1:
         rows = rows + exchanged(rows, axis, distance)
-        distance *= 2
+        distance //= 2
     return rows
 
 

time: 72.3 us -> 72.9 us (level)
  transfers between devices with their start and end apart: 11 -> 11, of which waited for: 7 -> 7; matrix products, arithmetic and copies ran while one was open for 22% -> 21% of each run, Pallas kernels for 0% -> 0%
where the time goes in v16:
time: 72.9 us; the launch traced here: 72.4 us
  starting transfers between devices  18.9 us (26%)
  matrix products  14.7 us (20%)
  other arithmetic  13.1 us (18%)
  waiting for transfers between devices  12 us (16%)
  between operations  9.69 us (13%)
  local copies, waits for them, and re-layouts  3.94 us (5%)
    ppermute x9, starting transfers between devices, exchanged(): return lax.ppermute(block, axis, [(i, i ^ distance) for i in devices])  15.4 us
    ppermute x9, waiting for transfers between devices, exchanged(): return lax.ppermute(block, axis, [(i, i ^ distance) for i in devices])  12 us
    dot_general x1, matrix products, local(): lax.dot_general(cal_table, high_hot, (((0,), (0,)), ((), ())), precision=...  5.59 us
    dot_general x1, matrix products, local(): lax.dot_general(high_hot, cal_weighted, (((1,), (1,)), ((), ())), precisi...  4.49 us
    dot_general x1, other arithmetic, local(): lax.dot_general(high_hot, cal_weighted, (((1,), (1,)), ((), ())), precisi...  4.09 us
    ppermute x2, starting transfers between devices, passed_along(): return lax.ppermute(block, axis, route)  3.54 us
    dot_general x1, matrix products, local(): lax.dot_general(spread, knot_hot, (((1,), (1,)), ((), ())), precision=ONE...  2.43 us
    dot_general x1, matrix products, local(): jnp.dot(table, knot_hot, precision=ONE_HOT_PRECISION)  2.16 us
  transfers between devices with their start and end apart: 11, of which 7 were waited for; matrix products, arithmetic and copies ran while one was open for 21% of the time, Pallas kernels for 0%

profile of v16, /device:TPU:0, one launch (start us, length us, event | category | flops | bytes accessed | tf_op | source)
XLA Modules:
  0.0 72.4 jit_solution(13249089491985144041)
XLA Ops:
  0.7 3.0 %collective-permute-start.1 = (f32[1,2,4096]{2,1,0:T(2,128)}, f32[1,2,4096]{2,1,0:T(2,128)S(1)}, u32[]{:S(2)}, u32[]{:S(2)}) collective-permute-start(f32[1,2,4096]{2,1,0:T(2,128)} %bitcast.111), channel_id=1, source_target_pairs={{0,2},{1,3},{2,0},{3,1},{4,6},{5,7},{6,4},{7,5},{8,10},{9,11},{10,... | collective-permute-start | bytes 98312 | tf_op jit(solution)/shard_map/ppermute | solution.py:18
  3.7 1.3 %collective-permute-start = (f32[3,3]{1,0:T(4,128)}, f32[3,3]{1,0:T(4,128)S(1)}, u32[]{:S(2)}, u32[]{:S(2)}) collective-permute-start(f32[3,3]{1,0:T(4,128)} %bitcast.113), channel_id=1, source_target_pairs={{1,0},{2,1},{3,2},{4,3},{5,4},{6,5},{7,6},{8,7},{9,8},{10,9},{11,1... | collective-permute-start | bytes 116 | tf_op jit(solution)/shard_map/ppermute | solution.py:13
  5.0 0.7 constant_dynamic-update-slice_fusion.1
  5.7 1.4 %multiply_reduce_fusion.4 = f32[]{:T(128)} fusion(f32[2,4096]{1,0:T(2,128)} %param.26), kind=kLoop, calls=%fused_computation.82 | loop fusion | flops 16383 | bytes 32772 | tf_op jit(solution)/shard_map/reduce_sum | solution.py:153
  7.1 0.9 %add_select_fusion = (s32[16384]{0:T(1024)S(1)}, s32[16384]{0:T(1024)S(1)}) fusion(s32[128,128]{1,0:T(8,128)} %param.22, s32[128,128]{1,0:T(8,128)} %param.21), kind=kLoop, calls=%fused_computation.39 | loop fusion | flops 344064 | bytes 262144 | tf_op jit(solution)/shard_map/jit(remainder)/select_n | solution.py:129
  8.0 4.1 %iota_compare_fusion.14 = pred[256,16384]{1,0:T(32,128)(4,1)} fusion(s32[16384]{0:T(1024)S(1)} %get-tuple-element.38), kind=kLoop, calls=%fused_computation.1.clone.clone.2 | loop fusion | flops 4194304 | bytes 4259840 | tf_op jit(solution)/shard_map/dot_general | solution.py:151
  13.1 2.2 %fusion.3 = f32[12,16384]{1,0:T(8,128)S(1)} fusion(f32[12,128]{1,0:T(8,128)S(1)} %reshape.269, s32[16384]{0:T(1024)S(1)} %subtract_bitcast_fusion), kind=kOutput, calls=%fused_computation.6 | convolution fusion | flops 153092096 | bytes 858112 | tf_op jit(solution)/shard_map/dot_general | solution.py:122
  15.5 1.2 %collective-permute-start.2 = (f32[1,4,4096]{2,1,0:T(4,128)S(1)}, f32[1,4,4096]{2,1,0:T(4,128)S(1)}, u32[]{:S(2)}, u32[]{:S(2)}) collective-permute-start(f32[1,4,4096]{2,1,0:T(4,128)S(1)} %maximum_select_fusion.1), channel_id=1, source_target_pairs={{0,1},{1,0},{2,3},{3,2},{4,5},{5,4},{6,7},{7,6},{8,9},{9,8},{10,11... | collective-permute-start | bytes 196616 | tf_op jit(solution)/shard_map/ppermute | solution.py:18
  16.8 0.8 %collective-permute-done.2 = f32[1,4,4096]{2,1,0:T(4,128)S(1)} collective-permute-done((f32[1,4,4096]{2,1,0:T(4,128)S(1)}, f32[1,4,4096]{2,1,0:T(4,128)S(1)}, u32[]{:S(2)}, u32[]{:S(2)}) %collective-permute-start.2) | collective-permute-done | bytes 65568 | tf_op jit(solution)/shard_map/ppermute | solution.py:18
  17.9 5.6 %fusion.11 = f32[16384]{0:T(1024)S(1)} fusion(f32[256,128]{1,0:T(8,128)S(1)} %reshape_squeeze.3, s32[16384]{0:T(1024)S(1)} %get-tuple-element.38, s32[16384]{0:T(1024)S(1)} %get-tuple-element.37), kind=kOutput, calls=%fused_computation.15 | convolution fusion | flops 3231694848 | bytes 327680 | tf_op jit(solution)/shard_map/dot_general | solution.py:131
  24.7 2.4 %fusion.2 = f32[12,128]{1,0:T(8,128)S(1)} fusion(f32[12,16384]{1,0:T(8,128)S(1)} %bitcast.110, s32[16384]{0:T(1024)S(1)} %subtract_bitcast_fusion), kind=kOutput, calls=%fused_computation.5 | convolution fusion | flops 153092096 | bytes 858112 | tf_op jit(solution)/shard_map/dot_general | solution.py:142
  27.3 2.3 %collective-permute-start.3 = (f32[3,3]{1,0:T(4,128)S(1)}, f32[3,3]{1,0:T(4,128)S(1)}, u32[]{:S(2)}, u32[]{:S(2)}) collective-permute-start(f32[3,3]{1,0:T(4,128)S(1)} %slice.168), channel_id=1, source_target_pairs={{0,1},{1,2},{2,3},{3,4},{4,5},{5,6},{6,7},{7,8},{8,9},{9,10},{10,1... | collective-permute-start | bytes 116 | tf_op jit(solution)/shard_map/ppermute | solution.py:13
  30.2 4.5 %fusion = f32[256,128]{1,0:T(8,128)S(1)} fusion(f32[16384]{0:T(1024)S(1)} %get-tuple-element.22, s32[16384]{0:T(1024)S(1)} %get-tuple-element.37, pred[256,16384]{1,0:T(32,128)(4,1)S(1)} %copy-done), kind=kOutput, calls=%fused_computation.2 | convolution fusion | flops 3225419776 | bytes 4456448 | tf_op jit(solution)/shard_map/dot_general | solution.py:151
  35.4 0.7 multiply_reduce_fusion.8
  40.0 0.7 concatenate.73
  40.7 0.9 %collective-permute-start.4 = (f32[129,128]{1,0:T(8,128)S(1)}, f32[129,128]{1,0:T(8,128)S(1)}, u32[]{:S(2)}, u32[]{:S(2)}) collective-permute-start(f32[129,128]{1,0:T(8,128)S(1)} %pad_maximum_fusion.3), channel_id=1, source_target_pairs={{0,1},{1,0},{2,3},{3,2},{4,5},{5,4},{6,7},{7,6},{8,9},{9,8},{10,11... | collective-permute-start | bytes 198152 | tf_op jit(solution)/shard_map/ppermute | solution.py:18
  41.6 0.9 %collective-permute-done.4 = f32[129,128]{1,0:T(8,128)S(1)} collective-permute-done((f32[129,128]{1,0:T(8,128)S(1)}, f32[129,128]{1,0:T(8,128)S(1)}, u32[]{:S(2)}, u32[]{:S(2)}) %collective-permute-start.4) | collective-permute-done | bytes 66080 | tf_op jit(solution)/shard_map/ppermute | solution.py:18
  42.5 2.0 %collective-permute-start.5 = (f32[65,128]{1,0:T(8,128)S(1)}, f32[65,128]{1,0:T(8,128)S(1)}, u32[]{:S(2)}, u32[]{:S(2)}) collective-permute-start(f32[65,128]{1,0:T(8,128)S(1)} %pad_maximum_fusion.4), channel_id=1, source_target_pairs={{0,2},{1,3},{2,0},{3,1},{4,6},{5,7},{6,4},{7,5},{8,10},{9,11},{10,... | collective-permute-start | bytes 99848 | tf_op jit(solution)/shard_map/ppermute | solution.py:18
  44.5 2.0 %collective-permute-done.5 = f32[65,128]{1,0:T(8,128)S(1)} collective-permute-done((f32[65,128]{1,0:T(8,128)S(1)}, f32[65,128]{1,0:T(8,128)S(1)}, u32[]{:S(2)}, u32[]{:S(2)}) %collective-permute-start.5) | collective-permute-done | bytes 33312 | tf_op jit(solution)/shard_map/ppermute | solution.py:18
  46.6 2.7 %collective-permute-start.6 = (f32[65,128]{1,0:T(8,128)S(1)}, f32[65,128]{1,0:T(8,128)S(1)}, u32[]{:S(2)}, u32[]{:S(2)}) collective-permute-start(f32[65,128]{1,0:T(8,128)S(1)} %pad_maximum_fusion.5), channel_id=1, source_target_pairs={{0,16},{4,20},{8,24},{12,28},{16,0},{20,4},{24,8},{28,12},{1,17},{... | collective-permute-start | bytes 99848 | tf_op jit(solution)/shard_map/ppermute | solution.py:18
  49.2 2.3 %collective-permute-done.6 = f32[65,128]{1,0:T(8,128)S(1)} collective-permute-done((f32[65,128]{1,0:T(8,128)S(1)}, f32[65,128]{1,0:T(8,128)S(1)}, u32[]{:S(2)}, u32[]{:S(2)}) %collective-permute-start.6) | collective-permute-done | bytes 33312 | tf_op jit(solution)/shard_map/ppermute | solution.py:18
  51.5 1.6 %collective-permute-start.7 = (f32[65,128]{1,0:T(8,128)S(1)}, f32[65,128]{1,0:T(8,128)S(1)}, u32[]{:S(2)}, u32[]{:S(2)}) collective-permute-start(f32[65,128]{1,0:T(8,128)S(1)} %fusion.31), channel_id=1, source_target_pairs={{0,8},{4,12},{8,0},{12,4},{16,24},{20,28},{24,16},{28,20},{1,9},{5... | collective-permute-start | bytes 99848 | tf_op jit(solution)/shard_map/ppermute | solution.py:18
  53.1 2.4 %collective-permute-done.7 = f32[65,128]{1,0:T(8,128)S(1)} collective-permute-done((f32[65,128]{1,0:T(8,128)S(1)}, f32[65,128]{1,0:T(8,128)S(1)}, u32[]{:S(2)}, u32[]{:S(2)}) %collective-permute-start.7) | collective-permute-done | bytes 33312 | tf_op jit(solution)/shard_map/ppermute | solution.py:18
  55.5 2.1 %collective-permute-start.8 = (f32[65,128]{1,0:T(8,128)S(1)}, f32[65,128]{1,0:T(8,128)S(1)}, u32[]{:S(2)}, u32[]{:S(2)}) collective-permute-start(f32[65,128]{1,0:T(8,128)S(1)} %add.178), channel_id=1, source_target_pairs={{0,4},{4,0},{8,12},{12,8},{16,20},{20,16},{24,28},{28,24},{1,5},{5... | collective-permute-start | bytes 99848 | tf_op jit(solution)/shard_map/ppermute | solution.py:18
  57.6 1.9 %collective-permute-done.8 = f32[65,128]{1,0:T(8,128)S(1)} collective-permute-done((f32[65,128]{1,0:T(8,128)S(1)}, f32[65,128]{1,0:T(8,128)S(1)}, u32[]{:S(2)}, u32[]{:S(2)}) %collective-permute-start.8) | collective-permute-done | bytes 33312 | tf_op jit(solution)/shard_map/ppermute | solution.py:18
  62.2 0.6 multiply_reduce_fusion.3
  62.8 0.7 broadcast_in_dim.5
  63.5 1.9 %collective-permute-start.9 = (f32[1,128]{1,0:T(1,128)S(1)}, f32[1,128]{1,0:T(1,128)S(1)}, u32[]{:S(2)}, u32[]{:S(2)}) collective-permute-start(f32[1,128]{1,0:T(1,128)S(1)} %broadcast_in_dim.5), channel_id=1, source_target_pairs={{0,2},{1,3},{2,0},{3,1},{4,6},{5,7},{6,4},{7,5},{8,10},{9,11},{10,... | collective-permute-start | bytes 1544 | tf_op jit(solution)/shard_map/ppermute | solution.py:18
  65.4 1.7 %collective-permute-done.9 = f32[1,128]{1,0:T(1,128)S(1)} collective-permute-done((f32[1,128]{1,0:T(1,128)S(1)}, f32[1,128]{1,0:T(1,128)S(1)}, u32[]{:S(2)}, u32[]{:S(2)}) %collective-permute-start.9) | collective-permute-done | bytes 544 | tf_op jit(solution)/shard_map/ppermute | solution.py:18
  67.1 0.6 broadcast_add_fusion
  69.8 0.7 fusion.39
  71.1 0.7 multiply_add_fusion.3
  (82 shorter events, 5.4 us)
Async XLA Ops:
  0.6 12.4 %copy-start.10 = (f32[3,128]{1,0:T(4,128)S(1)}, f32[3,128]{1,0:T(4,128)}, u32[]{:S(2)}) copy-start(f32[3,128]{1,0:T(4,128)} %param.28) | copy-start | bytes 4612
  0.6 11.5 %copy-start.11 = (f32[5,128]{1,0:T(8,128)S(1)}, f32[5,128]{1,0:T(8,128)}, u32[]{:S(2)}) copy-start(f32[5,128]{1,0:T(8,128)} %param.27) | copy-start | bytes 7684
  0.7 11.5 %copy-start.1 = (f32[5,128,128]{2,1,0:T(8,128)S(1)}, f32[5,128,128]{2,1,0:T(8,128)}, u32[]{:S(2)}) copy-start(f32[5,128,128]{2,1,0:T(8,128)} %param.15) | copy-start | bytes 983044
  0.7 11.6 %copy-start.6 = (s32[128,128]{1,0:T(8,128)S(1)}, s32[128,128]{1,0:T(8,128)}, u32[]{:S(2)}) copy-start(s32[128,128]{1,0:T(8,128)} %param.20) | copy-start | bytes 196612
  0.7 14.8 %collective-permute-start.1 = (f32[1,2,4096]{2,1,0:T(2,128)}, f32[1,2,4096]{2,1,0:T(2,128)S(1)}, u32[]{:S(2)}, u32[]{:S(2)}) collective-permute-start(f32[1,2,4096]{2,1,0:T(2,128)} %bitcast.111), channel_id=1, source_target_pairs={{0,2},{1,3},{2,0},{3,1},{4,6},{5,7},{6,4},{7,5},{8,10},{9,11},{10,... | collective-permute-start | bytes 98312 | tf_op jit(solution)/shard_map/ppermute | solution.py:18
  3.7 9.3 %collective-permute-start = (f32[3,3]{1,0:T(4,128)}, f32[3,3]{1,0:T(4,128)S(1)}, u32[]{:S(2)}, u32[]{:S(2)}) collective-permute-start(f32[3,3]{1,0:T(4,128)} %bitcast.113), channel_id=1, source_target_pairs={{1,0},{2,1},{3,2},{4,3},{5,4},{6,5},{7,6},{8,7},{9,8},{10,9},{11,1... | collective-permute-start | bytes 116 | tf_op jit(solution)/shard_map/ppermute | solution.py:13
  8.0 7.4 %copy-start.5 = (f32[2,4096]{1,0:T(2,128)S(1)}, f32[2,4096]{1,0:T(2,128)}, u32[]{:S(2)}) copy-start(f32[2,4096]{1,0:T(2,128)} %param.29) | copy-start | bytes 98308
  8.0 8.7 %copy-start.2 = (f32[3,128,128]{2,1,0:T(8,128)S(1)}, f32[3,128,128]{2,1,0:T(8,128)}, u32[]{:S(2)}) copy-start(f32[3,128,128]{2,1,0:T(8,128)} %param.16) | copy-start | bytes 589828
  15.5 2.1 %collective-permute-start.2 = (f32[1,4,4096]{2,1,0:T(4,128)S(1)}, f32[1,4,4096]{2,1,0:T(4,128)S(1)}, u32[]{:S(2)}, u32[]{:S(2)}) collective-permute-start(f32[1,4,4096]{2,1,0:T(4,128)S(1)} %maximum_select_fusion.1), channel_id=1, source_target_pairs={{0,1},{1,0},{2,3},{3,2},{4,5},{5,4},{6,7},{7,6},{8,9},{9,8},{10,11... | collective-permute-start | bytes 196616 | tf_op jit(solution)/shard_map/ppermute | solution.py:18
  17.9 5.6 %copy-start.7 = (f32[128,128]{1,0:T(8,128)S(1)}, f32[128,128]{1,0:T(8,128)}, u32[]{:S(2)}) copy-start(f32[128,128]{1,0:T(8,128)} %param.18) | copy-start | bytes 196612
  17.9 5.6 %copy-start.8 = (f32[128,128]{1,0:T(8,128)S(1)}, f32[128,128]{1,0:T(8,128)}, u32[]{:S(2)}) copy-start(f32[128,128]{1,0:T(8,128)} %param.19) | copy-start | bytes 196612
  17.9 5.6 %copy-start.9 = (f32[128,128]{1,0:T(8,128)S(1)}, f32[128,128]{1,0:T(8,128)}, u32[]{:S(2)}) copy-start(f32[128,128]{1,0:T(8,128)} %param.17) | copy-start | bytes 196612
  17.9 5.6 %copy-start.14 = (s32[128]{0:T(128)S(1)}, s32[128]{0:T(128)}, u32[]{:S(2)}) copy-start(s32[128]{0:T(128)} %param.23) | copy-start | bytes 1540
  23.9 6.3 %copy-start = (pred[256,16384]{1,0:T(32,128)(4,1)S(1)}, pred[256,16384]{1,0:T(32,128)(4,1)}, u32[]{:S(2)}) copy-start(pred[256,16384]{1,0:T(32,128)(4,1)} %iota_compare_fusion.14) | copy-start | bytes 12582916
  27.3 8.1 %collective-permute-start.3 = (f32[3,3]{1,0:T(4,128)S(1)}, f32[3,3]{1,0:T(4,128)S(1)}, u32[]{:S(2)}, u32[]{:S(2)}) collective-permute-start(f32[3,3]{1,0:T(4,128)S(1)} %slice.168), channel_id=1, source_target_pairs={{0,1},{1,2},{2,3},{3,4},{4,5},{5,6},{6,7},{7,8},{8,9},{9,10},{10,1... | collective-permute-start | bytes 116 | tf_op jit(solution)/shard_map/ppermute | solution.py:13
  30.2 4.5 %copy-start.12 = (f32[5,128]{1,0:T(8,128)S(1)}, f32[5,128]{1,0:T(8,128)}, u32[]{:S(2)}) copy-start(f32[5,128]{1,0:T(8,128)} %param.24) | copy-start | bytes 7684
  30.2 5.2 %copy-start.13 = (f32[3,128]{1,0:T(4,128)S(1)}, f32[3,128]{1,0:T(4,128)}, u32[]{:S(2)}) copy-start(f32[3,128]{1,0:T(4,128)} %param.25) | copy-start | bytes 4612
  30.2 32.0 %copy-start.4 = (f32[2,4096]{1,0:T(2,128)S(1)}, f32[2,4096]{1,0:T(2,128)}, u32[]{:S(2)}) copy-start(f32[2,4096]{1,0:T(2,128)} %param.26) | copy-start | bytes 98308
  40.7 1.8 %collective-permute-start.4 = (f32[129,128]{1,0:T(8,128)S(1)}, f32[129,128]{1,0:T(8,128)S(1)}, u32[]{:S(2)}, u32[]{:S(2)}) collective-permute-start(f32[129,128]{1,0:T(8,128)S(1)} %pad_maximum_fusion.3), channel_id=1, source_target_pairs={{0,1},{1,0},{2,3},{3,2},{4,5},{5,4},{6,7},{7,6},{8,9},{9,8},{10,11... | collective-permute-start | bytes 198152 | tf_op jit(solution)/shard_map/ppermute | solution.py:18
  42.5 4.0 %collective-permute-start.5 = (f32[65,128]{1,0:T(8,128)S(1)}, f32[65,128]{1,0:T(8,128)S(1)}, u32[]{:S(2)}, u32[]{:S(2)}) collective-permute-start(f32[65,128]{1,0:T(8,128)S(1)} %pad_maximum_fusion.4), channel_id=1, source_target_pairs={{0,2},{1,3},{2,0},{3,1},{4,6},{5,7},{6,4},{7,5},{8,10},{9,11},{10,... | collective-permute-start | bytes 99848 | tf_op jit(solution)/shard_map/ppermute | solution.py:18
  46.6 4.9 %collective-permute-start.6 = (f32[65,128]{1,0:T(8,128)S(1)}, f32[65,128]{1,0:T(8,128)S(1)}, u32[]{:S(2)}, u32[]{:S(2)}) collective-permute-start(f32[65,128]{1,0:T(8,128)S(1)} %pad_maximum_fusion.5), channel_id=1, source_target_pairs={{0,16},{4,20},{8,24},{12,28},{16,0},{20,4},{24,8},{28,12},{1,17},{... | collective-permute-start | bytes 99848 | tf_op jit(solution)/shard_map/ppermute | solution.py:18
  51.5 4.0 %collective-permute-start.7 = (f32[65,128]{1,0:T(8,128)S(1)}, f32[65,128]{1,0:T(8,128)S(1)}, u32[]{:S(2)}, u32[]{:S(2)}) collective-permute-start(f32[65,128]{1,0:T(8,128)S(1)} %fusion.31), channel_id=1, source_target_pairs={{0,8},{4,12},{8,0},{12,4},{16,24},{20,28},{24,16},{28,20},{1,9},{5... | collective-permute-start | bytes 99848 | tf_op jit(solution)/shard_map/ppermute | solution.py:18
  55.5 4.0 %collective-permute-start.8 = (f32[65,128]{1,0:T(8,128)S(1)}, f32[65,128]{1,0:T(8,128)S(1)}, u32[]{:S(2)}, u32[]{:S(2)}) collective-permute-start(f32[65,128]{1,0:T(8,128)S(1)} %add.178), channel_id=1, source_target_pairs={{0,4},{4,0},{8,12},{12,8},{16,20},{20,16},{24,28},{28,24},{1,5},{5... | collective-permute-start | bytes 99848 | tf_op jit(solution)/shard_map/ppermute | solution.py:18
  62.8 9.6 %copy-start.3 = (f32[2,4096]{1,0:T(2,128)}, f32[2,4096]{1,0:T(2,128)S(1)}, u32[]{:S(2)}) copy-start(f32[2,4096]{1,0:T(2,128)S(1)} %get-tuple-element.21) | copy-start | bytes 98308
  63.5 3.6 %collective-permute-start.9 = (f32[1,128]{1,0:T(1,128)S(1)}, f32[1,128]{1,0:T(1,128)S(1)}, u32[]{:S(2)}, u32[]{:S(2)}) collective-permute-start(f32[1,128]{1,0:T(1,128)S(1)} %broadcast_in_dim.5), channel_id=1, source_target_pairs={{0,2},{1,3},{2,0},{3,1},{4,6},{5,7},{6,4},{7,5},{8,10},{9,11},{10,... | collective-permute-start | bytes 1544 | tf_op jit(solution)/shard_map/ppermute | solution.py:18
  67.7 2.0 %collective-permute-start.10 = (f32[1,128]{1,0:T(1,128)S(1)}, f32[1,128]{1,0:T(1,128)S(1)}, u32[]{:S(2)}, u32[]{:S(2)}) collective-permute-start(f32[1,128]{1,0:T(1,128)S(1)} %broadcast_add_fusion), channel_id=1, source_target_pairs={{0,1},{1,0},{2,3},{3,2},{4,5},{5,4},{6,7},{7,6},{8,9},{9,8},{10,11... | collective-permute-start | bytes 1544 | tf_op jit(solution)/shard_map/ppermute | solution.py:18

commit v17 on v15

--- a/solution.py
+++ b/solution.py
@@ -167,7 +167,8 @@
     new_cal_res = cal_res - step_len * q_cal
     kept = res_sq - step_len * (2.0 * res_q - step_len * q_sq)
     cal_next = jnp.broadcast_to(jnp.sum(new_cal_res * new_cal_res), (1, lane))
-    norm_next = kept + doubling_sum(cal_next, "cal")[0, 0]
+    cal_next = cal_next + exchanged(cal_next, "cal", 2)
+    norm_next = kept + (cal_next + exchanged(cal_next, "cal", 1))[0, 0]
     ratio = norm_next / norm_now
     return (
         new_src_res,

time: 72.3 us -> 73 us (level)
    add x0 -> x2, other arithmetic: none -> 1.3 us  [the longest x1 0.65 us: local(): norm_next = kept + (cal_next + exchanged(cal_next, 'cal', 1))[0, 0]]
    add x5 -> x3, other arithmetic: 1.32 us -> 0.02 us  [doubling_sum(): rows = rows + exchanged(rows, axis, distance)]
  transfers between devices with their start and end apart: 11 -> 11, of which waited for: 7 -> 7; matrix products, arithmetic and copies ran while one was open for 22% -> 21% of each run, Pallas kernels for 0% -> 0%
where the time goes in v17:
time: 73 us; the launch traced here: 72.3 us
  starting transfers between devices  18.8 us (26%)
  matrix products  14.7 us (20%)
  other arithmetic  13.1 us (18%)
  waiting for transfers between devices  12.1 us (17%)
  between operations  9.69 us (13%)
  local copies, waits for them, and re-layouts  3.94 us (5%)
    ppermute x9, starting transfers between devices, exchanged(): return lax.ppermute(block, axis, [(i, i ^ distance) for i in devices])  15.3 us
    ppermute x9, waiting for transfers between devices, exchanged(): return lax.ppermute(block, axis, [(i, i ^ distance) for i in devices])  12.1 us
    dot_general x1, matrix products, local(): lax.dot_general(cal_table, high_hot, (((0,), (0,)), ((), ())), precision=...  5.59 us
    dot_general x1, matrix products, local(): lax.dot_general(high_hot, cal_weighted, (((1,), (1,)), ((), ())), precisi...  4.49 us
    dot_general x1, other arithmetic, local(): lax.dot_general(high_hot, cal_weighted, (((1,), (1,)), ((), ())), precisi...  4.09 us
    ppermute x2, starting transfers between devices, passed_along(): return lax.ppermute(block, axis, route)  3.54 us
    dot_general x1, matrix products, local(): lax.dot_general(spread, knot_hot, (((1,), (1,)), ((), ())), precision=ONE...  2.43 us
    dot_general x1, matrix products, local(): jnp.dot(table, knot_hot, precision=ONE_HOT_PRECISION)  2.16 us
  transfers between devices with their start and end apart: 11, of which 7 were waited for; matrix products, arithmetic and copies ran while one was open for 21% of the time, Pallas kernels for 0%

profile of v17, /device:TPU:0, one launch (start us, length us, event | category | flops | bytes accessed | tf_op | source)
XLA Modules:
  0.0 72.3 jit_solution(7741178766918995989)
XLA Ops:
  0.7 3.0 %collective-permute-start.1 = (f32[1,2,4096]{2,1,0:T(2,128)}, f32[1,2,4096]{2,1,0:T(2,128)S(1)}, u32[]{:S(2)}, u32[]{:S(2)}) collective-permute-start(f32[1,2,4096]{2,1,0:T(2,128)} %bitcast.111), channel_id=1, source_target_pairs={{0,2},{1,3},{2,0},{3,1},{4,6},{5,7},{6,4},{7,5},{8,10},{9,11},{10,... | collective-permute-start | bytes 98312 | tf_op jit(solution)/shard_map/ppermute | solution.py:18
  3.7 1.3 %collective-permute-start = (f32[3,3]{1,0:T(4,128)}, f32[3,3]{1,0:T(4,128)S(1)}, u32[]{:S(2)}, u32[]{:S(2)}) collective-permute-start(f32[3,3]{1,0:T(4,128)} %bitcast.113), channel_id=1, source_target_pairs={{1,0},{2,1},{3,2},{4,3},{5,4},{6,5},{7,6},{8,7},{9,8},{10,9},{11,1... | collective-permute-start | bytes 116 | tf_op jit(solution)/shard_map/ppermute | solution.py:13
  5.0 0.7 constant_dynamic-update-slice_fusion.1
  5.7 1.4 %multiply_reduce_fusion.4 = f32[]{:T(128)} fusion(f32[2,4096]{1,0:T(2,128)} %param.26), kind=kLoop, calls=%fused_computation.82 | loop fusion | flops 16383 | bytes 32772 | tf_op jit(solution)/shard_map/reduce_sum | solution.py:153
  7.1 0.9 %add_select_fusion = (s32[16384]{0:T(1024)S(1)}, s32[16384]{0:T(1024)S(1)}) fusion(s32[128,128]{1,0:T(8,128)} %param.22, s32[128,128]{1,0:T(8,128)} %param.21), kind=kLoop, calls=%fused_computation.39 | loop fusion | flops 344064 | bytes 262144 | tf_op jit(solution)/shard_map/jit(remainder)/select_n | solution.py:129
  8.0 4.1 %iota_compare_fusion.14 = pred[256,16384]{1,0:T(32,128)(4,1)} fusion(s32[16384]{0:T(1024)S(1)} %get-tuple-element.38), kind=kLoop, calls=%fused_computation.1.clone.clone.2 | loop fusion | flops 4194304 | bytes 4259840 | tf_op jit(solution)/shard_map/dot_general | solution.py:151
  13.1 2.2 %fusion.3 = f32[12,16384]{1,0:T(8,128)S(1)} fusion(f32[12,128]{1,0:T(8,128)S(1)} %reshape.269, s32[16384]{0:T(1024)S(1)} %subtract_bitcast_fusion), kind=kOutput, calls=%fused_computation.6 | convolution fusion | flops 153092096 | bytes 858112 | tf_op jit(solution)/shard_map/dot_general | solution.py:122
  15.5 1.2 %collective-permute-start.2 = (f32[1,4,4096]{2,1,0:T(4,128)S(1)}, f32[1,4,4096]{2,1,0:T(4,128)S(1)}, u32[]{:S(2)}, u32[]{:S(2)}) collective-permute-start(f32[1,4,4096]{2,1,0:T(4,128)S(1)} %maximum_select_fusion.1), channel_id=1, source_target_pairs={{0,1},{1,0},{2,3},{3,2},{4,5},{5,4},{6,7},{7,6},{8,9},{9,8},{10,11... | collective-permute-start | bytes 196616 | tf_op jit(solution)/shard_map/ppermute | solution.py:18
  16.8 0.8 %collective-permute-done.2 = f32[1,4,4096]{2,1,0:T(4,128)S(1)} collective-permute-done((f32[1,4,4096]{2,1,0:T(4,128)S(1)}, f32[1,4,4096]{2,1,0:T(4,128)S(1)}, u32[]{:S(2)}, u32[]{:S(2)}) %collective-permute-start.2) | collective-permute-done | bytes 65568 | tf_op jit(solution)/shard_map/ppermute | solution.py:18
  17.9 5.6 %fusion.11 = f32[16384]{0:T(1024)S(1)} fusion(f32[256,128]{1,0:T(8,128)S(1)} %reshape_squeeze.3, s32[16384]{0:T(1024)S(1)} %get-tuple-element.38, s32[16384]{0:T(1024)S(1)} %get-tuple-element.37), kind=kOutput, calls=%fused_computation.15 | convolution fusion | flops 3231694848 | bytes 327680 | tf_op jit(solution)/shard_map/dot_general | solution.py:131
  24.7 2.4 %fusion.2 = f32[12,128]{1,0:T(8,128)S(1)} fusion(f32[12,16384]{1,0:T(8,128)S(1)} %bitcast.110, s32[16384]{0:T(1024)S(1)} %subtract_bitcast_fusion), kind=kOutput, calls=%fused_computation.5 | convolution fusion | flops 153092096 | bytes 858112 | tf_op jit(solution)/shard_map/dot_general | solution.py:142
  27.3 2.3 %collective-permute-start.3 = (f32[3,3]{1,0:T(4,128)S(1)}, f32[3,3]{1,0:T(4,128)S(1)}, u32[]{:S(2)}, u32[]{:S(2)}) collective-permute-start(f32[3,3]{1,0:T(4,128)S(1)} %slice.168), channel_id=1, source_target_pairs={{0,1},{1,2},{2,3},{3,4},{4,5},{5,6},{6,7},{7,8},{8,9},{9,10},{10,1... | collective-permute-start | bytes 116 | tf_op jit(solution)/shard_map/ppermute | solution.py:13
  30.2 4.5 %fusion = f32[256,128]{1,0:T(8,128)S(1)} fusion(f32[16384]{0:T(1024)S(1)} %get-tuple-element.22, s32[16384]{0:T(1024)S(1)} %get-tuple-element.37, pred[256,16384]{1,0:T(32,128)(4,1)S(1)} %copy-done), kind=kOutput, calls=%fused_computation.2 | convolution fusion | flops 3225419776 | bytes 4456448 | tf_op jit(solution)/shard_map/dot_general | solution.py:151
  35.4 0.7 multiply_reduce_fusion.8
  40.0 0.7 concatenate.73
  40.7 0.9 %collective-permute-start.4 = (f32[129,128]{1,0:T(8,128)S(1)}, f32[129,128]{1,0:T(8,128)S(1)}, u32[]{:S(2)}, u32[]{:S(2)}) collective-permute-start(f32[129,128]{1,0:T(8,128)S(1)} %pad_maximum_fusion.3), channel_id=1, source_target_pairs={{0,1},{1,0},{2,3},{3,2},{4,5},{5,4},{6,7},{7,6},{8,9},{9,8},{10,11... | collective-permute-start | bytes 198152 | tf_op jit(solution)/shard_map/ppermute | solution.py:18
  41.6 0.9 %collective-permute-done.4 = f32[129,128]{1,0:T(8,128)S(1)} collective-permute-done((f32[129,128]{1,0:T(8,128)S(1)}, f32[129,128]{1,0:T(8,128)S(1)}, u32[]{:S(2)}, u32[]{:S(2)}) %collective-permute-start.4) | collective-permute-done | bytes 66080 | tf_op jit(solution)/shard_map/ppermute | solution.py:18
  42.5 2.0 %collective-permute-start.5 = (f32[65,128]{1,0:T(8,128)S(1)}, f32[65,128]{1,0:T(8,128)S(1)}, u32[]{:S(2)}, u32[]{:S(2)}) collective-permute-start(f32[65,128]{1,0:T(8,128)S(1)} %pad_maximum_fusion.4), channel_id=1, source_target_pairs={{0,2},{1,3},{2,0},{3,1},{4,6},{5,7},{6,4},{7,5},{8,10},{9,11},{10,... | collective-permute-start | bytes 99848 | tf_op jit(solution)/shard_map/ppermute | solution.py:18
  44.5 2.0 %collective-permute-done.5 = f32[65,128]{1,0:T(8,128)S(1)} collective-permute-done((f32[65,128]{1,0:T(8,128)S(1)}, f32[65,128]{1,0:T(8,128)S(1)}, u32[]{:S(2)}, u32[]{:S(2)}) %collective-permute-start.5) | collective-permute-done | bytes 33312 | tf_op jit(solution)/shard_map/ppermute | solution.py:18
  46.6 2.0 %collective-permute-start.6 = (f32[65,128]{1,0:T(8,128)S(1)}, f32[65,128]{1,0:T(8,128)S(1)}, u32[]{:S(2)}, u32[]{:S(2)}) collective-permute-start(f32[65,128]{1,0:T(8,128)S(1)} %pad_maximum_fusion.5), channel_id=1, source_target_pairs={{0,4},{4,0},{8,12},{12,8},{16,20},{20,16},{24,28},{28,24},{1,5},{5... | collective-permute-start | bytes 99848 | tf_op jit(solution)/shard_map/ppermute | solution.py:18
  48.5 2.1 %collective-permute-done.6 = f32[65,128]{1,0:T(8,128)S(1)} collective-permute-done((f32[65,128]{1,0:T(8,128)S(1)}, f32[65,128]{1,0:T(8,128)S(1)}, u32[]{:S(2)}, u32[]{:S(2)}) %collective-permute-start.6) | collective-permute-done | bytes 33312 | tf_op jit(solution)/shard_map/ppermute | solution.py:18
  50.6 1.6 %collective-permute-start.7 = (f32[65,128]{1,0:T(8,128)S(1)}, f32[65,128]{1,0:T(8,128)S(1)}, u32[]{:S(2)}, u32[]{:S(2)}) collective-permute-start(f32[65,128]{1,0:T(8,128)S(1)} %fusion.31), channel_id=1, source_target_pairs={{0,8},{4,12},{8,0},{12,4},{16,24},{20,28},{24,16},{28,20},{1,9},{5... | collective-permute-start | bytes 99848 | tf_op jit(solution)/shard_map/ppermute | solution.py:18
  52.2 2.4 %collective-permute-done.7 = f32[65,128]{1,0:T(8,128)S(1)} collective-permute-done((f32[65,128]{1,0:T(8,128)S(1)}, f32[65,128]{1,0:T(8,128)S(1)}, u32[]{:S(2)}, u32[]{:S(2)}) %collective-permute-start.7) | collective-permute-done | bytes 33312 | tf_op jit(solution)/shard_map/ppermute | solution.py:18
  54.6 2.6 %collective-permute-start.8 = (f32[65,128]{1,0:T(8,128)S(1)}, f32[65,128]{1,0:T(8,128)S(1)}, u32[]{:S(2)}, u32[]{:S(2)}) collective-permute-start(f32[65,128]{1,0:T(8,128)S(1)} %add.178), channel_id=1, source_target_pairs={{0,16},{4,20},{8,24},{12,28},{16,0},{20,4},{24,8},{28,12},{1,17},{... | collective-permute-start | bytes 99848 | tf_op jit(solution)/shard_map/ppermute | solution.py:18
  57.2 2.3 %collective-permute-done.8 = f32[65,128]{1,0:T(8,128)S(1)} collective-permute-done((f32[65,128]{1,0:T(8,128)S(1)}, f32[65,128]{1,0:T(8,128)S(1)}, u32[]{:S(2)}, u32[]{:S(2)}) %collective-permute-start.8) | collective-permute-done | bytes 33312 | tf_op jit(solution)/shard_map/ppermute | solution.py:18
  62.1 0.6 multiply_reduce_fusion.3
  62.7 0.7 broadcast_in_dim.5
  63.4 2.0 %collective-permute-start.9 = (f32[1,128]{1,0:T(1,128)S(1)}, f32[1,128]{1,0:T(1,128)S(1)}, u32[]{:S(2)}, u32[]{:S(2)}) collective-permute-start(f32[1,128]{1,0:T(1,128)S(1)} %broadcast_in_dim.5), channel_id=1, source_target_pairs={{0,2},{1,3},{2,0},{3,1},{4,6},{5,7},{6,4},{7,5},{8,10},{9,11},{10,... | collective-permute-start | bytes 1544 | tf_op jit(solution)/shard_map/ppermute | solution.py:18
  65.4 1.6 %collective-permute-done.9 = f32[1,128]{1,0:T(1,128)S(1)} collective-permute-done((f32[1,128]{1,0:T(1,128)S(1)}, f32[1,128]{1,0:T(1,128)S(1)}, u32[]{:S(2)}, u32[]{:S(2)}) %collective-permute-start.9) | collective-permute-done | bytes 544 | tf_op jit(solution)/shard_map/ppermute | solution.py:18
  67.0 0.6 broadcast_add_fusion
  69.7 0.7 fusion.39
  71.0 0.7 multiply_add_fusion.3
  (82 shorter events, 5.4 us)
Async XLA Ops:
  0.6 12.4 %copy-start.10 = (f32[3,128]{1,0:T(4,128)S(1)}, f32[3,128]{1,0:T(4,128)}, u32[]{:S(2)}) copy-start(f32[3,128]{1,0:T(4,128)} %param.28) | copy-start | bytes 4612
  0.6 11.5 %copy-start.11 = (f32[5,128]{1,0:T(8,128)S(1)}, f32[5,128]{1,0:T(8,128)}, u32[]{:S(2)}) copy-start(f32[5,128]{1,0:T(8,128)} %param.27) | copy-start | bytes 7684
  0.7 11.5 %copy-start.1 = (f32[5,128,128]{2,1,0:T(8,128)S(1)}, f32[5,128,128]{2,1,0:T(8,128)}, u32[]{:S(2)}) copy-start(f32[5,128,128]{2,1,0:T(8,128)} %param.15) | copy-start | bytes 983044
  0.7 11.6 %copy-start.6 = (s32[128,128]{1,0:T(8,128)S(1)}, s32[128,128]{1,0:T(8,128)}, u32[]{:S(2)}) copy-start(s32[128,128]{1,0:T(8,128)} %param.20) | copy-start | bytes 196612
  0.7 14.8 %collective-permute-start.1 = (f32[1,2,4096]{2,1,0:T(2,128)}, f32[1,2,4096]{2,1,0:T(2,128)S(1)}, u32[]{:S(2)}, u32[]{:S(2)}) collective-permute-start(f32[1,2,4096]{2,1,0:T(2,128)} %bitcast.111), channel_id=1, source_target_pairs={{0,2},{1,3},{2,0},{3,1},{4,6},{5,7},{6,4},{7,5},{8,10},{9,11},{10,... | collective-permute-start | bytes 98312 | tf_op jit(solution)/shard_map/ppermute | solution.py:18
  3.7 9.3 %collective-permute-start = (f32[3,3]{1,0:T(4,128)}, f32[3,3]{1,0:T(4,128)S(1)}, u32[]{:S(2)}, u32[]{:S(2)}) collective-permute-start(f32[3,3]{1,0:T(4,128)} %bitcast.113), channel_id=1, source_target_pairs={{1,0},{2,1},{3,2},{4,3},{5,4},{6,5},{7,6},{8,7},{9,8},{10,9},{11,1... | collective-permute-start | bytes 116 | tf_op jit(solution)/shard_map/ppermute | solution.py:13
  8.0 7.4 %copy-start.5 = (f32[2,4096]{1,0:T(2,128)S(1)}, f32[2,4096]{1,0:T(2,128)}, u32[]{:S(2)}) copy-start(f32[2,4096]{1,0:T(2,128)} %param.29) | copy-start | bytes 98308
  8.0 8.7 %copy-start.2 = (f32[3,128,128]{2,1,0:T(8,128)S(1)}, f32[3,128,128]{2,1,0:T(8,128)}, u32[]{:S(2)}) copy-start(f32[3,128,128]{2,1,0:T(8,128)} %param.16) | copy-start | bytes 589828
  15.5 2.1 %collective-permute-start.2 = (f32[1,4,4096]{2,1,0:T(4,128)S(1)}, f32[1,4,4096]{2,1,0:T(4,128)S(1)}, u32[]{:S(2)}, u32[]{:S(2)}) collective-permute-start(f32[1,4,4096]{2,1,0:T(4,128)S(1)} %maximum_select_fusion.1), channel_id=1, source_target_pairs={{0,1},{1,0},{2,3},{3,2},{4,5},{5,4},{6,7},{7,6},{8,9},{9,8},{10,11... | collective-permute-start | bytes 196616 | tf_op jit(solution)/shard_map/ppermute | solution.py:18
  17.9 5.6 %copy-start.7 = (f32[128,128]{1,0:T(8,128)S(1)}, f32[128,128]{1,0:T(8,128)}, u32[]{:S(2)}) copy-start(f32[128,128]{1,0:T(8,128)} %param.18) | copy-start | bytes 196612
  17.9 5.6 %copy-start.8 = (f32[128,128]{1,0:T(8,128)S(1)}, f32[128,128]{1,0:T(8,128)}, u32[]{:S(2)}) copy-start(f32[128,128]{1,0:T(8,128)} %param.19) | copy-start | bytes 196612
  17.9 5.6 %copy-start.9 = (f32[128,128]{1,0:T(8,128)S(1)}, f32[128,128]{1,0:T(8,128)}, u32[]{:S(2)}) copy-start(f32[128,128]{1,0:T(8,128)} %param.17) | copy-start | bytes 196612
  17.9 5.6 %copy-start.14 = (s32[128]{0:T(128)S(1)}, s32[128]{0:T(128)}, u32[]{:S(2)}) copy-start(s32[128]{0:T(128)} %param.23) | copy-start | bytes 1540
  23.9 6.3 %copy-start = (pred[256,16384]{1,0:T(32,128)(4,1)S(1)}, pred[256,16384]{1,0:T(32,128)(4,1)}, u32[]{:S(2)}) copy-start(pred[256,16384]{1,0:T(32,128)(4,1)} %iota_compare_fusion.14) | copy-start | bytes 12582916
  27.3 8.1 %collective-permute-start.3 = (f32[3,3]{1,0:T(4,128)S(1)}, f32[3,3]{1,0:T(4,128)S(1)}, u32[]{:S(2)}, u32[]{:S(2)}) collective-permute-start(f32[3,3]{1,0:T(4,128)S(1)} %slice.168), channel_id=1, source_target_pairs={{0,1},{1,2},{2,3},{3,4},{4,5},{5,6},{6,7},{7,8},{8,9},{9,10},{10,1... | collective-permute-start | bytes 116 | tf_op jit(solution)/shard_map/ppermute | solution.py:13
  30.2 4.5 %copy-start.12 = (f32[5,128]{1,0:T(8,128)S(1)}, f32[5,128]{1,0:T(8,128)}, u32[]{:S(2)}) copy-start(f32[5,128]{1,0:T(8,128)} %param.24) | copy-start | bytes 7684
  30.2 5.2 %copy-start.13 = (f32[3,128]{1,0:T(4,128)S(1)}, f32[3,128]{1,0:T(4,128)}, u32[]{:S(2)}) copy-start(f32[3,128]{1,0:T(4,128)} %param.25) | copy-start | bytes 4612
  30.2 31.9 %copy-start.4 = (f32[2,4096]{1,0:T(2,128)S(1)}, f32[2,4096]{1,0:T(2,128)}, u32[]{:S(2)}) copy-start(f32[2,4096]{1,0:T(2,128)} %param.26) | copy-start | bytes 98308
  40.7 1.8 %collective-permute-start.4 = (f32[129,128]{1,0:T(8,128)S(1)}, f32[129,128]{1,0:T(8,128)S(1)}, u32[]{:S(2)}, u32[]{:S(2)}) collective-permute-start(f32[129,128]{1,0:T(8,128)S(1)} %pad_maximum_fusion.3), channel_id=1, source_target_pairs={{0,1},{1,0},{2,3},{3,2},{4,5},{5,4},{6,7},{7,6},{8,9},{9,8},{10,11... | collective-permute-start | bytes 198152 | tf_op jit(solution)/shard_map/ppermute | solution.py:18
  42.5 4.0 %collective-permute-start.5 = (f32[65,128]{1,0:T(8,128)S(1)}, f32[65,128]{1,0:T(8,128)S(1)}, u32[]{:S(2)}, u32[]{:S(2)}) collective-permute-start(f32[65,128]{1,0:T(8,128)S(1)} %pad_maximum_fusion.4), channel_id=1, source_target_pairs={{0,2},{1,3},{2,0},{3,1},{4,6},{5,7},{6,4},{7,5},{8,10},{9,11},{10,... | collective-permute-start | bytes 99848 | tf_op jit(solution)/shard_map/ppermute | solution.py:18
  46.6 4.0 %collective-permute-start.6 = (f32[65,128]{1,0:T(8,128)S(1)}, f32[65,128]{1,0:T(8,128)S(1)}, u32[]{:S(2)}, u32[]{:S(2)}) collective-permute-start(f32[65,128]{1,0:T(8,128)S(1)} %pad_maximum_fusion.5), channel_id=1, source_target_pairs={{0,4},{4,0},{8,12},{12,8},{16,20},{20,16},{24,28},{28,24},{1,5},{5... | collective-permute-start | bytes 99848 | tf_op jit(solution)/shard_map/ppermute | solution.py:18
  50.6 4.0 %collective-permute-start.7 = (f32[65,128]{1,0:T(8,128)S(1)}, f32[65,128]{1,0:T(8,128)S(1)}, u32[]{:S(2)}, u32[]{:S(2)}) collective-permute-start(f32[65,128]{1,0:T(8,128)S(1)} %fusion.31), channel_id=1, source_target_pairs={{0,8},{4,12},{8,0},{12,4},{16,24},{20,28},{24,16},{28,20},{1,9},{5... | collective-permute-start | bytes 99848 | tf_op jit(solution)/shard_map/ppermute | solution.py:18
  54.6 4.9 %collective-permute-start.8 = (f32[65,128]{1,0:T(8,128)S(1)}, f32[65,128]{1,0:T(8,128)S(1)}, u32[]{:S(2)}, u32[]{:S(2)}) collective-permute-start(f32[65,128]{1,0:T(8,128)S(1)} %add.178), channel_id=1, source_target_pairs={{0,16},{4,20},{8,24},{12,28},{16,0},{20,4},{24,8},{28,12},{1,17},{... | collective-permute-start | bytes 99848 | tf_op jit(solution)/shard_map/ppermute | solution.py:18
  62.7 9.6 %copy-start.3 = (f32[2,4096]{1,0:T(2,128)}, f32[2,4096]{1,0:T(2,128)S(1)}, u32[]{:S(2)}) copy-start(f32[2,4096]{1,0:T(2,128)S(1)} %get-tuple-element.21) | copy-start | bytes 98308
  63.4 3.6 %collective-permute-start.9 = (f32[1,128]{1,0:T(1,128)S(1)}, f32[1,128]{1,0:T(1,128)S(1)}, u32[]{:S(2)}, u32[]{:S(2)}) collective-permute-start(f32[1,128]{1,0:T(1,128)S(1)} %broadcast_in_dim.5), channel_id=1, source_target_pairs={{0,2},{1,3},{2,0},{3,1},{4,6},{5,7},{6,4},{7,5},{8,10},{9,11},{10,... | collective-permute-start | bytes 1544 | tf_op jit(solution)/shard_map/ppermute | solution.py:18
  67.7 2.0 %collective-permute-start.10 = (f32[1,128]{1,0:T(1,128)S(1)}, f32[1,128]{1,0:T(1,128)S(1)}, u32[]{:S(2)}, u32[]{:S(2)}) collective-permute-start(f32[1,128]{1,0:T(1,128)S(1)} %broadcast_add_fusion), channel_id=1, source_target_pairs={{0,1},{1,0},{2,3},{3,2},{4,5},{5,4},{6,7},{7,6},{8,9},{9,8},{10,11... | collective-permute-start | bytes 1544 | tf_op jit(solution)/shard_map/ppermute | solution.py:18

commit v18 on v15

--- a/solution.py
+++ b/solution.py
@@ -31,9 +31,13 @@
         upper = (me // distance) % 2
         keep = lax.dynamic_slice_in_dim(rows, upper * half, half, 0)
         send = lax.dynamic_slice_in_dim(rows, (1 - upper) * half, half, 0)
-        got = exchanged(jnp.concatenate([send, extra], axis=0), axis, distance)
-        rows = keep + got[:half]
-        extra = extra + got[half:]
+        if distance == 1:
+            rows = keep + exchanged(send, axis, distance)
+            extra = extra + exchanged(extra, axis, distance)
+        else:
+            got = exchanged(jnp.concatenate([send, extra], axis=0), axis, distance)
+            rows = keep + got[:half]
+            extra = extra + got[half:]
         distance *= 2
     return rows, extra
 

time: 72.3 us -> 72.5 us (level)
    ppermute x9 -> x10, starting transfers between devices: 15.3 us -> 15.6 us  [exchanged(): return lax.ppermute(block, axis, [(i, i ^ distance) for i in devices])]
    ppermute x9 -> x10, waiting for transfers between devices: 11.6 us -> 11.5 us  [exchanged(): return lax.ppermute(block, axis, [(i, i ^ distance) for i in devices])]
  transfers between devices with their start and end apart: 11 -> 12, of which waited for: 7 -> 8; matrix products, arithmetic and copies ran while one was open for 22% -> 22% of each run, Pallas kernels for 0% -> 0%
where the time goes in v18:
time: 72.5 us; the launch traced here: 72.1 us
  starting transfers between devices  19.1 us (26%)
  matrix products  14.7 us (20%)
  other arithmetic  13.1 us (18%)
  waiting for transfers between devices  11.6 us (16%)
  between operations  9.69 us (13%)
  local copies, waits for them, and re-layouts  3.93 us (5%)
    ppermute x10, starting transfers between devices, exchanged(): return lax.ppermute(block, axis, [(i, i ^ distance) for i in devices])  15.6 us
    ppermute x10, waiting for transfers between devices, exchanged(): return lax.ppermute(block, axis, [(i, i ^ distance) for i in devices])  11.5 us
    dot_general x1, matrix products, local(): lax.dot_general(cal_table, high_hot, (((0,), (0,)), ((), ())), precision=...  5.58 us
    dot_general x1, matrix products, local(): lax.dot_general(high_hot, cal_weighted, (((1,), (1,)), ((), ())), precisi...  4.49 us
    dot_general x1, other arithmetic, local(): lax.dot_general(high_hot, cal_weighted, (((1,), (1,)), ((), ())), precisi...  4.09 us
    ppermute x2, starting transfers between devices, passed_along(): return lax.ppermute(block, axis, route)  3.53 us
    dot_general x1, matrix products, local(): lax.dot_general(spread, knot_hot, (((1,), (1,)), ((), ())), precision=ONE...  2.43 us
    dot_general x1, matrix products, local(): jnp.dot(table, knot_hot, precision=ONE_HOT_PRECISION)  2.16 us
  transfers between devices with their start and end apart: 12, of which 8 were waited for; matrix products, arithmetic and copies ran while one was open for 22% of the time, Pallas kernels for 0%

profile of v18, /device:TPU:0, one launch (start us, length us, event | category | flops | bytes accessed | tf_op | source)
XLA Modules:
  0.0 72.1 jit_solution(10575328541858511570)
XLA Ops:
  0.7 3.0 %collective-permute-start.1 = (f32[1,2,4096]{2,1,0:T(2,128)}, f32[1,2,4096]{2,1,0:T(2,128)S(1)}, u32[]{:S(2)}, u32[]{:S(2)}) collective-permute-start(f32[1,2,4096]{2,1,0:T(2,128)} %bitcast.111), channel_id=1, source_target_pairs={{0,2},{1,3},{2,0},{3,1},{4,6},{5,7},{6,4},{7,5},{8,10},{9,11},{10,... | collective-permute-start | bytes 98312 | tf_op jit(solution)/shard_map/ppermute | solution.py:18
  3.7 1.3 %collective-permute-start = (f32[3,3]{1,0:T(4,128)}, f32[3,3]{1,0:T(4,128)S(1)}, u32[]{:S(2)}, u32[]{:S(2)}) collective-permute-start(f32[3,3]{1,0:T(4,128)} %bitcast.113), channel_id=1, source_target_pairs={{1,0},{2,1},{3,2},{4,3},{5,4},{6,5},{7,6},{8,7},{9,8},{10,9},{11,1... | collective-permute-start | bytes 116 | tf_op jit(solution)/shard_map/ppermute | solution.py:13
  5.0 0.7 constant_dynamic-update-slice_fusion.1
  5.7 1.4 %multiply_reduce_fusion.4 = f32[]{:T(128)} fusion(f32[2,4096]{1,0:T(2,128)} %param.26), kind=kLoop, calls=%fused_computation.81 | loop fusion | flops 16383 | bytes 32772 | tf_op jit(solution)/shard_map/reduce_sum | solution.py:157
  7.1 0.9 %add_select_fusion = (s32[16384]{0:T(1024)S(1)}, s32[16384]{0:T(1024)S(1)}) fusion(s32[128,128]{1,0:T(8,128)} %param.22, s32[128,128]{1,0:T(8,128)} %param.21), kind=kLoop, calls=%fused_computation.39 | loop fusion | flops 344064 | bytes 262144 | tf_op jit(solution)/shard_map/jit(remainder)/select_n | solution.py:133
  8.0 4.1 %iota_compare_fusion.14 = pred[256,16384]{1,0:T(32,128)(4,1)} fusion(s32[16384]{0:T(1024)S(1)} %get-tuple-element.38), kind=kLoop, calls=%fused_computation.1.clone.clone.2 | loop fusion | flops 4194304 | bytes 4259840 | tf_op jit(solution)/shard_map/dot_general | solution.py:155
  13.1 2.2 %fusion.3 = f32[12,16384]{1,0:T(8,128)S(1)} fusion(f32[12,128]{1,0:T(8,128)S(1)} %reshape.269, s32[16384]{0:T(1024)S(1)} %subtract_bitcast_fusion), kind=kOutput, calls=%fused_computation.6 | convolution fusion | flops 153092096 | bytes 858112 | tf_op jit(solution)/shard_map/dot_general | solution.py:126
  15.5 1.2 %collective-permute-start.2 = (f32[1,4,4096]{2,1,0:T(4,128)S(1)}, f32[1,4,4096]{2,1,0:T(4,128)S(1)}, u32[]{:S(2)}, u32[]{:S(2)}) collective-permute-start(f32[1,4,4096]{2,1,0:T(4,128)S(1)} %maximum_select_fusion.1), channel_id=1, source_target_pairs={{0,1},{1,0},{2,3},{3,2},{4,5},{5,4},{6,7},{7,6},{8,9},{9,8},{10,11... | collective-permute-start | bytes 196616 | tf_op jit(solution)/shard_map/ppermute | solution.py:18
  16.8 0.8 %collective-permute-done.2 = f32[1,4,4096]{2,1,0:T(4,128)S(1)} collective-permute-done((f32[1,4,4096]{2,1,0:T(4,128)S(1)}, f32[1,4,4096]{2,1,0:T(4,128)S(1)}, u32[]{:S(2)}, u32[]{:S(2)}) %collective-permute-start.2) | collective-permute-done | bytes 65568 | tf_op jit(solution)/shard_map/ppermute | solution.py:18
  17.9 5.6 %fusion.11 = f32[16384]{0:T(1024)S(1)} fusion(f32[256,128]{1,0:T(8,128)S(1)} %reshape_squeeze.3, s32[16384]{0:T(1024)S(1)} %get-tuple-element.38, s32[16384]{0:T(1024)S(1)} %get-tuple-element.37), kind=kOutput, calls=%fused_computation.15 | convolution fusion | flops 3231694848 | bytes 327680 | tf_op jit(solution)/shard_map/dot_general | solution.py:135
  24.7 2.4 %fusion.2 = f32[12,128]{1,0:T(8,128)S(1)} fusion(f32[12,16384]{1,0:T(8,128)S(1)} %bitcast.110, s32[16384]{0:T(1024)S(1)} %subtract_bitcast_fusion), kind=kOutput, calls=%fused_computation.5 | convolution fusion | flops 153092096 | bytes 858112 | tf_op jit(solution)/shard_map/dot_general | solution.py:146
  27.3 2.3 %collective-permute-start.4 = (f32[3,3]{1,0:T(4,128)S(1)}, f32[3,3]{1,0:T(4,128)S(1)}, u32[]{:S(2)}, u32[]{:S(2)}) collective-permute-start(f32[3,3]{1,0:T(4,128)S(1)} %slice.160), channel_id=1, source_target_pairs={{0,1},{1,2},{2,3},{3,4},{4,5},{5,6},{6,7},{7,8},{8,9},{9,10},{10,1... | collective-permute-start | bytes 116 | tf_op jit(solution)/shard_map/ppermute | solution.py:13
  30.2 4.5 %fusion = f32[256,128]{1,0:T(8,128)S(1)} fusion(f32[16384]{0:T(1024)S(1)} %get-tuple-element.22, s32[16384]{0:T(1024)S(1)} %get-tuple-element.37, pred[256,16384]{1,0:T(32,128)(4,1)S(1)} %copy-done), kind=kOutput, calls=%fused_computation.2 | convolution fusion | flops 3225419776 | bytes 4456448 | tf_op jit(solution)/shard_map/dot_general | solution.py:155
  35.4 0.7 multiply_reduce_fusion.8
  40.0 0.7 concatenate.70
  40.7 0.8 %collective-permute-start.5 = (f32[1,128]{1,0:T(1,128)S(1)}, f32[1,128]{1,0:T(1,128)S(1)}, u32[]{:S(2)}, u32[]{:S(2)}) collective-permute-start(f32[1,128]{1,0:T(1,128)S(1)} %bitcast.115), channel_id=1, source_target_pairs={{0,1},{1,0},{2,3},{3,2},{4,5},{5,4},{6,7},{7,6},{8,9},{9,8},{10,11... | collective-permute-start | bytes 1544 | tf_op jit(solution)/shard_map/ppermute | solution.py:18
  41.6 0.7 collective-permute-done.5
  42.8 2.0 %collective-permute-start.6 = (f32[65,128]{1,0:T(8,128)S(1)}, f32[65,128]{1,0:T(8,128)S(1)}, u32[]{:S(2)}, u32[]{:S(2)}) collective-permute-start(f32[65,128]{1,0:T(8,128)S(1)} %pad_maximum_fusion.3), channel_id=1, source_target_pairs={{0,2},{1,3},{2,0},{3,1},{4,6},{5,7},{6,4},{7,5},{8,10},{9,11},{10,... | collective-permute-start | bytes 99848 | tf_op jit(solution)/shard_map/ppermute | solution.py:18
  44.8 2.0 %collective-permute-done.6 = f32[65,128]{1,0:T(8,128)S(1)} collective-permute-done((f32[65,128]{1,0:T(8,128)S(1)}, f32[65,128]{1,0:T(8,128)S(1)}, u32[]{:S(2)}, u32[]{:S(2)}) %collective-permute-start.6) | collective-permute-done | bytes 33312 | tf_op jit(solution)/shard_map/ppermute | solution.py:18
  46.8 1.9 %collective-permute-start.7 = (f32[65,128]{1,0:T(8,128)S(1)}, f32[65,128]{1,0:T(8,128)S(1)}, u32[]{:S(2)}, u32[]{:S(2)}) collective-permute-start(f32[65,128]{1,0:T(8,128)S(1)} %pad_maximum_fusion.4), channel_id=1, source_target_pairs={{0,4},{4,0},{8,12},{12,8},{16,20},{20,16},{24,28},{28,24},{1,5},{5... | collective-permute-start | bytes 99848 | tf_op jit(solution)/shard_map/ppermute | solution.py:18
  48.7 2.1 %collective-permute-done.7 = f32[65,128]{1,0:T(8,128)S(1)} collective-permute-done((f32[65,128]{1,0:T(8,128)S(1)}, f32[65,128]{1,0:T(8,128)S(1)}, u32[]{:S(2)}, u32[]{:S(2)}) %collective-permute-start.7) | collective-permute-done | bytes 33312 | tf_op jit(solution)/shard_map/ppermute | solution.py:18
  50.9 1.6 %collective-permute-start.8 = (f32[65,128]{1,0:T(8,128)S(1)}, f32[65,128]{1,0:T(8,128)S(1)}, u32[]{:S(2)}, u32[]{:S(2)}) collective-permute-start(f32[65,128]{1,0:T(8,128)S(1)} %fusion.31), channel_id=1, source_target_pairs={{0,8},{4,12},{8,0},{12,4},{16,24},{20,28},{24,16},{28,20},{1,9},{5... | collective-permute-start | bytes 99848 | tf_op jit(solution)/shard_map/ppermute | solution.py:18
  52.5 2.4 %collective-permute-done.8 = f32[65,128]{1,0:T(8,128)S(1)} collective-permute-done((f32[65,128]{1,0:T(8,128)S(1)}, f32[65,128]{1,0:T(8,128)S(1)}, u32[]{:S(2)}, u32[]{:S(2)}) %collective-permute-start.8) | collective-permute-done | bytes 33312 | tf_op jit(solution)/shard_map/ppermute | solution.py:18
  54.8 3.0 %collective-permute-start.9 = (f32[65,128]{1,0:T(8,128)S(1)}, f32[65,128]{1,0:T(8,128)S(1)}, u32[]{:S(2)}, u32[]{:S(2)}) collective-permute-start(f32[65,128]{1,0:T(8,128)S(1)} %add.178), channel_id=1, source_target_pairs={{0,16},{4,20},{8,24},{12,28},{16,0},{20,4},{24,8},{28,12},{1,17},{... | collective-permute-start | bytes 99848 | tf_op jit(solution)/shard_map/ppermute | solution.py:18
  57.8 1.9 %collective-permute-done.9 = f32[65,128]{1,0:T(8,128)S(1)} collective-permute-done((f32[65,128]{1,0:T(8,128)S(1)}, f32[65,128]{1,0:T(8,128)S(1)}, u32[]{:S(2)}, u32[]{:S(2)}) %collective-permute-start.9) | collective-permute-done | bytes 33312 | tf_op jit(solution)/shard_map/ppermute | solution.py:18
  62.4 0.6 multiply_reduce_fusion.3
  63.0 0.7 broadcast_in_dim.5
  63.8 1.1 %collective-permute-done.10 = f32[1,128]{1,0:T(1,128)S(1)} collective-permute-done((f32[1,128]{1,0:T(1,128)S(1)}, f32[1,128]{1,0:T(1,128)S(1)}, u32[]{:S(2)}, u32[]{:S(2)}) %collective-permute-start.10) | collective-permute-done | bytes 544 | tf_op jit(solution)/shard_map/ppermute | solution.py:18
  64.9 0.6 broadcast_add_fusion
  65.5 2.0 %collective-permute-start.11 = (f32[1,128]{1,0:T(1,128)S(1)}, f32[1,128]{1,0:T(1,128)S(1)}, u32[]{:S(2)}, u32[]{:S(2)}) collective-permute-start(f32[1,128]{1,0:T(1,128)S(1)} %broadcast_add_fusion), channel_id=1, source_target_pairs={{0,2},{1,3},{2,0},{3,1},{4,6},{5,7},{6,4},{7,5},{8,10},{9,11},{10,... | collective-permute-start | bytes 1544 | tf_op jit(solution)/shard_map/ppermute | solution.py:18
  69.5 0.7 fusion.39
  70.8 0.7 multiply_add_fusion.3
  (83 shorter events, 5.9 us)
Async XLA Ops:
  0.6 12.4 %copy-start.10 = (f32[3,128]{1,0:T(4,128)S(1)}, f32[3,128]{1,0:T(4,128)}, u32[]{:S(2)}) copy-start(f32[3,128]{1,0:T(4,128)} %param.28) | copy-start | bytes 4612
  0.6 11.5 %copy-start.11 = (f32[5,128]{1,0:T(8,128)S(1)}, f32[5,128]{1,0:T(8,128)}, u32[]{:S(2)}) copy-start(f32[5,128]{1,0:T(8,128)} %param.27) | copy-start | bytes 7684
  0.7 11.5 %copy-start.1 = (f32[5,128,128]{2,1,0:T(8,128)S(1)}, f32[5,128,128]{2,1,0:T(8,128)}, u32[]{:S(2)}) copy-start(f32[5,128,128]{2,1,0:T(8,128)} %param.15) | copy-start | bytes 983044
  0.7 11.6 %copy-start.6 = (s32[128,128]{1,0:T(8,128)S(1)}, s32[128,128]{1,0:T(8,128)}, u32[]{:S(2)}) copy-start(s32[128,128]{1,0:T(8,128)} %param.20) | copy-start | bytes 196612
  0.7 14.8 %collective-permute-start.1 = (f32[1,2,4096]{2,1,0:T(2,128)}, f32[1,2,4096]{2,1,0:T(2,128)S(1)}, u32[]{:S(2)}, u32[]{:S(2)}) collective-permute-start(f32[1,2,4096]{2,1,0:T(2,128)} %bitcast.111), channel_id=1, source_target_pairs={{0,2},{1,3},{2,0},{3,1},{4,6},{5,7},{6,4},{7,5},{8,10},{9,11},{10,... | collective-permute-start | bytes 98312 | tf_op jit(solution)/shard_map/ppermute | solution.py:18
  3.7 9.3 %collective-permute-start = (f32[3,3]{1,0:T(4,128)}, f32[3,3]{1,0:T(4,128)S(1)}, u32[]{:S(2)}, u32[]{:S(2)}) collective-permute-start(f32[3,3]{1,0:T(4,128)} %bitcast.113), channel_id=1, source_target_pairs={{1,0},{2,1},{3,2},{4,3},{5,4},{6,5},{7,6},{8,7},{9,8},{10,9},{11,1... | collective-permute-start | bytes 116 | tf_op jit(solution)/shard_map/ppermute | solution.py:13
  8.0 7.4 %copy-start.5 = (f32[2,4096]{1,0:T(2,128)S(1)}, f32[2,4096]{1,0:T(2,128)}, u32[]{:S(2)}) copy-start(f32[2,4096]{1,0:T(2,128)} %param.29) | copy-start | bytes 98308
  8.0 8.7 %copy-start.2 = (f32[3,128,128]{2,1,0:T(8,128)S(1)}, f32[3,128,128]{2,1,0:T(8,128)}, u32[]{:S(2)}) copy-start(f32[3,128,128]{2,1,0:T(8,128)} %param.16) | copy-start | bytes 589828
  15.5 2.1 %collective-permute-start.2 = (f32[1,4,4096]{2,1,0:T(4,128)S(1)}, f32[1,4,4096]{2,1,0:T(4,128)S(1)}, u32[]{:S(2)}, u32[]{:S(2)}) collective-permute-start(f32[1,4,4096]{2,1,0:T(4,128)S(1)} %maximum_select_fusion.1), channel_id=1, source_target_pairs={{0,1},{1,0},{2,3},{3,2},{4,5},{5,4},{6,7},{7,6},{8,9},{9,8},{10,11... | collective-permute-start | bytes 196616 | tf_op jit(solution)/shard_map/ppermute | solution.py:18
  17.9 5.6 %copy-start.7 = (f32[128,128]{1,0:T(8,128)S(1)}, f32[128,128]{1,0:T(8,128)}, u32[]{:S(2)}) copy-start(f32[128,128]{1,0:T(8,128)} %param.18) | copy-start | bytes 196612
  17.9 5.6 %copy-start.8 = (f32[128,128]{1,0:T(8,128)S(1)}, f32[128,128]{1,0:T(8,128)}, u32[]{:S(2)}) copy-start(f32[128,128]{1,0:T(8,128)} %param.19) | copy-start | bytes 196612
  17.9 5.6 %copy-start.9 = (f32[128,128]{1,0:T(8,128)S(1)}, f32[128,128]{1,0:T(8,128)}, u32[]{:S(2)}) copy-start(f32[128,128]{1,0:T(8,128)} %param.17) | copy-start | bytes 196612
  17.9 5.6 %copy-start.14 = (s32[128]{0:T(128)S(1)}, s32[128]{0:T(128)}, u32[]{:S(2)}) copy-start(s32[128]{0:T(128)} %param.23) | copy-start | bytes 1540
  23.9 6.3 %copy-start = (pred[256,16384]{1,0:T(32,128)(4,1)S(1)}, pred[256,16384]{1,0:T(32,128)(4,1)}, u32[]{:S(2)}) copy-start(pred[256,16384]{1,0:T(32,128)(4,1)} %iota_compare_fusion.14) | copy-start | bytes 12582916
  27.3 8.1 %collective-permute-start.4 = (f32[3,3]{1,0:T(4,128)S(1)}, f32[3,3]{1,0:T(4,128)S(1)}, u32[]{:S(2)}, u32[]{:S(2)}) collective-permute-start(f32[3,3]{1,0:T(4,128)S(1)} %slice.160), channel_id=1, source_target_pairs={{0,1},{1,2},{2,3},{3,4},{4,5},{5,6},{6,7},{7,8},{8,9},{9,10},{10,1... | collective-permute-start | bytes 116 | tf_op jit(solution)/shard_map/ppermute | solution.py:13
  30.2 4.5 %copy-start.12 = (f32[5,128]{1,0:T(8,128)S(1)}, f32[5,128]{1,0:T(8,128)}, u32[]{:S(2)}) copy-start(f32[5,128]{1,0:T(8,128)} %param.24) | copy-start | bytes 7684
  30.2 5.2 %copy-start.13 = (f32[3,128]{1,0:T(4,128)S(1)}, f32[3,128]{1,0:T(4,128)}, u32[]{:S(2)}) copy-start(f32[3,128]{1,0:T(4,128)} %param.25) | copy-start | bytes 4612
  30.2 32.2 %copy-start.4 = (f32[2,4096]{1,0:T(2,128)S(1)}, f32[2,4096]{1,0:T(2,128)}, u32[]{:S(2)}) copy-start(f32[2,4096]{1,0:T(2,128)} %param.26) | copy-start | bytes 98308
  40.7 1.6 %collective-permute-start.5 = (f32[1,128]{1,0:T(1,128)S(1)}, f32[1,128]{1,0:T(1,128)S(1)}, u32[]{:S(2)}, u32[]{:S(2)}) collective-permute-start(f32[1,128]{1,0:T(1,128)S(1)} %bitcast.115), channel_id=1, source_target_pairs={{0,1},{1,0},{2,3},{3,2},{4,5},{5,4},{6,7},{7,6},{8,9},{9,8},{10,11... | collective-permute-start | bytes 1544 | tf_op jit(solution)/shard_map/ppermute | solution.py:18
  41.5 1.3 %collective-permute-start.3 = (f32[128,128]{1,0:T(8,128)S(1)}, f32[128,128]{1,0:T(8,128)S(1)}, u32[]{:S(2)}, u32[]{:S(2)}) collective-permute-start(f32[128,128]{1,0:T(8,128)S(1)} %constant_dynamic-slice_fusion.1), channel_id=1, source_target_pairs={{0,1},{1,0},{2,3},{3,2},{4,5},{5,4},{6,7},{7,6},{8,9},{9,8},{10,11... | collective-permute-start | bytes 196616 | tf_op jit(solution)/shard_map/ppermute | solution.py:18
  42.8 4.0 %collective-permute-start.6 = (f32[65,128]{1,0:T(8,128)S(1)}, f32[65,128]{1,0:T(8,128)S(1)}, u32[]{:S(2)}, u32[]{:S(2)}) collective-permute-start(f32[65,128]{1,0:T(8,128)S(1)} %pad_maximum_fusion.3), channel_id=1, source_target_pairs={{0,2},{1,3},{2,0},{3,1},{4,6},{5,7},{6,4},{7,5},{8,10},{9,11},{10,... | collective-permute-start | bytes 99848 | tf_op jit(solution)/shard_map/ppermute | solution.py:18
  46.8 4.0 %collective-permute-start.7 = (f32[65,128]{1,0:T(8,128)S(1)}, f32[65,128]{1,0:T(8,128)S(1)}, u32[]{:S(2)}, u32[]{:S(2)}) collective-permute-start(f32[65,128]{1,0:T(8,128)S(1)} %pad_maximum_fusion.4), channel_id=1, source_target_pairs={{0,4},{4,0},{8,12},{12,8},{16,20},{20,16},{24,28},{28,24},{1,5},{5... | collective-permute-start | bytes 99848 | tf_op jit(solution)/shard_map/ppermute | solution.py:18
  50.9 4.0 %collective-permute-start.8 = (f32[65,128]{1,0:T(8,128)S(1)}, f32[65,128]{1,0:T(8,128)S(1)}, u32[]{:S(2)}, u32[]{:S(2)}) collective-permute-start(f32[65,128]{1,0:T(8,128)S(1)} %fusion.31), channel_id=1, source_target_pairs={{0,8},{4,12},{8,0},{12,4},{16,24},{20,28},{24,16},{28,20},{1,9},{5... | collective-permute-start | bytes 99848 | tf_op jit(solution)/shard_map/ppermute | solution.py:18
  54.8 4.9 %collective-permute-start.9 = (f32[65,128]{1,0:T(8,128)S(1)}, f32[65,128]{1,0:T(8,128)S(1)}, u32[]{:S(2)}, u32[]{:S(2)}) collective-permute-start(f32[65,128]{1,0:T(8,128)S(1)} %add.178), channel_id=1, source_target_pairs={{0,16},{4,20},{8,24},{12,28},{16,0},{20,4},{24,8},{28,12},{1,17},{... | collective-permute-start | bytes 99848 | tf_op jit(solution)/shard_map/ppermute | solution.py:18
  63.0 9.1 %copy-start.3 = (f32[2,4096]{1,0:T(2,128)}, f32[2,4096]{1,0:T(2,128)S(1)}, u32[]{:S(2)}) copy-start(f32[2,4096]{1,0:T(2,128)S(1)} %get-tuple-element.21) | copy-start | bytes 98308
  63.7 1.2 %collective-permute-start.10 = (f32[1,128]{1,0:T(1,128)S(1)}, f32[1,128]{1,0:T(1,128)S(1)}, u32[]{:S(2)}, u32[]{:S(2)}) collective-permute-start(f32[1,128]{1,0:T(1,128)S(1)} %broadcast_in_dim.5), channel_id=1, source_target_pairs={{0,1},{1,0},{2,3},{3,2},{4,5},{5,4},{6,7},{7,6},{8,9},{9,8},{10,11... | collective-permute-start | bytes 1544 | tf_op jit(solution)/shard_map/ppermute | solution.py:18
  65.5 3.9 %collective-permute-start.11 = (f32[1,128]{1,0:T(1,128)S(1)}, f32[1,128]{1,0:T(1,128)S(1)}, u32[]{:S(2)}, u32[]{:S(2)}) collective-permute-start(f32[1,128]{1,0:T(1,128)S(1)} %broadcast_add_fusion), channel_id=1, source_target_pairs={{0,2},{1,3},{2,0},{3,1},{4,6},{5,7},{6,4},{7,5},{8,10},{9,11},{10,... | collective-permute-start | bytes 1544 | tf_op jit(solution)/shard_map/ppermute | solution.py:18

commit v19 on v15

--- a/solution.py
+++ b/solution.py
@@ -166,7 +166,7 @@
     new_att_res = att_res - step_len * q_att
     new_cal_res = cal_res - step_len * q_cal
     kept = res_sq - step_len * (2.0 * res_q - step_len * q_sq)
-    cal_next = jnp.broadcast_to(jnp.sum(new_cal_res * new_cal_res), (1, lane))
+    cal_next = jnp.sum(new_cal_res * new_cal_res, keepdims=True)
     norm_next = kept + doubling_sum(cal_next, "cal")[0, 0]
     ratio = norm_next / norm_now
     return (

time: 72.3 us -> 73.9 us (1.022)
  between operations: 9.69 us -> 11.7 us
  starting transfers between devices: 18.8 us -> 20.1 us
  other arithmetic: 13.1 us -> 11.8 us
    add x5 -> x3, other arithmetic: 1.32 us -> 0.02 us  [doubling_sum(): rows = rows + exchanged(rows, axis, distance)]
    ppermute x9, starting transfers between devices: 15.3 us -> 16.5 us  [exchanged(): return lax.ppermute(block, axis, [(i, i ^ distance) for i in devices])]
  transfers between devices with their start and end apart: 11 -> 11, of which waited for: 7 -> 8; matrix products, arithmetic and copies ran while one was open for 22% -> 21% of each run, Pallas kernels for 0% -> 0%
where the time goes in v19:
time: 73.9 us; the launch traced here: 73.4 us
  starting transfers between devices  20.1 us (27%)
  matrix products  14.7 us (20%)
  waiting for transfers between devices  12 us (16%)
  other arithmetic  11.8 us (16%)
  between operations  11.7 us (16%)
  local copies, waits for them, and re-layouts  3.28 us (4%)
    ppermute x9, starting transfers between devices, exchanged(): return lax.ppermute(block, axis, [(i, i ^ distance) for i in devices])  16.5 us
    ppermute x9, waiting for transfers between devices, exchanged(): return lax.ppermute(block, axis, [(i, i ^ distance) for i in devices])  12 us
    dot_general x1, matrix products, local(): lax.dot_general(cal_table, high_hot, (((0,), (0,)), ((), ())), precision=...  5.59 us
    dot_general x1, matrix products, local(): lax.dot_general(high_hot, cal_weighted, (((1,), (1,)), ((), ())), precisi...  4.49 us
    dot_general x1, other arithmetic, local(): lax.dot_general(high_hot, cal_weighted, (((1,), (1,)), ((), ())), precisi...  4.09 us
    ppermute x2, starting transfers between devices, passed_along(): return lax.ppermute(block, axis, route)  3.54 us
    dot_general x1, matrix products, local(): lax.dot_general(spread, knot_hot, (((1,), (1,)), ((), ())), precision=ONE...  2.43 us
    dot_general x1, matrix products, local(): jnp.dot(table, knot_hot, precision=ONE_HOT_PRECISION)  2.16 us
  transfers between devices with their start and end apart: 11, of which 8 were waited for; matrix products, arithmetic and copies ran while one was open for 21% of the time, Pallas kernels for 0%

profile of v19, /device:TPU:0, one launch (start us, length us, event | category | flops | bytes accessed | tf_op | source)
XLA Modules:
  0.0 73.4 jit_solution(9024351514324059355)
XLA Ops:
  0.7 3.0 %collective-permute-start.1 = (f32[1,2,4096]{2,1,0:T(2,128)}, f32[1,2,4096]{2,1,0:T(2,128)S(1)}, u32[]{:S(2)}, u32[]{:S(2)}) collective-permute-start(f32[1,2,4096]{2,1,0:T(2,128)} %bitcast.111), channel_id=1, source_target_pairs={{0,2},{1,3},{2,0},{3,1},{4,6},{5,7},{6,4},{7,5},{8,10},{9,11},{10,... | collective-permute-start | bytes 98312 | tf_op jit(solution)/shard_map/ppermute | solution.py:18
  3.7 1.3 %collective-permute-start = (f32[3,3]{1,0:T(4,128)}, f32[3,3]{1,0:T(4,128)S(1)}, u32[]{:S(2)}, u32[]{:S(2)}) collective-permute-start(f32[3,3]{1,0:T(4,128)} %bitcast.113), channel_id=1, source_target_pairs={{1,0},{2,1},{3,2},{4,3},{5,4},{6,5},{7,6},{8,7},{9,8},{10,9},{11,1... | collective-permute-start | bytes 116 | tf_op jit(solution)/shard_map/ppermute | solution.py:13
  5.0 0.7 constant_dynamic-update-slice_fusion.1
  5.7 1.4 %multiply_reduce_fusion.4 = f32[]{:T(128)} fusion(f32[2,4096]{1,0:T(2,128)} %param.26), kind=kLoop, calls=%fused_computation.82 | loop fusion | flops 16383 | bytes 32772 | tf_op jit(solution)/shard_map/reduce_sum | solution.py:153
  7.1 0.9 %add_select_fusion = (s32[16384]{0:T(1024)S(1)}, s32[16384]{0:T(1024)S(1)}) fusion(s32[128,128]{1,0:T(8,128)} %param.22, s32[128,128]{1,0:T(8,128)} %param.21), kind=kLoop, calls=%fused_computation.39 | loop fusion | flops 344064 | bytes 262144 | tf_op jit(solution)/shard_map/jit(remainder)/select_n | solution.py:129
  8.0 4.1 %iota_compare_fusion.14 = pred[256,16384]{1,0:T(32,128)(4,1)} fusion(s32[16384]{0:T(1024)S(1)} %get-tuple-element.38), kind=kLoop, calls=%fused_computation.1.clone.clone.2 | loop fusion | flops 4194304 | bytes 4259840 | tf_op jit(solution)/shard_map/dot_general | solution.py:151
  13.1 2.2 %fusion.3 = f32[12,16384]{1,0:T(8,128)S(1)} fusion(f32[12,128]{1,0:T(8,128)S(1)} %reshape.269, s32[16384]{0:T(1024)S(1)} %subtract_bitcast_fusion), kind=kOutput, calls=%fused_computation.6 | convolution fusion | flops 153092096 | bytes 858112 | tf_op jit(solution)/shard_map/dot_general | solution.py:122
  15.5 1.2 %collective-permute-start.2 = (f32[1,4,4096]{2,1,0:T(4,128)S(1)}, f32[1,4,4096]{2,1,0:T(4,128)S(1)}, u32[]{:S(2)}, u32[]{:S(2)}) collective-permute-start(f32[1,4,4096]{2,1,0:T(4,128)S(1)} %maximum_select_fusion.1), channel_id=1, source_target_pairs={{0,1},{1,0},{2,3},{3,2},{4,5},{5,4},{6,7},{7,6},{8,9},{9,8},{10,11... | collective-permute-start | bytes 196616 | tf_op jit(solution)/shard_map/ppermute | solution.py:18
  16.8 0.8 %collective-permute-done.2 = f32[1,4,4096]{2,1,0:T(4,128)S(1)} collective-permute-done((f32[1,4,4096]{2,1,0:T(4,128)S(1)}, f32[1,4,4096]{2,1,0:T(4,128)S(1)}, u32[]{:S(2)}, u32[]{:S(2)}) %collective-permute-start.2) | collective-permute-done | bytes 65568 | tf_op jit(solution)/shard_map/ppermute | solution.py:18
  17.9 5.6 %fusion.11 = f32[16384]{0:T(1024)S(1)} fusion(f32[256,128]{1,0:T(8,128)S(1)} %reshape_squeeze.3, s32[16384]{0:T(1024)S(1)} %get-tuple-element.38, s32[16384]{0:T(1024)S(1)} %get-tuple-element.37), kind=kOutput, calls=%fused_computation.15 | convolution fusion | flops 3231694848 | bytes 327680 | tf_op jit(solution)/shard_map/dot_general | solution.py:131
  24.1 0.6 copy.25
  24.7 2.4 %fusion.2 = f32[12,128]{1,0:T(8,128)S(1)} fusion(f32[12,16384]{1,0:T(8,128)S(1)} %bitcast.110, s32[16384]{0:T(1024)S(1)} %subtract_bitcast_fusion), kind=kOutput, calls=%fused_computation.5 | convolution fusion | flops 153092096 | bytes 858112 | tf_op jit(solution)/shard_map/dot_general | solution.py:142
  27.3 2.3 %collective-permute-start.3 = (f32[3,3]{1,0:T(4,128)S(1)}, f32[3,3]{1,0:T(4,128)S(1)}, u32[]{:S(2)}, u32[]{:S(2)}) collective-permute-start(f32[3,3]{1,0:T(4,128)S(1)} %slice.164), channel_id=1, source_target_pairs={{0,1},{1,2},{2,3},{3,4},{4,5},{5,6},{6,7},{7,8},{8,9},{9,10},{10,1... | collective-permute-start | bytes 116 | tf_op jit(solution)/shard_map/ppermute | solution.py:13
  29.6 0.6 multiply_reduce_fusion.2
  30.2 4.5 %fusion = f32[256,128]{1,0:T(8,128)S(1)} fusion(f32[16384]{0:T(1024)S(1)} %get-tuple-element.22, s32[16384]{0:T(1024)S(1)} %get-tuple-element.37, pred[256,16384]{1,0:T(32,128)(4,1)S(1)} %copy-done), kind=kOutput, calls=%fused_computation.2 | convolution fusion | flops 3225419776 | bytes 4456448 | tf_op jit(solution)/shard_map/dot_general | solution.py:151
  35.4 0.7 multiply_reduce_fusion.8
  40.0 0.7 concatenate.73
  40.7 0.9 %collective-permute-start.4 = (f32[129,128]{1,0:T(8,128)S(1)}, f32[129,128]{1,0:T(8,128)S(1)}, u32[]{:S(2)}, u32[]{:S(2)}) collective-permute-start(f32[129,128]{1,0:T(8,128)S(1)} %pad_maximum_fusion.3), channel_id=1, source_target_pairs={{0,1},{1,0},{2,3},{3,2},{4,5},{5,4},{6,7},{7,6},{8,9},{9,8},{10,11... | collective-permute-start | bytes 198152 | tf_op jit(solution)/shard_map/ppermute | solution.py:18
  41.6 0.9 %collective-permute-done.4 = f32[129,128]{1,0:T(8,128)S(1)} collective-permute-done((f32[129,128]{1,0:T(8,128)S(1)}, f32[129,128]{1,0:T(8,128)S(1)}, u32[]{:S(2)}, u32[]{:S(2)}) %collective-permute-start.4) | collective-permute-done | bytes 66080 | tf_op jit(solution)/shard_map/ppermute | solution.py:18
  42.5 2.0 %collective-permute-start.5 = (f32[65,128]{1,0:T(8,128)S(1)}, f32[65,128]{1,0:T(8,128)S(1)}, u32[]{:S(2)}, u32[]{:S(2)}) collective-permute-start(f32[65,128]{1,0:T(8,128)S(1)} %pad_maximum_fusion.4), channel_id=1, source_target_pairs={{0,2},{1,3},{2,0},{3,1},{4,6},{5,7},{6,4},{7,5},{8,10},{9,11},{10,... | collective-permute-start | bytes 99848 | tf_op jit(solution)/shard_map/ppermute | solution.py:18
  44.5 2.0 %collective-permute-done.5 = f32[65,128]{1,0:T(8,128)S(1)} collective-permute-done((f32[65,128]{1,0:T(8,128)S(1)}, f32[65,128]{1,0:T(8,128)S(1)}, u32[]{:S(2)}, u32[]{:S(2)}) %collective-permute-start.5) | collective-permute-done | bytes 33312 | tf_op jit(solution)/shard_map/ppermute | solution.py:18
  46.6 2.0 %collective-permute-start.6 = (f32[65,128]{1,0:T(8,128)S(1)}, f32[65,128]{1,0:T(8,128)S(1)}, u32[]{:S(2)}, u32[]{:S(2)}) collective-permute-start(f32[65,128]{1,0:T(8,128)S(1)} %pad_maximum_fusion.5), channel_id=1, source_target_pairs={{0,4},{4,0},{8,12},{12,8},{16,20},{20,16},{24,28},{28,24},{1,5},{5... | collective-permute-start | bytes 99848 | tf_op jit(solution)/shard_map/ppermute | solution.py:18
  48.5 2.1 %collective-permute-done.6 = f32[65,128]{1,0:T(8,128)S(1)} collective-permute-done((f32[65,128]{1,0:T(8,128)S(1)}, f32[65,128]{1,0:T(8,128)S(1)}, u32[]{:S(2)}, u32[]{:S(2)}) %collective-permute-start.6) | collective-permute-done | bytes 33312 | tf_op jit(solution)/shard_map/ppermute | solution.py:18
  50.6 1.6 %collective-permute-start.7 = (f32[65,128]{1,0:T(8,128)S(1)}, f32[65,128]{1,0:T(8,128)S(1)}, u32[]{:S(2)}, u32[]{:S(2)}) collective-permute-start(f32[65,128]{1,0:T(8,128)S(1)} %fusion.31), channel_id=1, source_target_pairs={{0,8},{4,12},{8,0},{12,4},{16,24},{20,28},{24,16},{28,20},{1,9},{5... | collective-permute-start | bytes 99848 | tf_op jit(solution)/shard_map/ppermute | solution.py:18
  52.2 2.4 %collective-permute-done.7 = f32[65,128]{1,0:T(8,128)S(1)} collective-permute-done((f32[65,128]{1,0:T(8,128)S(1)}, f32[65,128]{1,0:T(8,128)S(1)}, u32[]{:S(2)}, u32[]{:S(2)}) %collective-permute-start.7) | collective-permute-done | bytes 33312 | tf_op jit(solution)/shard_map/ppermute | solution.py:18
  54.6 2.6 %collective-permute-start.8 = (f32[65,128]{1,0:T(8,128)S(1)}, f32[65,128]{1,0:T(8,128)S(1)}, u32[]{:S(2)}, u32[]{:S(2)}) collective-permute-start(f32[65,128]{1,0:T(8,128)S(1)} %add.178), channel_id=1, source_target_pairs={{0,16},{4,20},{8,24},{12,28},{16,0},{20,4},{24,8},{28,12},{1,17},{... | collective-permute-start | bytes 99848 | tf_op jit(solution)/shard_map/ppermute | solution.py:18
  57.2 2.3 %collective-permute-done.8 = f32[65,128]{1,0:T(8,128)S(1)} collective-permute-done((f32[65,128]{1,0:T(8,128)S(1)}, f32[65,128]{1,0:T(8,128)S(1)}, u32[]{:S(2)}, u32[]{:S(2)}) %collective-permute-start.8) | collective-permute-done | bytes 33312 | tf_op jit(solution)/shard_map/ppermute | solution.py:18
  64.0 0.6 multiply_reduce_fusion.3
  64.7 1.2 %collective-permute-done.9 = f32[1,1]{1,0:T(1,128)} collective-permute-done((f32[1,1]{1,0:T(1,128)}, f32[1,1]{1,0:T(1,128)}, u32[]{:S(2)}, u32[]{:S(2)}) %collective-permute-start.9) | collective-permute-done | bytes 36 | tf_op jit(solution)/shard_map/ppermute | solution.py:18
  67.2 3.3 %collective-permute-start.10 = (f32[1,1]{1,0:T(1,128)}, f32[1,1]{1,0:T(1,128)}, u32[]{:S(2)}, u32[]{:S(2)}) collective-permute-start(f32[1,1]{1,0:T(1,128)} %add.181), channel_id=1, source_target_pairs={{0,2},{1,3},{2,0},{3,1},{4,6},{5,7},{6,4},{7,5},{8,10},{9,11},{10,... | collective-permute-start | bytes 20 | tf_op jit(solution)/shard_map/ppermute | solution.py:18
  72.1 0.7 multiply_add_fusion.3
  72.8 0.6 multiply_add_fusion.1
  (79 shorter events, 3.7 us)
Async XLA Ops:
  0.6 12.4 %copy-start.10 = (f32[3,128]{1,0:T(4,128)S(1)}, f32[3,128]{1,0:T(4,128)}, u32[]{:S(2)}) copy-start(f32[3,128]{1,0:T(4,128)} %param.28) | copy-start | bytes 4612
  0.6 11.5 %copy-start.11 = (f32[5,128]{1,0:T(8,128)S(1)}, f32[5,128]{1,0:T(8,128)}, u32[]{:S(2)}) copy-start(f32[5,128]{1,0:T(8,128)} %param.27) | copy-start | bytes 7684
  0.7 11.5 %copy-start.1 = (f32[5,128,128]{2,1,0:T(8,128)S(1)}, f32[5,128,128]{2,1,0:T(8,128)}, u32[]{:S(2)}) copy-start(f32[5,128,128]{2,1,0:T(8,128)} %param.15) | copy-start | bytes 983044
  0.7 11.6 %copy-start.6 = (s32[128,128]{1,0:T(8,128)S(1)}, s32[128,128]{1,0:T(8,128)}, u32[]{:S(2)}) copy-start(s32[128,128]{1,0:T(8,128)} %param.20) | copy-start | bytes 196612
  0.7 14.8 %collective-permute-start.1 = (f32[1,2,4096]{2,1,0:T(2,128)}, f32[1,2,4096]{2,1,0:T(2,128)S(1)}, u32[]{:S(2)}, u32[]{:S(2)}) collective-permute-start(f32[1,2,4096]{2,1,0:T(2,128)} %bitcast.111), channel_id=1, source_target_pairs={{0,2},{1,3},{2,0},{3,1},{4,6},{5,7},{6,4},{7,5},{8,10},{9,11},{10,... | collective-permute-start | bytes 98312 | tf_op jit(solution)/shard_map/ppermute | solution.py:18
  3.7 9.3 %collective-permute-start = (f32[3,3]{1,0:T(4,128)}, f32[3,3]{1,0:T(4,128)S(1)}, u32[]{:S(2)}, u32[]{:S(2)}) collective-permute-start(f32[3,3]{1,0:T(4,128)} %bitcast.113), channel_id=1, source_target_pairs={{1,0},{2,1},{3,2},{4,3},{5,4},{6,5},{7,6},{8,7},{9,8},{10,9},{11,1... | collective-permute-start | bytes 116 | tf_op jit(solution)/shard_map/ppermute | solution.py:13
  8.0 7.4 %copy-start.5 = (f32[2,4096]{1,0:T(2,128)S(1)}, f32[2,4096]{1,0:T(2,128)}, u32[]{:S(2)}) copy-start(f32[2,4096]{1,0:T(2,128)} %param.29) | copy-start | bytes 98308
  8.0 8.7 %copy-start.2 = (f32[3,128,128]{2,1,0:T(8,128)S(1)}, f32[3,128,128]{2,1,0:T(8,128)}, u32[]{:S(2)}) copy-start(f32[3,128,128]{2,1,0:T(8,128)} %param.16) | copy-start | bytes 589828
  15.5 2.1 %collective-permute-start.2 = (f32[1,4,4096]{2,1,0:T(4,128)S(1)}, f32[1,4,4096]{2,1,0:T(4,128)S(1)}, u32[]{:S(2)}, u32[]{:S(2)}) collective-permute-start(f32[1,4,4096]{2,1,0:T(4,128)S(1)} %maximum_select_fusion.1), channel_id=1, source_target_pairs={{0,1},{1,0},{2,3},{3,2},{4,5},{5,4},{6,7},{7,6},{8,9},{9,8},{10,11... | collective-permute-start | bytes 196616 | tf_op jit(solution)/shard_map/ppermute | solution.py:18
  17.9 5.6 %copy-start.7 = (f32[128,128]{1,0:T(8,128)S(1)}, f32[128,128]{1,0:T(8,128)}, u32[]{:S(2)}) copy-start(f32[128,128]{1,0:T(8,128)} %param.18) | copy-start | bytes 196612
  17.9 5.6 %copy-start.8 = (f32[128,128]{1,0:T(8,128)S(1)}, f32[128,128]{1,0:T(8,128)}, u32[]{:S(2)}) copy-start(f32[128,128]{1,0:T(8,128)} %param.19) | copy-start | bytes 196612
  17.9 5.6 %copy-start.9 = (f32[128,128]{1,0:T(8,128)S(1)}, f32[128,128]{1,0:T(8,128)}, u32[]{:S(2)}) copy-start(f32[128,128]{1,0:T(8,128)} %param.17) | copy-start | bytes 196612
  17.9 5.6 %copy-start.14 = (s32[128]{0:T(128)S(1)}, s32[128]{0:T(128)}, u32[]{:S(2)}) copy-start(s32[128]{0:T(128)} %param.23) | copy-start | bytes 1540
  23.9 6.3 %copy-start = (pred[256,16384]{1,0:T(32,128)(4,1)S(1)}, pred[256,16384]{1,0:T(32,128)(4,1)}, u32[]{:S(2)}) copy-start(pred[256,16384]{1,0:T(32,128)(4,1)} %iota_compare_fusion.14) | copy-start | bytes 12582916
  27.3 8.1 %collective-permute-start.3 = (f32[3,3]{1,0:T(4,128)S(1)}, f32[3,3]{1,0:T(4,128)S(1)}, u32[]{:S(2)}, u32[]{:S(2)}) collective-permute-start(f32[3,3]{1,0:T(4,128)S(1)} %slice.164), channel_id=1, source_target_pairs={{0,1},{1,2},{2,3},{3,4},{4,5},{5,6},{6,7},{7,8},{8,9},{9,10},{10,1... | collective-permute-start | bytes 116 | tf_op jit(solution)/shard_map/ppermute | solution.py:13
  30.2 4.5 %copy-start.12 = (f32[5,128]{1,0:T(8,128)S(1)}, f32[5,128]{1,0:T(8,128)}, u32[]{:S(2)}) copy-start(f32[5,128]{1,0:T(8,128)} %param.24) | copy-start | bytes 7684
  30.2 5.2 %copy-start.13 = (f32[3,128]{1,0:T(4,128)S(1)}, f32[3,128]{1,0:T(4,128)}, u32[]{:S(2)}) copy-start(f32[3,128]{1,0:T(4,128)} %param.25) | copy-start | bytes 4612
  30.2 33.8 %copy-start.4 = (f32[2,4096]{1,0:T(2,128)S(1)}, f32[2,4096]{1,0:T(2,128)}, u32[]{:S(2)}) copy-start(f32[2,4096]{1,0:T(2,128)} %param.26) | copy-start | bytes 98308
  40.7 1.8 %collective-permute-start.4 = (f32[129,128]{1,0:T(8,128)S(1)}, f32[129,128]{1,0:T(8,128)S(1)}, u32[]{:S(2)}, u32[]{:S(2)}) collective-permute-start(f32[129,128]{1,0:T(8,128)S(1)} %pad_maximum_fusion.3), channel_id=1, source_target_pairs={{0,1},{1,0},{2,3},{3,2},{4,5},{5,4},{6,7},{7,6},{8,9},{9,8},{10,11... | collective-permute-start | bytes 198152 | tf_op jit(solution)/shard_map/ppermute | solution.py:18
  42.5 4.0 %collective-permute-start.5 = (f32[65,128]{1,0:T(8,128)S(1)}, f32[65,128]{1,0:T(8,128)S(1)}, u32[]{:S(2)}, u32[]{:S(2)}) collective-permute-start(f32[65,128]{1,0:T(8,128)S(1)} %pad_maximum_fusion.4), channel_id=1, source_target_pairs={{0,2},{1,3},{2,0},{3,1},{4,6},{5,7},{6,4},{7,5},{8,10},{9,11},{10,... | collective-permute-start | bytes 99848 | tf_op jit(solution)/shard_map/ppermute | solution.py:18
  46.6 4.0 %collective-permute-start.6 = (f32[65,128]{1,0:T(8,128)S(1)}, f32[65,128]{1,0:T(8,128)S(1)}, u32[]{:S(2)}, u32[]{:S(2)}) collective-permute-start(f32[65,128]{1,0:T(8,128)S(1)} %pad_maximum_fusion.5), channel_id=1, source_target_pairs={{0,4},{4,0},{8,12},{12,8},{16,20},{20,16},{24,28},{28,24},{1,5},{5... | collective-permute-start | bytes 99848 | tf_op jit(solution)/shard_map/ppermute | solution.py:18
  50.6 4.0 %collective-permute-start.7 = (f32[65,128]{1,0:T(8,128)S(1)}, f32[65,128]{1,0:T(8,128)S(1)}, u32[]{:S(2)}, u32[]{:S(2)}) collective-permute-start(f32[65,128]{1,0:T(8,128)S(1)} %fusion.31), channel_id=1, source_target_pairs={{0,8},{4,12},{8,0},{12,4},{16,24},{20,28},{24,16},{28,20},{1,9},{5... | collective-permute-start | bytes 99848 | tf_op jit(solution)/shard_map/ppermute | solution.py:18
  54.6 4.9 %collective-permute-start.8 = (f32[65,128]{1,0:T(8,128)S(1)}, f32[65,128]{1,0:T(8,128)S(1)}, u32[]{:S(2)}, u32[]{:S(2)}) collective-permute-start(f32[65,128]{1,0:T(8,128)S(1)} %add.178), channel_id=1, source_target_pairs={{0,16},{4,20},{8,24},{12,28},{16,0},{20,4},{24,8},{28,12},{1,17},{... | collective-permute-start | bytes 99848 | tf_op jit(solution)/shard_map/ppermute | solution.py:18
  64.7 8.8 %copy-start.3 = (f32[2,4096]{1,0:T(2,128)}, f32[2,4096]{1,0:T(2,128)S(1)}, u32[]{:S(2)}) copy-start(f32[2,4096]{1,0:T(2,128)S(1)} %get-tuple-element.21) | copy-start | bytes 98308
  64.7 1.2 %collective-permute-start.9 = (f32[1,1]{1,0:T(1,128)}, f32[1,1]{1,0:T(1,128)}, u32[]{:S(2)}, u32[]{:S(2)}) collective-permute-start(f32[1,1]{1,0:T(1,128)} %bitcast.28), channel_id=1, source_target_pairs={{0,1},{1,0},{2,3},{3,2},{4,5},{5,4},{6,7},{7,6},{8,9},{9,8},{10,11... | collective-permute-start | bytes 20 | tf_op jit(solution)/shard_map/ppermute | solution.py:18
  67.2 3.6 %collective-permute-start.10 = (f32[1,1]{1,0:T(1,128)}, f32[1,1]{1,0:T(1,128)}, u32[]{:S(2)}, u32[]{:S(2)}) collective-permute-start(f32[1,1]{1,0:T(1,128)} %add.181), channel_id=1, source_target_pairs={{0,2},{1,3},{2,0},{3,1},{4,6},{5,7},{6,4},{7,5},{8,10},{9,11},{10,... | collective-permute-start | bytes 20 | tf_op jit(solution)/shard_map/ppermute | solution.py:18

commit v20 on v15

--- a/solution.py
+++ b/solution.py
@@ -156,7 +156,11 @@
     scalars = jnp.stack([res_sq, curv_local, res_q, q_sq, cal_sq])
     scalars = jnp.concatenate([scalars, jnp.zeros((lane - 5,), jnp.float32)]).reshape(1, lane)
     own_rows, scalars = halving_sum(cal_term, scalars, "cal")
-    summed = doubling_sum(jnp.concatenate([own_rows, scalars], axis=0), "tm")
+    summed = jnp.concatenate([own_rows, scalars], axis=0)
+    distance = lax.axis_size("tm") // 2
+    while distance >= 1:
+        summed = summed + exchanged(summed, "tm", distance)
+        distance //= 2
     res_sq, curvature, res_q, q_sq, cal_sq = (summed[-1, k] for k in range(5))
     q_cal = summed[:-1].reshape(blocks, col_width)
 

time: 72.3 us -> 72.3 us (level)
  no operation moved by 1% of the time
where the time goes in v20:
time: 72.3 us; the launch traced here: 71.8 us
  starting transfers between devices  18.9 us (26%)
  matrix products  14.7 us (20%)
  other arithmetic  13.1 us (18%)
  waiting for transfers between devices  11.5 us (16%)
  between operations  9.69 us (13%)
  local copies, waits for them, and re-layouts  3.94 us (5%)
    ppermute x9, starting transfers between devices, exchanged(): return lax.ppermute(block, axis, [(i, i ^ distance) for i in devices])  15.4 us
    ppermute x9, waiting for transfers between devices, exchanged(): return lax.ppermute(block, axis, [(i, i ^ distance) for i in devices])  11.5 us
    dot_general x1, matrix products, local(): lax.dot_general(cal_table, high_hot, (((0,), (0,)), ((), ())), precision=...  5.59 us
    dot_general x1, matrix products, local(): lax.dot_general(high_hot, cal_weighted, (((1,), (1,)), ((), ())), precisi...  4.49 us
    dot_general x1, other arithmetic, local(): lax.dot_general(high_hot, cal_weighted, (((1,), (1,)), ((), ())), precisi...  4.09 us
    ppermute x2, starting transfers between devices, passed_along(): return lax.ppermute(block, axis, route)  3.54 us
    dot_general x1, matrix products, local(): lax.dot_general(spread, knot_hot, (((1,), (1,)), ((), ())), precision=ONE...  2.43 us
    dot_general x1, matrix products, local(): jnp.dot(table, knot_hot, precision=ONE_HOT_PRECISION)  2.16 us
  transfers between devices with their start and end apart: 11, of which 7 were waited for; matrix products, arithmetic and copies ran while one was open for 22% of the time, Pallas kernels for 0%

profile of v20, /device:TPU:0, one launch (start us, length us, event | category | flops | bytes accessed | tf_op | source)
XLA Modules:
  0.0 71.8 jit_solution(5916317440740644385)
XLA Ops:
  0.7 3.0 %collective-permute-start.1 = (f32[1,2,4096]{2,1,0:T(2,128)}, f32[1,2,4096]{2,1,0:T(2,128)S(1)}, u32[]{:S(2)}, u32[]{:S(2)}) collective-permute-start(f32[1,2,4096]{2,1,0:T(2,128)} %bitcast.111), channel_id=1, source_target_pairs={{0,2},{1,3},{2,0},{3,1},{4,6},{5,7},{6,4},{7,5},{8,10},{9,11},{10,... | collective-permute-start | bytes 98312 | tf_op jit(solution)/shard_map/ppermute | solution.py:18
  3.7 1.3 %collective-permute-start = (f32[3,3]{1,0:T(4,128)}, f32[3,3]{1,0:T(4,128)S(1)}, u32[]{:S(2)}, u32[]{:S(2)}) collective-permute-start(f32[3,3]{1,0:T(4,128)} %bitcast.113), channel_id=1, source_target_pairs={{1,0},{2,1},{3,2},{4,3},{5,4},{6,5},{7,6},{8,7},{9,8},{10,9},{11,1... | collective-permute-start | bytes 116 | tf_op jit(solution)/shard_map/ppermute | solution.py:13
  5.0 0.7 constant_dynamic-update-slice_fusion.1
  5.7 1.4 %multiply_reduce_fusion.4 = f32[]{:T(128)} fusion(f32[2,4096]{1,0:T(2,128)} %param.26), kind=kLoop, calls=%fused_computation.82 | loop fusion | flops 16383 | bytes 32772 | tf_op jit(solution)/shard_map/reduce_sum | solution.py:153
  7.1 0.9 %add_select_fusion = (s32[16384]{0:T(1024)S(1)}, s32[16384]{0:T(1024)S(1)}) fusion(s32[128,128]{1,0:T(8,128)} %param.22, s32[128,128]{1,0:T(8,128)} %param.21), kind=kLoop, calls=%fused_computation.39 | loop fusion | flops 344064 | bytes 262144 | tf_op jit(solution)/shard_map/jit(remainder)/select_n | solution.py:129
  8.0 4.1 %iota_compare_fusion.14 = pred[256,16384]{1,0:T(32,128)(4,1)} fusion(s32[16384]{0:T(1024)S(1)} %get-tuple-element.38), kind=kLoop, calls=%fused_computation.1.clone.clone.2 | loop fusion | flops 4194304 | bytes 4259840 | tf_op jit(solution)/shard_map/dot_general | solution.py:151
  13.1 2.2 %fusion.3 = f32[12,16384]{1,0:T(8,128)S(1)} fusion(f32[12,128]{1,0:T(8,128)S(1)} %reshape.269, s32[16384]{0:T(1024)S(1)} %subtract_bitcast_fusion), kind=kOutput, calls=%fused_computation.6 | convolution fusion | flops 153092096 | bytes 858112 | tf_op jit(solution)/shard_map/dot_general | solution.py:122
  15.5 1.2 %collective-permute-start.2 = (f32[1,4,4096]{2,1,0:T(4,128)S(1)}, f32[1,4,4096]{2,1,0:T(4,128)S(1)}, u32[]{:S(2)}, u32[]{:S(2)}) collective-permute-start(f32[1,4,4096]{2,1,0:T(4,128)S(1)} %maximum_select_fusion.1), channel_id=1, source_target_pairs={{0,1},{1,0},{2,3},{3,2},{4,5},{5,4},{6,7},{7,6},{8,9},{9,8},{10,11... | collective-permute-start | bytes 196616 | tf_op jit(solution)/shard_map/ppermute | solution.py:18
  16.8 0.8 %collective-permute-done.2 = f32[1,4,4096]{2,1,0:T(4,128)S(1)} collective-permute-done((f32[1,4,4096]{2,1,0:T(4,128)S(1)}, f32[1,4,4096]{2,1,0:T(4,128)S(1)}, u32[]{:S(2)}, u32[]{:S(2)}) %collective-permute-start.2) | collective-permute-done | bytes 65568 | tf_op jit(solution)/shard_map/ppermute | solution.py:18
  17.9 5.6 %fusion.11 = f32[16384]{0:T(1024)S(1)} fusion(f32[256,128]{1,0:T(8,128)S(1)} %reshape_squeeze.3, s32[16384]{0:T(1024)S(1)} %get-tuple-element.38, s32[16384]{0:T(1024)S(1)} %get-tuple-element.37), kind=kOutput, calls=%fused_computation.15 | convolution fusion | flops 3231694848 | bytes 327680 | tf_op jit(solution)/shard_map/dot_general | solution.py:131
  24.7 2.4 %fusion.2 = f32[12,128]{1,0:T(8,128)S(1)} fusion(f32[12,16384]{1,0:T(8,128)S(1)} %bitcast.110, s32[16384]{0:T(1024)S(1)} %subtract_bitcast_fusion), kind=kOutput, calls=%fused_computation.5 | convolution fusion | flops 153092096 | bytes 858112 | tf_op jit(solution)/shard_map/dot_general | solution.py:142
  27.3 2.3 %collective-permute-start.3 = (f32[3,3]{1,0:T(4,128)S(1)}, f32[3,3]{1,0:T(4,128)S(1)}, u32[]{:S(2)}, u32[]{:S(2)}) collective-permute-start(f32[3,3]{1,0:T(4,128)S(1)} %slice.168), channel_id=1, source_target_pairs={{0,1},{1,2},{2,3},{3,4},{4,5},{5,6},{6,7},{7,8},{8,9},{9,10},{10,1... | collective-permute-start | bytes 116 | tf_op jit(solution)/shard_map/ppermute | solution.py:13
  30.2 4.5 %fusion = f32[256,128]{1,0:T(8,128)S(1)} fusion(f32[16384]{0:T(1024)S(1)} %get-tuple-element.22, s32[16384]{0:T(1024)S(1)} %get-tuple-element.37, pred[256,16384]{1,0:T(32,128)(4,1)S(1)} %copy-done), kind=kOutput, calls=%fused_computation.2 | convolution fusion | flops 3225419776 | bytes 4456448 | tf_op jit(solution)/shard_map/dot_general | solution.py:151
  35.4 0.7 multiply_reduce_fusion.8
  40.0 0.7 concatenate.73
  40.7 0.9 %collective-permute-start.4 = (f32[129,128]{1,0:T(8,128)S(1)}, f32[129,128]{1,0:T(8,128)S(1)}, u32[]{:S(2)}, u32[]{:S(2)}) collective-permute-start(f32[129,128]{1,0:T(8,128)S(1)} %pad_maximum_fusion.3), channel_id=1, source_target_pairs={{0,1},{1,0},{2,3},{3,2},{4,5},{5,4},{6,7},{7,6},{8,9},{9,8},{10,11... | collective-permute-start | bytes 198152 | tf_op jit(solution)/shard_map/ppermute | solution.py:18
  41.6 0.9 %collective-permute-done.4 = f32[129,128]{1,0:T(8,128)S(1)} collective-permute-done((f32[129,128]{1,0:T(8,128)S(1)}, f32[129,128]{1,0:T(8,128)S(1)}, u32[]{:S(2)}, u32[]{:S(2)}) %collective-permute-start.4) | collective-permute-done | bytes 66080 | tf_op jit(solution)/shard_map/ppermute | solution.py:18
  42.5 2.0 %collective-permute-start.5 = (f32[65,128]{1,0:T(8,128)S(1)}, f32[65,128]{1,0:T(8,128)S(1)}, u32[]{:S(2)}, u32[]{:S(2)}) collective-permute-start(f32[65,128]{1,0:T(8,128)S(1)} %pad_maximum_fusion.4), channel_id=1, source_target_pairs={{0,2},{1,3},{2,0},{3,1},{4,6},{5,7},{6,4},{7,5},{8,10},{9,11},{10,... | collective-permute-start | bytes 99848 | tf_op jit(solution)/shard_map/ppermute | solution.py:18
  44.5 2.0 %collective-permute-done.5 = f32[65,128]{1,0:T(8,128)S(1)} collective-permute-done((f32[65,128]{1,0:T(8,128)S(1)}, f32[65,128]{1,0:T(8,128)S(1)}, u32[]{:S(2)}, u32[]{:S(2)}) %collective-permute-start.5) | collective-permute-done | bytes 33312 | tf_op jit(solution)/shard_map/ppermute | solution.py:18
  46.6 2.7 %collective-permute-start.6 = (f32[65,128]{1,0:T(8,128)S(1)}, f32[65,128]{1,0:T(8,128)S(1)}, u32[]{:S(2)}, u32[]{:S(2)}) collective-permute-start(f32[65,128]{1,0:T(8,128)S(1)} %pad_maximum_fusion.5), channel_id=1, source_target_pairs={{0,16},{4,20},{8,24},{12,28},{16,0},{20,4},{24,8},{28,12},{1,17},{... | collective-permute-start | bytes 99848 | tf_op jit(solution)/shard_map/ppermute | solution.py:18
  49.2 2.3 %collective-permute-done.6 = f32[65,128]{1,0:T(8,128)S(1)} collective-permute-done((f32[65,128]{1,0:T(8,128)S(1)}, f32[65,128]{1,0:T(8,128)S(1)}, u32[]{:S(2)}, u32[]{:S(2)}) %collective-permute-start.6) | collective-permute-done | bytes 33312 | tf_op jit(solution)/shard_map/ppermute | solution.py:18
  51.5 1.6 %collective-permute-start.7 = (f32[65,128]{1,0:T(8,128)S(1)}, f32[65,128]{1,0:T(8,128)S(1)}, u32[]{:S(2)}, u32[]{:S(2)}) collective-permute-start(f32[65,128]{1,0:T(8,128)S(1)} %fusion.31), channel_id=1, source_target_pairs={{0,8},{4,12},{8,0},{12,4},{16,24},{20,28},{24,16},{28,20},{1,9},{5... | collective-permute-start | bytes 99848 | tf_op jit(solution)/shard_map/ppermute | solution.py:18
  53.1 2.4 %collective-permute-done.7 = f32[65,128]{1,0:T(8,128)S(1)} collective-permute-done((f32[65,128]{1,0:T(8,128)S(1)}, f32[65,128]{1,0:T(8,128)S(1)}, u32[]{:S(2)}, u32[]{:S(2)}) %collective-permute-start.7) | collective-permute-done | bytes 33312 | tf_op jit(solution)/shard_map/ppermute | solution.py:18
  55.5 2.1 %collective-permute-start.8 = (f32[65,128]{1,0:T(8,128)S(1)}, f32[65,128]{1,0:T(8,128)S(1)}, u32[]{:S(2)}, u32[]{:S(2)}) collective-permute-start(f32[65,128]{1,0:T(8,128)S(1)} %add.178), channel_id=1, source_target_pairs={{0,4},{4,0},{8,12},{12,8},{16,20},{20,16},{24,28},{28,24},{1,5},{5... | collective-permute-start | bytes 99848 | tf_op jit(solution)/shard_map/ppermute | solution.py:18
  57.6 1.9 %collective-permute-done.8 = f32[65,128]{1,0:T(8,128)S(1)} collective-permute-done((f32[65,128]{1,0:T(8,128)S(1)}, f32[65,128]{1,0:T(8,128)S(1)}, u32[]{:S(2)}, u32[]{:S(2)}) %collective-permute-start.8) | collective-permute-done | bytes 33312 | tf_op jit(solution)/shard_map/ppermute | solution.py:18
  62.2 0.6 multiply_reduce_fusion.3
  62.8 0.7 broadcast_in_dim.5
  63.5 1.1 %collective-permute-done.9 = f32[1,128]{1,0:T(1,128)S(1)} collective-permute-done((f32[1,128]{1,0:T(1,128)S(1)}, f32[1,128]{1,0:T(1,128)S(1)}, u32[]{:S(2)}, u32[]{:S(2)}) %collective-permute-start.9) | collective-permute-done | bytes 544 | tf_op jit(solution)/shard_map/ppermute | solution.py:18
  64.7 0.6 broadcast_add_fusion
  65.3 1.9 %collective-permute-start.10 = (f32[1,128]{1,0:T(1,128)S(1)}, f32[1,128]{1,0:T(1,128)S(1)}, u32[]{:S(2)}, u32[]{:S(2)}) collective-permute-start(f32[1,128]{1,0:T(1,128)S(1)} %broadcast_add_fusion), channel_id=1, source_target_pairs={{0,2},{1,3},{2,0},{3,1},{4,6},{5,7},{6,4},{7,5},{8,10},{9,11},{10,... | collective-permute-start | bytes 1544 | tf_op jit(solution)/shard_map/ppermute | solution.py:18
  69.2 0.7 fusion.39
  70.5 0.7 multiply_add_fusion.3
  (82 shorter events, 5.4 us)
Async XLA Ops:
  0.6 12.4 %copy-start.10 = (f32[3,128]{1,0:T(4,128)S(1)}, f32[3,128]{1,0:T(4,128)}, u32[]{:S(2)}) copy-start(f32[3,128]{1,0:T(4,128)} %param.28) | copy-start | bytes 4612
  0.6 11.5 %copy-start.11 = (f32[5,128]{1,0:T(8,128)S(1)}, f32[5,128]{1,0:T(8,128)}, u32[]{:S(2)}) copy-start(f32[5,128]{1,0:T(8,128)} %param.27) | copy-start | bytes 7684
  0.7 11.5 %copy-start.1 = (f32[5,128,128]{2,1,0:T(8,128)S(1)}, f32[5,128,128]{2,1,0:T(8,128)}, u32[]{:S(2)}) copy-start(f32[5,128,128]{2,1,0:T(8,128)} %param.15) | copy-start | bytes 983044
  0.7 11.6 %copy-start.6 = (s32[128,128]{1,0:T(8,128)S(1)}, s32[128,128]{1,0:T(8,128)}, u32[]{:S(2)}) copy-start(s32[128,128]{1,0:T(8,128)} %param.20) | copy-start | bytes 196612
  0.7 14.8 %collective-permute-start.1 = (f32[1,2,4096]{2,1,0:T(2,128)}, f32[1,2,4096]{2,1,0:T(2,128)S(1)}, u32[]{:S(2)}, u32[]{:S(2)}) collective-permute-start(f32[1,2,4096]{2,1,0:T(2,128)} %bitcast.111), channel_id=1, source_target_pairs={{0,2},{1,3},{2,0},{3,1},{4,6},{5,7},{6,4},{7,5},{8,10},{9,11},{10,... | collective-permute-start | bytes 98312 | tf_op jit(solution)/shard_map/ppermute | solution.py:18
  3.7 9.3 %collective-permute-start = (f32[3,3]{1,0:T(4,128)}, f32[3,3]{1,0:T(4,128)S(1)}, u32[]{:S(2)}, u32[]{:S(2)}) collective-permute-start(f32[3,3]{1,0:T(4,128)} %bitcast.113), channel_id=1, source_target_pairs={{1,0},{2,1},{3,2},{4,3},{5,4},{6,5},{7,6},{8,7},{9,8},{10,9},{11,1... | collective-permute-start | bytes 116 | tf_op jit(solution)/shard_map/ppermute | solution.py:13
  8.0 7.4 %copy-start.5 = (f32[2,4096]{1,0:T(2,128)S(1)}, f32[2,4096]{1,0:T(2,128)}, u32[]{:S(2)}) copy-start(f32[2,4096]{1,0:T(2,128)} %param.29) | copy-start | bytes 98308
  8.0 8.7 %copy-start.2 = (f32[3,128,128]{2,1,0:T(8,128)S(1)}, f32[3,128,128]{2,1,0:T(8,128)}, u32[]{:S(2)}) copy-start(f32[3,128,128]{2,1,0:T(8,128)} %param.16) | copy-start | bytes 589828
  15.5 2.1 %collective-permute-start.2 = (f32[1,4,4096]{2,1,0:T(4,128)S(1)}, f32[1,4,4096]{2,1,0:T(4,128)S(1)}, u32[]{:S(2)}, u32[]{:S(2)}) collective-permute-start(f32[1,4,4096]{2,1,0:T(4,128)S(1)} %maximum_select_fusion.1), channel_id=1, source_target_pairs={{0,1},{1,0},{2,3},{3,2},{4,5},{5,4},{6,7},{7,6},{8,9},{9,8},{10,11... | collective-permute-start | bytes 196616 | tf_op jit(solution)/shard_map/ppermute | solution.py:18
  17.9 5.6 %copy-start.7 = (f32[128,128]{1,0:T(8,128)S(1)}, f32[128,128]{1,0:T(8,128)}, u32[]{:S(2)}) copy-start(f32[128,128]{1,0:T(8,128)} %param.18) | copy-start | bytes 196612
  17.9 5.6 %copy-start.8 = (f32[128,128]{1,0:T(8,128)S(1)}, f32[128,128]{1,0:T(8,128)}, u32[]{:S(2)}) copy-start(f32[128,128]{1,0:T(8,128)} %param.19) | copy-start | bytes 196612
  17.9 5.6 %copy-start.9 = (f32[128,128]{1,0:T(8,128)S(1)}, f32[128,128]{1,0:T(8,128)}, u32[]{:S(2)}) copy-start(f32[128,128]{1,0:T(8,128)} %param.17) | copy-start | bytes 196612
  17.9 5.6 %copy-start.14 = (s32[128]{0:T(128)S(1)}, s32[128]{0:T(128)}, u32[]{:S(2)}) copy-start(s32[128]{0:T(128)} %param.23) | copy-start | bytes 1540
  23.9 6.3 %copy-start = (pred[256,16384]{1,0:T(32,128)(4,1)S(1)}, pred[256,16384]{1,0:T(32,128)(4,1)}, u32[]{:S(2)}) copy-start(pred[256,16384]{1,0:T(32,128)(4,1)} %iota_compare_fusion.14) | copy-start | bytes 12582916
  27.3 8.1 %collective-permute-start.3 = (f32[3,3]{1,0:T(4,128)S(1)}, f32[3,3]{1,0:T(4,128)S(1)}, u32[]{:S(2)}, u32[]{:S(2)}) collective-permute-start(f32[3,3]{1,0:T(4,128)S(1)} %slice.168), channel_id=1, source_target_pairs={{0,1},{1,2},{2,3},{3,4},{4,5},{5,6},{6,7},{7,8},{8,9},{9,10},{10,1... | collective-permute-start | bytes 116 | tf_op jit(solution)/shard_map/ppermute | solution.py:13
  30.2 4.5 %copy-start.12 = (f32[5,128]{1,0:T(8,128)S(1)}, f32[5,128]{1,0:T(8,128)}, u32[]{:S(2)}) copy-start(f32[5,128]{1,0:T(8,128)} %param.24) | copy-start | bytes 7684
  30.2 5.2 %copy-start.13 = (f32[3,128]{1,0:T(4,128)S(1)}, f32[3,128]{1,0:T(4,128)}, u32[]{:S(2)}) copy-start(f32[3,128]{1,0:T(4,128)} %param.25) | copy-start | bytes 4612
  30.2 32.0 %copy-start.4 = (f32[2,4096]{1,0:T(2,128)S(1)}, f32[2,4096]{1,0:T(2,128)}, u32[]{:S(2)}) copy-start(f32[2,4096]{1,0:T(2,128)} %param.26) | copy-start | bytes 98308
  40.7 1.8 %collective-permute-start.4 = (f32[129,128]{1,0:T(8,128)S(1)}, f32[129,128]{1,0:T(8,128)S(1)}, u32[]{:S(2)}, u32[]{:S(2)}) collective-permute-start(f32[129,128]{1,0:T(8,128)S(1)} %pad_maximum_fusion.3), channel_id=1, source_target_pairs={{0,1},{1,0},{2,3},{3,2},{4,5},{5,4},{6,7},{7,6},{8,9},{9,8},{10,11... | collective-permute-start | bytes 198152 | tf_op jit(solution)/shard_map/ppermute | solution.py:18
  42.5 4.0 %collective-permute-start.5 = (f32[65,128]{1,0:T(8,128)S(1)}, f32[65,128]{1,0:T(8,128)S(1)}, u32[]{:S(2)}, u32[]{:S(2)}) collective-permute-start(f32[65,128]{1,0:T(8,128)S(1)} %pad_maximum_fusion.4), channel_id=1, source_target_pairs={{0,2},{1,3},{2,0},{3,1},{4,6},{5,7},{6,4},{7,5},{8,10},{9,11},{10,... | collective-permute-start | bytes 99848 | tf_op jit(solution)/shard_map/ppermute | solution.py:18
  46.6 4.9 %collective-permute-start.6 = (f32[65,128]{1,0:T(8,128)S(1)}, f32[65,128]{1,0:T(8,128)S(1)}, u32[]{:S(2)}, u32[]{:S(2)}) collective-permute-start(f32[65,128]{1,0:T(8,128)S(1)} %pad_maximum_fusion.5), channel_id=1, source_target_pairs={{0,16},{4,20},{8,24},{12,28},{16,0},{20,4},{24,8},{28,12},{1,17},{... | collective-permute-start | bytes 99848 | tf_op jit(solution)/shard_map/ppermute | solution.py:18
  51.5 4.0 %collective-permute-start.7 = (f32[65,128]{1,0:T(8,128)S(1)}, f32[65,128]{1,0:T(8,128)S(1)}, u32[]{:S(2)}, u32[]{:S(2)}) collective-permute-start(f32[65,128]{1,0:T(8,128)S(1)} %fusion.31), channel_id=1, source_target_pairs={{0,8},{4,12},{8,0},{12,4},{16,24},{20,28},{24,16},{28,20},{1,9},{5... | collective-permute-start | bytes 99848 | tf_op jit(solution)/shard_map/ppermute | solution.py:18
  55.5 4.0 %collective-permute-start.8 = (f32[65,128]{1,0:T(8,128)S(1)}, f32[65,128]{1,0:T(8,128)S(1)}, u32[]{:S(2)}, u32[]{:S(2)}) collective-permute-start(f32[65,128]{1,0:T(8,128)S(1)} %add.178), channel_id=1, source_target_pairs={{0,4},{4,0},{8,12},{12,8},{16,20},{20,16},{24,28},{28,24},{1,5},{5... | collective-permute-start | bytes 99848 | tf_op jit(solution)/shard_map/ppermute | solution.py:18
  62.8 9.0 %copy-start.3 = (f32[2,4096]{1,0:T(2,128)}, f32[2,4096]{1,0:T(2,128)S(1)}, u32[]{:S(2)}) copy-start(f32[2,4096]{1,0:T(2,128)S(1)} %get-tuple-element.21) | copy-start | bytes 98308
  63.5 1.2 %collective-permute-start.9 = (f32[1,128]{1,0:T(1,128)S(1)}, f32[1,128]{1,0:T(1,128)S(1)}, u32[]{:S(2)}, u32[]{:S(2)}) collective-permute-start(f32[1,128]{1,0:T(1,128)S(1)} %broadcast_in_dim.5), channel_id=1, source_target_pairs={{0,1},{1,0},{2,3},{3,2},{4,5},{5,4},{6,7},{7,6},{8,9},{9,8},{10,11... | collective-permute-start | bytes 1544 | tf_op jit(solution)/shard_map/ppermute | solution.py:18
  65.3 3.9 %collective-permute-start.10 = (f32[1,128]{1,0:T(1,128)S(1)}, f32[1,128]{1,0:T(1,128)S(1)}, u32[]{:S(2)}, u32[]{:S(2)}) collective-permute-start(f32[1,128]{1,0:T(1,128)S(1)} %broadcast_add_fusion), channel_id=1, source_target_pairs={{0,2},{1,3},{2,0},{3,1},{4,6},{5,7},{6,4},{7,5},{8,10},{9,11},{10,... | collective-permute-start | bytes 1544 | tf_op jit(solution)/shard_map/ppermute | solution.py:18
